TPU v7x, 32 devices: a whole 2x2x4 slice. The times are simulated.
32 devices in a mesh: home: 4 (over z), pair: 8 (over y, x, core).
Axes of the slice: x: 2, y: 2, z: 4, core: 2. Of those that a mesh axis runs over, the one named last changes fastest.
Arguments:
- orbitals: bfloat16 [64, 32768], P('home'), may hold values from -4 to 4
- offsets: int32 [64, 3], P('home'), may hold values from 0 to 16
- sends: int32 [4, 4, 1], P('home'), may hold values from 0 to 15
- pair_home: int32 [4, 8, 4], P('home', 'pair'), may hold values from 0 to 15
- pair_visit: int32 [4, 8, 4], P('home', 'pair'), may hold values from 0 to 3
- pair_count: int32 [4, 8], P('home', 'pair'), may hold values from 1 to 4, as said below
Outputs:
- fields: float32 [64, 32768], P('home', 'pair')
Inputs may be any that keep to these rules, and one draw needn't show every extreme that they name: `pair_count`: slots from this number on hold no pair; some device holds 4 live pairs.
All inputs are finite; a program needn't handle non-finite values.
Results may differ from a plain program's by a relative error of at most 0.0003.
Values may be sent and summed in bfloat16 or wider, within the bound.
No kernel may reach another device: no remote copies, remote signals or barrier semaphores. Data moves between devices by JAX's collectives and lax.ppermute only.
A program may use at most 64 MiB of HBM per device.

v0:
```python
import functools

import jax
import jax.numpy as jnp
from jax import lax
from jax.experimental import pallas as pl
from jax.experimental.pallas import tpu as pltpu
from jax.sharding import PartitionSpec as P

B = 32
PLANE = B * B


PRECISE = lax.Precision.HIGHEST


def sine_table():
    grid = jnp.arange(B, dtype=jnp.float32) + 1.0
    return jnp.sqrt(2.0 / (B + 1.0)) * jnp.sin(jnp.pi * grid[:, None] * grid[None, :] / (B + 1.0))


def eigen_sum():
    grid = jnp.arange(B, dtype=jnp.float32) + 1.0
    single = 2.0 - 2.0 * jnp.cos(jnp.pi * grid / (B + 1.0))
    return single[:, None, None] + single[None, :, None] + single[None, None, :]


def split(values):
    high = values.astype(jnp.bfloat16)
    low = (values - high.astype(jnp.float32)).astype(jnp.bfloat16)
    return high, low


def split_outside(values):
    high = lax.reduce_precision(values, exponent_bits=8, mantissa_bits=7)
    return high.astype(jnp.bfloat16), (values - high).astype(jnp.bfloat16)


def dot3(left, right_high, right_low):
    high, low = split(left)
    out = jnp.dot(high, right_high, preferred_element_type=jnp.float32)
    out = out + jnp.dot(low, right_high, preferred_element_type=jnp.float32)
    return out + jnp.dot(high, right_low, preferred_element_type=jnp.float32)


def dot3_left(left_high, left_low, right):
    high, low = split(right)
    out = jnp.dot(left_high, high, preferred_element_type=jnp.float32)
    out = out + jnp.dot(left_low, high, preferred_element_type=jnp.float32)
    return out + jnp.dot(left_high, low, preferred_element_type=jnp.float32)


def exact_rows(matrix, values):
    first = values.astype(jnp.bfloat16)
    rest = values - first.astype(jnp.float32)
    second = rest.astype(jnp.bfloat16)
    third = (rest - second.astype(jnp.float32)).astype(jnp.bfloat16)
    out = jnp.dot(matrix, first, preferred_element_type=jnp.float32)
    out = out + jnp.dot(matrix, second, preferred_element_type=jnp.float32)
    return out + jnp.dot(matrix, third, preferred_element_type=jnp.float32)


def pair_kernel(
    delta_ref,
    live_ref,
    home_ref,
    part_ref,
    kron_high_ref,
    kron_low_ref,
    rows_high_ref,
    rows_low_ref,
    eigen_ref,
    to_home_ref,
    to_partner_ref,
    shifted_ref,
    work_ref,
):
    slots = home_ref.shape[0]
    lane = lax.broadcasted_iota(jnp.int32, (B, PLANE), 1)
    lane_b = lane // B
    lane_c = lane % B
    row = lax.broadcasted_iota(jnp.int32, (B, B), 0)
    col = lax.broadcasted_iota(jnp.int32, (B, B), 1)
    for slot in range(slots):
        d_a = delta_ref[slot, 0]
        d_b = delta_ref[slot, 1]
        d_c = delta_ref[slot, 2]
        pick = (col == row + d_a).astype(jnp.bfloat16)
        moved = jnp.dot(pick, part_ref[slot], preferred_element_type=jnp.float32)
        step = d_b * B + d_c
        moved = pltpu.roll(moved, (PLANE - step) % PLANE, 1)
        inside = (
            (lane_b + d_b >= 0) & (lane_b + d_b < B) & (lane_c + d_c >= 0) & (lane_c + d_c < B)
        )
        moved = jnp.where(inside, moved, 0.0)
        shifted_ref[slot] = moved
        work_ref[slot * B : (slot + 1) * B, :] = home_ref[slot].astype(jnp.float32) * moved

    kron_high = kron_high_ref[...]
    kron_low = kron_low_ref[...]
    rows_high = rows_high_ref[...]
    rows_low = rows_low_ref[...]
    coef = dot3_left(rows_high, rows_low, dot3(work_ref[...], kron_high, kron_low))
    eigen = eigen_ref[...]
    for slot in range(slots):
        work_ref[slot * B : (slot + 1) * B, :] = coef[slot * B : (slot + 1) * B, :] / eigen
    potential = dot3_left(rows_high, rows_low, dot3(work_ref[...], kron_high, kron_low))

    for slot in range(slots):
        d_a = delta_ref[slot, 0]
        d_b = delta_ref[slot, 1]
        d_c = delta_ref[slot, 2]
        live = live_ref[slot] > 0
        here = potential[slot * B : (slot + 1) * B, :]
        to_home_ref[slot] = jnp.where(live, here * shifted_ref[slot], 0.0)
        product = here * home_ref[slot].astype(jnp.float32)
        pick = (col == row - d_a).astype(jnp.bfloat16)
        moved = exact_rows(pick, product)
        step = d_b * B + d_c
        moved = pltpu.roll(moved, (PLANE + step) % PLANE, 1)
        inside = (
            (lane_b - d_b >= 0) & (lane_b - d_b < B) & (lane_c - d_c >= 0) & (lane_c - d_c < B)
        )
        to_partner_ref[slot] = jnp.where(live & inside, moved, 0.0)


def pair_fields(delta, live, home, part):
    slots = home.shape[0]
    table = sine_table()
    kron_high, kron_low = split_outside(jnp.kron(table, table))
    rows_high, rows_low = split_outside(jnp.kron(jnp.eye(slots, dtype=jnp.float32), table))
    eigen = eigen_sum().reshape(B, PLANE)
    smem = pl.BlockSpec(memory_space=pltpu.SMEM)
    vmem = pl.BlockSpec(memory_space=pltpu.VMEM)
    box = jax.ShapeDtypeStruct((slots, B, PLANE), jnp.float32)
    return pl.pallas_call(
        pair_kernel,
        out_shape=(box, box),
        in_specs=[smem, smem] + [vmem] * 7,
        out_specs=(vmem, vmem),
        scratch_shapes=[
            pltpu.VMEM((slots, B, PLANE), jnp.float32),
            pltpu.VMEM((slots * B, PLANE), jnp.float32),
        ],
    )(delta, live, home, part, kron_high, kron_low, rows_high, rows_low, eigen)


def per_device(orbitals, offsets, sends, pair_home, pair_visit, pair_count):
    home_count = orbitals.shape[0]
    cell_count = orbitals.shape[1]
    chosen = sends[0].reshape(-1)
    slot_total = chosen.shape[0]
    slots = pair_home.shape[2]
    extra = 128
    outgoing = jnp.concatenate(
        [
            orbitals[chosen],
            jnp.pad(offsets[chosen].astype(jnp.bfloat16), ((0, 0), (0, extra - 3))),
        ],
        axis=1,
    )
    arrived = lax.all_to_all(outgoing, "home", split_axis=0, concat_axis=0, tiled=True)
    visitors = arrived[:, :cell_count]
    visit_offsets = arrived[:, cell_count : cell_count + 3].astype(jnp.int32)

    home_slot = pair_home[0, 0]
    visit_slot = pair_visit[0, 0]
    live = (jnp.arange(slots, dtype=jnp.int32) < pair_count[0, 0]).astype(jnp.int32)
    home_orb = orbitals[home_slot].reshape(slots, B, PLANE)
    part_orb = visitors[visit_slot].reshape(slots, B, PLANE)
    delta = offsets[home_slot] - visit_offsets[visit_slot]
    to_home, to_partner = pair_fields(delta, live, home_orb, part_orb)

    fields = jnp.concatenate([to_home, to_partner], axis=0).reshape(2 * slots, cell_count)
    rows = jnp.arange(home_count + slot_total, dtype=jnp.int32)
    targets = jnp.concatenate([home_slot, home_count + visit_slot])
    picker = (targets[:, None] == rows[None, :]).astype(jnp.float32)
    totals = jnp.dot(picker.T, fields, precision=PRECISE)
    totals = lax.psum_scatter(totals, "pair", scatter_dimension=1, tiled=True)
    home_totals = totals[:home_count]
    visit_totals = totals[home_count:]
    chooser = (chosen[:, None] == jnp.arange(home_count, dtype=jnp.int32)[None, :]).astype(
        jnp.float32
    )
    returned = lax.all_to_all(visit_totals, "home", split_axis=0, concat_axis=0, tiled=True)
    return home_totals + jnp.dot(chooser.T, returned, precision=PRECISE)


def solution(mesh):
    in_specs = (
        P("home", None),
        P("home", None),
        P("home", None, None),
        P("home", "pair", None),
        P("home", "pair", None),
        P("home", "pair"),
    )
    out_specs = P("home", "pair")
    return jax.shard_map(
        per_device, mesh=mesh, in_specs=in_specs, out_specs=out_specs, check_vma=False
    )
```

profile of v0, /device:TPU:0, one launch (start us, length us, event | category | flops | bytes accessed | tf_op | source)
XLA Modules:
  0.0 134.1 jit_solution(10705510580115987698)
XLA Ops:
  6.5 0.8 copy.13
  7.4 0.7 fusion.12
  8.1 0.6 gather_fusion.2
  8.6 0.8 gather_fusion.1
  9.6 0.5 broadcast.259
  10.1 1.0 reduce
  11.1 1.0 reshape.297
  12.1 6.3 %all-to-all-start = ((bf16[4,2,16448]{2,1,0:T(2,128)(2,1)}), bf16[4,2,16448]{2,1,0:T(2,128)(2,1)S(1)}, u32[]{:S(2)}, u32[]{:S(2)}) async-start(bf16[4,2,16448]{2,1,0:T(2,128)(2,1)} %reshape.297), calls=%async_computation | async-start | bytes 528384 | tf_op jit(solution)/shard_map/all_to_all | solution.py:162
  18.4 0.8 gather_fusion.4
  19.2 0.6 gather_fusion
  20.0 8.0 %broadcast_multiply_fusion = f32[32,32,32,32]{3,2,1,0:T(8,128)} fusion(f32[32,32]{1,0:T(8,128)S(1)} %sine_multiply_fusion), kind=kLoop, calls=%fused_computation.6 | loop fusion | flops 1048576 | bytes 4198400 | tf_op jit(solution)/shard_map/jit(kron)/mul | solution.py:130
  28.0 13.7 %mul.170 = f32[1024,1024]{1,0:T(8,128)} reshape(f32[32,32,32,32]{3,2,1,0:T(8,128)} %broadcast_multiply_fusion) | data formatting | bytes 8388608 | tf_op jit(solution)/shard_map/jit(kron)/mul | solution.py:130
  41.8 0.2 mul.174
  42.0 0.6 fusion.4
  42.7 0.2 add.123
  42.9 0.2 add.124
  43.9 0.6 compare_convert_fusion.live_ref
  44.5 0.7 broadcast_add_fusion.eigen_ref
  45.2 5.1 %fusion = (bf16[1024,1024]{1,0:T(8,128)(2,1)}, bf16[1024,1024]{1,0:T(8,128)(2,1)}) fusion(f32[1024,1024]{1,0:T(8,128)} %mul.170), kind=kLoop, calls=%fused_computation.10 | loop fusion | flops 4194304 | bytes 8388608 | tf_op jit(solution)/shard_map/convert_element_type | solution.py:36
  50.3 1.0 reshape.298
  51.5 0.8 gather_fusion.5
  52.4 0.6 gather_fusion.3
  52.9 1.0 copy_bitcast_fusion.1
  53.9 0.6 sub.24.delta_ref
  54.5 6.6 %shard_map.64 = (f32[4,32,1024]{2,1,0:T(8,128)}, f32[4,32,1024]{2,1,0:T(8,128)}) custom-call(s32[4,3]{1,0:T(4,128)} %sub.24.delta_ref, s32[4]{0:T(128)} %compare_convert_fusion.live_ref, bf16[4,32,1024]{2,1,0:T(8,128)(2,1)} %get-tuple-element.16.home_ref, bf16[4,32,1024]{2,1,0:T(8,128)(2,1)} %get-tuple-element.15.part_ref, ...), custom_call_target="tpu_custom_call" | custom-call | tf_op jit(solution)/shard_map/pallas_call | solution.py:136
  61.1 1.3 maximum_bitcast_fusion
  62.4 0.6 copy.21
  63.0 3.1 %fusion.7 = f32[20,32768]{1,0:T(8,128)} fusion(f32[8,32768]{1,0:T(8,128)S(1)} %bitcast.40, s32[8]{0:T(128)S(1)} %pad_add_fusion), kind=kOutput, calls=%fused_computation.33 | convolution fusion | flops 62914720 | bytes 3670048 | tf_op jit(solution)/shard_map/dot_general | solution.py:178
  66.2 47.9 %reduce-scatter.2.cloned.1.call-done = f32[20,4096]{1,0:T(8,128)} async-done(((f32[20,32768]{1,0:T(8,128)}), f32[20,4096]{1,0:T(8,128)}) %reduce-scatter.2.cloned.1.call-update) | async-done | bytes 327696 | tf_op jit(solution)/shard_map/reduce_scatter | solution.py:179
  114.0 0.9 slice_bitcast_fusion
  115.0 10.1 %all_to_all.24 = f32[4,1,4096]{2,1,0:T(1,128)S(1)} all-to-all(f32[4,1,4096]{2,1,0:T(1,128)S(1)} %copy.16), channel_id=1, replica_groups=mesh['home'=4,'pair'=8] {'home'}, dimensions={0} | all-to-all | bytes 131072 | tf_op jit(solution)/shard_map/all_to_all | solution.py:185
  125.2 2.1 %convolution_add_fusion = f32[16,4096]{1,0:T(8,128)} fusion(f32[20,4096]{1,0:T(8,128)} %reduce-scatter.2.cloned.1.call-done, f32[4,1,4096]{2,1,0:T(1,128)S(1)} %all_to_all.24, s32[4]{0:T(128)S(1)} %bitcast.45), kind=kOutput, calls=%fused_computation.9 | convolution fusion | flops 3211328 | bytes 589840 | tf_op jit(solution)/shard_map/dot_general | solution.py:186
  (32 shorter events, 1.0 us)
Async XLA Ops:
  6.5 2.1 %copy-start = (bf16[16,32768]{1,0:T(8,128)(2,1)S(1)}, bf16[16,32768]{1,0:T(8,128)(2,1)}, u32[]{:S(2)}) copy-start(bf16[16,32768]{1,0:T(8,128)(2,1)} %param.6) | copy-start | bytes 3145732
  6.5 11.9 %copy-start.3 = (s32[1,1,4]{2,1,0:T(1,128)S(1)}, s32[1,1,4]{2,1,0:T(1,128)}, u32[]{:S(2)}) copy-start(s32[1,1,4]{2,1,0:T(1,128)} %param.9) | copy-start | bytes 52
  6.5 13.3 %copy-start.2 = (s32[1,1,4]{2,1,0:T(1,128)S(1)}, s32[1,1,4]{2,1,0:T(1,128)}, u32[]{:S(2)}) copy-start(s32[1,1,4]{2,1,0:T(1,128)} %param.10) | copy-start | bytes 52
  12.1 38.2 %all-to-all-start = ((bf16[4,2,16448]{2,1,0:T(2,128)(2,1)}), bf16[4,2,16448]{2,1,0:T(2,128)(2,1)S(1)}, u32[]{:S(2)}, u32[]{:S(2)}) async-start(bf16[4,2,16448]{2,1,0:T(2,128)(2,1)} %reshape.297), calls=%async_computation | async-start | bytes 528384 | tf_op jit(solution)/shard_map/all_to_all | solution.py:162
  18.4 95.6 %reduce-scatter.2.cloned.1.call-start = ((), (), s32[]{:S(2)}) async-start(), calls=%async_computation.3 | async-start | bytes 3538944 | tf_op jit(solution)/shard_map/reduce_scatter | solution.py:179
  63.0 62.2 %copy-start.1 = (s32[1,4,1]{1,2,0:T(1,128)S(1)}, s32[1,4,1]{1,2,0:T(1,128)}, u32[]{:S(2)}) copy-start(s32[1,4,1]{1,2,0:T(1,128)} %param.8) | copy-start | bytes 52
Sparse Core Ops, SparseCore 0:
  66.3 47.7 reduce-scatter.1
where the time goes:
time: 135 us; the launch traced here: 134 us
  waiting for transfers between devices  47.9 us (35%)
  local copies, waits for them, and re-layouts  24.6 us (18%)
  other arithmetic  19.1 us (14%)
  between operations  14.2 us (11%)
  blocking collectives  10.1 us (7%)
  Pallas kernels  6.61 us (5%)
  starting transfers between devices  6.32 us (5%)
  matrix products  5.23 us (4%)
    reduce_scatter x1, waiting for transfers between devices, per_device(): totals = lax.psum_scatter(totals, 'pair', scatter_dimension=1, tiled=True)  47.9 us
    mul x1, local copies, waits for them, and re-layouts, pair_fields(): kron_high, kron_low = split_outside(jnp.kron(table, table))  13.7 us
    all_to_all x1, blocking collectives, per_device(): lax.all_to_all(visit_totals, 'home', split_axis=0, concat_axis=0, tiled=T...  10.1 us
    mul x1, other arithmetic, pair_fields(): kron_high, kron_low = split_outside(jnp.kron(table, table))  7.99 us
    pallas_call x1, Pallas kernels, pair_fields(): pl.pallas_call(pair_kernel, out_shape=(box, box), in_specs=[smem, smem] +...  6.61 us
    all_to_all x1, starting transfers between devices, per_device(): lax.all_to_all(outgoing, 'home', split_axis=0, concat_axis=0, tiled=True)  6.32 us
    convert_element_type x2, other arithmetic, split_outside(): return (high.astype(jnp.bfloat16), (values - high).astype(jnp.bfloat16))  5.72 us
    unnamed x13, local copies, waits for them, and re-layouts  3.63 us
  transfers between devices with their start and end apart: 2, of which 1 were waited for; matrix products, arithmetic and copies ran while one was open for 23% of the time, Pallas kernels for 0%

commit v1 on v0

--- a/solution.py
+++ b/solution.py
@@ -2,6 +2,8 @@
 
 import jax
 import jax.numpy as jnp
+import ml_dtypes
+import numpy as np
 from jax import lax
 from jax.experimental import pallas as pl
 from jax.experimental.pallas import tpu as pltpu
@@ -23,6 +25,20 @@
     grid = jnp.arange(B, dtype=jnp.float32) + 1.0
     single = 2.0 - 2.0 * jnp.cos(jnp.pi * grid / (B + 1.0))
     return single[:, None, None] + single[None, :, None] + single[None, None, :]
+
+
+def host_tables(slots):
+    grid = np.arange(B, dtype=np.float32) + np.float32(1.0)
+    angle = np.float32(np.pi) * grid[:, None] * grid[None, :] / np.float32(B + 1.0)
+    table = (np.sqrt(np.float32(2.0 / (B + 1.0))) * np.sin(angle)).astype(np.float32)
+    tiled = np.tile(table, (1, B))
+    spread = np.repeat(table, B, axis=1)
+    rows = np.kron(np.eye(slots, dtype=np.float32), table).astype(np.float32)
+    rows_high = rows.astype(ml_dtypes.bfloat16)
+    rows_low = (rows - rows_high.astype(np.float32)).astype(ml_dtypes.bfloat16)
+    single = (np.float32(2.0) - np.float32(2.0) * np.cos(np.float32(np.pi) * grid / np.float32(B + 1.0))).astype(np.float32)
+    eigen = (single[:, None, None] + single[None, :, None] + single[None, None, :]).reshape(B, PLANE)
+    return tiled, spread, rows_high, rows_low, eigen.astype(np.float32)
 
 
 def split(values):
@@ -65,8 +81,8 @@
     live_ref,
     home_ref,
     part_ref,
-    kron_high_ref,
-    kron_low_ref,
+    tiled_ref,
+    spread_ref,
     rows_high_ref,
     rows_low_ref,
     eigen_ref,
@@ -74,8 +90,18 @@
     to_partner_ref,
     shifted_ref,
     work_ref,
+    kron_high_ref,
+    kron_low_ref,
 ):
     slots = home_ref.shape[0]
+    tiled = tiled_ref[...]
+    for block in range(B):
+        values = tiled * spread_ref[block : block + 1, :]
+        high = values.astype(jnp.bfloat16)
+        kron_high_ref[block * B : (block + 1) * B, :] = high
+        kron_low_ref[block * B : (block + 1) * B, :] = (
+            values - high.astype(jnp.float32)
+        ).astype(jnp.bfloat16)
     lane = lax.broadcasted_iota(jnp.int32, (B, PLANE), 1)
     lane_b = lane // B
     lane_c = lane % B
@@ -126,10 +152,7 @@
 
 def pair_fields(delta, live, home, part):
     slots = home.shape[0]
-    table = sine_table()
-    kron_high, kron_low = split_outside(jnp.kron(table, table))
-    rows_high, rows_low = split_outside(jnp.kron(jnp.eye(slots, dtype=jnp.float32), table))
-    eigen = eigen_sum().reshape(B, PLANE)
+    tiled, spread, rows_high, rows_low, eigen = host_tables(slots)
     smem = pl.BlockSpec(memory_space=pltpu.SMEM)
     vmem = pl.BlockSpec(memory_space=pltpu.VMEM)
     box = jax.ShapeDtypeStruct((slots, B, PLANE), jnp.float32)
@@ -141,8 +164,10 @@
         scratch_shapes=[
             pltpu.VMEM((slots, B, PLANE), jnp.float32),
             pltpu.VMEM((slots * B, PLANE), jnp.float32),
+            pltpu.VMEM((PLANE, PLANE), jnp.bfloat16),
+            pltpu.VMEM((PLANE, PLANE), jnp.bfloat16),
         ],
-    )(delta, live, home, part, kron_high, kron_low, rows_high, rows_low, eigen)
+    )(delta, live, home, part, tiled, spread, rows_high, rows_low, eigen)
 
 
 def per_device(orbitals, offsets, sends, pair_home, pair_visit, pair_count):

time: 135 us -> 108 us (0.80)
  other arithmetic: 19.1 us -> 4.4 us
  local copies, waits for them, and re-layouts: 24.6 us -> 10.1 us
  waiting for transfers between devices: 47.9 us -> 51.7 us
    mul x2 -> x0, local copies, waits for them, and re-layouts: 13.8 us -> none  [the longest x1 13.7 us: pair_fields(): kron_high, kron_low = split_outside(jnp.kron(table, table))]
    mul x3 -> x0, other arithmetic: 8.24 us -> none  [the longest x1 7.99 us: pair_fields(): kron_high, kron_low = split_outside(jnp.kron(table, table))]
    all_to_all x1, waiting for transfers between devices: 0.01 us -> 6.25 us  [per_device(): lax.all_to_all(outgoing, 'home', split_axis=0, concat_axis=0, tiled=True)]
    convert_element_type x3 -> x0, other arithmetic: 5.73 us -> none  [the longest x2 5.72 us: split_outside(): return (high.astype(jnp.bfloat16), (values - high).astype(jnp.bfloat16))]
    reduce_scatter x1, waiting for transfers between devices: 47.9 us -> 45.5 us  [per_device(): totals = lax.psum_scatter(totals, 'pair', scatter_dimension=1, tiled=True)]
  transfers between devices with their start and end apart: 2 -> 2, of which waited for: 1 -> 2; matrix products, arithmetic and copies ran while one was open for 23% -> 2% of each run, Pallas kernels for 0% -> 0%
where the time goes in v1:
time: 108 us
  waiting for transfers between devices  51.7 us (48%)
  between operations  14.2 us (13%)
  blocking collectives  10.2 us (9%)
  local copies, waits for them, and re-layouts  10.1 us (9%)
  starting transfers between devices  6.32 us (6%)
  Pallas kernels  5.58 us (5%)
  matrix products  5.24 us (5%)
  other arithmetic  4.4 us (4%)
    reduce_scatter x1, waiting for transfers between devices, per_device(): totals = lax.psum_scatter(totals, 'pair', scatter_dimension=1, tiled=True)  45.5 us
    all_to_all x1, blocking collectives, per_device(): lax.all_to_all(visit_totals, 'home', split_axis=0, concat_axis=0, tiled=T...  10.2 us
    all_to_all x1, starting transfers between devices, per_device(): lax.all_to_all(outgoing, 'home', split_axis=0, concat_axis=0, tiled=True)  6.32 us
    all_to_all x1, waiting for transfers between devices, per_device(): lax.all_to_all(outgoing, 'home', split_axis=0, concat_axis=0, tiled=True)  6.25 us
    pallas_call x1, Pallas kernels, pair_fields(): pl.pallas_call(pair_kernel, out_shape=(box, box), in_specs=[smem, smem] +...  5.58 us
    unnamed x13, local copies, waits for them, and re-layouts  3.54 us
    dot_general x1, matrix products, per_device(): totals = jnp.dot(picker.T, fields, precision=PRECISE)  3.16 us
  transfers between devices with their start and end apart: 2, of which 2 were waited for; matrix products, arithmetic and copies ran while one was open for 2% of the time, Pallas kernels for 0%

profile of v1, /device:TPU:0, one launch (start us, length us, event | category | flops | bytes accessed | tf_op | source)
XLA Modules:
  0.0 107.7 jit_solution(10130718842117039801)
XLA Ops:
  6.5 0.7 fusion.9
  7.3 0.8 copy.18
  8.1 0.6 gather_fusion.2
  8.6 0.0 copy-start.3
  8.6 0.8 gather_fusion.1
  9.4 0.1 fusion.2
  9.6 0.5 broadcast.91
  10.1 1.0 reduce
  11.1 1.0 reshape.152
  12.1 6.3 %all-to-all-start = ((bf16[4,2,16448]{2,1,0:T(2,128)(2,1)}), bf16[4,2,16448]{2,1,0:T(2,128)(2,1)S(1)}, u32[]{:S(2)}, u32[]{:S(2)}) async-start(bf16[4,2,16448]{2,1,0:T(2,128)(2,1)} %reshape.152), calls=%async_computation | async-start | bytes 528384 | tf_op jit(solution)/shard_map/all_to_all | solution.py:187
  18.4 0.6 gather_fusion
  19.0 0.8 gather_fusion.4
  20.4 0.6 compare_convert_fusion.live_ref
  21.0 0.1 pad_add_fusion
  21.1 6.2 %all-to-all-done = bf16[4,2,16448]{2,1,0:T(2,128)(2,1)S(1)} async-done(((bf16[4,2,16448]{2,1,0:T(2,128)(2,1)}), bf16[4,2,16448]{2,1,0:T(2,128)(2,1)S(1)}, u32[]{:S(2)}, u32[]{:S(2)}) %all-to-all-start) | async-done | bytes 263200 | tf_op jit(solution)/shard_map/all_to_all | solution.py:187
  27.4 1.0 reshape.153
  28.4 0.1 copy.34
  28.5 0.1 slice.29
  28.6 0.8 gather_fusion.5
  29.4 0.6 gather_fusion.3
  30.0 0.6 sub.3.delta_ref
  30.6 0.9 copy_bitcast_fusion.1
  31.5 5.6 %shard_map.109 = (f32[4,32,1024]{2,1,0:T(8,128)}, f32[4,32,1024]{2,1,0:T(8,128)}) custom-call(s32[4,3]{1,0:T(4,128)} %sub.3.delta_ref, s32[4]{0:T(128)} %compare_convert_fusion.live_ref, bf16[4,32,1024]{2,1,0:T(8,128)(2,1)} %get-tuple-element.10.home_ref, bf16[4,32,1024]{2,1,0:T(8,128)(2,1)} %get-tuple-element.9.part_ref, ...), custom_call_target="tpu_custom_call" | custom-call | tf_op jit(solution)/shard_map/pallas_call | solution.py:159
  37.1 1.3 %maximum_bitcast_fusion = f32[1,8,32,1024]{3,2,1,0:T(8,128)S(1)} fusion(f32[4,32,1024]{2,1,0:T(8,128)} %get-tuple-element.8, f32[4,32,1024]{2,1,0:T(8,128)} %get-tuple-element.7), kind=kLoop, calls=%fused_computation.7 | loop fusion | flops 262144 | bytes 2097152
  38.4 0.6 copy.26
  39.0 3.2 %fusion.5 = f32[20,32768]{1,0:T(8,128)} fusion(f32[8,32768]{1,0:T(8,128)S(1)} %bitcast.38, s32[8]{0:T(128)S(1)} %pad_add_fusion), kind=kOutput, calls=%fused_computation.22 | convolution fusion | flops 62914720 | bytes 3670048 | tf_op jit(solution)/shard_map/dot_general | solution.py:203
  42.2 0.0 reduce-scatter.2.cloned.1.call-update
  42.2 45.5 %reduce-scatter.2.cloned.1.call-done = f32[20,4096]{1,0:T(8,128)} async-done(((f32[20,32768]{1,0:T(8,128)}), f32[20,4096]{1,0:T(8,128)}) %reduce-scatter.2.cloned.1.call-update) | async-done | bytes 327696 | tf_op jit(solution)/shard_map/reduce_scatter | solution.py:204
  87.7 0.9 slice_bitcast_fusion
  88.6 0.1 copy.21
  88.7 10.2 %all_to_all.24 = f32[4,1,4096]{2,1,0:T(1,128)S(1)} all-to-all(f32[4,1,4096]{2,1,0:T(1,128)S(1)} %copy.21), channel_id=1, replica_groups=mesh['home'=4,'pair'=8] {'home'}, dimensions={0} | all-to-all | bytes 131072 | tf_op jit(solution)/shard_map/all_to_all | solution.py:210
  98.8 2.1 %convolution_add_fusion = f32[16,4096]{1,0:T(8,128)} fusion(f32[20,4096]{1,0:T(8,128)} %reduce-scatter.2.cloned.1.call-done, f32[4,1,4096]{2,1,0:T(1,128)S(1)} %all_to_all.24, s32[4]{0:T(128)S(1)} %bitcast.43), kind=kOutput, calls=%fused_computation.6 | convolution fusion | flops 3211328 | bytes 589840 | tf_op jit(solution)/shard_map/dot_general | solution.py:211
  (16 shorter events, 0.1 us)
Async XLA Ops:
  6.5 2.1 %copy-start = (bf16[16,32768]{1,0:T(8,128)(2,1)S(1)}, bf16[16,32768]{1,0:T(8,128)(2,1)}, u32[]{:S(2)}) copy-start(bf16[16,32768]{1,0:T(8,128)(2,1)} %param.11) | copy-start | bytes 3145732
  6.5 11.9 %copy-start.2 = (s32[1,1,4]{2,1,0:T(1,128)S(1)}, s32[1,1,4]{2,1,0:T(1,128)}, u32[]{:S(2)}) copy-start(s32[1,1,4]{2,1,0:T(1,128)} %param.14) | copy-start | bytes 52
  8.6 12.4 %copy-start.3 = (s32[1,1,4]{2,1,0:T(1,128)S(1)}, s32[1,1,4]{2,1,0:T(1,128)}, u32[]{:S(2)}) copy-start(s32[1,1,4]{2,1,0:T(1,128)} %param.15) | copy-start | bytes 52
  12.1 15.3 %all-to-all-start = ((bf16[4,2,16448]{2,1,0:T(2,128)(2,1)}), bf16[4,2,16448]{2,1,0:T(2,128)(2,1)S(1)}, u32[]{:S(2)}, u32[]{:S(2)}) async-start(bf16[4,2,16448]{2,1,0:T(2,128)(2,1)} %reshape.152), calls=%async_computation | async-start | bytes 528384 | tf_op jit(solution)/shard_map/all_to_all | solution.py:187
  18.4 69.3 %reduce-scatter.2.cloned.1.call-start = ((), (), s32[]{:S(2)}) async-start(), calls=%async_computation.3 | async-start | bytes 3538944 | tf_op jit(solution)/shard_map/reduce_scatter | solution.py:204
  39.0 59.8 %copy-start.1 = (s32[1,4,1]{1,2,0:T(1,128)S(1)}, s32[1,4,1]{1,2,0:T(1,128)}, u32[]{:S(2)}) copy-start(s32[1,4,1]{1,2,0:T(1,128)} %param.13) | copy-start | bytes 52
Sparse Core Ops, SparseCore 0:
  42.3 45.2 reduce-scatter.1

commit v2 on v1

--- a/solution.py
+++ b/solution.py
@@ -196,12 +196,19 @@
     delta = offsets[home_slot] - visit_offsets[visit_slot]
     to_home, to_partner = pair_fields(delta, live, home_orb, part_orb)
 
-    fields = jnp.concatenate([to_home, to_partner], axis=0).reshape(2 * slots, cell_count)
-    rows = jnp.arange(home_count + slot_total, dtype=jnp.int32)
-    targets = jnp.concatenate([home_slot, home_count + visit_slot])
-    picker = (targets[:, None] == rows[None, :]).astype(jnp.float32)
-    totals = jnp.dot(picker.T, fields, precision=PRECISE)
-    totals = lax.psum_scatter(totals, "pair", scatter_dimension=1, tiled=True)
+    rows_out = 2 * slots
+    fields = jnp.concatenate([to_home, to_partner], axis=0).reshape(rows_out, cell_count)
+    pair_total = lax.psum(1, "pair")
+    chunk = cell_count // pair_total
+    targets = jnp.concatenate([home_slot, home_count + visit_slot]).astype(jnp.float32)
+    body = fields.reshape(rows_out, pair_total, chunk).transpose(1, 0, 2)
+    tags = jnp.broadcast_to(targets[None, :, None], (pair_total, rows_out, extra))
+    payload = jnp.concatenate([body, tags], axis=2)
+    got = lax.all_to_all(payload, "pair", split_axis=0, concat_axis=0, tiled=True)
+    got_ids = got[:, :, chunk].astype(jnp.int32)
+    all_rows = jnp.arange(home_count + slot_total, dtype=jnp.int32)
+    picker = (got_ids[:, :, None] == all_rows[None, None, :]).astype(jnp.float32)
+    totals = jnp.einsum("srk,srl->kl", picker, got[:, :, :chunk], precision=PRECISE)
     home_totals = totals[:home_count]
     visit_totals = totals[home_count:]
     chooser = (chosen[:, None] == jnp.arange(home_count, dtype=jnp.int32)[None, :]).astype(

time: 108 us -> 63.5 us (0.59)
  waiting for transfers between devices: 51.7 us -> 6.24 us
  blocking collectives: 10.2 us -> 27.5 us
  between operations: 14.2 us -> 0.83 us
  matrix products: 5.24 us -> 2.18 us
    reduce_scatter x1 -> x0, waiting for transfers between devices: 45.5 us -> none  [per_device(): totals = lax.psum_scatter(totals, 'pair', scatter_dimension=1, tiled=True)]
    all_to_all x0 -> x1, blocking collectives: none -> 19.2 us  [per_device(): lax.all_to_all(payload, 'pair', split_axis=0, concat_axis=0, tiled=True)]
    dot_general x1, matrix products: 3.16 us -> 1.04 us  [per_device(): jnp.einsum('srk,srl->kl', picker, got[:, :, :chunk], precision=PRECISE)]
    all_to_all x1, blocking collectives: 10.2 us -> 8.23 us  [per_device(): lax.all_to_all(visit_totals, 'home', split_axis=0, concat_axis=0, tiled=T...]
    unnamed x1 -> x0, other arithmetic: 1.27 us -> none
    concatenate x1 -> x2, other arithmetic: 0.08 us -> 1.34 us  [the longest x1 1.27 us: per_device(): jnp.concatenate([to_home, to_partner], axis=0).reshape(rows_out, cell_count)]
    another operation x0 -> x2, local copies, waits for them, and re-layouts: none -> 1.09 us  [per_device(): body = fields.reshape(rows_out, pair_total, chunk).transpose(1, 0, 2)]
  transfers between devices with their start and end apart: 2 -> 1, of which waited for: 2 -> 1; matrix products, arithmetic and copies ran while one was open for 2% -> 3% of each run, Pallas kernels for 0% -> 0%
where the time goes in v2:
time: 63.5 us; the launch traced here: 63.1 us
  blocking collectives  27.5 us (43%)
  local copies, waits for them, and re-layouts  10 us (16%)
  starting transfers between devices  6.32 us (10%)
  waiting for transfers between devices  6.24 us (10%)
  Pallas kernels  5.58 us (9%)
  other arithmetic  4.48 us (7%)
  matrix products  2.18 us (3%)
  between operations  0.83 us (1%)
    all_to_all x1, blocking collectives, per_device(): lax.all_to_all(payload, 'pair', split_axis=0, concat_axis=0, tiled=True)  19.2 us
    all_to_all x1, blocking collectives, per_device(): lax.all_to_all(visit_totals, 'home', split_axis=0, concat_axis=0, tiled=T...  8.23 us
    all_to_all x1, starting transfers between devices, per_device(): lax.all_to_all(outgoing, 'home', split_axis=0, concat_axis=0, tiled=True)  6.32 us
    all_to_all x1, waiting for transfers between devices, per_device(): lax.all_to_all(outgoing, 'home', split_axis=0, concat_axis=0, tiled=True)  6.24 us
    pallas_call x1, Pallas kernels, pair_fields(): pl.pallas_call(pair_kernel, out_shape=(box, box), in_specs=[smem, smem] +...  5.58 us
    unnamed x13, local copies, waits for them, and re-layouts  3.05 us
  transfers between devices with their start and end apart: 1, of which 1 were waited for; matrix products, arithmetic and copies ran while one was open for 3% of the time, Pallas kernels for 0%

profile of v2, /device:TPU:0, one launch (start us, length us, event | category | flops | bytes accessed | tf_op | source)
XLA Modules:
  0.0 63.1 jit_solution(5175556678823877731)
XLA Ops:
  0.0 0.7 %fusion.9 = s32[4]{0:T(128)S(1)} fusion(s32[1,4,1]{1,2,0:T(1,128)} %param.13), kind=kLoop, calls=%fused_computation.36 | loop fusion | flops 12 | bytes 32 | tf_op jit(solution)/shard_map/select_n | solution.py:182
  0.8 0.8 %copy.24 = s32[16,3]{1,0:T(8,128)S(1)} copy(s32[16,3]{0,1:T(4,128)} %param.12) | data formatting | bytes 384 | tf_op args[1]
  1.5 0.6 gather_fusion.2
  2.1 0.8 %gather_fusion.1 = bf16[4,32768]{1,0:T(4,128)(2,1)S(1)} fusion(bf16[16,32768]{1,0:T(8,128)(2,1)S(1)} %copy-done, s32[1024]{0:T(1024)S(1)} %pad_clamp_fusion.1), kind=kCustom, calls=%fused_computation.1 | custom fusion | bytes 524304 | tf_op jit(solution)/shard_map/gather | solution.py:182
  2.9 0.1 fusion.3
  3.0 0.5 broadcast.92
  3.6 1.0 %reduce = bf16[4,32896]{1,0:T(4,128)(2,1)S(1)} reduce(bf16[4,1,32896]{2,0,1:T(4,128)(2,1)S(1)} %fusion.3, bf16[]{:T(256)} %broadcast.92), dimensions={1}, to_apply=%copy.26.reduce_sub_computation | reduce | bytes 526338 | tf_op jit(solution)/shard_map/all_to_all | solution.py:187
  4.5 1.0 %reshape.164 = bf16[4,2,16448]{2,1,0:T(2,128)(2,1)} reshape(bf16[4,32896]{1,0:T(4,128)(2,1)S(1)} %reduce) | data formatting | bytes 526336
  5.5 6.3 %all-to-all-start = ((bf16[4,2,16448]{2,1,0:T(2,128)(2,1)}), bf16[4,2,16448]{2,1,0:T(2,128)(2,1)S(1)}, u32[]{:S(2)}, u32[]{:S(2)}) async-start(bf16[4,2,16448]{2,1,0:T(2,128)(2,1)} %reshape.164), calls=%async_computation | async-start | bytes 528384 | tf_op jit(solution)/shard_map/all_to_all | solution.py:187
  11.9 0.6 gather_fusion
  12.5 0.8 %gather_fusion.4 = bf16[4,32768]{1,0:T(4,128)(2,1)S(1)} fusion(bf16[16,32768]{1,0:T(8,128)(2,1)S(1)} %copy-done, s32[1024]{0:T(1024)S(1)} %pad_clamp_fusion.2), kind=kCustom, calls=%fused_computation.4 | custom fusion | bytes 524304 | tf_op jit(solution)/shard_map/gather | solution.py:194
  13.9 0.6 compare_convert_fusion.live_ref
  14.5 0.1 add_convert_fusion
  14.6 6.2 %all-to-all-done = bf16[4,2,16448]{2,1,0:T(2,128)(2,1)S(1)} async-done(((bf16[4,2,16448]{2,1,0:T(2,128)(2,1)}), bf16[4,2,16448]{2,1,0:T(2,128)(2,1)S(1)}, u32[]{:S(2)}, u32[]{:S(2)}) %all-to-all-start) | async-done | bytes 263200 | tf_op jit(solution)/shard_map/all_to_all | solution.py:187
  20.8 1.0 %reshape.165 = bf16[4,1,32896]{2,1,0:T(2,128)(2,1)S(1)} reshape(bf16[4,2,16448]{2,1,0:T(2,128)(2,1)S(1)} %all-to-all-done) | data formatting | bytes 526336
  21.8 0.1 copy.49
  22.0 0.1 slice.37
  22.1 0.8 %gather_fusion.5 = bf16[4,32768]{1,0:T(4,128)(2,1)S(1)} fusion(bf16[4,32768]{1,0:T(4,128)(2,1)S(1)} %slice.37, s32[1024]{0:T(1024)S(1)} %pad_clamp_fusion), kind=kCustom, calls=%fused_computation.5 | custom fusion | bytes 524304 | tf_op jit(solution)/shard_map/gather | solution.py:195
  22.9 0.6 gather_fusion.3
  23.5 0.6 sub.3.delta_ref
  24.1 0.9 %copy_bitcast_fusion.2 = (bf16[4,32,1024]{2,1,0:T(8,128)(2,1)}, bf16[4,32,1024]{2,1,0:T(8,128)(2,1)}) fusion(bf16[1,4,32,1024]{3,1,2,0:T(4,128)(2,1)S(1)} %bitcast.45, bf16[1,4,32,1024]{3,1,2,0:T(4,128)(2,1)S(1)} %bitcast.44), kind=kLoop, calls=%fused_computation.17 | loop fusion | bytes 1048576 | tf_op jit(solution)/shard_map/reshape | solution.py:195
  25.0 5.6 %shard_map.109 = (f32[4,32,1024]{2,1,0:T(8,128)}, f32[4,32,1024]{2,1,0:T(8,128)}) custom-call(s32[4,3]{1,0:T(4,128)} %sub.3.delta_ref, s32[4]{0:T(128)} %compare_convert_fusion.live_ref, bf16[4,32,1024]{2,1,0:T(8,128)(2,1)} %get-tuple-element.10.home_ref, bf16[4,32,1024]{2,1,0:T(8,128)(2,1)} %get-tuple-element.9.part_ref, ...), custom_call_target="tpu_custom_call" | custom-call | tf_op jit(solution)/shard_map/pallas_call | solution.py:159
  30.6 1.3 %pad_maximum_fusion.1 = f32[8,32,1024]{2,1,0:T(8,128)S(1)} fusion(f32[4,32,1024]{2,1,0:T(8,128)} %get-tuple-element.8, f32[4,32,1024]{2,1,0:T(8,128)} %get-tuple-element.7), kind=kLoop, calls=%fused_computation.9 | loop fusion | flops 262144 | bytes 2097152 | tf_op jit(solution)/shard_map/concatenate | solution.py:200
  31.8 0.5 reshape_reshape.3
  32.3 0.6 copy.48
  33.0 0.1 pad_maximum_fusion
  33.1 19.2 %all_to_all.29 = f32[8,8,4224]{2,1,0:T(8,128)S(1)} all-to-all(f32[8,8,4224]{2,1,0:T(8,128)S(1)} %pad_maximum_fusion), channel_id=1, replica_groups=mesh['home'=4,'pair'=8] {'pair'}, dimensions={0} | all-to-all | bytes 2162688 | tf_op jit(solution)/shard_map/all_to_all | solution.py:207
  52.3 0.1 copy.34
  52.5 0.1 copy.29
  52.6 1.0 %convolution_bitcast_fusion = f32[20,4096]{1,0:T(8,128)S(1)} fusion(f32[8,8,4096]{2,1,0:T(8,128)S(1)} %slice.39, s32[8,8]{0,1:T(8,128)S(1)} %copy.29), kind=kOutput, calls=%fused_computation.6 | convolution fusion | flops 62915840 | bytes 1376512 | tf_op jit(solution)/shard_map/srk,srl->kl/dot_general | solution.py:211
  53.8 8.2 %all_to_all.30 = f32[4,1,4096]{2,1,0:T(1,128)S(1)} all-to-all(f32[4,1,4096]{2,1,0:T(1,128)S(1)} %copy.31), channel_id=1, replica_groups=mesh['home'=4,'pair'=8] {'home'}, dimensions={0} | all-to-all | bytes 131072 | tf_op jit(solution)/shard_map/all_to_all | solution.py:217
  62.0 1.1 %convolution_add_fusion = f32[16,4096]{1,0:T(8,128)} fusion(f32[20,4096]{1,0:T(8,128)S(1)} %convolution_bitcast_fusion, f32[4,1,4096]{2,1,0:T(1,128)S(1)} %all_to_all.30, s32[4]{0:T(128)S(1)} %bitcast.46), kind=kOutput, calls=%fused_computation.7 | convolution fusion | flops 3211328 | bytes 589840 | tf_op jit(solution)/shard_map/dot_general | solution.py:218
  (22 shorter events, 0.3 us)
Async XLA Ops:
  0.0 2.1 %copy-start = (bf16[16,32768]{1,0:T(8,128)(2,1)S(1)}, bf16[16,32768]{1,0:T(8,128)(2,1)}, u32[]{:S(2)}) copy-start(bf16[16,32768]{1,0:T(8,128)(2,1)} %param.11) | copy-start | bytes 3145732
  2.9 9.0 %copy-start.2 = (s32[1,1,4]{2,1,0:T(1,128)S(1)}, s32[1,1,4]{2,1,0:T(1,128)}, u32[]{:S(2)}) copy-start(s32[1,1,4]{2,1,0:T(1,128)} %param.14) | copy-start | bytes 52
  5.5 15.3 %all-to-all-start = ((bf16[4,2,16448]{2,1,0:T(2,128)(2,1)}), bf16[4,2,16448]{2,1,0:T(2,128)(2,1)S(1)}, u32[]{:S(2)}, u32[]{:S(2)}) async-start(bf16[4,2,16448]{2,1,0:T(2,128)(2,1)} %reshape.164), calls=%async_computation | async-start | bytes 528384 | tf_op jit(solution)/shard_map/all_to_all | solution.py:187
  12.4 2.0 %copy-start.3 = (s32[1,1,4]{2,1,0:T(1,128)S(1)}, s32[1,1,4]{2,1,0:T(1,128)}, u32[]{:S(2)}) copy-start(s32[1,1,4]{2,1,0:T(1,128)} %param.15) | copy-start | bytes 52
  52.6 9.4 %copy-start.1 = (s32[1,4,1]{1,2,0:T(1,128)S(1)}, s32[1,4,1]{1,2,0:T(1,128)}, u32[]{:S(2)}) copy-start(s32[1,4,1]{1,2,0:T(1,128)} %param.13) | copy-start | bytes 52

commit v3 on v2

--- a/solution.py
+++ b/solution.py
@@ -170,26 +170,42 @@
     )(delta, live, home, part, tiled, spread, rows_high, rows_low, eigen)
 
 
+def exchange(blocks, axis):
+    count = blocks.shape[0]
+    received = [blocks[0]]
+    for step in range(1, count):
+        pairs = [(source, (source + step) % count) for source in range(count)]
+        received.append(lax.ppermute(blocks[step], axis, pairs))
+    return jnp.stack(received)
+
+
 def per_device(orbitals, offsets, sends, pair_home, pair_visit, pair_count):
     home_count = orbitals.shape[0]
     cell_count = orbitals.shape[1]
-    chosen = sends[0].reshape(-1)
-    slot_total = chosen.shape[0]
+    section_total = sends.shape[1]
+    per_target = sends.shape[2]
+    slot_total = section_total * per_target
     slots = pair_home.shape[2]
     extra = 128
+    me = lax.axis_index("home")
+    ahead = (me + jnp.arange(section_total, dtype=jnp.int32)) % section_total
+    chosen = sends[0][ahead]
+    flat_chosen = chosen.reshape(-1)
     outgoing = jnp.concatenate(
         [
-            orbitals[chosen],
-            jnp.pad(offsets[chosen].astype(jnp.bfloat16), ((0, 0), (0, extra - 3))),
+            orbitals[flat_chosen],
+            jnp.pad(offsets[flat_chosen].astype(jnp.bfloat16), ((0, 0), (0, extra - 3))),
         ],
         axis=1,
-    )
-    arrived = lax.all_to_all(outgoing, "home", split_axis=0, concat_axis=0, tiled=True)
+    ).reshape(section_total, per_target, cell_count + extra)
+    arrived = exchange(outgoing, "home").reshape(slot_total, cell_count + extra)
     visitors = arrived[:, :cell_count]
     visit_offsets = arrived[:, cell_count : cell_count + 3].astype(jnp.int32)
 
     home_slot = pair_home[0, 0]
-    visit_slot = pair_visit[0, 0]
+    visit_code = pair_visit[0, 0]
+    source = visit_code // per_target
+    visit_slot = ((me - source) % section_total) * per_target + visit_code % per_target
     live = (jnp.arange(slots, dtype=jnp.int32) < pair_count[0, 0]).astype(jnp.int32)
     home_orb = orbitals[home_slot].reshape(slots, B, PLANE)
     part_orb = visitors[visit_slot].reshape(slots, B, PLANE)
@@ -200,21 +216,26 @@
     fields = jnp.concatenate([to_home, to_partner], axis=0).reshape(rows_out, cell_count)
     pair_total = lax.psum(1, "pair")
     chunk = cell_count // pair_total
+    pair_me = lax.axis_index("pair")
     targets = jnp.concatenate([home_slot, home_count + visit_slot]).astype(jnp.float32)
     body = fields.reshape(rows_out, pair_total, chunk).transpose(1, 0, 2)
+    body = body[(pair_me + jnp.arange(pair_total, dtype=jnp.int32)) % pair_total]
     tags = jnp.broadcast_to(targets[None, :, None], (pair_total, rows_out, extra))
     payload = jnp.concatenate([body, tags], axis=2)
-    got = lax.all_to_all(payload, "pair", split_axis=0, concat_axis=0, tiled=True)
+    got = exchange(payload, "pair")
     got_ids = got[:, :, chunk].astype(jnp.int32)
     all_rows = jnp.arange(home_count + slot_total, dtype=jnp.int32)
     picker = (got_ids[:, :, None] == all_rows[None, None, :]).astype(jnp.float32)
     totals = jnp.einsum("srk,srl->kl", picker, got[:, :, :chunk], precision=PRECISE)
     home_totals = totals[:home_count]
-    visit_totals = totals[home_count:]
-    chooser = (chosen[:, None] == jnp.arange(home_count, dtype=jnp.int32)[None, :]).astype(
+    back = (-jnp.arange(section_total, dtype=jnp.int32)) % section_total
+    back_rows = (back[:, None] * per_target + jnp.arange(per_target)[None, :]).reshape(-1)
+    visit_totals = totals[home_count:][back_rows].reshape(section_total, per_target, chunk)
+    returned = exchange(visit_totals, "home").reshape(slot_total, chunk)
+    owners = chosen[back].reshape(-1)
+    chooser = (owners[:, None] == jnp.arange(home_count, dtype=jnp.int32)[None, :]).astype(
         jnp.float32
     )
-    returned = lax.all_to_all(visit_totals, "home", split_axis=0, concat_axis=0, tiled=True)
     return home_totals + jnp.dot(chooser.T, returned, precision=PRECISE)
 
 

time: 63.5 us -> 58.1 us (0.915)
  blocking collectives: 27.5 us -> 0 us
  starting transfers between devices: 6.32 us -> 21.4 us
  waiting for transfers between devices: 6.24 us -> 11.9 us
  local copies, waits for them, and re-layouts: 10 us -> 11.6 us
    all_to_all x2 -> x0, blocking collectives: 27.5 us -> none  [the longest x1 19.2 us: per_device(): lax.all_to_all(payload, 'pair', split_axis=0, concat_axis=0, tiled=True)]
    ppermute x0 -> x13, starting transfers between devices: none -> 21.4 us  [exchange(): received.append(lax.ppermute(blocks[step], axis, pairs))]
    ppermute x0 -> x13, waiting for transfers between devices: none -> 11.9 us  [exchange(): received.append(lax.ppermute(blocks[step], axis, pairs))]
    all_to_all x1 -> x0, starting transfers between devices: 6.32 us -> none  [per_device(): lax.all_to_all(outgoing, 'home', split_axis=0, concat_axis=0, tiled=True)]
    all_to_all x1 -> x0, waiting for transfers between devices: 6.24 us -> none  [per_device(): lax.all_to_all(outgoing, 'home', split_axis=0, concat_axis=0, tiled=True)]
    gather x2 -> x6, local copies, waits for them, and re-layouts: 1.35 us -> 4.57 us  [the longest x1 1.38 us: per_device(): chosen = sends[0][ahead]]
    all_to_all x2 -> x0, other arithmetic: 1.09 us -> none  [per_device(): lax.all_to_all(outgoing, 'home', split_axis=0, concat_axis=0, tiled=True)]
    reshape x1 -> x0, local copies, waits for them, and re-layouts: 0.94 us -> none  [per_device(): part_orb = visitors[visit_slot].reshape(slots, B, PLANE)]
  transfers between devices with their start and end apart: 1 -> 13, of which waited for: 1 -> 7; matrix products, arithmetic and copies ran while one was open for 3% -> 6% of each run, Pallas kernels for 0% -> 0%
where the time goes in v3:
time: 58.1 us; the launch traced here: 57.8 us
  starting transfers between devices  21.4 us (37%)
  waiting for transfers between devices  11.9 us (20%)
  local copies, waits for them, and re-layouts  11.6 us (20%)
  Pallas kernels  5.57 us (10%)
  other arithmetic  4.17 us (7%)
  matrix products  2.18 us (4%)
  between operations  0.94 us (2%)
    ppermute x13, starting transfers between devices, exchange(): received.append(lax.ppermute(blocks[step], axis, pairs))  21.4 us
    ppermute x13, waiting for transfers between devices, exchange(): received.append(lax.ppermute(blocks[step], axis, pairs))  11.9 us
    pallas_call x1, Pallas kernels, pair_fields(): pl.pallas_call(pair_kernel, out_shape=(box, box), in_specs=[smem, smem] +...  5.57 us
    unnamed x16, local copies, waits for them, and re-layouts  2.52 us
    gather x1, local copies, waits for them, and re-layouts, per_device(): chosen = sends[0][ahead]  1.38 us
    concatenate x1, other arithmetic, per_device(): jnp.concatenate([to_home, to_partner], axis=0).reshape(rows_out, cell_count)  1.27 us
  transfers between devices with their start and end apart: 13, of which 7 were waited for; matrix products, arithmetic and copies ran while one was open for 6% of the time, Pallas kernels for 0%

profile of v3, /device:TPU:0, one launch (start us, length us, event | category | flops | bytes accessed | tf_op | source)
XLA Modules:
  0.0 57.8 jit_solution(10842915966125084316)
XLA Ops:
  0.0 1.4 %gather_fusion.1 = s32[4]{0:T(128)S(1)} fusion(s32[4]{0:T(128)} %bitcast.82, s32[1024]{0:T(1024)S(1)} %pad_clamp_fusion.4), kind=kCustom, calls=%fused_computation.1 | custom fusion | bytes 48 | tf_op jit(solution)/shard_map/gather | solution.py:192
  1.4 0.7 %fusion.29 = s32[4]{0:T(128)S(1)} fusion(s32[1,1,4]{2,1,0:T(1,128)} %param.14), kind=kLoop, calls=%fused_computation.105 | loop fusion | flops 12 | bytes 32 | tf_op jit(solution)/shard_map/select_n | solution.py:212
  2.1 0.8 %copy.48 = s32[16,3]{1,0:T(8,128)S(1)} copy(s32[16,3]{0,1:T(4,128)} %param.12) | data formatting | bytes 384 | tf_op args[1]
  3.4 0.8 %gather_fusion.2 = bf16[4,32768]{1,0:T(4,128)(2,1)S(1)} fusion(bf16[16,32768]{1,0:T(8,128)(2,1)S(1)} %copy-done, s32[1024]{0:T(1024)S(1)} %get-tuple-element.27), kind=kCustom, calls=%fused_computation.2 | custom fusion | bytes 524304 | tf_op jit(solution)/shard_map/gather | solution.py:196
  4.7 3.1 %collective-permute-start = (bf16[1,32896]{1,0:T(2,128)(2,1)S(1)}, bf16[1,32896]{1,0:T(2,128)(2,1)S(1)}, u32[]{:S(2)}, u32[]{:S(2)}) collective-permute-start(bf16[1,32896]{1,0:T(2,128)(2,1)S(1)} %get-tuple-element.20), channel_id=1, source_target_pairs={{0,8},{8,16},{16,24},{24,0},{1,9},{9,17},{17,25},{25,1},{2,10},{10... | collective-permute-start | bytes 197384 | tf_op jit(solution)/shard_map/ppermute | solution.py:178
  7.8 2.6 %collective-permute-start.1 = (bf16[1,32896]{1,0:T(2,128)(2,1)S(1)}, bf16[1,32896]{1,0:T(2,128)(2,1)S(1)}, u32[]{:S(2)}, u32[]{:S(2)}) collective-permute-start(bf16[1,32896]{1,0:T(2,128)(2,1)S(1)} %get-tuple-element.19), channel_id=1, source_target_pairs={{0,16},{8,24},{16,0},{24,8},{1,17},{9,25},{17,1},{25,9},{2,18},{10... | collective-permute-start | bytes 197384 | tf_op jit(solution)/shard_map/ppermute | solution.py:178
  10.4 1.3 %collective-permute-start.2 = (bf16[1,32896]{1,0:T(2,128)(2,1)S(1)}, bf16[1,32896]{1,0:T(2,128)(2,1)S(1)}, u32[]{:S(2)}, u32[]{:S(2)}) collective-permute-start(bf16[1,32896]{1,0:T(2,128)(2,1)S(1)} %get-tuple-element.18), channel_id=1, source_target_pairs={{0,24},{8,0},{16,8},{24,16},{1,25},{9,1},{17,9},{25,17},{2,26},{10... | collective-permute-start | bytes 197384 | tf_op jit(solution)/shard_map/ppermute | solution.py:178
  12.3 0.8 %gather_fusion.5 = bf16[4,32768]{1,0:T(4,128)(2,1)S(1)} fusion(bf16[16,32768]{1,0:T(8,128)(2,1)S(1)} %copy-done, s32[1024]{0:T(1024)S(1)} %get-tuple-element.28), kind=kCustom, calls=%fused_computation.5 | custom fusion | bytes 524304 | tf_op jit(solution)/shard_map/gather | solution.py:210
  13.2 0.8 %copy.70 = bf16[1,4,32,1024]{3,2,1,0:T(8,128)(2,1)} copy(bf16[1,4,32,1024]{3,1,2,0:T(4,128)(2,1)S(1)} %bitcast.86) | data formatting | bytes 524288
  15.3 3.8 %collective-permute-done.1 = bf16[1,32896]{1,0:T(2,128)(2,1)S(1)} collective-permute-done((bf16[1,32896]{1,0:T(2,128)(2,1)S(1)}, bf16[1,32896]{1,0:T(2,128)(2,1)S(1)}, u32[]{:S(2)}, u32[]{:S(2)}) %collective-permute-start.1) | collective-permute-done | bytes 65824 | tf_op jit(solution)/shard_map/ppermute | solution.py:178
  19.1 0.6 %maximum_bitcast_fusion = bf16[4,32896]{1,0:T(4,128)(2,1)S(1)} fusion(bf16[1,1,32896]{2,0,1:T(2,128)(2,1)S(1)} %bitcast.90, bf16[1,1,32896]{2,0,1:T(2,128)(2,1)S(1)} %bitcast.89, bf16[1,1,32896]{2,0,1:T(2,128)(2,1)S(1)} %bitcast.88, bf16[1,1,32896]{2,0,1:T(2,128)(2,1)S(1)} %get-tuple-element.17), kind=kLoop, calls=%fused_computation.32 | loop fusion | flops 1052672 | bytes 526336 | tf_op jit(solution)/shard_map/reshape | solution.py:201
  20.4 0.8 %gather_fusion.6 = bf16[4,32768]{1,0:T(4,128)(2,1)S(1)} fusion(bf16[4,32768]{1,0:T(4,128)(2,1)S(1)} %slice.127, s32[1024]{0:T(1024)S(1)} %get-tuple-element.26), kind=kCustom, calls=%fused_computation.6 | custom fusion | bytes 524304 | tf_op jit(solution)/shard_map/gather | solution.py:211
  21.2 0.8 %copy.69 = bf16[1,4,32,1024]{3,2,1,0:T(8,128)(2,1)} copy(bf16[1,4,32,1024]{3,1,2,0:T(4,128)(2,1)S(1)} %bitcast.87) | data formatting | bytes 524288
  22.0 0.6 %sub.26.delta_ref = s32[4,3]{1,0:T(4,128)} subtract(s32[4,3]{1,0:T(4,128)S(1)} %gather_fusion, s32[4,3]{1,0:T(4,128)S(1)} %gather_fusion.4) | non-fusion elementwise | flops 12 | bytes 144 | tf_op jit(solution)/shard_map/sub | solution.py:212
  22.6 5.6 %shard_map.109 = (f32[4,32,1024]{2,1,0:T(8,128)}, f32[4,32,1024]{2,1,0:T(8,128)}) custom-call(s32[4,3]{1,0:T(4,128)} %sub.26.delta_ref, s32[4]{0:T(128)} %compare_convert_fusion.live_ref, bf16[4,32,1024]{2,1,0:T(8,128)(2,1)} %bitcast.84, bf16[4,32,1024]{2,1,0:T(8,128)(2,1)} %bitcast.85, f32[32,1024]{1,0:T(8,128)} %constant.91.clone.tiled_ref, ...), custom_call_target="tpu_custom_call" | custom-call | tf_op jit(solution)/shard_map/pallas_call | solution.py:159
  28.1 1.3 %pad_maximum_fusion = f32[8,32,1024]{2,1,0:T(8,128)S(1)} fusion(f32[4,32,1024]{2,1,0:T(8,128)} %get-tuple-element.8, f32[4,32,1024]{2,1,0:T(8,128)} %get-tuple-element.7), kind=kLoop, calls=%fused_computation.19 | loop fusion | flops 262144 | bytes 2097152 | tf_op jit(solution)/shard_map/concatenate | solution.py:216
  29.9 0.6 %copy.68 = f32[8,8,4096]{2,0,1:T(8,128)S(1)} copy(f32[8,8,4096]{2,1,0:T(8,128)S(1)} %reshape_reshape.3) | data formatting | bytes 2097152 | tf_op jit(solution)/shard_map/reshape;reshape | solution.py:221
  30.5 0.6 %gather_fusion.7 = f32[8,8,4096]{2,1,0:T(8,128)S(1)} fusion(f32[8,8,4096]{2,1,0:T(8,128)S(1)} %bitcast.83, s32[1024]{0:T(1024)S(1)} %get-tuple-element.25), kind=kCustom, calls=%fused_computation.7 | custom fusion | bytes 2097184 | tf_op jit(solution)/shard_map/gather | solution.py:222
  31.4 1.5 %collective-permute-start.4 = (f32[8,4224]{1,0:T(8,128)S(1)}, f32[8,4224]{1,0:T(8,128)S(1)}, u32[]{:S(2)}, u32[]{:S(2)}) collective-permute-start(f32[8,4224]{1,0:T(8,128)S(1)} %get-tuple-element.12), channel_id=1, source_target_pairs={{0,2},{1,3},{2,4},{3,5},{4,6},{5,7},{6,0},{7,1},{8,10},{9,11},{10,... | collective-permute-start | bytes 405512 | tf_op jit(solution)/shard_map/ppermute | solution.py:178
  32.9 2.4 %collective-permute-start.5 = (f32[8,4224]{1,0:T(8,128)S(1)}, f32[8,4224]{1,0:T(8,128)S(1)}, u32[]{:S(2)}, u32[]{:S(2)}) collective-permute-start(f32[8,4224]{1,0:T(8,128)S(1)} %get-tuple-element.13), channel_id=1, source_target_pairs={{0,3},{1,4},{2,5},{3,6},{4,7},{5,0},{6,1},{7,2},{8,11},{9,12},{10,... | collective-permute-start | bytes 405512 | tf_op jit(solution)/shard_map/ppermute | solution.py:178
  35.9 1.7 %collective-permute-done.3 = f32[8,4224]{1,0:T(8,128)S(1)} collective-permute-done((f32[8,4224]{1,0:T(8,128)S(1)}, f32[8,4224]{1,0:T(8,128)S(1)}, u32[]{:S(2)}, u32[]{:S(2)}) %collective-permute-start.3) | collective-permute-done | bytes 135200 | tf_op jit(solution)/shard_map/ppermute | solution.py:178
  37.6 1.4 %collective-permute-start.8 = (f32[8,4224]{1,0:T(8,128)S(1)}, f32[8,4224]{1,0:T(8,128)S(1)}, u32[]{:S(2)}, u32[]{:S(2)}) collective-permute-start(f32[8,4224]{1,0:T(8,128)S(1)} %get-tuple-element.16), channel_id=1, source_target_pairs={{0,6},{1,7},{2,0},{3,1},{4,2},{5,3},{6,4},{7,5},{8,14},{9,15},{10,... | collective-permute-start | bytes 405512 | tf_op jit(solution)/shard_map/ppermute | solution.py:178
  39.1 2.6 %collective-permute-start.9 = (f32[8,4224]{1,0:T(8,128)S(1)}, f32[8,4224]{1,0:T(8,128)S(1)}, u32[]{:S(2)}, u32[]{:S(2)}) collective-permute-start(f32[8,4224]{1,0:T(8,128)S(1)} %get-tuple-element.9), channel_id=1, source_target_pairs={{0,7},{1,0},{2,1},{3,2},{4,3},{5,4},{6,5},{7,6},{8,15},{9,8},{10,9... | collective-permute-start | bytes 405512 | tf_op jit(solution)/shard_map/ppermute | solution.py:178
  41.7 2.1 %collective-permute-done.5 = f32[8,4224]{1,0:T(8,128)S(1)} collective-permute-done((f32[8,4224]{1,0:T(8,128)S(1)}, f32[8,4224]{1,0:T(8,128)S(1)}, u32[]{:S(2)}, u32[]{:S(2)}) %collective-permute-start.5) | collective-permute-done | bytes 135200 | tf_op jit(solution)/shard_map/ppermute | solution.py:178
  44.0 1.8 %collective-permute-done.7 = f32[8,4224]{1,0:T(8,128)S(1)} collective-permute-done((f32[8,4224]{1,0:T(8,128)S(1)}, f32[8,4224]{1,0:T(8,128)S(1)}, u32[]{:S(2)}, u32[]{:S(2)}) %collective-permute-start.7) | collective-permute-done | bytes 135200 | tf_op jit(solution)/shard_map/ppermute | solution.py:178
  46.2 1.1 %convolution_bitcast_fusion = f32[20,4096]{1,0:T(8,128)S(1)} fusion(f32[8,8,4096]{2,1,0:T(8,128)S(1)} %slice.143, s32[8,8]{0,1:T(8,128)S(1)} %copy.52), kind=kOutput, calls=%fused_computation.10 | convolution fusion | flops 62915840 | bytes 1376512 | tf_op jit(solution)/shard_map/srk,srl->kl/dot_general | solution.py:229
  47.9 3.3 %collective-permute-start.10 = (f32[1,4096]{1,0:T(1,128)S(1)}, f32[1,4096]{1,0:T(1,128)S(1)}, u32[]{:S(2)}, u32[]{:S(2)}) collective-permute-start(f32[1,4096]{1,0:T(1,128)S(1)} %get-tuple-element.23), channel_id=1, source_target_pairs={{0,8},{8,16},{16,24},{24,0},{1,9},{9,17},{17,25},{25,1},{2,10},{10... | collective-permute-start | bytes 49160 | tf_op jit(solution)/shard_map/ppermute | solution.py:178
  51.3 1.6 %collective-permute-start.11 = (f32[1,4096]{1,0:T(1,128)S(1)}, f32[1,4096]{1,0:T(1,128)S(1)}, u32[]{:S(2)}, u32[]{:S(2)}) collective-permute-start(f32[1,4096]{1,0:T(1,128)S(1)} %get-tuple-element.22), channel_id=1, source_target_pairs={{0,16},{8,24},{16,0},{24,8},{1,17},{9,25},{17,1},{25,9},{2,18},{10... | collective-permute-start | bytes 49160 | tf_op jit(solution)/shard_map/ppermute | solution.py:178
  52.9 0.8 %collective-permute-start.12 = (f32[1,4096]{1,0:T(1,128)S(1)}, f32[1,4096]{1,0:T(1,128)S(1)}, u32[]{:S(2)}, u32[]{:S(2)}) collective-permute-start(f32[1,4096]{1,0:T(1,128)S(1)} %get-tuple-element.24), channel_id=1, source_target_pairs={{0,24},{8,0},{16,8},{24,16},{1,25},{9,1},{17,9},{25,17},{2,26},{10... | collective-permute-start | bytes 49160 | tf_op jit(solution)/shard_map/ppermute | solution.py:178
  53.7 0.6 %gather_fusion.8 = s32[4]{0:T(128)S(1)} fusion(s32[4]{0:T(128)S(1)} %gather_fusion.1, s32[1024]{0:T(1024)S(1)} %pad_clamp_fusion), kind=kCustom, calls=%fused_computation.8 | custom fusion | bytes 48 | tf_op jit(solution)/shard_map/gather | solution.py:235
  54.4 1.7 %collective-permute-done.11 = f32[1,4096]{1,0:T(1,128)S(1)} collective-permute-done((f32[1,4096]{1,0:T(1,128)S(1)}, f32[1,4096]{1,0:T(1,128)S(1)}, u32[]{:S(2)}, u32[]{:S(2)}) %collective-permute-start.11) | collective-permute-done | bytes 16416 | tf_op jit(solution)/shard_map/ppermute | solution.py:178
  56.7 1.1 %convolution_add_fusion = f32[16,4096]{1,0:T(8,128)} fusion(f32[20,4096]{1,0:T(8,128)S(1)} %convolution_bitcast_fusion, f32[4,1,4096]{2,1,0:T(1,128)S(1)} %pad_maximum_fusion.2, s32[4]{0:T(128)S(1)} %gather_fusion.8), kind=kOutput, calls=%fused_computation.11 | convolution fusion | flops 3211328 | bytes 589840 | tf_op jit(solution)/shard_map/dot_general | solution.py:239
  (56 shorter events, 6.1 us)
Async XLA Ops:
  0.0 3.4 %copy-start = (bf16[16,32768]{1,0:T(8,128)(2,1)S(1)}, bf16[16,32768]{1,0:T(8,128)(2,1)}, u32[]{:S(2)}) copy-start(bf16[16,32768]{1,0:T(8,128)(2,1)} %param.11) | copy-start | bytes 3145732
  4.7 10.6 %collective-permute-start = (bf16[1,32896]{1,0:T(2,128)(2,1)S(1)}, bf16[1,32896]{1,0:T(2,128)(2,1)S(1)}, u32[]{:S(2)}, u32[]{:S(2)}) collective-permute-start(bf16[1,32896]{1,0:T(2,128)(2,1)S(1)} %get-tuple-element.20), channel_id=1, source_target_pairs={{0,8},{8,16},{16,24},{24,0},{1,9},{9,17},{17,25},{25,1},{2,10},{10... | collective-permute-start | bytes 197384 | tf_op jit(solution)/shard_map/ppermute | solution.py:178
  7.8 11.3 %collective-permute-start.1 = (bf16[1,32896]{1,0:T(2,128)(2,1)S(1)}, bf16[1,32896]{1,0:T(2,128)(2,1)S(1)}, u32[]{:S(2)}, u32[]{:S(2)}) collective-permute-start(bf16[1,32896]{1,0:T(2,128)(2,1)S(1)} %get-tuple-element.19), channel_id=1, source_target_pairs={{0,16},{8,24},{16,0},{24,8},{1,17},{9,25},{17,1},{25,9},{2,18},{10... | collective-permute-start | bytes 197384 | tf_op jit(solution)/shard_map/ppermute | solution.py:178
  10.4 8.7 %collective-permute-start.2 = (bf16[1,32896]{1,0:T(2,128)(2,1)S(1)}, bf16[1,32896]{1,0:T(2,128)(2,1)S(1)}, u32[]{:S(2)}, u32[]{:S(2)}) collective-permute-start(bf16[1,32896]{1,0:T(2,128)(2,1)S(1)} %get-tuple-element.18), channel_id=1, source_target_pairs={{0,24},{8,0},{16,8},{24,16},{1,25},{9,1},{17,9},{25,17},{2,26},{10... | collective-permute-start | bytes 197384 | tf_op jit(solution)/shard_map/ppermute | solution.py:178
  12.3 0.8 %copy-start.1 = (s32[1,1,4]{2,1,0:T(1,128)S(1)}, s32[1,1,4]{2,1,0:T(1,128)}, u32[]{:S(2)}) copy-start(s32[1,1,4]{2,1,0:T(1,128)} %param.15) | copy-start | bytes 52
  12.3 2.9 %copy-start.2 = (s32[1,1,4]{2,1,0:T(1,128)S(1)}, s32[1,1,4]{2,1,0:T(1,128)}, u32[]{:S(2)}) copy-start(s32[1,1,4]{2,1,0:T(1,128)} %param.14) | copy-start | bytes 52
  31.3 6.3 %collective-permute-start.3 = (f32[8,4224]{1,0:T(8,128)S(1)}, f32[8,4224]{1,0:T(8,128)S(1)}, u32[]{:S(2)}, u32[]{:S(2)}) collective-permute-start(f32[8,4224]{1,0:T(8,128)S(1)} %get-tuple-element.11), channel_id=1, source_target_pairs={{0,1},{1,2},{2,3},{3,4},{4,5},{5,6},{6,7},{7,0},{8,9},{9,10},{10,1... | collective-permute-start | bytes 405512 | tf_op jit(solution)/shard_map/ppermute | solution.py:178
  31.4 7.7 %collective-permute-start.4 = (f32[8,4224]{1,0:T(8,128)S(1)}, f32[8,4224]{1,0:T(8,128)S(1)}, u32[]{:S(2)}, u32[]{:S(2)}) collective-permute-start(f32[8,4224]{1,0:T(8,128)S(1)} %get-tuple-element.12), channel_id=1, source_target_pairs={{0,2},{1,3},{2,4},{3,5},{4,6},{5,7},{6,0},{7,1},{8,10},{9,11},{10,... | collective-permute-start | bytes 405512 | tf_op jit(solution)/shard_map/ppermute | solution.py:178
  32.9 10.9 %collective-permute-start.5 = (f32[8,4224]{1,0:T(8,128)S(1)}, f32[8,4224]{1,0:T(8,128)S(1)}, u32[]{:S(2)}, u32[]{:S(2)}) collective-permute-start(f32[8,4224]{1,0:T(8,128)S(1)} %get-tuple-element.13), channel_id=1, source_target_pairs={{0,3},{1,4},{2,5},{3,6},{4,7},{5,0},{6,1},{7,2},{8,11},{9,12},{10,... | collective-permute-start | bytes 405512 | tf_op jit(solution)/shard_map/ppermute | solution.py:178
  35.3 8.7 %collective-permute-start.6 = (f32[8,4224]{1,0:T(8,128)S(1)}, f32[8,4224]{1,0:T(8,128)S(1)}, u32[]{:S(2)}, u32[]{:S(2)}) collective-permute-start(f32[8,4224]{1,0:T(8,128)S(1)} %get-tuple-element.14), channel_id=1, source_target_pairs={{0,4},{1,5},{2,6},{3,7},{4,0},{5,1},{6,2},{7,3},{8,12},{9,13},{10,... | collective-permute-start | bytes 405512 | tf_op jit(solution)/shard_map/ppermute | solution.py:178
  35.8 10.0 %collective-permute-start.7 = (f32[8,4224]{1,0:T(8,128)S(1)}, f32[8,4224]{1,0:T(8,128)S(1)}, u32[]{:S(2)}, u32[]{:S(2)}) collective-permute-start(f32[8,4224]{1,0:T(8,128)S(1)} %get-tuple-element.15), channel_id=1, source_target_pairs={{0,5},{1,6},{2,7},{3,0},{4,1},{5,2},{6,3},{7,4},{8,13},{9,14},{10,... | collective-permute-start | bytes 405512 | tf_op jit(solution)/shard_map/ppermute | solution.py:178
  37.6 8.3 %collective-permute-start.8 = (f32[8,4224]{1,0:T(8,128)S(1)}, f32[8,4224]{1,0:T(8,128)S(1)}, u32[]{:S(2)}, u32[]{:S(2)}) collective-permute-start(f32[8,4224]{1,0:T(8,128)S(1)} %get-tuple-element.16), channel_id=1, source_target_pairs={{0,6},{1,7},{2,0},{3,1},{4,2},{5,3},{6,4},{7,5},{8,14},{9,15},{10,... | collective-permute-start | bytes 405512 | tf_op jit(solution)/shard_map/ppermute | solution.py:178
  39.1 6.8 %collective-permute-start.9 = (f32[8,4224]{1,0:T(8,128)S(1)}, f32[8,4224]{1,0:T(8,128)S(1)}, u32[]{:S(2)}, u32[]{:S(2)}) collective-permute-start(f32[8,4224]{1,0:T(8,128)S(1)} %get-tuple-element.9), channel_id=1, source_target_pairs={{0,7},{1,0},{2,1},{3,2},{4,3},{5,4},{6,5},{7,6},{8,15},{9,8},{10,9... | collective-permute-start | bytes 405512 | tf_op jit(solution)/shard_map/ppermute | solution.py:178
  47.9 6.4 %collective-permute-start.10 = (f32[1,4096]{1,0:T(1,128)S(1)}, f32[1,4096]{1,0:T(1,128)S(1)}, u32[]{:S(2)}, u32[]{:S(2)}) collective-permute-start(f32[1,4096]{1,0:T(1,128)S(1)} %get-tuple-element.23), channel_id=1, source_target_pairs={{0,8},{8,16},{16,24},{24,0},{1,9},{9,17},{17,25},{25,1},{2,10},{10... | collective-permute-start | bytes 49160 | tf_op jit(solution)/shard_map/ppermute | solution.py:178
  51.3 4.8 %collective-permute-start.11 = (f32[1,4096]{1,0:T(1,128)S(1)}, f32[1,4096]{1,0:T(1,128)S(1)}, u32[]{:S(2)}, u32[]{:S(2)}) collective-permute-start(f32[1,4096]{1,0:T(1,128)S(1)} %get-tuple-element.22), channel_id=1, source_target_pairs={{0,16},{8,24},{16,0},{24,8},{1,17},{9,25},{17,1},{25,9},{2,18},{10... | collective-permute-start | bytes 49160 | tf_op jit(solution)/shard_map/ppermute | solution.py:178
  52.9 3.7 %collective-permute-start.12 = (f32[1,4096]{1,0:T(1,128)S(1)}, f32[1,4096]{1,0:T(1,128)S(1)}, u32[]{:S(2)}, u32[]{:S(2)}) collective-permute-start(f32[1,4096]{1,0:T(1,128)S(1)} %get-tuple-element.24), channel_id=1, source_target_pairs={{0,24},{8,0},{16,8},{24,16},{1,25},{9,1},{17,9},{25,17},{2,26},{10... | collective-permute-start | bytes 49160 | tf_op jit(solution)/shard_map/ppermute | solution.py:178

commit v4 on v3

--- a/solution.py
+++ b/solution.py
@@ -179,6 +179,25 @@
     return jnp.stack(received)
 
 
+def pair_exchange(blocks, axis):
+    chips = blocks.shape[0]
+    count = 2 * chips
+    partner = [(source, source ^ 1) for source in range(count)]
+    mine = [blocks[0, 0], lax.ppermute(blocks[0, 1], axis, partner)]
+    forward = []
+    for step in range(1, chips):
+        pairs = [
+            (source, ((source // 2 + step) % chips) * 2 + source % 2) for source in range(count)
+        ]
+        got = lax.ppermute(blocks[step], axis, pairs)
+        mine.append(got[0])
+        forward.append(got[1])
+    if forward:
+        passed = lax.ppermute(jnp.stack(forward), axis, partner)
+        mine.extend(passed[index] for index in range(chips - 1))
+    return jnp.stack(mine)
+
+
 def per_device(orbitals, offsets, sends, pair_home, pair_visit, pair_count):
     home_count = orbitals.shape[0]
     cell_count = orbitals.shape[1]
@@ -219,10 +238,14 @@
     pair_me = lax.axis_index("pair")
     targets = jnp.concatenate([home_slot, home_count + visit_slot]).astype(jnp.float32)
     body = fields.reshape(rows_out, pair_total, chunk).transpose(1, 0, 2)
-    body = body[(pair_me + jnp.arange(pair_total, dtype=jnp.int32)) % pair_total]
+    chips = pair_total // 2
+    chip_me = pair_me // 2
+    ahead_chip = (chip_me + jnp.arange(chips, dtype=jnp.int32)) % chips
+    ahead_core = (pair_me + jnp.arange(2, dtype=jnp.int32)) % 2
+    body = body[(ahead_chip[:, None] * 2 + ahead_core[None, :]).reshape(-1)]
     tags = jnp.broadcast_to(targets[None, :, None], (pair_total, rows_out, extra))
-    payload = jnp.concatenate([body, tags], axis=2)
-    got = exchange(payload, "pair")
+    payload = jnp.concatenate([body, tags], axis=2).reshape(chips, 2, rows_out, chunk + extra)
+    got = pair_exchange(payload, "pair")
     got_ids = got[:, :, chunk].astype(jnp.int32)
     all_rows = jnp.arange(home_count + slot_total, dtype=jnp.int32)
     picker = (got_ids[:, :, None] == all_rows[None, None, :]).astype(jnp.float32)

time: 58.1 us -> 66.3 us (1.14)
  waiting for transfers between devices: 11.9 us -> 24.4 us
  starting transfers between devices: 21.4 us -> 14.6 us
  local copies, waits for them, and re-layouts: 11.6 us -> 14 us
    ppermute x0 -> x5, waiting for transfers between devices: none -> 14.9 us  [the longest x3 13.2 us: pair_exchange(): got = lax.ppermute(blocks[step], axis, pairs)]
    ppermute x13 -> x6, starting transfers between devices: 21.4 us -> 10.8 us  [exchange(): received.append(lax.ppermute(blocks[step], axis, pairs))]
    ppermute x0 -> x5, starting transfers between devices: none -> 3.74 us  [the longest x3 3.6 us: pair_exchange(): got = lax.ppermute(blocks[step], axis, pairs)]
    ppermute x13 -> x6, waiting for transfers between devices: 11.9 us -> 9.48 us  [exchange(): received.append(lax.ppermute(blocks[step], axis, pairs))]
    another operation x2, local copies, waits for them, and re-layouts: 1.09 us -> 3.31 us  [per_device(): body = fields.reshape(rows_out, pair_total, chunk).transpose(1, 0, 2)]
    unnamed x16 -> x12, local copies, waits for them, and re-layouts: 2.52 us -> 2.56 us
  transfers between devices with their start and end apart: 13 -> 11, of which waited for: 7 -> 6; matrix products, arithmetic and copies ran while one was open for 6% -> 6% of each run, Pallas kernels for 0% -> 0%
where the time goes in v4:
time: 66.3 us; the launch traced here: 66 us
  waiting for transfers between devices  24.4 us (37%)
  starting transfers between devices  14.6 us (22%)
  local copies, waits for them, and re-layouts  14 us (21%)
  Pallas kernels  5.59 us (8%)
  other arithmetic  4.31 us (7%)
  matrix products  2.19 us (3%)
  between operations  0.95 us (1%)
    ppermute x3, waiting for transfers between devices, pair_exchange(): got = lax.ppermute(blocks[step], axis, pairs)  13.2 us
    ppermute x6, starting transfers between devices, exchange(): received.append(lax.ppermute(blocks[step], axis, pairs))  10.8 us
    ppermute x6, waiting for transfers between devices, exchange(): received.append(lax.ppermute(blocks[step], axis, pairs))  9.48 us
    pallas_call x1, Pallas kernels, pair_fields(): pl.pallas_call(pair_kernel, out_shape=(box, box), in_specs=[smem, smem] +...  5.59 us
    ppermute x3, starting transfers between devices, pair_exchange(): got = lax.ppermute(blocks[step], axis, pairs)  3.6 us
    another operation x2, local copies, waits for them, and re-layouts, per_device(): body = fields.reshape(rows_out, pair_total, chunk).transpose(1, 0, 2)  3.31 us
    unnamed x12, local copies, waits for them, and re-layouts  2.56 us
    ppermute x1, waiting for transfers between devices, pair_exchange(): passed = lax.ppermute(jnp.stack(forward), axis, partner)  1.7 us
  transfers between devices with their start and end apart: 11, of which 6 were waited for; matrix products, arithmetic and copies ran while one was open for 6% of the time, Pallas kernels for 0%

profile of v4, /device:TPU:0, one launch (start us, length us, event | category | flops | bytes accessed | tf_op | source)
XLA Modules:
  0.0 66.0 jit_solution(15493740791485334745)
XLA Ops:
  0.0 0.8 %copy.46 = s32[16,3]{1,0:T(8,128)S(1)} copy(s32[16,3]{0,1:T(4,128)} %param.12) | data formatting | bytes 384 | tf_op args[1]
  0.9 1.3 %gather_fusion.1 = s32[4]{0:T(128)S(1)} fusion(s32[4]{0:T(128)} %bitcast.65, s32[1024]{0:T(1024)S(1)} %pad_clamp_fusion.4), kind=kCustom, calls=%fused_computation.1 | custom fusion | bytes 48 | tf_op jit(solution)/shard_map/gather | solution.py:211
  2.2 0.7 fusion.23
  3.4 0.8 %gather_fusion.2 = bf16[4,32768]{1,0:T(4,128)(2,1)S(1)} fusion(bf16[16,32768]{1,0:T(8,128)(2,1)S(1)} %copy-done, s32[1024]{0:T(1024)S(1)} %get-tuple-element.28), kind=kCustom, calls=%fused_computation.2 | custom fusion | bytes 524304 | tf_op jit(solution)/shard_map/gather | solution.py:215
  4.7 5.1 %collective-permute-start.2 = (bf16[1,32896]{1,0:T(2,128)(2,1)S(1)}, bf16[1,32896]{1,0:T(2,128)(2,1)S(1)}, u32[]{:S(2)}, u32[]{:S(2)}) collective-permute-start(bf16[1,32896]{1,0:T(2,128)(2,1)S(1)} %get-tuple-element.19), channel_id=1, source_target_pairs={{0,24},{8,0},{16,8},{24,16},{1,25},{9,1},{17,9},{25,17},{2,26},{10... | collective-permute-start | bytes 197384 | tf_op jit(solution)/shard_map/ppermute | solution.py:178
  9.9 1.0 %collective-permute-start = (bf16[1,32896]{1,0:T(2,128)(2,1)S(1)}, bf16[1,32896]{1,0:T(2,128)(2,1)S(1)}, u32[]{:S(2)}, u32[]{:S(2)}) collective-permute-start(bf16[1,32896]{1,0:T(2,128)(2,1)S(1)} %get-tuple-element.21), channel_id=1, source_target_pairs={{0,8},{8,16},{16,24},{24,0},{1,9},{9,17},{17,25},{25,1},{2,10},{10... | collective-permute-start | bytes 197384 | tf_op jit(solution)/shard_map/ppermute | solution.py:178
  11.5 0.8 %gather_fusion.5 = bf16[4,32768]{1,0:T(4,128)(2,1)S(1)} fusion(bf16[16,32768]{1,0:T(8,128)(2,1)S(1)} %copy-done, s32[1024]{0:T(1024)S(1)} %get-tuple-element.29), kind=kCustom, calls=%fused_computation.5 | custom fusion | bytes 524304 | tf_op jit(solution)/shard_map/gather | solution.py:229
  13.7 0.8 %copy.68 = bf16[1,4,32,1024]{3,2,1,0:T(8,128)(2,1)} copy(bf16[1,4,32,1024]{3,1,2,0:T(4,128)(2,1)S(1)} %bitcast.70) | data formatting | bytes 524288
  14.6 6.5 %collective-permute-done.1 = bf16[1,32896]{1,0:T(2,128)(2,1)S(1)} collective-permute-done((bf16[1,32896]{1,0:T(2,128)(2,1)S(1)}, bf16[1,32896]{1,0:T(2,128)(2,1)S(1)}, u32[]{:S(2)}, u32[]{:S(2)}) %collective-permute-start.1) | collective-permute-done | bytes 65824 | tf_op jit(solution)/shard_map/ppermute | solution.py:178
  21.1 0.6 maximum_bitcast_fusion
  22.4 0.8 %gather_fusion.6 = bf16[4,32768]{1,0:T(4,128)(2,1)S(1)} fusion(bf16[4,32768]{1,0:T(4,128)(2,1)S(1)} %slice.146, s32[1024]{0:T(1024)S(1)} %get-tuple-element.27), kind=kCustom, calls=%fused_computation.6 | custom fusion | bytes 524304 | tf_op jit(solution)/shard_map/gather | solution.py:230
  23.2 0.8 %copy.67 = bf16[1,4,32,1024]{3,2,1,0:T(8,128)(2,1)} copy(bf16[1,4,32,1024]{3,1,2,0:T(4,128)(2,1)S(1)} %bitcast.72) | data formatting | bytes 524288
  24.0 0.6 sub.30.delta_ref
  24.6 5.6 %shard_map.109 = (f32[4,32,1024]{2,1,0:T(8,128)}, f32[4,32,1024]{2,1,0:T(8,128)}) custom-call(s32[4,3]{1,0:T(4,128)} %sub.30.delta_ref, s32[4]{0:T(128)} %compare_convert_fusion.live_ref, bf16[4,32,1024]{2,1,0:T(8,128)(2,1)} %bitcast.69, bf16[4,32,1024]{2,1,0:T(8,128)(2,1)} %bitcast.71, f32[32,1024]{1,0:T(8,128)} %constant.109.clone.tiled_ref, ...), custom_call_target="tpu_custom_call" | custom-call | tf_op jit(solution)/shard_map/pallas_call | solution.py:159
  30.1 1.3 %pad_maximum_fusion.1 = f32[8,32,1024]{2,1,0:T(8,128)S(1)} fusion(f32[4,32,1024]{2,1,0:T(8,128)} %get-tuple-element.8, f32[4,32,1024]{2,1,0:T(8,128)} %get-tuple-element.7), kind=kLoop, calls=%fused_computation.15 | loop fusion | flops 262144 | bytes 2097152 | tf_op jit(solution)/shard_map/concatenate | solution.py:235
  31.4 1.5 %reshape_reshape.3 = f32[8,8,4096]{2,1,0:T(8,128)} reshape(f32[8,32,1024]{2,1,0:T(8,128)S(1)} %pad_maximum_fusion.1) | data formatting | bytes 2097152 | tf_op jit(solution)/shard_map/reshape;reshape | solution.py:240
  32.9 1.8 %copy.66 = f32[8,8,4096]{2,0,1:T(8,128)S(1)} copy(f32[8,8,4096]{2,1,0:T(8,128)} %reshape_reshape.3) | data formatting | bytes 2097152 | tf_op jit(solution)/shard_map/reshape;reshape | solution.py:240
  34.7 0.6 gather_fusion.7
  35.7 2.5 %collective-permute-start.6 = (f32[2,8,4224]{2,1,0:T(8,128)S(1)}, f32[2,8,4224]{2,1,0:T(8,128)S(1)}, u32[]{:S(2)}, u32[]{:S(2)}) collective-permute-start(f32[2,8,4224]{2,1,0:T(8,128)S(1)} %get-tuple-element.9), channel_id=1, source_target_pairs={{0,6},{1,7},{2,0},{3,1},{4,2},{5,3},{6,4},{7,5},{8,14},{9,15},{10,... | collective-permute-start | bytes 811016 | tf_op jit(solution)/shard_map/ppermute | solution.py:192
  38.7 0.6 collective-permute-start.4
  39.3 12.2 %collective-permute-done.4 = f32[2,8,4224]{2,1,0:T(8,128)S(1)} collective-permute-done((f32[2,8,4224]{2,1,0:T(8,128)S(1)}, f32[2,8,4224]{2,1,0:T(8,128)S(1)}, u32[]{:S(2)}, u32[]{:S(2)}) %collective-permute-start.4) | collective-permute-done | bytes 270368 | tf_op jit(solution)/shard_map/ppermute | solution.py:192
  51.5 1.1 %collective-permute-done.5 = f32[2,8,4224]{2,1,0:T(8,128)S(1)} collective-permute-done((f32[2,8,4224]{2,1,0:T(8,128)S(1)}, f32[2,8,4224]{2,1,0:T(8,128)S(1)}, u32[]{:S(2)}, u32[]{:S(2)}) %collective-permute-start.5) | collective-permute-done | bytes 270368 | tf_op jit(solution)/shard_map/ppermute | solution.py:192
  52.8 1.7 %collective-permute-done.7 = f32[3,8,4224]{2,1,0:T(8,128)S(1)} collective-permute-done((f32[3,8,4224]{2,1,0:T(8,128)S(1)}, f32[3,8,4224]{2,1,0:T(8,128)S(1)}, u32[]{:S(2)}, u32[]{:S(2)}) %collective-permute-start.7) | collective-permute-done | bytes 405536 | tf_op jit(solution)/shard_map/ppermute | solution.py:196
  54.8 1.1 %convolution_bitcast_fusion = f32[20,4096]{1,0:T(8,128)S(1)} fusion(f32[8,8,4096]{2,1,0:T(8,128)S(1)} %slice.162, s32[8,8]{0,1:T(8,128)S(1)} %copy.50), kind=kOutput, calls=%fused_computation.10 | convolution fusion | flops 62915840 | bytes 1376512 | tf_op jit(solution)/shard_map/srk,srl->kl/dot_general | solution.py:252
  55.9 0.6 gather_fusion.9
  56.5 1.7 %collective-permute-start.10 = (f32[1,4096]{1,0:T(1,128)S(1)}, f32[1,4096]{1,0:T(1,128)S(1)}, u32[]{:S(2)}, u32[]{:S(2)}) collective-permute-start(f32[1,4096]{1,0:T(1,128)S(1)} %get-tuple-element.25), channel_id=1, source_target_pairs={{0,24},{8,0},{16,8},{24,16},{1,25},{9,1},{17,9},{25,17},{2,26},{10... | collective-permute-start | bytes 49160 | tf_op jit(solution)/shard_map/ppermute | solution.py:178
  58.2 1.1 %collective-permute-start.9 = (f32[1,4096]{1,0:T(1,128)S(1)}, f32[1,4096]{1,0:T(1,128)S(1)}, u32[]{:S(2)}, u32[]{:S(2)}) collective-permute-start(f32[1,4096]{1,0:T(1,128)S(1)} %get-tuple-element.23), channel_id=1, source_target_pairs={{0,16},{8,24},{16,0},{24,8},{1,17},{9,25},{17,1},{25,9},{2,18},{10... | collective-permute-start | bytes 49160 | tf_op jit(solution)/shard_map/ppermute | solution.py:178
  59.3 1.9 %collective-permute-start.8 = (f32[1,4096]{1,0:T(1,128)S(1)}, f32[1,4096]{1,0:T(1,128)S(1)}, u32[]{:S(2)}, u32[]{:S(2)}) collective-permute-start(f32[1,4096]{1,0:T(1,128)S(1)} %get-tuple-element.24), channel_id=1, source_target_pairs={{0,8},{8,16},{16,24},{24,0},{1,9},{9,17},{17,25},{25,1},{2,10},{10... | collective-permute-start | bytes 49160 | tf_op jit(solution)/shard_map/ppermute | solution.py:178
  61.2 0.6 gather_fusion.8
  61.9 1.0 %collective-permute-done.9 = f32[1,4096]{1,0:T(1,128)S(1)} collective-permute-done((f32[1,4096]{1,0:T(1,128)S(1)}, f32[1,4096]{1,0:T(1,128)S(1)}, u32[]{:S(2)}, u32[]{:S(2)}) %collective-permute-start.9) | collective-permute-done | bytes 16416 | tf_op jit(solution)/shard_map/ppermute | solution.py:178
  62.8 2.0 %collective-permute-done.8 = f32[1,4096]{1,0:T(1,128)S(1)} collective-permute-done((f32[1,4096]{1,0:T(1,128)S(1)}, f32[1,4096]{1,0:T(1,128)S(1)}, u32[]{:S(2)}, u32[]{:S(2)}) %collective-permute-start.8) | collective-permute-done | bytes 16416 | tf_op jit(solution)/shard_map/ppermute | solution.py:178
  64.9 1.1 %slice_add_fusion = f32[16,4096]{1,0:T(8,128)} fusion(f32[20,4096]{1,0:T(8,128)S(1)} %convolution_bitcast_fusion, f32[4,1,4096]{2,1,0:T(1,128)S(1)} %pad_maximum_fusion.3, s32[4]{0:T(128)S(1)} %gather_fusion.8), kind=kOutput, calls=%fused_computation.31 | convolution fusion | flops 3211328 | bytes 589840 | tf_op jit(solution)/shard_map/dot_general | solution.py:262
  (58 shorter events, 4.6 us)
Async XLA Ops:
  0.0 3.4 %copy-start = (bf16[16,32768]{1,0:T(8,128)(2,1)S(1)}, bf16[16,32768]{1,0:T(8,128)(2,1)}, u32[]{:S(2)}) copy-start(bf16[16,32768]{1,0:T(8,128)(2,1)} %param.11) | copy-start | bytes 3145732
  4.7 9.8 %collective-permute-start.2 = (bf16[1,32896]{1,0:T(2,128)(2,1)S(1)}, bf16[1,32896]{1,0:T(2,128)(2,1)S(1)}, u32[]{:S(2)}, u32[]{:S(2)}) collective-permute-start(bf16[1,32896]{1,0:T(2,128)(2,1)S(1)} %get-tuple-element.19), channel_id=1, source_target_pairs={{0,24},{8,0},{16,8},{24,16},{1,25},{9,1},{17,9},{25,17},{2,26},{10... | collective-permute-start | bytes 197384 | tf_op jit(solution)/shard_map/ppermute | solution.py:178
  9.8 11.2 %collective-permute-start.1 = (bf16[1,32896]{1,0:T(2,128)(2,1)S(1)}, bf16[1,32896]{1,0:T(2,128)(2,1)S(1)}, u32[]{:S(2)}, u32[]{:S(2)}) collective-permute-start(bf16[1,32896]{1,0:T(2,128)(2,1)S(1)} %get-tuple-element.20), channel_id=1, source_target_pairs={{0,16},{8,24},{16,0},{24,8},{1,17},{9,25},{17,1},{25,9},{2,18},{10... | collective-permute-start | bytes 197384 | tf_op jit(solution)/shard_map/ppermute | solution.py:178
  9.9 11.2 %collective-permute-start = (bf16[1,32896]{1,0:T(2,128)(2,1)S(1)}, bf16[1,32896]{1,0:T(2,128)(2,1)S(1)}, u32[]{:S(2)}, u32[]{:S(2)}) collective-permute-start(bf16[1,32896]{1,0:T(2,128)(2,1)S(1)} %get-tuple-element.21), channel_id=1, source_target_pairs={{0,8},{8,16},{16,24},{24,0},{1,9},{9,17},{17,25},{25,1},{2,10},{10... | collective-permute-start | bytes 197384 | tf_op jit(solution)/shard_map/ppermute | solution.py:178
  11.4 0.8 %copy-start.1 = (s32[1,1,4]{2,1,0:T(1,128)S(1)}, s32[1,1,4]{2,1,0:T(1,128)}, u32[]{:S(2)}) copy-start(s32[1,1,4]{2,1,0:T(1,128)} %param.15) | copy-start | bytes 52
  11.4 3.0 %copy-start.2 = (s32[1,1,4]{2,1,0:T(1,128)S(1)}, s32[1,1,4]{2,1,0:T(1,128)}, u32[]{:S(2)}) copy-start(s32[1,1,4]{2,1,0:T(1,128)} %param.14) | copy-start | bytes 52
  35.5 3.7 %collective-permute-start.3 = (f32[8,4224]{1,0:T(8,128)S(1)}, f32[8,4224]{1,0:T(8,128)S(1)}, u32[]{:S(2)}, u32[]{:S(2)}) collective-permute-start(f32[8,4224]{1,0:T(8,128)S(1)} %slice_bitcast_fusion), channel_id=1, source_target_pairs={{0,1},{1,0},{2,3},{3,2},{4,5},{5,4},{6,7},{7,6},{8,9},{9,8},{10,11... | collective-permute-start | bytes 405512 | tf_op jit(solution)/shard_map/ppermute | solution.py:186
  35.7 16.9 %collective-permute-start.6 = (f32[2,8,4224]{2,1,0:T(8,128)S(1)}, f32[2,8,4224]{2,1,0:T(8,128)S(1)}, u32[]{:S(2)}, u32[]{:S(2)}) collective-permute-start(f32[2,8,4224]{2,1,0:T(8,128)S(1)} %get-tuple-element.9), channel_id=1, source_target_pairs={{0,6},{1,7},{2,0},{3,1},{4,2},{5,3},{6,4},{7,5},{8,14},{9,15},{10,... | collective-permute-start | bytes 811016 | tf_op jit(solution)/shard_map/ppermute | solution.py:192
  38.2 14.4 %collective-permute-start.5 = (f32[2,8,4224]{2,1,0:T(8,128)S(1)}, f32[2,8,4224]{2,1,0:T(8,128)S(1)}, u32[]{:S(2)}, u32[]{:S(2)}) collective-permute-start(f32[2,8,4224]{2,1,0:T(8,128)S(1)} %get-tuple-element.11), channel_id=1, source_target_pairs={{0,4},{1,5},{2,6},{3,7},{4,0},{5,1},{6,2},{7,3},{8,12},{9,13},{10,... | collective-permute-start | bytes 811016 | tf_op jit(solution)/shard_map/ppermute | solution.py:192
  38.7 12.8 %collective-permute-start.4 = (f32[2,8,4224]{2,1,0:T(8,128)S(1)}, f32[2,8,4224]{2,1,0:T(8,128)S(1)}, u32[]{:S(2)}, u32[]{:S(2)}) collective-permute-start(f32[2,8,4224]{2,1,0:T(8,128)S(1)} %get-tuple-element.10), channel_id=1, source_target_pairs={{0,2},{1,3},{2,4},{3,5},{4,6},{5,7},{6,0},{7,1},{8,10},{9,11},{10,... | collective-permute-start | bytes 811016 | tf_op jit(solution)/shard_map/ppermute | solution.py:192
  52.7 1.8 %collective-permute-start.7 = (f32[3,8,4224]{2,1,0:T(8,128)S(1)}, f32[3,8,4224]{2,1,0:T(8,128)S(1)}, u32[]{:S(2)}, u32[]{:S(2)}) collective-permute-start(f32[3,8,4224]{2,1,0:T(8,128)S(1)} %pad_maximum_fusion.2), channel_id=1, source_target_pairs={{0,1},{1,0},{2,3},{3,2},{4,5},{5,4},{6,7},{7,6},{8,9},{9,8},{10,11... | collective-permute-start | bytes 1216520 | tf_op jit(solution)/shard_map/ppermute | solution.py:196
  56.5 5.4 %collective-permute-start.10 = (f32[1,4096]{1,0:T(1,128)S(1)}, f32[1,4096]{1,0:T(1,128)S(1)}, u32[]{:S(2)}, u32[]{:S(2)}) collective-permute-start(f32[1,4096]{1,0:T(1,128)S(1)} %get-tuple-element.25), channel_id=1, source_target_pairs={{0,24},{8,0},{16,8},{24,16},{1,25},{9,1},{17,9},{25,17},{2,26},{10... | collective-permute-start | bytes 49160 | tf_op jit(solution)/shard_map/ppermute | solution.py:178
  58.2 4.7 %collective-permute-start.9 = (f32[1,4096]{1,0:T(1,128)S(1)}, f32[1,4096]{1,0:T(1,128)S(1)}, u32[]{:S(2)}, u32[]{:S(2)}) collective-permute-start(f32[1,4096]{1,0:T(1,128)S(1)} %get-tuple-element.23), channel_id=1, source_target_pairs={{0,16},{8,24},{16,0},{24,8},{1,17},{9,25},{17,1},{25,9},{2,18},{10... | collective-permute-start | bytes 49160 | tf_op jit(solution)/shard_map/ppermute | solution.py:178
  59.3 5.5 %collective-permute-start.8 = (f32[1,4096]{1,0:T(1,128)S(1)}, f32[1,4096]{1,0:T(1,128)S(1)}, u32[]{:S(2)}, u32[]{:S(2)}) collective-permute-start(f32[1,4096]{1,0:T(1,128)S(1)} %get-tuple-element.24), channel_id=1, source_target_pairs={{0,8},{8,16},{16,24},{24,0},{1,9},{9,17},{17,25},{25,1},{2,10},{10... | collective-permute-start | bytes 49160 | tf_op jit(solution)/shard_map/ppermute | solution.py:178

commit v5 on v3

--- a/solution.py
+++ b/solution.py
@@ -76,9 +76,28 @@
     return out + jnp.dot(matrix, third, preferred_element_type=jnp.float32)
 
 
+def emit(payload_ref, row, values, tag, me):
+    count, _, width = payload_ref.shape
+    chunk = width - 128
+    for index in range(count):
+        place = lax.rem(index - me + count, count)
+        if chunk >= PLANE:
+            per = chunk // PLANE
+            for part in range(per):
+                payload_ref[place, pl.ds(row, 1), pl.ds(part * PLANE, PLANE)] = values[
+                    index * per + part : index * per + part + 1, :
+                ]
+        else:
+            per = PLANE // chunk
+            line, piece = divmod(index, per)
+            payload_ref[place, pl.ds(row, 1), pl.ds(0, chunk)] = values[
+                line : line + 1, piece * chunk : (piece + 1) * chunk
+            ]
+        payload_ref[place, pl.ds(row, 1), pl.ds(chunk, 128)] = tag
+
+
 def pair_kernel(
-    delta_ref,
-    live_ref,
+    meta_ref,
     home_ref,
     part_ref,
     tiled_ref,
@@ -86,14 +105,14 @@
     rows_high_ref,
     rows_low_ref,
     eigen_ref,
-    to_home_ref,
-    to_partner_ref,
+    payload_ref,
     shifted_ref,
     work_ref,
     kron_high_ref,
     kron_low_ref,
 ):
     slots = home_ref.shape[0]
+    me = meta_ref[6 * slots]
     tiled = tiled_ref[...]
     for block in range(B):
         values = tiled * spread_ref[block : block + 1, :]
@@ -108,9 +127,9 @@
     row = lax.broadcasted_iota(jnp.int32, (B, B), 0)
     col = lax.broadcasted_iota(jnp.int32, (B, B), 1)
     for slot in range(slots):
-        d_a = delta_ref[slot, 0]
-        d_b = delta_ref[slot, 1]
-        d_c = delta_ref[slot, 2]
+        d_a = meta_ref[3 * slot]
+        d_b = meta_ref[3 * slot + 1]
+        d_c = meta_ref[3 * slot + 2]
         pick = (col == row + d_a).astype(jnp.bfloat16)
         moved = jnp.dot(pick, part_ref[slot], preferred_element_type=jnp.float32)
         step = d_b * B + d_c
@@ -133,12 +152,14 @@
     potential = dot3_left(rows_high, rows_low, dot3(work_ref[...], kron_high, kron_low))
 
     for slot in range(slots):
-        d_a = delta_ref[slot, 0]
-        d_b = delta_ref[slot, 1]
-        d_c = delta_ref[slot, 2]
-        live = live_ref[slot] > 0
+        d_a = meta_ref[3 * slot]
+        d_b = meta_ref[3 * slot + 1]
+        d_c = meta_ref[3 * slot + 2]
+        live = meta_ref[3 * slots + slot] > 0
         here = potential[slot * B : (slot + 1) * B, :]
-        to_home_ref[slot] = jnp.where(live, here * shifted_ref[slot], 0.0)
+        tag_home = jnp.full((1, 128), meta_ref[4 * slots + slot].astype(jnp.float32))
+        tag_part = jnp.full((1, 128), meta_ref[5 * slots + slot].astype(jnp.float32))
+        emit(payload_ref, slot, jnp.where(live, here * shifted_ref[slot], 0.0), tag_home, me)
         product = here * home_ref[slot].astype(jnp.float32)
         pick = (col == row - d_a).astype(jnp.bfloat16)
         moved = exact_rows(pick, product)
@@ -147,27 +168,27 @@
         inside = (
             (lane_b - d_b >= 0) & (lane_b - d_b < B) & (lane_c - d_c >= 0) & (lane_c - d_c < B)
         )
-        to_partner_ref[slot] = jnp.where(live & inside, moved, 0.0)
-
-
-def pair_fields(delta, live, home, part):
+        emit(payload_ref, slots + slot, jnp.where(live & inside, moved, 0.0), tag_part, me)
+
+
+def pair_fields(meta, home, part, count, chunk):
     slots = home.shape[0]
     tiled, spread, rows_high, rows_low, eigen = host_tables(slots)
     smem = pl.BlockSpec(memory_space=pltpu.SMEM)
     vmem = pl.BlockSpec(memory_space=pltpu.VMEM)
-    box = jax.ShapeDtypeStruct((slots, B, PLANE), jnp.float32)
+    box = jax.ShapeDtypeStruct((count, 2 * slots, chunk + 128), jnp.float32)
     return pl.pallas_call(
         pair_kernel,
-        out_shape=(box, box),
-        in_specs=[smem, smem] + [vmem] * 7,
-        out_specs=(vmem, vmem),
+        out_shape=box,
+        in_specs=[smem] + [vmem] * 7,
+        out_specs=vmem,
         scratch_shapes=[
             pltpu.VMEM((slots, B, PLANE), jnp.float32),
             pltpu.VMEM((slots * B, PLANE), jnp.float32),
             pltpu.VMEM((PLANE, PLANE), jnp.bfloat16),
             pltpu.VMEM((PLANE, PLANE), jnp.bfloat16),
         ],
-    )(delta, live, home, part, tiled, spread, rows_high, rows_low, eigen)
+    )(meta, home, part, tiled, spread, rows_high, rows_low, eigen)
 
 
 def exchange(blocks, axis):
@@ -210,18 +231,19 @@
     home_orb = orbitals[home_slot].reshape(slots, B, PLANE)
     part_orb = visitors[visit_slot].reshape(slots, B, PLANE)
     delta = offsets[home_slot] - visit_offsets[visit_slot]
-    to_home, to_partner = pair_fields(delta, live, home_orb, part_orb)
-
-    rows_out = 2 * slots
-    fields = jnp.concatenate([to_home, to_partner], axis=0).reshape(rows_out, cell_count)
     pair_total = lax.psum(1, "pair")
     chunk = cell_count // pair_total
     pair_me = lax.axis_index("pair")
-    targets = jnp.concatenate([home_slot, home_count + visit_slot]).astype(jnp.float32)
-    body = fields.reshape(rows_out, pair_total, chunk).transpose(1, 0, 2)
-    body = body[(pair_me + jnp.arange(pair_total, dtype=jnp.int32)) % pair_total]
-    tags = jnp.broadcast_to(targets[None, :, None], (pair_total, rows_out, extra))
-    payload = jnp.concatenate([body, tags], axis=2)
+    meta = jnp.concatenate(
+        [
+            delta.reshape(-1),
+            live,
+            home_slot,
+            home_count + visit_slot,
+            jnp.reshape(pair_me, (1,)).astype(jnp.int32),
+        ]
+    )
+    payload = pair_fields(meta, home_orb, part_orb, pair_total, chunk)
     got = exchange(payload, "pair")
     got_ids = got[:, :, chunk].astype(jnp.int32)
     all_rows = jnp.arange(home_count + slot_total, dtype=jnp.int32)

time: 58.1 us -> 56.9 us (0.979)
  other arithmetic: 4.17 us -> 1.57 us
  waiting for transfers between devices: 11.9 us -> 12.6 us
    squeeze x0 -> x1, local copies, waits for them, and re-layouts: none -> 1.37 us  [exchange(): received.append(lax.ppermute(blocks[step], axis, pairs))]
    concatenate x1 -> x0, other arithmetic: 1.27 us -> none  [per_device(): jnp.concatenate([to_home, to_partner], axis=0).reshape(rows_out, cell_count)]
    another operation x2 -> x0, local copies, waits for them, and re-layouts: 1.09 us -> none  [per_device(): body = fields.reshape(rows_out, pair_total, chunk).transpose(1, 0, 2)]
    ppermute x13, waiting for transfers between devices: 11.9 us -> 12.6 us  [exchange(): received.append(lax.ppermute(blocks[step], axis, pairs))]
    gather x1 -> x0, local copies, waits for them, and re-layouts: 0.62 us -> none  [per_device(): body[(pair_me + jnp.arange(pair_total, dtype=jnp.int32)) % pair_total]]
    concatenate x0 -> x1, local copies, waits for them, and re-layouts: none -> 0.61 us  [per_device(): jnp.concatenate([delta.reshape(-1), live, home_slot, home_count + visit_s...]
    sub x1, other arithmetic: 0.6 us -> 0.01 us  [per_device(): delta = offsets[home_slot] - visit_offsets[visit_slot]]
    unnamed x16 -> x15, local copies, waits for them, and re-layouts: 2.52 us -> 2.4 us
  transfers between devices with their start and end apart: 13 -> 13, of which waited for: 7 -> 7; matrix products, arithmetic and copies ran while one was open for 6% -> 5% of each run, Pallas kernels for 0% -> 0%
where the time goes in v5:
time: 56.9 us; the launch traced here: 56.7 us
  starting transfers between devices  21.4 us (38%)
  waiting for transfers between devices  12.6 us (22%)
  local copies, waits for them, and re-layouts  11.9 us (21%)
  Pallas kernels  6.12 us (11%)
  matrix products  2.18 us (4%)
  other arithmetic  1.57 us (3%)
  between operations  0.91 us (2%)
    ppermute x13, starting transfers between devices, exchange(): received.append(lax.ppermute(blocks[step], axis, pairs))  21.4 us
    ppermute x13, waiting for transfers between devices, exchange(): received.append(lax.ppermute(blocks[step], axis, pairs))  12.6 us
    pallas_call x1, Pallas kernels, pair_fields(): pl.pallas_call(pair_kernel, out_shape=box, in_specs=[smem] + [vmem] * 7,...  6.12 us
    unnamed x15, local copies, waits for them, and re-layouts  2.4 us
    gather x1, local copies, waits for them, and re-layouts, per_device(): chosen = sends[0][ahead]  1.38 us
    squeeze x1, local copies, waits for them, and re-layouts, exchange(): received.append(lax.ppermute(blocks[step], axis, pairs))  1.37 us
  transfers between devices with their start and end apart: 13, of which 7 were waited for; matrix products, arithmetic and copies ran while one was open for 5% of the time, Pallas kernels for 0%

profile of v5, /device:TPU:0, one launch (start us, length us, event | category | flops | bytes accessed | tf_op | source)
XLA Modules:
  0.0 56.7 jit_solution(17346818322011355995)
XLA Ops:
  0.0 1.4 %gather_fusion.1 = s32[4]{0:T(128)S(1)} fusion(s32[4]{0:T(128)} %bitcast.77, s32[1024]{0:T(1024)S(1)} %pad_clamp_fusion.3), kind=kCustom, calls=%fused_computation.1 | custom fusion | bytes 48 | tf_op jit(solution)/shard_map/gather | solution.py:213
  1.4 0.7 %fusion.16 = s32[4]{0:T(128)S(1)} fusion(s32[1,1,4]{2,1,0:T(1,128)} %param.15, s32[]{:T(128)S(6)} %axis_index.23), kind=kLoop, calls=%fused_computation.77 | loop fusion | flops 60 | bytes 36 | tf_op jit(solution)/shard_map/select_n | solution.py:233
  2.1 0.8 %copy.16 = s32[16,3]{1,0:T(8,128)S(1)} copy(s32[16,3]{0,1:T(4,128)} %param.12) | data formatting | bytes 384 | tf_op args[1]
  3.4 0.8 %gather_fusion.2 = bf16[4,32768]{1,0:T(4,128)(2,1)S(1)} fusion(bf16[16,32768]{1,0:T(8,128)(2,1)S(1)} %copy-done, s32[1024]{0:T(1024)S(1)} %get-tuple-element.22), kind=kCustom, calls=%fused_computation.2 | custom fusion | bytes 524304 | tf_op jit(solution)/shard_map/gather | solution.py:217
  4.8 3.1 %collective-permute-start = (bf16[1,32896]{1,0:T(2,128)(2,1)S(1)}, bf16[1,32896]{1,0:T(2,128)(2,1)S(1)}, u32[]{:S(2)}, u32[]{:S(2)}) collective-permute-start(bf16[1,32896]{1,0:T(2,128)(2,1)S(1)} %get-tuple-element.16), channel_id=1, source_target_pairs={{0,8},{8,16},{16,24},{24,0},{1,9},{9,17},{17,25},{25,1},{2,10},{10... | collective-permute-start | bytes 197384 | tf_op jit(solution)/shard_map/ppermute | solution.py:199
  7.9 2.6 %collective-permute-start.1 = (bf16[1,32896]{1,0:T(2,128)(2,1)S(1)}, bf16[1,32896]{1,0:T(2,128)(2,1)S(1)}, u32[]{:S(2)}, u32[]{:S(2)}) collective-permute-start(bf16[1,32896]{1,0:T(2,128)(2,1)S(1)} %get-tuple-element.15), channel_id=1, source_target_pairs={{0,16},{8,24},{16,0},{24,8},{1,17},{9,25},{17,1},{25,9},{2,18},{10... | collective-permute-start | bytes 197384 | tf_op jit(solution)/shard_map/ppermute | solution.py:199
  10.4 1.3 %collective-permute-start.2 = (bf16[1,32896]{1,0:T(2,128)(2,1)S(1)}, bf16[1,32896]{1,0:T(2,128)(2,1)S(1)}, u32[]{:S(2)}, u32[]{:S(2)}) collective-permute-start(bf16[1,32896]{1,0:T(2,128)(2,1)S(1)} %get-tuple-element.14), channel_id=1, source_target_pairs={{0,24},{8,0},{16,8},{24,16},{1,25},{9,1},{17,9},{25,17},{2,26},{10... | collective-permute-start | bytes 197384 | tf_op jit(solution)/shard_map/ppermute | solution.py:199
  12.4 0.8 %gather_fusion.5 = bf16[4,32768]{1,0:T(4,128)(2,1)S(1)} fusion(bf16[16,32768]{1,0:T(8,128)(2,1)S(1)} %copy-done, s32[1024]{0:T(1024)S(1)} %pad_clamp_fusion.4), kind=kCustom, calls=%fused_computation.5 | custom fusion | bytes 524304 | tf_op jit(solution)/shard_map/gather | solution.py:231
  13.8 0.8 %copy.33 = bf16[1,4,32,1024]{3,2,1,0:T(8,128)(2,1)} copy(bf16[1,4,32,1024]{3,1,2,0:T(4,128)(2,1)S(1)} %bitcast.80) | data formatting | bytes 524288
  14.6 4.5 %collective-permute-done.1 = bf16[1,32896]{1,0:T(2,128)(2,1)S(1)} collective-permute-done((bf16[1,32896]{1,0:T(2,128)(2,1)S(1)}, bf16[1,32896]{1,0:T(2,128)(2,1)S(1)}, u32[]{:S(2)}, u32[]{:S(2)}) %collective-permute-start.1) | collective-permute-done | bytes 65824 | tf_op jit(solution)/shard_map/ppermute | solution.py:199
  19.1 0.6 %maximum_bitcast_fusion = bf16[4,32896]{1,0:T(4,128)(2,1)S(1)} fusion(bf16[1,1,32896]{2,0,1:T(2,128)(2,1)S(1)} %bitcast.84, bf16[1,1,32896]{2,0,1:T(2,128)(2,1)S(1)} %bitcast.83, bf16[1,1,32896]{2,0,1:T(2,128)(2,1)S(1)} %bitcast.82, bf16[1,1,32896]{2,0,1:T(2,128)(2,1)S(1)} %get-tuple-element.13), kind=kLoop, calls=%fused_computation.15 | loop fusion | flops 1052672 | bytes 526336 | tf_op jit(solution)/shard_map/reshape | solution.py:222
  20.5 0.8 %gather_fusion.6 = bf16[4,32768]{1,0:T(4,128)(2,1)S(1)} fusion(bf16[4,32768]{1,0:T(4,128)(2,1)S(1)} %slice.125, s32[1024]{0:T(1024)S(1)} %get-tuple-element.21), kind=kCustom, calls=%fused_computation.6 | custom fusion | bytes 524304 | tf_op jit(solution)/shard_map/gather | solution.py:232
  21.3 0.8 %copy.32 = bf16[1,4,32,1024]{3,2,1,0:T(8,128)(2,1)} copy(bf16[1,4,32,1024]{3,1,2,0:T(4,128)(2,1)S(1)} %bitcast.81) | data formatting | bytes 524288
  22.1 0.6 %concatenate.7.meta_ref = s32[25]{0:T(128)} concatenate(s32[12]{0:T(128)S(1)} %sub.29, s32[4]{0:T(128)S(1)} %compare_convert_fusion, s32[4]{0:T(128)S(1)} %bitcast.89, s32[4]{0:T(128)S(1)} %fusion.9, s32[1]{0:T(128)} %bitcast.16), dimensions={0} | concatenate | bytes 200 | tf_op jit(solution)/shard_map/concatenate | solution.py:237
  22.7 6.1 %shard_map.109 = f32[8,8,4224]{2,1,0:T(8,128)} custom-call(s32[25]{0:T(128)} %concatenate.7.meta_ref, bf16[4,32,1024]{2,1,0:T(8,128)(2,1)} %bitcast.78, bf16[4,32,1024]{2,1,0:T(8,128)(2,1)} %bitcast.79, f32[32,1024]{1,0:T(8,128)} %constant.75.clone.tiled_ref, f32[32,1024]{1,0:T(8,128)} %constant.76.clone.spread_ref, ...), custom_call_target="tpu_custom_call" | custom-call | tf_op jit(solution)/shard_map/pallas_call | solution.py:180
  28.8 1.4 %slice_bitcast_fusion = (f32[8,4224]{1,0:T(8,128)S(1)}, f32[8,4224]{1,0:T(8,128)S(1)}, f32[8,4224]{1,0:T(8,128)S(1)}, f32[8,4224]{1,0:T(8,128)S(1)}, f32[8,4224]...) fusion(f32[8,8,4224]{2,1,0:T(8,128)} %shard_map.109), kind=kLoop, calls=%fused_computation.18 | loop fusion | bytes 2162688 | tf_op jit(solution)/shard_map/squeeze | solution.py:199
  30.3 1.5 %collective-permute-start.4 = (f32[8,4224]{1,0:T(8,128)S(1)}, f32[8,4224]{1,0:T(8,128)S(1)}, u32[]{:S(2)}, u32[]{:S(2)}) collective-permute-start(f32[8,4224]{1,0:T(8,128)S(1)} %get-tuple-element.10), channel_id=1, source_target_pairs={{0,2},{1,3},{2,4},{3,5},{4,6},{5,7},{6,0},{7,1},{8,10},{9,11},{10,... | collective-permute-start | bytes 405512 | tf_op jit(solution)/shard_map/ppermute | solution.py:199
  31.8 2.4 %collective-permute-start.5 = (f32[8,4224]{1,0:T(8,128)S(1)}, f32[8,4224]{1,0:T(8,128)S(1)}, u32[]{:S(2)}, u32[]{:S(2)}) collective-permute-start(f32[8,4224]{1,0:T(8,128)S(1)} %get-tuple-element.9), channel_id=1, source_target_pairs={{0,3},{1,4},{2,5},{3,6},{4,7},{5,0},{6,1},{7,2},{8,11},{9,12},{10,... | collective-permute-start | bytes 405512 | tf_op jit(solution)/shard_map/ppermute | solution.py:199
  34.8 1.7 %collective-permute-done.3 = f32[8,4224]{1,0:T(8,128)S(1)} collective-permute-done((f32[8,4224]{1,0:T(8,128)S(1)}, f32[8,4224]{1,0:T(8,128)S(1)}, u32[]{:S(2)}, u32[]{:S(2)}) %collective-permute-start.3) | collective-permute-done | bytes 135200 | tf_op jit(solution)/shard_map/ppermute | solution.py:199
  36.5 1.5 %collective-permute-start.8 = (f32[8,4224]{1,0:T(8,128)S(1)}, f32[8,4224]{1,0:T(8,128)S(1)}, u32[]{:S(2)}, u32[]{:S(2)}) collective-permute-start(f32[8,4224]{1,0:T(8,128)S(1)} %get-tuple-element.6), channel_id=1, source_target_pairs={{0,6},{1,7},{2,0},{3,1},{4,2},{5,3},{6,4},{7,5},{8,14},{9,15},{10,... | collective-permute-start | bytes 405512 | tf_op jit(solution)/shard_map/ppermute | solution.py:199
  38.0 2.6 %collective-permute-start.9 = (f32[8,4224]{1,0:T(8,128)S(1)}, f32[8,4224]{1,0:T(8,128)S(1)}, u32[]{:S(2)}, u32[]{:S(2)}) collective-permute-start(f32[8,4224]{1,0:T(8,128)S(1)} %get-tuple-element.5), channel_id=1, source_target_pairs={{0,7},{1,0},{2,1},{3,2},{4,3},{5,4},{6,5},{7,6},{8,15},{9,8},{10,9... | collective-permute-start | bytes 405512 | tf_op jit(solution)/shard_map/ppermute | solution.py:199
  40.6 2.1 %collective-permute-done.5 = f32[8,4224]{1,0:T(8,128)S(1)} collective-permute-done((f32[8,4224]{1,0:T(8,128)S(1)}, f32[8,4224]{1,0:T(8,128)S(1)}, u32[]{:S(2)}, u32[]{:S(2)}) %collective-permute-start.5) | collective-permute-done | bytes 135200 | tf_op jit(solution)/shard_map/ppermute | solution.py:199
  42.9 1.8 %collective-permute-done.7 = f32[8,4224]{1,0:T(8,128)S(1)} collective-permute-done((f32[8,4224]{1,0:T(8,128)S(1)}, f32[8,4224]{1,0:T(8,128)S(1)}, u32[]{:S(2)}, u32[]{:S(2)}) %collective-permute-start.7) | collective-permute-done | bytes 135200 | tf_op jit(solution)/shard_map/ppermute | solution.py:199
  45.1 1.0 %convolution_bitcast_fusion = f32[20,4096]{1,0:T(8,128)S(1)} fusion(f32[8,8,4096]{2,1,0:T(8,128)S(1)} %slice.135, s32[8,8]{0,1:T(8,128)S(1)} %bitcast.85), kind=kOutput, calls=%fused_computation.9 | convolution fusion | flops 62915840 | bytes 1376512 | tf_op jit(solution)/shard_map/srk,srl->kl/dot_general | solution.py:251
  46.1 0.6 %gather_fusion.8 = f32[4,4096]{1,0:T(4,128)S(1)} fusion(f32[4,4096]{1,0:T(4,128)S(1)} %slice.137, s32[1024]{0:T(1024)S(1)} %pad_clamp_fusion), kind=kCustom, calls=%fused_computation.8 | custom fusion | bytes 131088 | tf_op jit(solution)/shard_map/gather | solution.py:255
  46.8 3.3 %collective-permute-start.10 = (f32[1,4096]{1,0:T(1,128)S(1)}, f32[1,4096]{1,0:T(1,128)S(1)}, u32[]{:S(2)}, u32[]{:S(2)}) collective-permute-start(f32[1,4096]{1,0:T(1,128)S(1)} %get-tuple-element.19), channel_id=1, source_target_pairs={{0,8},{8,16},{16,24},{24,0},{1,9},{9,17},{17,25},{25,1},{2,10},{10... | collective-permute-start | bytes 49160 | tf_op jit(solution)/shard_map/ppermute | solution.py:199
  50.1 1.6 %collective-permute-start.11 = (f32[1,4096]{1,0:T(1,128)S(1)}, f32[1,4096]{1,0:T(1,128)S(1)}, u32[]{:S(2)}, u32[]{:S(2)}) collective-permute-start(f32[1,4096]{1,0:T(1,128)S(1)} %get-tuple-element.18), channel_id=1, source_target_pairs={{0,16},{8,24},{16,0},{24,8},{1,17},{9,25},{17,1},{25,9},{2,18},{10... | collective-permute-start | bytes 49160 | tf_op jit(solution)/shard_map/ppermute | solution.py:199
  51.8 0.8 %collective-permute-start.12 = (f32[1,4096]{1,0:T(1,128)S(1)}, f32[1,4096]{1,0:T(1,128)S(1)}, u32[]{:S(2)}, u32[]{:S(2)}) collective-permute-start(f32[1,4096]{1,0:T(1,128)S(1)} %get-tuple-element.20), channel_id=1, source_target_pairs={{0,24},{8,0},{16,8},{24,16},{1,25},{9,1},{17,9},{25,17},{2,26},{10... | collective-permute-start | bytes 49160 | tf_op jit(solution)/shard_map/ppermute | solution.py:199
  52.6 0.6 %gather_fusion.7 = s32[4]{0:T(128)S(1)} fusion(s32[4]{0:T(128)S(1)} %gather_fusion.1, s32[1024]{0:T(1024)S(1)} %pad_clamp_fusion), kind=kCustom, calls=%fused_computation.7 | custom fusion | bytes 48 | tf_op jit(solution)/shard_map/gather | solution.py:257
  53.2 1.7 %collective-permute-done.11 = f32[1,4096]{1,0:T(1,128)S(1)} collective-permute-done((f32[1,4096]{1,0:T(1,128)S(1)}, f32[1,4096]{1,0:T(1,128)S(1)}, u32[]{:S(2)}, u32[]{:S(2)}) %collective-permute-start.11) | collective-permute-done | bytes 16416 | tf_op jit(solution)/shard_map/ppermute | solution.py:199
  54.9 0.6 collective-permute-done.12
  55.6 1.1 %convolution_add_fusion = f32[16,4096]{1,0:T(8,128)} fusion(f32[20,4096]{1,0:T(8,128)S(1)} %convolution_bitcast_fusion, f32[4,1,4096]{2,1,0:T(1,128)S(1)} %pad_maximum_fusion, s32[4]{0:T(128)S(1)} %gather_fusion.7), kind=kOutput, calls=%fused_computation.10 | convolution fusion | flops 3211328 | bytes 589840 | tf_op jit(solution)/shard_map/dot_general | solution.py:261
  (49 shorter events, 3.7 us)
Async XLA Ops:
  0.0 3.4 %copy-start = (bf16[16,32768]{1,0:T(8,128)(2,1)S(1)}, bf16[16,32768]{1,0:T(8,128)(2,1)}, u32[]{:S(2)}) copy-start(bf16[16,32768]{1,0:T(8,128)(2,1)} %param.11) | copy-start | bytes 3145732
  4.2 7.6 %copy-start.2 = (s32[1,1,4]{2,1,0:T(1,128)S(1)}, s32[1,1,4]{2,1,0:T(1,128)}, u32[]{:S(2)}) copy-start(s32[1,1,4]{2,1,0:T(1,128)} %param.15) | copy-start | bytes 52
  4.2 7.6 %copy-start.1 = (s32[1,1,4]{2,1,0:T(1,128)S(1)}, s32[1,1,4]{2,1,0:T(1,128)}, u32[]{:S(2)}) copy-start(s32[1,1,4]{2,1,0:T(1,128)} %param.14) | copy-start | bytes 52
  4.8 9.9 %collective-permute-start = (bf16[1,32896]{1,0:T(2,128)(2,1)S(1)}, bf16[1,32896]{1,0:T(2,128)(2,1)S(1)}, u32[]{:S(2)}, u32[]{:S(2)}) collective-permute-start(bf16[1,32896]{1,0:T(2,128)(2,1)S(1)} %get-tuple-element.16), channel_id=1, source_target_pairs={{0,8},{8,16},{16,24},{24,0},{1,9},{9,17},{17,25},{25,1},{2,10},{10... | collective-permute-start | bytes 197384 | tf_op jit(solution)/shard_map/ppermute | solution.py:199
  7.9 11.3 %collective-permute-start.1 = (bf16[1,32896]{1,0:T(2,128)(2,1)S(1)}, bf16[1,32896]{1,0:T(2,128)(2,1)S(1)}, u32[]{:S(2)}, u32[]{:S(2)}) collective-permute-start(bf16[1,32896]{1,0:T(2,128)(2,1)S(1)} %get-tuple-element.15), channel_id=1, source_target_pairs={{0,16},{8,24},{16,0},{24,8},{1,17},{9,25},{17,1},{25,9},{2,18},{10... | collective-permute-start | bytes 197384 | tf_op jit(solution)/shard_map/ppermute | solution.py:199
  10.4 8.7 %collective-permute-start.2 = (bf16[1,32896]{1,0:T(2,128)(2,1)S(1)}, bf16[1,32896]{1,0:T(2,128)(2,1)S(1)}, u32[]{:S(2)}, u32[]{:S(2)}) collective-permute-start(bf16[1,32896]{1,0:T(2,128)(2,1)S(1)} %get-tuple-element.14), channel_id=1, source_target_pairs={{0,24},{8,0},{16,8},{24,16},{1,25},{9,1},{17,9},{25,17},{2,26},{10... | collective-permute-start | bytes 197384 | tf_op jit(solution)/shard_map/ppermute | solution.py:199
  30.2 6.3 %collective-permute-start.3 = (f32[8,4224]{1,0:T(8,128)S(1)}, f32[8,4224]{1,0:T(8,128)S(1)}, u32[]{:S(2)}, u32[]{:S(2)}) collective-permute-start(f32[8,4224]{1,0:T(8,128)S(1)} %get-tuple-element.11), channel_id=1, source_target_pairs={{0,1},{1,2},{2,3},{3,4},{4,5},{5,6},{6,7},{7,0},{8,9},{9,10},{10,1... | collective-permute-start | bytes 405512 | tf_op jit(solution)/shard_map/ppermute | solution.py:199
  30.3 7.7 %collective-permute-start.4 = (f32[8,4224]{1,0:T(8,128)S(1)}, f32[8,4224]{1,0:T(8,128)S(1)}, u32[]{:S(2)}, u32[]{:S(2)}) collective-permute-start(f32[8,4224]{1,0:T(8,128)S(1)} %get-tuple-element.10), channel_id=1, source_target_pairs={{0,2},{1,3},{2,4},{3,5},{4,6},{5,7},{6,0},{7,1},{8,10},{9,11},{10,... | collective-permute-start | bytes 405512 | tf_op jit(solution)/shard_map/ppermute | solution.py:199
  31.8 10.9 %collective-permute-start.5 = (f32[8,4224]{1,0:T(8,128)S(1)}, f32[8,4224]{1,0:T(8,128)S(1)}, u32[]{:S(2)}, u32[]{:S(2)}) collective-permute-start(f32[8,4224]{1,0:T(8,128)S(1)} %get-tuple-element.9), channel_id=1, source_target_pairs={{0,3},{1,4},{2,5},{3,6},{4,7},{5,0},{6,1},{7,2},{8,11},{9,12},{10,... | collective-permute-start | bytes 405512 | tf_op jit(solution)/shard_map/ppermute | solution.py:199
  34.2 8.7 %collective-permute-start.6 = (f32[8,4224]{1,0:T(8,128)S(1)}, f32[8,4224]{1,0:T(8,128)S(1)}, u32[]{:S(2)}, u32[]{:S(2)}) collective-permute-start(f32[8,4224]{1,0:T(8,128)S(1)} %get-tuple-element.8), channel_id=1, source_target_pairs={{0,4},{1,5},{2,6},{3,7},{4,0},{5,1},{6,2},{7,3},{8,12},{9,13},{10,... | collective-permute-start | bytes 405512 | tf_op jit(solution)/shard_map/ppermute | solution.py:199
  34.8 10.0 %collective-permute-start.7 = (f32[8,4224]{1,0:T(8,128)S(1)}, f32[8,4224]{1,0:T(8,128)S(1)}, u32[]{:S(2)}, u32[]{:S(2)}) collective-permute-start(f32[8,4224]{1,0:T(8,128)S(1)} %get-tuple-element.7), channel_id=1, source_target_pairs={{0,5},{1,6},{2,7},{3,0},{4,1},{5,2},{6,3},{7,4},{8,13},{9,14},{10,... | collective-permute-start | bytes 405512 | tf_op jit(solution)/shard_map/ppermute | solution.py:199
  36.5 8.3 %collective-permute-start.8 = (f32[8,4224]{1,0:T(8,128)S(1)}, f32[8,4224]{1,0:T(8,128)S(1)}, u32[]{:S(2)}, u32[]{:S(2)}) collective-permute-start(f32[8,4224]{1,0:T(8,128)S(1)} %get-tuple-element.6), channel_id=1, source_target_pairs={{0,6},{1,7},{2,0},{3,1},{4,2},{5,3},{6,4},{7,5},{8,14},{9,15},{10,... | collective-permute-start | bytes 405512 | tf_op jit(solution)/shard_map/ppermute | solution.py:199
  38.0 6.8 %collective-permute-start.9 = (f32[8,4224]{1,0:T(8,128)S(1)}, f32[8,4224]{1,0:T(8,128)S(1)}, u32[]{:S(2)}, u32[]{:S(2)}) collective-permute-start(f32[8,4224]{1,0:T(8,128)S(1)} %get-tuple-element.5), channel_id=1, source_target_pairs={{0,7},{1,0},{2,1},{3,2},{4,3},{5,4},{6,5},{7,6},{8,15},{9,8},{10,9... | collective-permute-start | bytes 405512 | tf_op jit(solution)/shard_map/ppermute | solution.py:199
  46.8 6.4 %collective-permute-start.10 = (f32[1,4096]{1,0:T(1,128)S(1)}, f32[1,4096]{1,0:T(1,128)S(1)}, u32[]{:S(2)}, u32[]{:S(2)}) collective-permute-start(f32[1,4096]{1,0:T(1,128)S(1)} %get-tuple-element.19), channel_id=1, source_target_pairs={{0,8},{8,16},{16,24},{24,0},{1,9},{9,17},{17,25},{25,1},{2,10},{10... | collective-permute-start | bytes 49160 | tf_op jit(solution)/shard_map/ppermute | solution.py:199
  50.1 4.8 %collective-permute-start.11 = (f32[1,4096]{1,0:T(1,128)S(1)}, f32[1,4096]{1,0:T(1,128)S(1)}, u32[]{:S(2)}, u32[]{:S(2)}) collective-permute-start(f32[1,4096]{1,0:T(1,128)S(1)} %get-tuple-element.18), channel_id=1, source_target_pairs={{0,16},{8,24},{16,0},{24,8},{1,17},{9,25},{17,1},{25,9},{2,18},{10... | collective-permute-start | bytes 49160 | tf_op jit(solution)/shard_map/ppermute | solution.py:199
  51.8 3.7 %collective-permute-start.12 = (f32[1,4096]{1,0:T(1,128)S(1)}, f32[1,4096]{1,0:T(1,128)S(1)}, u32[]{:S(2)}, u32[]{:S(2)}) collective-permute-start(f32[1,4096]{1,0:T(1,128)S(1)} %get-tuple-element.20), channel_id=1, source_target_pairs={{0,24},{8,0},{16,8},{24,16},{1,25},{9,1},{17,9},{25,17},{2,26},{10... | collective-permute-start | bytes 49160 | tf_op jit(solution)/shard_map/ppermute | solution.py:199

commit v6 on v5

--- a/solution.py
+++ b/solution.py
@@ -80,7 +80,10 @@
     count, _, width = payload_ref.shape
     chunk = width - 128
     for index in range(count):
-        place = lax.rem(index - me + count, count)
+        if flips(count):
+            place = lax.bitwise_xor(me, jnp.int32(index))
+        else:
+            place = lax.rem(index - me + count, count)
         if chunk >= PLANE:
             per = chunk // PLANE
             for part in range(per):
@@ -191,11 +194,21 @@
     )(meta, home, part, tiled, spread, rows_high, rows_low, eigen)
 
 
+def flips(count):
+    return count & (count - 1) == 0
+
+
+def toward(index, step, count):
+    if flips(count):
+        return index ^ step
+    return (index + step) % count
+
+
 def exchange(blocks, axis):
     count = blocks.shape[0]
     received = [blocks[0]]
     for step in range(1, count):
-        pairs = [(source, (source + step) % count) for source in range(count)]
+        pairs = [(source, toward(source, step, count)) for source in range(count)]
         received.append(lax.ppermute(blocks[step], axis, pairs))
     return jnp.stack(received)
 
@@ -209,7 +222,11 @@
     slots = pair_home.shape[2]
     extra = 128
     me = lax.axis_index("home")
-    ahead = (me + jnp.arange(section_total, dtype=jnp.int32)) % section_total
+    steps = jnp.arange(section_total, dtype=jnp.int32)
+    if flips(section_total):
+        ahead = me ^ steps
+    else:
+        ahead = (me + steps) % section_total
     chosen = sends[0][ahead]
     flat_chosen = chosen.reshape(-1)
     outgoing = jnp.concatenate(
@@ -226,7 +243,11 @@
     home_slot = pair_home[0, 0]
     visit_code = pair_visit[0, 0]
     source = visit_code // per_target
-    visit_slot = ((me - source) % section_total) * per_target + visit_code % per_target
+    if flips(section_total):
+        arrival = me ^ source
+    else:
+        arrival = (me - source) % section_total
+    visit_slot = arrival * per_target + visit_code % per_target
     live = (jnp.arange(slots, dtype=jnp.int32) < pair_count[0, 0]).astype(jnp.int32)
     home_orb = orbitals[home_slot].reshape(slots, B, PLANE)
     part_orb = visitors[visit_slot].reshape(slots, B, PLANE)
@@ -250,9 +271,15 @@
     picker = (got_ids[:, :, None] == all_rows[None, None, :]).astype(jnp.float32)
     totals = jnp.einsum("srk,srl->kl", picker, got[:, :, :chunk], precision=PRECISE)
     home_totals = totals[:home_count]
-    back = (-jnp.arange(section_total, dtype=jnp.int32)) % section_total
+    if flips(section_total):
+        back = steps
+    else:
+        back = (-steps) % section_total
     back_rows = (back[:, None] * per_target + jnp.arange(per_target)[None, :]).reshape(-1)
-    visit_totals = totals[home_count:][back_rows].reshape(section_total, per_target, chunk)
+    visit_totals = totals[home_count:]
+    if not flips(section_total):
+        visit_totals = visit_totals[back_rows]
+    visit_totals = visit_totals.reshape(section_total, per_target, chunk)
     returned = exchange(visit_totals, "home").reshape(slot_total, chunk)
     owners = chosen[back].reshape(-1)
     chooser = (owners[:, None] == jnp.arange(home_count, dtype=jnp.int32)[None, :]).astype(

time: 56.9 us -> 60.8 us (1.069)
  waiting for transfers between devices: 12.6 us -> 21.6 us
  starting transfers between devices: 21.4 us -> 17 us
  local copies, waits for them, and re-layouts: 11.9 us -> 11.2 us
    ppermute x13, waiting for transfers between devices: 12.6 us -> 21.6 us  [exchange(): received.append(lax.ppermute(blocks[step], axis, pairs))]
    ppermute x13, starting transfers between devices: 21.4 us -> 17 us  [exchange(): received.append(lax.ppermute(blocks[step], axis, pairs))]
  transfers between devices with their start and end apart: 13 -> 13, of which waited for: 7 -> 6; matrix products, arithmetic and copies ran while one was open for 5% -> 5% of each run, Pallas kernels for 0% -> 0%
where the time goes in v6:
time: 60.8 us; the launch traced here: 60.6 us
  waiting for transfers between devices  21.6 us (36%)
  starting transfers between devices  17 us (28%)
  local copies, waits for them, and re-layouts  11.2 us (18%)
  Pallas kernels  6.12 us (10%)
  matrix products  2.18 us (4%)
  other arithmetic  1.62 us (3%)
  between operations  0.9 us (1%)
    ppermute x13, waiting for transfers between devices, exchange(): received.append(lax.ppermute(blocks[step], axis, pairs))  21.6 us
    ppermute x13, starting transfers between devices, exchange(): received.append(lax.ppermute(blocks[step], axis, pairs))  17 us
    pallas_call x1, Pallas kernels, pair_fields(): pl.pallas_call(pair_kernel, out_shape=box, in_specs=[smem] + [vmem] * 7,...  6.12 us
    unnamed x15, local copies, waits for them, and re-layouts  2.41 us
    squeeze x1, local copies, waits for them, and re-layouts, exchange(): received.append(lax.ppermute(blocks[step], axis, pairs))  1.37 us
    gather x1, local copies, waits for them, and re-layouts, per_device(): chosen = sends[0][ahead]  1.29 us
  transfers between devices with their start and end apart: 13, of which 6 were waited for; matrix products, arithmetic and copies ran while one was open for 5% of the time, Pallas kernels for 0%

profile of v6, /device:TPU:0, one launch (start us, length us, event | category | flops | bytes accessed | tf_op | source)
XLA Modules:
  0.0 60.6 jit_solution(1574272785254918351)
XLA Ops:
  0.0 0.7 %fusion.10 = s32[4]{0:T(128)S(1)} fusion(s32[1,1,4]{2,1,0:T(1,128)} %param.15, s32[]{:T(128)S(6)} %axis_index.23), kind=kLoop, calls=%fused_computation.56 | loop fusion | flops 16 | bytes 36 | tf_op jit(solution)/shard_map/select_n | solution.py:254
  0.8 1.3 %gather_fusion.1 = s32[4]{0:T(128)S(1)} fusion(s32[4]{0:T(128)} %bitcast.75, s32[1024]{0:T(1024)S(1)} %pad_clamp_fusion.3), kind=kCustom, calls=%fused_computation.1 | custom fusion | bytes 48 | tf_op jit(solution)/shard_map/gather | solution.py:230
  2.1 0.8 %copy.16 = s32[16,3]{1,0:T(8,128)S(1)} copy(s32[16,3]{0,1:T(4,128)} %param.12) | data formatting | bytes 384 | tf_op args[1]
  2.8 0.6 gather_fusion.3
  3.4 0.8 %gather_fusion.2 = bf16[4,32768]{1,0:T(4,128)(2,1)S(1)} fusion(bf16[16,32768]{1,0:T(8,128)(2,1)S(1)} %copy-done, s32[1024]{0:T(1024)S(1)} %get-tuple-element.22), kind=kCustom, calls=%fused_computation.2 | custom fusion | bytes 524304 | tf_op jit(solution)/shard_map/gather | solution.py:234
  4.8 5.1 %collective-permute-start.2 = (bf16[1,32896]{1,0:T(2,128)(2,1)S(1)}, bf16[1,32896]{1,0:T(2,128)(2,1)S(1)}, u32[]{:S(2)}, u32[]{:S(2)}) collective-permute-start(bf16[1,32896]{1,0:T(2,128)(2,1)S(1)} %get-tuple-element.18), channel_id=1, source_target_pairs={{0,24},{8,16},{16,8},{24,0},{1,25},{9,17},{17,9},{25,1},{2,26},{10... | collective-permute-start | bytes 197384 | tf_op jit(solution)/shard_map/ppermute | solution.py:212
  9.9 0.6 %collective-permute-start = (bf16[1,32896]{1,0:T(2,128)(2,1)S(1)}, bf16[1,32896]{1,0:T(2,128)(2,1)S(1)}, u32[]{:S(2)}, u32[]{:S(2)}) collective-permute-start(bf16[1,32896]{1,0:T(2,128)(2,1)S(1)} %get-tuple-element.20), channel_id=1, source_target_pairs={{0,8},{8,0},{16,24},{24,16},{1,9},{9,1},{17,25},{25,17},{2,10},{10... | collective-permute-start | bytes 197384 | tf_op jit(solution)/shard_map/ppermute | solution.py:212
  10.6 0.6 gather_fusion
  11.1 0.8 %gather_fusion.5 = bf16[4,32768]{1,0:T(4,128)(2,1)S(1)} fusion(bf16[16,32768]{1,0:T(8,128)(2,1)S(1)} %copy-done, s32[1024]{0:T(1024)S(1)} %pad_clamp_fusion.4), kind=kCustom, calls=%fused_computation.5 | custom fusion | bytes 524304 | tf_op jit(solution)/shard_map/gather | solution.py:252
  12.6 0.8 %copy.33 = bf16[1,4,32,1024]{3,2,1,0:T(8,128)(2,1)} copy(bf16[1,4,32,1024]{3,1,2,0:T(4,128)(2,1)S(1)} %bitcast.79) | data formatting | bytes 524288
  13.4 1.0 %collective-permute-done.2 = bf16[1,32896]{1,0:T(2,128)(2,1)S(1)} collective-permute-done((bf16[1,32896]{1,0:T(2,128)(2,1)S(1)}, bf16[1,32896]{1,0:T(2,128)(2,1)S(1)}, u32[]{:S(2)}, u32[]{:S(2)}) %collective-permute-start.2) | collective-permute-done | bytes 65824 | tf_op jit(solution)/shard_map/ppermute | solution.py:212
  14.3 6.7 %collective-permute-done.1 = bf16[1,32896]{1,0:T(2,128)(2,1)S(1)} collective-permute-done((bf16[1,32896]{1,0:T(2,128)(2,1)S(1)}, bf16[1,32896]{1,0:T(2,128)(2,1)S(1)}, u32[]{:S(2)}, u32[]{:S(2)}) %collective-permute-start.1) | collective-permute-done | bytes 65824 | tf_op jit(solution)/shard_map/ppermute | solution.py:212
  21.0 0.6 %maximum_bitcast_fusion = bf16[4,32896]{1,0:T(4,128)(2,1)S(1)} fusion(bf16[1,1,32896]{2,0,1:T(2,128)(2,1)S(1)} %bitcast.80, bf16[1,1,32896]{2,0,1:T(2,128)(2,1)S(1)} %bitcast.81, bf16[1,1,32896]{2,0,1:T(2,128)(2,1)S(1)} %bitcast.82, bf16[1,1,32896]{2,0,1:T(2,128)(2,1)S(1)} %get-tuple-element.17), kind=kLoop, calls=%fused_computation.14 | loop fusion | flops 1052672 | bytes 526336 | tf_op jit(solution)/shard_map/reshape | solution.py:239
  21.7 0.8 %gather_fusion.6 = bf16[4,32768]{1,0:T(4,128)(2,1)S(1)} fusion(bf16[4,32768]{1,0:T(4,128)(2,1)S(1)} %slice.124, s32[1024]{0:T(1024)S(1)} %get-tuple-element.21), kind=kCustom, calls=%fused_computation.6 | custom fusion | bytes 524304 | tf_op jit(solution)/shard_map/gather | solution.py:253
  22.5 0.6 gather_fusion.4
  23.2 0.8 %copy.32 = bf16[1,4,32,1024]{3,2,1,0:T(8,128)(2,1)} copy(bf16[1,4,32,1024]{3,1,2,0:T(4,128)(2,1)S(1)} %bitcast.78) | data formatting | bytes 524288
  24.0 0.6 %concatenate.7.meta_ref = s32[25]{0:T(128)} concatenate(s32[12]{0:T(128)S(1)} %sub.10, s32[4]{0:T(128)S(1)} %compare_convert_fusion, s32[4]{0:T(128)S(1)} %bitcast.87, s32[4]{0:T(128)S(1)} %add_bitcast_fusion, s32[1]{0:T(128)} %bitcast.16), dimensions={0} | concatenate | bytes 200 | tf_op jit(solution)/shard_map/concatenate | solution.py:258
  24.6 6.1 %shard_map.109 = f32[8,8,4224]{2,1,0:T(8,128)} custom-call(s32[25]{0:T(128)} %concatenate.7.meta_ref, bf16[4,32,1024]{2,1,0:T(8,128)(2,1)} %bitcast.76, bf16[4,32,1024]{2,1,0:T(8,128)(2,1)} %bitcast.77, f32[32,1024]{1,0:T(8,128)} %constant.54.clone.tiled_ref, f32[32,1024]{1,0:T(8,128)} %constant.55.clone.spread_ref, ...), custom_call_target="tpu_custom_call" | custom-call | tf_op jit(solution)/shard_map/pallas_call | solution.py:183
  30.7 1.4 %slice_bitcast_fusion = (f32[8,4224]{1,0:T(8,128)S(1)}, f32[8,4224]{1,0:T(8,128)S(1)}, f32[8,4224]{1,0:T(8,128)S(1)}, f32[8,4224]{1,0:T(8,128)S(1)}, f32[8,4224]...) fusion(f32[8,8,4224]{2,1,0:T(8,128)} %shard_map.109), kind=kLoop, calls=%fused_computation.17 | loop fusion | bytes 2162688 | tf_op jit(solution)/shard_map/squeeze | solution.py:212
  32.2 2.6 %collective-permute-start.9 = (f32[8,4224]{1,0:T(8,128)S(1)}, f32[8,4224]{1,0:T(8,128)S(1)}, u32[]{:S(2)}, u32[]{:S(2)}) collective-permute-start(f32[8,4224]{1,0:T(8,128)S(1)} %get-tuple-element.5), channel_id=1, source_target_pairs={{0,7},{1,6},{2,5},{3,4},{4,3},{5,2},{6,1},{7,0},{8,15},{9,14},{10,... | collective-permute-start | bytes 405512 | tf_op jit(solution)/shard_map/ppermute | solution.py:212
  35.2 0.9 %collective-permute-start.7 = (f32[8,4224]{1,0:T(8,128)S(1)}, f32[8,4224]{1,0:T(8,128)S(1)}, u32[]{:S(2)}, u32[]{:S(2)}) collective-permute-start(f32[8,4224]{1,0:T(8,128)S(1)} %get-tuple-element.7), channel_id=1, source_target_pairs={{0,5},{1,4},{2,7},{3,6},{4,1},{5,0},{6,3},{7,2},{8,13},{9,12},{10,... | collective-permute-start | bytes 405512 | tf_op jit(solution)/shard_map/ppermute | solution.py:212
  36.1 0.6 %collective-permute-start.6 = (f32[8,4224]{1,0:T(8,128)S(1)}, f32[8,4224]{1,0:T(8,128)S(1)}, u32[]{:S(2)}, u32[]{:S(2)}) collective-permute-start(f32[8,4224]{1,0:T(8,128)S(1)} %get-tuple-element.8), channel_id=1, source_target_pairs={{0,4},{1,5},{2,6},{3,7},{4,0},{5,1},{6,2},{7,3},{8,12},{9,13},{10,... | collective-permute-start | bytes 405512 | tf_op jit(solution)/shard_map/ppermute | solution.py:212
  36.8 1.5 %collective-permute-start.4 = (f32[8,4224]{1,0:T(8,128)S(1)}, f32[8,4224]{1,0:T(8,128)S(1)}, u32[]{:S(2)}, u32[]{:S(2)}) collective-permute-start(f32[8,4224]{1,0:T(8,128)S(1)} %get-tuple-element.10), channel_id=1, source_target_pairs={{0,2},{1,3},{2,0},{3,1},{4,6},{5,7},{6,4},{7,5},{8,10},{9,11},{10,... | collective-permute-start | bytes 405512 | tf_op jit(solution)/shard_map/ppermute | solution.py:212
  38.3 6.7 %collective-permute-done.4 = f32[8,4224]{1,0:T(8,128)S(1)} collective-permute-done((f32[8,4224]{1,0:T(8,128)S(1)}, f32[8,4224]{1,0:T(8,128)S(1)}, u32[]{:S(2)}, u32[]{:S(2)}) %collective-permute-start.4) | collective-permute-done | bytes 135200 | tf_op jit(solution)/shard_map/ppermute | solution.py:212
  44.9 0.6 %collective-permute-start.5 = (f32[8,4224]{1,0:T(8,128)S(1)}, f32[8,4224]{1,0:T(8,128)S(1)}, u32[]{:S(2)}, u32[]{:S(2)}) collective-permute-start(f32[8,4224]{1,0:T(8,128)S(1)} %get-tuple-element.9), channel_id=1, source_target_pairs={{0,3},{1,2},{2,1},{3,0},{4,7},{5,6},{6,5},{7,4},{8,11},{9,10},{10,... | collective-permute-start | bytes 405512 | tf_op jit(solution)/shard_map/ppermute | solution.py:212
  45.5 5.2 %collective-permute-done.5 = f32[8,4224]{1,0:T(8,128)S(1)} collective-permute-done((f32[8,4224]{1,0:T(8,128)S(1)}, f32[8,4224]{1,0:T(8,128)S(1)}, u32[]{:S(2)}, u32[]{:S(2)}) %collective-permute-start.5) | collective-permute-done | bytes 135200 | tf_op jit(solution)/shard_map/ppermute | solution.py:212
  51.1 1.0 %convolution_bitcast_fusion = f32[20,4096]{1,0:T(8,128)S(1)} fusion(f32[8,8,4096]{2,1,0:T(8,128)S(1)} %slice.134, s32[8,8]{0,1:T(8,128)S(1)} %bitcast.83), kind=kOutput, calls=%fused_computation.8 | convolution fusion | flops 62915840 | bytes 1376512 | tf_op jit(solution)/shard_map/srk,srl->kl/dot_general | solution.py:272
  52.2 2.5 %collective-permute-start.12 = (f32[1,4096]{1,0:T(1,128)S(1)}, f32[1,4096]{1,0:T(1,128)S(1)}, u32[]{:S(2)}, u32[]{:S(2)}) collective-permute-start(f32[1,4096]{1,0:T(1,128)S(1)} %get-tuple-element.14), channel_id=1, source_target_pairs={{0,24},{8,16},{16,8},{24,0},{1,25},{9,17},{17,9},{25,1},{2,26},{10... | collective-permute-start | bytes 49160 | tf_op jit(solution)/shard_map/ppermute | solution.py:212
  54.8 1.9 %collective-permute-start.10 = (f32[1,4096]{1,0:T(1,128)S(1)}, f32[1,4096]{1,0:T(1,128)S(1)}, u32[]{:S(2)}, u32[]{:S(2)}) collective-permute-start(f32[1,4096]{1,0:T(1,128)S(1)} %get-tuple-element.16), channel_id=1, source_target_pairs={{0,8},{8,0},{16,24},{24,16},{1,9},{9,1},{17,25},{25,17},{2,10},{10... | collective-permute-start | bytes 49160 | tf_op jit(solution)/shard_map/ppermute | solution.py:212
  56.7 0.6 %gather_fusion.7 = s32[4]{0:T(128)S(1)} fusion(s32[4]{0:T(128)S(1)} %gather_fusion.1, s32[1024]{0:T(1024)S(1)} %pad_clamp_fusion), kind=kCustom, calls=%fused_computation.7 | custom fusion | bytes 48 | tf_op jit(solution)/shard_map/gather | solution.py:284
  57.8 1.6 %collective-permute-done.11 = f32[1,4096]{1,0:T(1,128)S(1)} collective-permute-done((f32[1,4096]{1,0:T(1,128)S(1)}, f32[1,4096]{1,0:T(1,128)S(1)}, u32[]{:S(2)}, u32[]{:S(2)}) %collective-permute-start.11) | collective-permute-done | bytes 16416 | tf_op jit(solution)/shard_map/ppermute | solution.py:212
  59.5 1.1 %convolution_add_fusion = f32[16,4096]{1,0:T(8,128)} fusion(f32[20,4096]{1,0:T(8,128)S(1)} %convolution_bitcast_fusion, f32[4,1,4096]{2,1,0:T(1,128)S(1)} %pad_maximum_fusion, s32[4]{0:T(128)S(1)} %gather_fusion.7), kind=kOutput, calls=%fused_computation.9 | convolution fusion | flops 3211328 | bytes 589840 | tf_op jit(solution)/shard_map/dot_general | solution.py:288
  (47 shorter events, 2.2 us)
Async XLA Ops:
  0.0 3.4 %copy-start = (bf16[16,32768]{1,0:T(8,128)(2,1)S(1)}, bf16[16,32768]{1,0:T(8,128)(2,1)}, u32[]{:S(2)}) copy-start(bf16[16,32768]{1,0:T(8,128)(2,1)} %param.11) | copy-start | bytes 3145732
  4.2 6.3 %copy-start.2 = (s32[1,1,4]{2,1,0:T(1,128)S(1)}, s32[1,1,4]{2,1,0:T(1,128)}, u32[]{:S(2)}) copy-start(s32[1,1,4]{2,1,0:T(1,128)} %param.15) | copy-start | bytes 52
  4.2 6.3 %copy-start.1 = (s32[1,1,4]{2,1,0:T(1,128)S(1)}, s32[1,1,4]{2,1,0:T(1,128)}, u32[]{:S(2)}) copy-start(s32[1,1,4]{2,1,0:T(1,128)} %param.14) | copy-start | bytes 52
  4.8 9.6 %collective-permute-start.2 = (bf16[1,32896]{1,0:T(2,128)(2,1)S(1)}, bf16[1,32896]{1,0:T(2,128)(2,1)S(1)}, u32[]{:S(2)}, u32[]{:S(2)}) collective-permute-start(bf16[1,32896]{1,0:T(2,128)(2,1)S(1)} %get-tuple-element.18), channel_id=1, source_target_pairs={{0,24},{8,16},{16,8},{24,0},{1,25},{9,17},{17,9},{25,1},{2,26},{10... | collective-permute-start | bytes 197384 | tf_op jit(solution)/shard_map/ppermute | solution.py:212
  9.9 11.1 %collective-permute-start.1 = (bf16[1,32896]{1,0:T(2,128)(2,1)S(1)}, bf16[1,32896]{1,0:T(2,128)(2,1)S(1)}, u32[]{:S(2)}, u32[]{:S(2)}) collective-permute-start(bf16[1,32896]{1,0:T(2,128)(2,1)S(1)} %get-tuple-element.19), channel_id=1, source_target_pairs={{0,16},{8,24},{16,0},{24,8},{1,17},{9,25},{17,1},{25,9},{2,18},{10... | collective-permute-start | bytes 197384 | tf_op jit(solution)/shard_map/ppermute | solution.py:212
  9.9 11.1 %collective-permute-start = (bf16[1,32896]{1,0:T(2,128)(2,1)S(1)}, bf16[1,32896]{1,0:T(2,128)(2,1)S(1)}, u32[]{:S(2)}, u32[]{:S(2)}) collective-permute-start(bf16[1,32896]{1,0:T(2,128)(2,1)S(1)} %get-tuple-element.20), channel_id=1, source_target_pairs={{0,8},{8,0},{16,24},{24,16},{1,9},{9,1},{17,25},{25,17},{2,10},{10... | collective-permute-start | bytes 197384 | tf_op jit(solution)/shard_map/ppermute | solution.py:212
  32.1 4.7 %collective-permute-start.3 = (f32[8,4224]{1,0:T(8,128)S(1)}, f32[8,4224]{1,0:T(8,128)S(1)}, u32[]{:S(2)}, u32[]{:S(2)}) collective-permute-start(f32[8,4224]{1,0:T(8,128)S(1)} %get-tuple-element.11), channel_id=1, source_target_pairs={{0,1},{1,0},{2,3},{3,2},{4,5},{5,4},{6,7},{7,6},{8,9},{9,8},{10,11... | collective-permute-start | bytes 405512 | tf_op jit(solution)/shard_map/ppermute | solution.py:212
  32.2 18.7 %collective-permute-start.9 = (f32[8,4224]{1,0:T(8,128)S(1)}, f32[8,4224]{1,0:T(8,128)S(1)}, u32[]{:S(2)}, u32[]{:S(2)}) collective-permute-start(f32[8,4224]{1,0:T(8,128)S(1)} %get-tuple-element.5), channel_id=1, source_target_pairs={{0,7},{1,6},{2,5},{3,4},{4,3},{5,2},{6,1},{7,0},{8,15},{9,14},{10,... | collective-permute-start | bytes 405512 | tf_op jit(solution)/shard_map/ppermute | solution.py:212
  34.7 16.1 %collective-permute-start.8 = (f32[8,4224]{1,0:T(8,128)S(1)}, f32[8,4224]{1,0:T(8,128)S(1)}, u32[]{:S(2)}, u32[]{:S(2)}) collective-permute-start(f32[8,4224]{1,0:T(8,128)S(1)} %get-tuple-element.6), channel_id=1, source_target_pairs={{0,6},{1,7},{2,4},{3,5},{4,2},{5,3},{6,0},{7,1},{8,14},{9,15},{10,... | collective-permute-start | bytes 405512 | tf_op jit(solution)/shard_map/ppermute | solution.py:212
  35.2 15.6 %collective-permute-start.7 = (f32[8,4224]{1,0:T(8,128)S(1)}, f32[8,4224]{1,0:T(8,128)S(1)}, u32[]{:S(2)}, u32[]{:S(2)}) collective-permute-start(f32[8,4224]{1,0:T(8,128)S(1)} %get-tuple-element.7), channel_id=1, source_target_pairs={{0,5},{1,4},{2,7},{3,6},{4,1},{5,0},{6,3},{7,2},{8,13},{9,12},{10,... | collective-permute-start | bytes 405512 | tf_op jit(solution)/shard_map/ppermute | solution.py:212
  36.1 14.7 %collective-permute-start.6 = (f32[8,4224]{1,0:T(8,128)S(1)}, f32[8,4224]{1,0:T(8,128)S(1)}, u32[]{:S(2)}, u32[]{:S(2)}) collective-permute-start(f32[8,4224]{1,0:T(8,128)S(1)} %get-tuple-element.8), channel_id=1, source_target_pairs={{0,4},{1,5},{2,6},{3,7},{4,0},{5,1},{6,2},{7,3},{8,12},{9,13},{10,... | collective-permute-start | bytes 405512 | tf_op jit(solution)/shard_map/ppermute | solution.py:212
  36.8 8.1 %collective-permute-start.4 = (f32[8,4224]{1,0:T(8,128)S(1)}, f32[8,4224]{1,0:T(8,128)S(1)}, u32[]{:S(2)}, u32[]{:S(2)}) collective-permute-start(f32[8,4224]{1,0:T(8,128)S(1)} %get-tuple-element.10), channel_id=1, source_target_pairs={{0,2},{1,3},{2,0},{3,1},{4,6},{5,7},{6,4},{7,5},{8,10},{9,11},{10,... | collective-permute-start | bytes 405512 | tf_op jit(solution)/shard_map/ppermute | solution.py:212
  44.9 5.9 %collective-permute-start.5 = (f32[8,4224]{1,0:T(8,128)S(1)}, f32[8,4224]{1,0:T(8,128)S(1)}, u32[]{:S(2)}, u32[]{:S(2)}) collective-permute-start(f32[8,4224]{1,0:T(8,128)S(1)} %get-tuple-element.9), channel_id=1, source_target_pairs={{0,3},{1,2},{2,1},{3,0},{4,7},{5,6},{6,5},{7,4},{8,11},{9,10},{10,... | collective-permute-start | bytes 405512 | tf_op jit(solution)/shard_map/ppermute | solution.py:212
  52.2 5.6 %collective-permute-start.12 = (f32[1,4096]{1,0:T(1,128)S(1)}, f32[1,4096]{1,0:T(1,128)S(1)}, u32[]{:S(2)}, u32[]{:S(2)}) collective-permute-start(f32[1,4096]{1,0:T(1,128)S(1)} %get-tuple-element.14), channel_id=1, source_target_pairs={{0,24},{8,16},{16,8},{24,0},{1,25},{9,17},{17,9},{25,1},{2,26},{10... | collective-permute-start | bytes 49160 | tf_op jit(solution)/shard_map/ppermute | solution.py:212
  54.7 4.6 %collective-permute-start.11 = (f32[1,4096]{1,0:T(1,128)S(1)}, f32[1,4096]{1,0:T(1,128)S(1)}, u32[]{:S(2)}, u32[]{:S(2)}) collective-permute-start(f32[1,4096]{1,0:T(1,128)S(1)} %get-tuple-element.15), channel_id=1, source_target_pairs={{0,16},{8,24},{16,0},{24,8},{1,17},{9,25},{17,1},{25,9},{2,18},{10... | collective-permute-start | bytes 49160 | tf_op jit(solution)/shard_map/ppermute | solution.py:212
  54.8 4.6 %collective-permute-start.10 = (f32[1,4096]{1,0:T(1,128)S(1)}, f32[1,4096]{1,0:T(1,128)S(1)}, u32[]{:S(2)}, u32[]{:S(2)}) collective-permute-start(f32[1,4096]{1,0:T(1,128)S(1)} %get-tuple-element.16), channel_id=1, source_target_pairs={{0,8},{8,0},{16,24},{24,16},{1,9},{9,1},{17,25},{25,17},{2,10},{10... | collective-permute-start | bytes 49160 | tf_op jit(solution)/shard_map/ppermute | solution.py:212

commit v7 on v5

--- a/solution.py
+++ b/solution.py
@@ -76,27 +76,32 @@
     return out + jnp.dot(matrix, third, preferred_element_type=jnp.float32)
 
 
-def emit(payload_ref, row, values, tag, me):
-    count, _, width = payload_ref.shape
-    chunk = width - 128
-    for index in range(count):
-        place = lax.rem(index - me + count, count)
+def emit(payload_refs, stage_ref, row, values, tag, me):
+    count = len(payload_refs)
+    chunk = payload_refs[0].shape[1] - 128
+    stage_ref[...] = values
+    for step in range(count):
+        index = lax.rem(me + step, count)
+        out = payload_refs[step]
         if chunk >= PLANE:
             per = chunk // PLANE
             for part in range(per):
-                payload_ref[place, pl.ds(row, 1), pl.ds(part * PLANE, PLANE)] = values[
-                    index * per + part : index * per + part + 1, :
+                out[pl.ds(row, 1), pl.ds(part * PLANE, PLANE)] = stage_ref[
+                    pl.ds(index * per + part, 1), :
                 ]
         else:
             per = PLANE // chunk
-            line, piece = divmod(index, per)
-            payload_ref[place, pl.ds(row, 1), pl.ds(0, chunk)] = values[
-                line : line + 1, piece * chunk : (piece + 1) * chunk
-            ]
-        payload_ref[place, pl.ds(row, 1), pl.ds(chunk, 128)] = tag
+            full = stage_ref[pl.ds(index // per, 1), :]
+            piece = index % per
+            pick = full[:, 0:chunk]
+            for other in range(1, per):
+                pick = jnp.where(piece == other, full[:, other * chunk : (other + 1) * chunk], pick)
+            out[pl.ds(row, 1), pl.ds(0, chunk)] = pick
+        out[pl.ds(row, 1), pl.ds(chunk, 128)] = tag
 
 
 def pair_kernel(
+    count,
     meta_ref,
     home_ref,
     part_ref,
@@ -105,12 +110,10 @@
     rows_high_ref,
     rows_low_ref,
     eigen_ref,
-    payload_ref,
-    shifted_ref,
-    work_ref,
-    kron_high_ref,
-    kron_low_ref,
+    *rest,
 ):
+    payload_ref = rest[:count]
+    shifted_ref, work_ref, kron_high_ref, kron_low_ref, stage_ref = rest[count:]
     slots = home_ref.shape[0]
     me = meta_ref[6 * slots]
     tiled = tiled_ref[...]
@@ -159,7 +162,7 @@
         here = potential[slot * B : (slot + 1) * B, :]
         tag_home = jnp.full((1, 128), meta_ref[4 * slots + slot].astype(jnp.float32))
         tag_part = jnp.full((1, 128), meta_ref[5 * slots + slot].astype(jnp.float32))
-        emit(payload_ref, slot, jnp.where(live, here * shifted_ref[slot], 0.0), tag_home, me)
+        emit(payload_ref, stage_ref, slot, jnp.where(live, here * shifted_ref[slot], 0.0), tag_home, me)
         product = here * home_ref[slot].astype(jnp.float32)
         pick = (col == row - d_a).astype(jnp.bfloat16)
         moved = exact_rows(pick, product)
@@ -168,7 +171,9 @@
         inside = (
             (lane_b - d_b >= 0) & (lane_b - d_b < B) & (lane_c - d_c >= 0) & (lane_c - d_c < B)
         )
-        emit(payload_ref, slots + slot, jnp.where(live & inside, moved, 0.0), tag_part, me)
+        emit(
+            payload_ref, stage_ref, slots + slot, jnp.where(live & inside, moved, 0.0), tag_part, me
+        )
 
 
 def pair_fields(meta, home, part, count, chunk):
@@ -176,23 +181,24 @@
     tiled, spread, rows_high, rows_low, eigen = host_tables(slots)
     smem = pl.BlockSpec(memory_space=pltpu.SMEM)
     vmem = pl.BlockSpec(memory_space=pltpu.VMEM)
-    box = jax.ShapeDtypeStruct((count, 2 * slots, chunk + 128), jnp.float32)
+    box = jax.ShapeDtypeStruct((2 * slots, chunk + 128), jnp.float32)
     return pl.pallas_call(
-        pair_kernel,
-        out_shape=box,
+        functools.partial(pair_kernel, count),
+        out_shape=tuple([box] * count),
         in_specs=[smem] + [vmem] * 7,
-        out_specs=vmem,
+        out_specs=tuple([vmem] * count),
         scratch_shapes=[
             pltpu.VMEM((slots, B, PLANE), jnp.float32),
             pltpu.VMEM((slots * B, PLANE), jnp.float32),
             pltpu.VMEM((PLANE, PLANE), jnp.bfloat16),
             pltpu.VMEM((PLANE, PLANE), jnp.bfloat16),
+            pltpu.VMEM((B, PLANE), jnp.float32),
         ],
     )(meta, home, part, tiled, spread, rows_high, rows_low, eigen)
 
 
 def exchange(blocks, axis):
-    count = blocks.shape[0]
+    count = len(blocks)
     received = [blocks[0]]
     for step in range(1, count):
         pairs = [(source, (source + step) % count) for source in range(count)]

time: 56.9 us -> 55.8 us (0.981)
  starting transfers between devices: 21.4 us -> 20.4 us
    squeeze x1 -> x0, local copies, waits for them, and re-layouts: 1.37 us -> none  [exchange(): received.append(lax.ppermute(blocks[step], axis, pairs))]
    ppermute x13, starting transfers between devices: 21.4 us -> 20.4 us  [exchange(): received.append(lax.ppermute(blocks[step], axis, pairs))]
    unnamed x15 -> x16, local copies, waits for them, and re-layouts: 2.4 us -> 3.31 us
  transfers between devices with their start and end apart: 13 -> 13, of which waited for: 7 -> 8; matrix products, arithmetic and copies ran while one was open for 5% -> 7% of each run, Pallas kernels for 0% -> 0%
where the time goes in v7:
time: 55.8 us; the launch traced here: 55.6 us
  starting transfers between devices  20.4 us (37%)
  waiting for transfers between devices  13.1 us (23%)
  local copies, waits for them, and re-layouts  11.4 us (20%)
  Pallas kernels  6.03 us (11%)
  matrix products  2.18 us (4%)
  other arithmetic  1.57 us (3%)
  between operations  0.9 us (2%)
    ppermute x13, starting transfers between devices, exchange(): received.append(lax.ppermute(blocks[step], axis, pairs))  20.4 us
    ppermute x13, waiting for transfers between devices, exchange(): received.append(lax.ppermute(blocks[step], axis, pairs))  13.1 us
    pallas_call x1, Pallas kernels, pair_fields(): pl.pallas_call(functools.partial(pair_kernel, count), out_shape=tuple([bo...  6.03 us
    unnamed x16, local copies, waits for them, and re-layouts  3.31 us
    gather x1, local copies, waits for them, and re-layouts, per_device(): chosen = sends[0][ahead]  1.38 us
    dot_general x1, matrix products, per_device(): return home_totals + jnp.dot(chooser.T, returned, precision=PRECISE)  1.13 us
    gather x2, local copies, waits for them, and re-layouts, per_device(): delta = offsets[home_slot] - visit_offsets[visit_slot]  1.12 us
  transfers between devices with their start and end apart: 13, of which 8 were waited for; matrix products, arithmetic and copies ran while one was open for 7% of the time, Pallas kernels for 0%

profile of v7, /device:TPU:0, one launch (start us, length us, event | category | flops | bytes accessed | tf_op | source)
XLA Modules:
  0.0 55.6 jit_solution(16445240797650486353)
XLA Ops:
  0.0 1.4 %gather_fusion.1 = s32[4]{0:T(128)S(1)} fusion(s32[4]{0:T(128)} %bitcast.65, s32[1024]{0:T(1024)S(1)} %pad_clamp_fusion.3), kind=kCustom, calls=%fused_computation.1 | custom fusion | bytes 48 | tf_op jit(solution)/shard_map/gather | solution.py:219
  1.4 0.7 %fusion.16 = s32[4]{0:T(128)S(1)} fusion(s32[1,1,4]{2,1,0:T(1,128)} %param.15, s32[]{:T(128)S(6)} %axis_index.23), kind=kLoop, calls=%fused_computation.70 | loop fusion | flops 60 | bytes 36 | tf_op jit(solution)/shard_map/select_n | solution.py:239
  2.1 0.8 %copy.16 = s32[16,3]{1,0:T(8,128)S(1)} copy(s32[16,3]{0,1:T(4,128)} %param.12) | data formatting | bytes 384 | tf_op args[1]
  3.4 0.8 %gather_fusion.2 = bf16[4,32768]{1,0:T(4,128)(2,1)S(1)} fusion(bf16[16,32768]{1,0:T(8,128)(2,1)S(1)} %copy-done, s32[1024]{0:T(1024)S(1)} %get-tuple-element.30), kind=kCustom, calls=%fused_computation.2 | custom fusion | bytes 524304 | tf_op jit(solution)/shard_map/gather | solution.py:223
  4.8 3.1 %collective-permute-start = (bf16[1,32896]{1,0:T(2,128)(2,1)S(1)}, bf16[1,32896]{1,0:T(2,128)(2,1)S(1)}, u32[]{:S(2)}, u32[]{:S(2)}) collective-permute-start(bf16[1,32896]{1,0:T(2,128)(2,1)S(1)} %get-tuple-element.24), channel_id=1, source_target_pairs={{0,8},{8,16},{16,24},{24,0},{1,9},{9,17},{17,25},{25,1},{2,10},{10... | collective-permute-start | bytes 197384 | tf_op jit(solution)/shard_map/ppermute | solution.py:205
  7.8 2.6 %collective-permute-start.1 = (bf16[1,32896]{1,0:T(2,128)(2,1)S(1)}, bf16[1,32896]{1,0:T(2,128)(2,1)S(1)}, u32[]{:S(2)}, u32[]{:S(2)}) collective-permute-start(bf16[1,32896]{1,0:T(2,128)(2,1)S(1)} %get-tuple-element.23), channel_id=1, source_target_pairs={{0,16},{8,24},{16,0},{24,8},{1,17},{9,25},{17,1},{25,9},{2,18},{10... | collective-permute-start | bytes 197384 | tf_op jit(solution)/shard_map/ppermute | solution.py:205
  10.4 1.3 %collective-permute-start.2 = (bf16[1,32896]{1,0:T(2,128)(2,1)S(1)}, bf16[1,32896]{1,0:T(2,128)(2,1)S(1)}, u32[]{:S(2)}, u32[]{:S(2)}) collective-permute-start(bf16[1,32896]{1,0:T(2,128)(2,1)S(1)} %get-tuple-element.22), channel_id=1, source_target_pairs={{0,24},{8,0},{16,8},{24,16},{1,25},{9,1},{17,9},{25,17},{2,26},{10... | collective-permute-start | bytes 197384 | tf_op jit(solution)/shard_map/ppermute | solution.py:205
  12.4 0.8 %gather_fusion.5 = bf16[4,32768]{1,0:T(4,128)(2,1)S(1)} fusion(bf16[16,32768]{1,0:T(8,128)(2,1)S(1)} %copy-done, s32[1024]{0:T(1024)S(1)} %pad_clamp_fusion.4), kind=kCustom, calls=%fused_computation.5 | custom fusion | bytes 524304 | tf_op jit(solution)/shard_map/gather | solution.py:237
  13.9 0.8 %copy.33 = bf16[1,4,32,1024]{3,2,1,0:T(8,128)(2,1)} copy(bf16[1,4,32,1024]{3,1,2,0:T(4,128)(2,1)S(1)} %bitcast.68) | data formatting | bytes 524288
  14.7 4.4 %collective-permute-done.1 = bf16[1,32896]{1,0:T(2,128)(2,1)S(1)} collective-permute-done((bf16[1,32896]{1,0:T(2,128)(2,1)S(1)}, bf16[1,32896]{1,0:T(2,128)(2,1)S(1)}, u32[]{:S(2)}, u32[]{:S(2)}) %collective-permute-start.1) | collective-permute-done | bytes 65824 | tf_op jit(solution)/shard_map/ppermute | solution.py:205
  19.1 0.6 %maximum_bitcast_fusion = bf16[4,32896]{1,0:T(4,128)(2,1)S(1)} fusion(bf16[1,1,32896]{2,0,1:T(2,128)(2,1)S(1)} %bitcast.72, bf16[1,1,32896]{2,0,1:T(2,128)(2,1)S(1)} %bitcast.71, bf16[1,1,32896]{2,0,1:T(2,128)(2,1)S(1)} %bitcast.70, bf16[1,1,32896]{2,0,1:T(2,128)(2,1)S(1)} %get-tuple-element.21), kind=kLoop, calls=%fused_computation.15 | loop fusion | flops 1052672 | bytes 526336 | tf_op jit(solution)/shard_map/reshape | solution.py:228
  20.5 0.8 %gather_fusion.6 = bf16[4,32768]{1,0:T(4,128)(2,1)S(1)} fusion(bf16[4,32768]{1,0:T(4,128)(2,1)S(1)} %slice.93, s32[1024]{0:T(1024)S(1)} %get-tuple-element.29), kind=kCustom, calls=%fused_computation.6 | custom fusion | bytes 524304 | tf_op jit(solution)/shard_map/gather | solution.py:238
  21.3 0.8 %copy.32 = bf16[1,4,32,1024]{3,2,1,0:T(8,128)(2,1)} copy(bf16[1,4,32,1024]{3,1,2,0:T(4,128)(2,1)S(1)} %bitcast.69) | data formatting | bytes 524288
  22.1 0.6 %concatenate.7.meta_ref = s32[25]{0:T(128)} concatenate(s32[12]{0:T(128)S(1)} %sub.29, s32[4]{0:T(128)S(1)} %compare_convert_fusion, s32[4]{0:T(128)S(1)} %bitcast.77, s32[4]{0:T(128)S(1)} %fusion.9, s32[1]{0:T(128)} %bitcast.16), dimensions={0} | concatenate | bytes 200 | tf_op jit(solution)/shard_map/concatenate | solution.py:243
  22.7 6.0 %shard_map.109 = (f32[8,4224]{1,0:T(8,128)}, f32[8,4224]{1,0:T(8,128)}, f32[8,4224]{1,0:T(8,128)}, f32[8,4224]{1,0:T(8,128)}, f32[8,4224]{1,0:T(8,128)}, /*index...) custom-call(s32[25]{0:T(128)} %concatenate.7.meta_ref, bf16[4,32,1024]{2,1,0:T(8,128)(2,1)} %bitcast.66, ...), custom_call_target="tpu_custom_call" | custom-call | tf_op jit(solution)/shard_map/pallas_call | solution.py:185
  28.8 0.9 %bitcast_dynamic-update-slice_fusion.7 = f32[8,8,4224]{2,1,0:T(8,128)S(1)} fusion(f32[8,4224]{1,0:T(8,128)} %get-tuple-element.13), kind=kLoop, calls=%fused_computation.25 | loop fusion | bytes 270336
  29.7 1.5 %collective-permute-start.4 = (f32[8,4224]{1,0:T(8,128)}, f32[8,4224]{1,0:T(8,128)S(1)}, u32[]{:S(2)}, u32[]{:S(2)}) collective-permute-start(f32[8,4224]{1,0:T(8,128)} %get-tuple-element.15), channel_id=1, source_target_pairs={{0,2},{1,3},{2,4},{3,5},{4,6},{5,7},{6,0},{7,1},{8,10},{9,11},{10,... | collective-permute-start | bytes 405512 | tf_op jit(solution)/shard_map/ppermute | solution.py:205
  31.2 2.4 %collective-permute-start.5 = (f32[8,4224]{1,0:T(8,128)}, f32[8,4224]{1,0:T(8,128)S(1)}, u32[]{:S(2)}, u32[]{:S(2)}) collective-permute-start(f32[8,4224]{1,0:T(8,128)} %get-tuple-element.16), channel_id=1, source_target_pairs={{0,3},{1,4},{2,5},{3,6},{4,7},{5,0},{6,1},{7,2},{8,11},{9,12},{10,... | collective-permute-start | bytes 405512 | tf_op jit(solution)/shard_map/ppermute | solution.py:205
  34.3 1.6 %collective-permute-start.8 = (f32[8,4224]{1,0:T(8,128)}, f32[8,4224]{1,0:T(8,128)S(1)}, u32[]{:S(2)}, u32[]{:S(2)}) collective-permute-start(f32[8,4224]{1,0:T(8,128)} %get-tuple-element.19), channel_id=1, source_target_pairs={{0,6},{1,7},{2,0},{3,1},{4,2},{5,3},{6,4},{7,5},{8,14},{9,15},{10,... | collective-permute-start | bytes 405512 | tf_op jit(solution)/shard_map/ppermute | solution.py:205
  35.9 0.9 %collective-permute-done.4 = f32[8,4224]{1,0:T(8,128)S(1)} collective-permute-done((f32[8,4224]{1,0:T(8,128)}, f32[8,4224]{1,0:T(8,128)S(1)}, u32[]{:S(2)}, u32[]{:S(2)}) %collective-permute-start.4) | collective-permute-done | bytes 135200 | tf_op jit(solution)/shard_map/ppermute | solution.py:205
  36.8 1.5 %collective-permute-start.9 = (f32[8,4224]{1,0:T(8,128)}, f32[8,4224]{1,0:T(8,128)S(1)}, u32[]{:S(2)}, u32[]{:S(2)}) collective-permute-start(f32[8,4224]{1,0:T(8,128)} %get-tuple-element.20), channel_id=1, source_target_pairs={{0,7},{1,0},{2,1},{3,2},{4,3},{5,4},{6,5},{7,6},{8,15},{9,8},{10,9... | collective-permute-start | bytes 405512 | tf_op jit(solution)/shard_map/ppermute | solution.py:205
  38.3 3.2 %collective-permute-done.5 = f32[8,4224]{1,0:T(8,128)S(1)} collective-permute-done((f32[8,4224]{1,0:T(8,128)}, f32[8,4224]{1,0:T(8,128)S(1)}, u32[]{:S(2)}, u32[]{:S(2)}) %collective-permute-start.5) | collective-permute-done | bytes 135200 | tf_op jit(solution)/shard_map/ppermute | solution.py:205
  41.7 1.9 %collective-permute-done.7 = f32[8,4224]{1,0:T(8,128)S(1)} collective-permute-done((f32[8,4224]{1,0:T(8,128)}, f32[8,4224]{1,0:T(8,128)S(1)}, u32[]{:S(2)}, u32[]{:S(2)}) %collective-permute-start.7) | collective-permute-done | bytes 135200 | tf_op jit(solution)/shard_map/ppermute | solution.py:205
  44.0 1.0 %convolution_bitcast_fusion = f32[20,4096]{1,0:T(8,128)S(1)} fusion(f32[8,8,4096]{2,1,0:T(8,128)S(1)} %slice.95, s32[8,8]{0,1:T(8,128)S(1)} %bitcast.73), kind=kOutput, calls=%fused_computation.9 | convolution fusion | flops 62915840 | bytes 1376512 | tf_op jit(solution)/shard_map/srk,srl->kl/dot_general | solution.py:257
  45.1 0.6 %gather_fusion.8 = f32[4,4096]{1,0:T(4,128)S(1)} fusion(f32[4,4096]{1,0:T(4,128)S(1)} %slice.97, s32[1024]{0:T(1024)S(1)} %pad_clamp_fusion), kind=kCustom, calls=%fused_computation.8 | custom fusion | bytes 131088 | tf_op jit(solution)/shard_map/gather | solution.py:261
  45.7 3.3 %collective-permute-start.10 = (f32[1,4096]{1,0:T(1,128)S(1)}, f32[1,4096]{1,0:T(1,128)S(1)}, u32[]{:S(2)}, u32[]{:S(2)}) collective-permute-start(f32[1,4096]{1,0:T(1,128)S(1)} %get-tuple-element.27), channel_id=1, source_target_pairs={{0,8},{8,16},{16,24},{24,0},{1,9},{9,17},{17,25},{25,1},{2,10},{10... | collective-permute-start | bytes 49160 | tf_op jit(solution)/shard_map/ppermute | solution.py:205
  49.0 1.6 %collective-permute-start.11 = (f32[1,4096]{1,0:T(1,128)S(1)}, f32[1,4096]{1,0:T(1,128)S(1)}, u32[]{:S(2)}, u32[]{:S(2)}) collective-permute-start(f32[1,4096]{1,0:T(1,128)S(1)} %get-tuple-element.26), channel_id=1, source_target_pairs={{0,16},{8,24},{16,0},{24,8},{1,17},{9,25},{17,1},{25,9},{2,18},{10... | collective-permute-start | bytes 49160 | tf_op jit(solution)/shard_map/ppermute | solution.py:205
  50.7 0.8 %collective-permute-start.12 = (f32[1,4096]{1,0:T(1,128)S(1)}, f32[1,4096]{1,0:T(1,128)S(1)}, u32[]{:S(2)}, u32[]{:S(2)}) collective-permute-start(f32[1,4096]{1,0:T(1,128)S(1)} %get-tuple-element.28), channel_id=1, source_target_pairs={{0,24},{8,0},{16,8},{24,16},{1,25},{9,1},{17,9},{25,17},{2,26},{10... | collective-permute-start | bytes 49160 | tf_op jit(solution)/shard_map/ppermute | solution.py:205
  51.5 0.6 %gather_fusion.7 = s32[4]{0:T(128)S(1)} fusion(s32[4]{0:T(128)S(1)} %gather_fusion.1, s32[1024]{0:T(1024)S(1)} %pad_clamp_fusion), kind=kCustom, calls=%fused_computation.7 | custom fusion | bytes 48 | tf_op jit(solution)/shard_map/gather | solution.py:263
  52.1 1.6 %collective-permute-done.11 = f32[1,4096]{1,0:T(1,128)S(1)} collective-permute-done((f32[1,4096]{1,0:T(1,128)S(1)}, f32[1,4096]{1,0:T(1,128)S(1)}, u32[]{:S(2)}, u32[]{:S(2)}) %collective-permute-start.11) | collective-permute-done | bytes 16416 | tf_op jit(solution)/shard_map/ppermute | solution.py:205
  53.8 0.6 %collective-permute-done.12 = f32[1,4096]{1,0:T(1,128)S(1)} collective-permute-done((f32[1,4096]{1,0:T(1,128)S(1)}, f32[1,4096]{1,0:T(1,128)S(1)}, u32[]{:S(2)}, u32[]{:S(2)}) %collective-permute-start.12) | collective-permute-done | bytes 16416 | tf_op jit(solution)/shard_map/ppermute | solution.py:205
  54.5 1.1 %convolution_add_fusion = f32[16,4096]{1,0:T(8,128)} fusion(f32[20,4096]{1,0:T(8,128)S(1)} %convolution_bitcast_fusion, f32[4,1,4096]{2,1,0:T(1,128)S(1)} %pad_maximum_fusion, s32[4]{0:T(128)S(1)} %gather_fusion.7), kind=kOutput, calls=%fused_computation.10 | convolution fusion | flops 3211328 | bytes 589840 | tf_op jit(solution)/shard_map/dot_general | solution.py:267
  (49 shorter events, 3.7 us)
Async XLA Ops:
  0.0 3.4 %copy-start = (bf16[16,32768]{1,0:T(8,128)(2,1)S(1)}, bf16[16,32768]{1,0:T(8,128)(2,1)}, u32[]{:S(2)}) copy-start(bf16[16,32768]{1,0:T(8,128)(2,1)} %param.11) | copy-start | bytes 3145732
  4.2 7.6 %copy-start.2 = (s32[1,1,4]{2,1,0:T(1,128)S(1)}, s32[1,1,4]{2,1,0:T(1,128)}, u32[]{:S(2)}) copy-start(s32[1,1,4]{2,1,0:T(1,128)} %param.15) | copy-start | bytes 52
  4.2 7.6 %copy-start.1 = (s32[1,1,4]{2,1,0:T(1,128)S(1)}, s32[1,1,4]{2,1,0:T(1,128)}, u32[]{:S(2)}) copy-start(s32[1,1,4]{2,1,0:T(1,128)} %param.14) | copy-start | bytes 52
  4.8 9.9 %collective-permute-start = (bf16[1,32896]{1,0:T(2,128)(2,1)S(1)}, bf16[1,32896]{1,0:T(2,128)(2,1)S(1)}, u32[]{:S(2)}, u32[]{:S(2)}) collective-permute-start(bf16[1,32896]{1,0:T(2,128)(2,1)S(1)} %get-tuple-element.24), channel_id=1, source_target_pairs={{0,8},{8,16},{16,24},{24,0},{1,9},{9,17},{17,25},{25,1},{2,10},{10... | collective-permute-start | bytes 197384 | tf_op jit(solution)/shard_map/ppermute | solution.py:205
  7.8 11.3 %collective-permute-start.1 = (bf16[1,32896]{1,0:T(2,128)(2,1)S(1)}, bf16[1,32896]{1,0:T(2,128)(2,1)S(1)}, u32[]{:S(2)}, u32[]{:S(2)}) collective-permute-start(bf16[1,32896]{1,0:T(2,128)(2,1)S(1)} %get-tuple-element.23), channel_id=1, source_target_pairs={{0,16},{8,24},{16,0},{24,8},{1,17},{9,25},{17,1},{25,9},{2,18},{10... | collective-permute-start | bytes 197384 | tf_op jit(solution)/shard_map/ppermute | solution.py:205
  10.4 8.7 %collective-permute-start.2 = (bf16[1,32896]{1,0:T(2,128)(2,1)S(1)}, bf16[1,32896]{1,0:T(2,128)(2,1)S(1)}, u32[]{:S(2)}, u32[]{:S(2)}) collective-permute-start(bf16[1,32896]{1,0:T(2,128)(2,1)S(1)} %get-tuple-element.22), channel_id=1, source_target_pairs={{0,24},{8,0},{16,8},{24,16},{1,25},{9,1},{17,9},{25,17},{2,26},{10... | collective-permute-start | bytes 197384 | tf_op jit(solution)/shard_map/ppermute | solution.py:205
  28.8 5.5 %collective-permute-start.3 = (f32[8,4224]{1,0:T(8,128)}, f32[8,4224]{1,0:T(8,128)S(1)}, u32[]{:S(2)}, u32[]{:S(2)}) collective-permute-start(f32[8,4224]{1,0:T(8,128)} %get-tuple-element.14), channel_id=1, source_target_pairs={{0,1},{1,2},{2,3},{3,4},{4,5},{5,6},{6,7},{7,0},{8,9},{9,10},{10,1... | collective-permute-start | bytes 405512 | tf_op jit(solution)/shard_map/ppermute | solution.py:205
  29.7 7.1 %collective-permute-start.4 = (f32[8,4224]{1,0:T(8,128)}, f32[8,4224]{1,0:T(8,128)S(1)}, u32[]{:S(2)}, u32[]{:S(2)}) collective-permute-start(f32[8,4224]{1,0:T(8,128)} %get-tuple-element.15), channel_id=1, source_target_pairs={{0,2},{1,3},{2,4},{3,5},{4,6},{5,7},{6,0},{7,1},{8,10},{9,11},{10,... | collective-permute-start | bytes 405512 | tf_op jit(solution)/shard_map/ppermute | solution.py:205
  31.2 10.3 %collective-permute-start.5 = (f32[8,4224]{1,0:T(8,128)}, f32[8,4224]{1,0:T(8,128)S(1)}, u32[]{:S(2)}, u32[]{:S(2)}) collective-permute-start(f32[8,4224]{1,0:T(8,128)} %get-tuple-element.16), channel_id=1, source_target_pairs={{0,3},{1,4},{2,5},{3,6},{4,7},{5,0},{6,1},{7,2},{8,11},{9,12},{10,... | collective-permute-start | bytes 405512 | tf_op jit(solution)/shard_map/ppermute | solution.py:205
  33.6 8.1 %collective-permute-start.6 = (f32[8,4224]{1,0:T(8,128)}, f32[8,4224]{1,0:T(8,128)S(1)}, u32[]{:S(2)}, u32[]{:S(2)}) collective-permute-start(f32[8,4224]{1,0:T(8,128)} %get-tuple-element.17), channel_id=1, source_target_pairs={{0,4},{1,5},{2,6},{3,7},{4,0},{5,1},{6,2},{7,3},{8,12},{9,13},{10,... | collective-permute-start | bytes 405512 | tf_op jit(solution)/shard_map/ppermute | solution.py:205
  34.1 9.5 %collective-permute-start.7 = (f32[8,4224]{1,0:T(8,128)}, f32[8,4224]{1,0:T(8,128)S(1)}, u32[]{:S(2)}, u32[]{:S(2)}) collective-permute-start(f32[8,4224]{1,0:T(8,128)} %get-tuple-element.18), channel_id=1, source_target_pairs={{0,5},{1,6},{2,7},{3,0},{4,1},{5,2},{6,3},{7,4},{8,13},{9,14},{10,... | collective-permute-start | bytes 405512 | tf_op jit(solution)/shard_map/ppermute | solution.py:205
  34.3 9.4 %collective-permute-start.8 = (f32[8,4224]{1,0:T(8,128)}, f32[8,4224]{1,0:T(8,128)S(1)}, u32[]{:S(2)}, u32[]{:S(2)}) collective-permute-start(f32[8,4224]{1,0:T(8,128)} %get-tuple-element.19), channel_id=1, source_target_pairs={{0,6},{1,7},{2,0},{3,1},{4,2},{5,3},{6,4},{7,5},{8,14},{9,15},{10,... | collective-permute-start | bytes 405512 | tf_op jit(solution)/shard_map/ppermute | solution.py:205
  36.8 6.9 %collective-permute-start.9 = (f32[8,4224]{1,0:T(8,128)}, f32[8,4224]{1,0:T(8,128)S(1)}, u32[]{:S(2)}, u32[]{:S(2)}) collective-permute-start(f32[8,4224]{1,0:T(8,128)} %get-tuple-element.20), channel_id=1, source_target_pairs={{0,7},{1,0},{2,1},{3,2},{4,3},{5,4},{6,5},{7,6},{8,15},{9,8},{10,9... | collective-permute-start | bytes 405512 | tf_op jit(solution)/shard_map/ppermute | solution.py:205
  45.7 6.4 %collective-permute-start.10 = (f32[1,4096]{1,0:T(1,128)S(1)}, f32[1,4096]{1,0:T(1,128)S(1)}, u32[]{:S(2)}, u32[]{:S(2)}) collective-permute-start(f32[1,4096]{1,0:T(1,128)S(1)} %get-tuple-element.27), channel_id=1, source_target_pairs={{0,8},{8,16},{16,24},{24,0},{1,9},{9,17},{17,25},{25,1},{2,10},{10... | collective-permute-start | bytes 49160 | tf_op jit(solution)/shard_map/ppermute | solution.py:205
  49.0 4.7 %collective-permute-start.11 = (f32[1,4096]{1,0:T(1,128)S(1)}, f32[1,4096]{1,0:T(1,128)S(1)}, u32[]{:S(2)}, u32[]{:S(2)}) collective-permute-start(f32[1,4096]{1,0:T(1,128)S(1)} %get-tuple-element.26), channel_id=1, source_target_pairs={{0,16},{8,24},{16,0},{24,8},{1,17},{9,25},{17,1},{25,9},{2,18},{10... | collective-permute-start | bytes 49160 | tf_op jit(solution)/shard_map/ppermute | solution.py:205
  50.7 3.7 %collective-permute-start.12 = (f32[1,4096]{1,0:T(1,128)S(1)}, f32[1,4096]{1,0:T(1,128)S(1)}, u32[]{:S(2)}, u32[]{:S(2)}) collective-permute-start(f32[1,4096]{1,0:T(1,128)S(1)} %get-tuple-element.28), channel_id=1, source_target_pairs={{0,24},{8,0},{16,8},{24,16},{1,25},{9,1},{17,9},{25,17},{2,26},{10... | collective-permute-start | bytes 49160 | tf_op jit(solution)/shard_map/ppermute | solution.py:205

commit v8 on v7

--- a/solution.py
+++ b/solution.py
@@ -100,22 +100,7 @@
         out[pl.ds(row, 1), pl.ds(chunk, 128)] = tag
 
 
-def pair_kernel(
-    count,
-    meta_ref,
-    home_ref,
-    part_ref,
-    tiled_ref,
-    spread_ref,
-    rows_high_ref,
-    rows_low_ref,
-    eigen_ref,
-    *rest,
-):
-    payload_ref = rest[:count]
-    shifted_ref, work_ref, kron_high_ref, kron_low_ref, stage_ref = rest[count:]
-    slots = home_ref.shape[0]
-    me = meta_ref[6 * slots]
+def kron_kernel(tiled_ref, spread_ref, kron_high_ref, kron_low_ref):
     tiled = tiled_ref[...]
     for block in range(B):
         values = tiled * spread_ref[block : block + 1, :]
@@ -124,6 +109,36 @@
         kron_low_ref[block * B : (block + 1) * B, :] = (
             values - high.astype(jnp.float32)
         ).astype(jnp.bfloat16)
+
+
+def kron_tables():
+    tiled, spread, _, _, _ = host_tables(1)
+    vmem = pl.BlockSpec(memory_space=pltpu.VMEM)
+    square = jax.ShapeDtypeStruct((PLANE, PLANE), jnp.bfloat16)
+    return pl.pallas_call(
+        kron_kernel,
+        out_shape=(square, square),
+        in_specs=[vmem, vmem],
+        out_specs=(vmem, vmem),
+    )(tiled, spread)
+
+
+def pair_kernel(
+    count,
+    meta_ref,
+    home_ref,
+    part_ref,
+    kron_high_ref,
+    kron_low_ref,
+    rows_high_ref,
+    rows_low_ref,
+    eigen_ref,
+    *rest,
+):
+    payload_ref = rest[:count]
+    shifted_ref, work_ref, stage_ref = rest[count:]
+    slots = home_ref.shape[0]
+    me = meta_ref[6 * slots]
     lane = lax.broadcasted_iota(jnp.int32, (B, PLANE), 1)
     lane_b = lane // B
     lane_c = lane % B
@@ -178,7 +193,8 @@
 
 def pair_fields(meta, home, part, count, chunk):
     slots = home.shape[0]
-    tiled, spread, rows_high, rows_low, eigen = host_tables(slots)
+    _, _, rows_high, rows_low, eigen = host_tables(slots)
+    kron_high, kron_low = kron_tables()
     smem = pl.BlockSpec(memory_space=pltpu.SMEM)
     vmem = pl.BlockSpec(memory_space=pltpu.VMEM)
     box = jax.ShapeDtypeStruct((2 * slots, chunk + 128), jnp.float32)
@@ -190,11 +206,9 @@
         scratch_shapes=[
             pltpu.VMEM((slots, B, PLANE), jnp.float32),
             pltpu.VMEM((slots * B, PLANE), jnp.float32),
-            pltpu.VMEM((PLANE, PLANE), jnp.bfloat16),
-            pltpu.VMEM((PLANE, PLANE), jnp.bfloat16),
             pltpu.VMEM((B, PLANE), jnp.float32),
         ],
-    )(meta, home, part, tiled, spread, rows_high, rows_low, eigen)
+    )(meta, home, part, kron_high, kron_low, rows_high, rows_low, eigen)
 
 
 def exchange(blocks, axis):

time: 55.8 us -> 56.9 us (1.020)
  Pallas kernels: 6.03 us -> 10.7 us
  waiting for transfers between devices: 13.1 us -> 9.54 us
    pallas_call x0 -> x1, Pallas kernels: none -> 3.58 us  [kron_tables(): pl.pallas_call(kron_kernel, out_shape=(square, square), in_specs=[vmem, v...]
    ppermute x13, waiting for transfers between devices: 13.1 us -> 9.54 us  [exchange(): received.append(lax.ppermute(blocks[step], axis, pairs))]
    pallas_call x1, Pallas kernels: 6.03 us -> 7.1 us  [pair_fields(): pl.pallas_call(functools.partial(pair_kernel, count), out_shape=tuple([bo...]
  transfers between devices with their start and end apart: 13 -> 13, of which waited for: 8 -> 8; matrix products, arithmetic and copies ran while one was open for 7% -> 7% of each run, Pallas kernels for 0% -> 6%
where the time goes in v8:
time: 56.9 us; the launch traced here: 56.7 us
  starting transfers between devices  20.4 us (36%)
  local copies, waits for them, and re-layouts  11.4 us (20%)
  Pallas kernels  10.7 us (19%)
  waiting for transfers between devices  9.54 us (17%)
  matrix products  2.18 us (4%)
  other arithmetic  1.57 us (3%)
  between operations  0.89 us (2%)
    ppermute x13, starting transfers between devices, exchange(): received.append(lax.ppermute(blocks[step], axis, pairs))  20.4 us
    ppermute x13, waiting for transfers between devices, exchange(): received.append(lax.ppermute(blocks[step], axis, pairs))  9.54 us
    pallas_call x1, Pallas kernels, pair_fields(): pl.pallas_call(functools.partial(pair_kernel, count), out_shape=tuple([bo...  7.1 us
    pallas_call x1, Pallas kernels, kron_tables(): pl.pallas_call(kron_kernel, out_shape=(square, square), in_specs=[vmem, v...  3.58 us
    unnamed x16, local copies, waits for them, and re-layouts  3.35 us
    gather x1, local copies, waits for them, and re-layouts, per_device(): chosen = sends[0][ahead]  1.38 us
  transfers between devices with their start and end apart: 13, of which 8 were waited for; matrix products, arithmetic and copies ran while one was open for 7% of the time, Pallas kernels for 6%

profile of v8, /device:TPU:0, one launch (start us, length us, event | category | flops | bytes accessed | tf_op | source)
XLA Modules:
  0.0 56.7 jit_solution(17523849222774025889)
XLA Ops:
  0.0 1.4 %gather_fusion.1 = s32[4]{0:T(128)S(1)} fusion(s32[4]{0:T(128)} %bitcast.65, s32[1024]{0:T(1024)S(1)} %pad_clamp_fusion.3), kind=kCustom, calls=%fused_computation.1 | custom fusion | bytes 48 | tf_op jit(solution)/shard_map/gather | solution.py:233
  1.4 0.7 %fusion.16 = s32[4]{0:T(128)S(1)} fusion(s32[1,1,4]{2,1,0:T(1,128)} %param.15, s32[]{:T(128)S(6)} %axis_index.23), kind=kLoop, calls=%fused_computation.70 | loop fusion | flops 60 | bytes 36 | tf_op jit(solution)/shard_map/select_n | solution.py:253
  2.1 0.8 %copy.16 = s32[16,3]{1,0:T(8,128)S(1)} copy(s32[16,3]{0,1:T(4,128)} %param.12) | data formatting | bytes 384 | tf_op args[1]
  3.4 0.8 %gather_fusion.2 = bf16[4,32768]{1,0:T(4,128)(2,1)S(1)} fusion(bf16[16,32768]{1,0:T(8,128)(2,1)S(1)} %copy-done, s32[1024]{0:T(1024)S(1)} %get-tuple-element.34), kind=kCustom, calls=%fused_computation.2 | custom fusion | bytes 524304 | tf_op jit(solution)/shard_map/gather | solution.py:237
  4.8 3.1 %collective-permute-start = (bf16[1,32896]{1,0:T(2,128)(2,1)S(1)}, bf16[1,32896]{1,0:T(2,128)(2,1)S(1)}, u32[]{:S(2)}, u32[]{:S(2)}) collective-permute-start(bf16[1,32896]{1,0:T(2,128)(2,1)S(1)} %get-tuple-element.28), channel_id=1, source_target_pairs={{0,8},{8,16},{16,24},{24,0},{1,9},{9,17},{17,25},{25,1},{2,10},{10... | collective-permute-start | bytes 197384 | tf_op jit(solution)/shard_map/ppermute | solution.py:219
  7.8 2.6 %collective-permute-start.1 = (bf16[1,32896]{1,0:T(2,128)(2,1)S(1)}, bf16[1,32896]{1,0:T(2,128)(2,1)S(1)}, u32[]{:S(2)}, u32[]{:S(2)}) collective-permute-start(bf16[1,32896]{1,0:T(2,128)(2,1)S(1)} %get-tuple-element.27), channel_id=1, source_target_pairs={{0,16},{8,24},{16,0},{24,8},{1,17},{9,25},{17,1},{25,9},{2,18},{10... | collective-permute-start | bytes 197384 | tf_op jit(solution)/shard_map/ppermute | solution.py:219
  10.4 1.3 %collective-permute-start.2 = (bf16[1,32896]{1,0:T(2,128)(2,1)S(1)}, bf16[1,32896]{1,0:T(2,128)(2,1)S(1)}, u32[]{:S(2)}, u32[]{:S(2)}) collective-permute-start(bf16[1,32896]{1,0:T(2,128)(2,1)S(1)} %get-tuple-element.26), channel_id=1, source_target_pairs={{0,24},{8,0},{16,8},{24,16},{1,25},{9,1},{17,9},{25,17},{2,26},{10... | collective-permute-start | bytes 197384 | tf_op jit(solution)/shard_map/ppermute | solution.py:219
  12.4 0.8 %gather_fusion.5 = bf16[4,32768]{1,0:T(4,128)(2,1)S(1)} fusion(bf16[16,32768]{1,0:T(8,128)(2,1)S(1)} %copy-done, s32[1024]{0:T(1024)S(1)} %pad_clamp_fusion.4), kind=kCustom, calls=%fused_computation.5 | custom fusion | bytes 524304 | tf_op jit(solution)/shard_map/gather | solution.py:251
  13.9 0.8 %copy.33 = bf16[1,4,32,1024]{3,2,1,0:T(8,128)(2,1)} copy(bf16[1,4,32,1024]{3,1,2,0:T(4,128)(2,1)S(1)} %bitcast.68) | data formatting | bytes 524288
  14.7 3.6 %shard_map.109 = (bf16[1024,1024]{1,0:T(8,128)(2,1)}, bf16[1024,1024]{1,0:T(8,128)(2,1)}) custom-call(f32[32,1024]{1,0:T(8,128)} %constant.75.clone.tiled_ref, f32[32,1024]{1,0:T(8,128)} %constant.76.clone.spread_ref), custom_call_target="tpu_custom_call" | custom-call | tf_op jit(solution)/shard_map/pallas_call | solution.py:118
  18.2 0.9 %collective-permute-done.1 = bf16[1,32896]{1,0:T(2,128)(2,1)S(1)} collective-permute-done((bf16[1,32896]{1,0:T(2,128)(2,1)S(1)}, bf16[1,32896]{1,0:T(2,128)(2,1)S(1)}, u32[]{:S(2)}, u32[]{:S(2)}) %collective-permute-start.1) | collective-permute-done | bytes 65824 | tf_op jit(solution)/shard_map/ppermute | solution.py:219
  19.1 0.6 %maximum_bitcast_fusion = bf16[4,32896]{1,0:T(4,128)(2,1)S(1)} fusion(bf16[1,1,32896]{2,0,1:T(2,128)(2,1)S(1)} %bitcast.72, bf16[1,1,32896]{2,0,1:T(2,128)(2,1)S(1)} %bitcast.71, bf16[1,1,32896]{2,0,1:T(2,128)(2,1)S(1)} %bitcast.70, bf16[1,1,32896]{2,0,1:T(2,128)(2,1)S(1)} %get-tuple-element.25), kind=kLoop, calls=%fused_computation.15 | loop fusion | flops 1052672 | bytes 526336 | tf_op jit(solution)/shard_map/reshape | solution.py:242
  20.5 0.8 %gather_fusion.6 = bf16[4,32768]{1,0:T(4,128)(2,1)S(1)} fusion(bf16[4,32768]{1,0:T(4,128)(2,1)S(1)} %slice.93, s32[1024]{0:T(1024)S(1)} %get-tuple-element.33), kind=kCustom, calls=%fused_computation.6 | custom fusion | bytes 524304 | tf_op jit(solution)/shard_map/gather | solution.py:252
  21.3 0.8 %copy.32 = bf16[1,4,32,1024]{3,2,1,0:T(8,128)(2,1)} copy(bf16[1,4,32,1024]{3,1,2,0:T(4,128)(2,1)S(1)} %bitcast.69) | data formatting | bytes 524288
  22.1 0.6 %concatenate.7.meta_ref = s32[25]{0:T(128)} concatenate(s32[12]{0:T(128)S(1)} %sub.29, s32[4]{0:T(128)S(1)} %compare_convert_fusion, s32[4]{0:T(128)S(1)} %bitcast.77, s32[4]{0:T(128)S(1)} %fusion.9, s32[1]{0:T(128)} %bitcast.16), dimensions={0} | concatenate | bytes 200 | tf_op jit(solution)/shard_map/concatenate | solution.py:257
  22.7 7.1 %shard_map.110 = (f32[8,4224]{1,0:T(8,128)}, f32[8,4224]{1,0:T(8,128)}, f32[8,4224]{1,0:T(8,128)}, f32[8,4224]{1,0:T(8,128)}, f32[8,4224]{1,0:T(8,128)}, /*index...) custom-call(s32[25]{0:T(128)} %concatenate.7.meta_ref, bf16[4,32,1024]{2,1,0:T(8,128)(2,1)} %bitcast.66, ...), custom_call_target="tpu_custom_call" | custom-call | tf_op jit(solution)/shard_map/pallas_call | solution.py:201
  29.8 0.9 %bitcast_dynamic-update-slice_fusion.7 = f32[8,8,4224]{2,1,0:T(8,128)S(1)} fusion(f32[8,4224]{1,0:T(8,128)} %get-tuple-element.17), kind=kLoop, calls=%fused_computation.25 | loop fusion | bytes 270336
  30.7 1.6 %collective-permute-start.4 = (f32[8,4224]{1,0:T(8,128)}, f32[8,4224]{1,0:T(8,128)S(1)}, u32[]{:S(2)}, u32[]{:S(2)}) collective-permute-start(f32[8,4224]{1,0:T(8,128)} %get-tuple-element.19), channel_id=1, source_target_pairs={{0,2},{1,3},{2,4},{3,5},{4,6},{5,7},{6,0},{7,1},{8,10},{9,11},{10,... | collective-permute-start | bytes 405512 | tf_op jit(solution)/shard_map/ppermute | solution.py:219
  32.3 2.4 %collective-permute-start.5 = (f32[8,4224]{1,0:T(8,128)}, f32[8,4224]{1,0:T(8,128)S(1)}, u32[]{:S(2)}, u32[]{:S(2)}) collective-permute-start(f32[8,4224]{1,0:T(8,128)} %get-tuple-element.20), channel_id=1, source_target_pairs={{0,3},{1,4},{2,5},{3,6},{4,7},{5,0},{6,1},{7,2},{8,11},{9,12},{10,... | collective-permute-start | bytes 405512 | tf_op jit(solution)/shard_map/ppermute | solution.py:219
  35.4 1.6 %collective-permute-start.8 = (f32[8,4224]{1,0:T(8,128)}, f32[8,4224]{1,0:T(8,128)S(1)}, u32[]{:S(2)}, u32[]{:S(2)}) collective-permute-start(f32[8,4224]{1,0:T(8,128)} %get-tuple-element.23), channel_id=1, source_target_pairs={{0,6},{1,7},{2,0},{3,1},{4,2},{5,3},{6,4},{7,5},{8,14},{9,15},{10,... | collective-permute-start | bytes 405512 | tf_op jit(solution)/shard_map/ppermute | solution.py:219
  36.9 0.9 %collective-permute-done.4 = f32[8,4224]{1,0:T(8,128)S(1)} collective-permute-done((f32[8,4224]{1,0:T(8,128)}, f32[8,4224]{1,0:T(8,128)S(1)}, u32[]{:S(2)}, u32[]{:S(2)}) %collective-permute-start.4) | collective-permute-done | bytes 135200 | tf_op jit(solution)/shard_map/ppermute | solution.py:219
  37.9 1.5 %collective-permute-start.9 = (f32[8,4224]{1,0:T(8,128)}, f32[8,4224]{1,0:T(8,128)S(1)}, u32[]{:S(2)}, u32[]{:S(2)}) collective-permute-start(f32[8,4224]{1,0:T(8,128)} %get-tuple-element.24), channel_id=1, source_target_pairs={{0,7},{1,0},{2,1},{3,2},{4,3},{5,4},{6,5},{7,6},{8,15},{9,8},{10,9... | collective-permute-start | bytes 405512 | tf_op jit(solution)/shard_map/ppermute | solution.py:219
  39.4 3.2 %collective-permute-done.5 = f32[8,4224]{1,0:T(8,128)S(1)} collective-permute-done((f32[8,4224]{1,0:T(8,128)}, f32[8,4224]{1,0:T(8,128)S(1)}, u32[]{:S(2)}, u32[]{:S(2)}) %collective-permute-start.5) | collective-permute-done | bytes 135200 | tf_op jit(solution)/shard_map/ppermute | solution.py:219
  42.8 1.9 %collective-permute-done.7 = f32[8,4224]{1,0:T(8,128)S(1)} collective-permute-done((f32[8,4224]{1,0:T(8,128)}, f32[8,4224]{1,0:T(8,128)S(1)}, u32[]{:S(2)}, u32[]{:S(2)}) %collective-permute-start.7) | collective-permute-done | bytes 135200 | tf_op jit(solution)/shard_map/ppermute | solution.py:219
  45.1 1.0 %convolution_bitcast_fusion = f32[20,4096]{1,0:T(8,128)S(1)} fusion(f32[8,8,4096]{2,1,0:T(8,128)S(1)} %slice.95, s32[8,8]{0,1:T(8,128)S(1)} %bitcast.73), kind=kOutput, calls=%fused_computation.9 | convolution fusion | flops 62915840 | bytes 1376512 | tf_op jit(solution)/shard_map/srk,srl->kl/dot_general | solution.py:271
  46.8 3.3 %collective-permute-start.10 = (f32[1,4096]{1,0:T(1,128)S(1)}, f32[1,4096]{1,0:T(1,128)S(1)}, u32[]{:S(2)}, u32[]{:S(2)}) collective-permute-start(f32[1,4096]{1,0:T(1,128)S(1)} %get-tuple-element.31), channel_id=1, source_target_pairs={{0,8},{8,16},{16,24},{24,0},{1,9},{9,17},{17,25},{25,1},{2,10},{10... | collective-permute-start | bytes 49160 | tf_op jit(solution)/shard_map/ppermute | solution.py:219
  50.1 1.6 %collective-permute-start.11 = (f32[1,4096]{1,0:T(1,128)S(1)}, f32[1,4096]{1,0:T(1,128)S(1)}, u32[]{:S(2)}, u32[]{:S(2)}) collective-permute-start(f32[1,4096]{1,0:T(1,128)S(1)} %get-tuple-element.30), channel_id=1, source_target_pairs={{0,16},{8,24},{16,0},{24,8},{1,17},{9,25},{17,1},{25,9},{2,18},{10... | collective-permute-start | bytes 49160 | tf_op jit(solution)/shard_map/ppermute | solution.py:219
  51.8 0.8 %collective-permute-start.12 = (f32[1,4096]{1,0:T(1,128)S(1)}, f32[1,4096]{1,0:T(1,128)S(1)}, u32[]{:S(2)}, u32[]{:S(2)}) collective-permute-start(f32[1,4096]{1,0:T(1,128)S(1)} %get-tuple-element.32), channel_id=1, source_target_pairs={{0,24},{8,0},{16,8},{24,16},{1,25},{9,1},{17,9},{25,17},{2,26},{10... | collective-permute-start | bytes 49160 | tf_op jit(solution)/shard_map/ppermute | solution.py:219
  52.6 0.6 %gather_fusion.7 = s32[4]{0:T(128)S(1)} fusion(s32[4]{0:T(128)S(1)} %gather_fusion.1, s32[1024]{0:T(1024)S(1)} %pad_clamp_fusion), kind=kCustom, calls=%fused_computation.7 | custom fusion | bytes 48 | tf_op jit(solution)/shard_map/gather | solution.py:277
  53.2 1.7 %collective-permute-done.11 = f32[1,4096]{1,0:T(1,128)S(1)} collective-permute-done((f32[1,4096]{1,0:T(1,128)S(1)}, f32[1,4096]{1,0:T(1,128)S(1)}, u32[]{:S(2)}, u32[]{:S(2)}) %collective-permute-start.11) | collective-permute-done | bytes 16416 | tf_op jit(solution)/shard_map/ppermute | solution.py:219
  54.9 0.6 %collective-permute-done.12 = f32[1,4096]{1,0:T(1,128)S(1)} collective-permute-done((f32[1,4096]{1,0:T(1,128)S(1)}, f32[1,4096]{1,0:T(1,128)S(1)}, u32[]{:S(2)}, u32[]{:S(2)}) %collective-permute-start.12) | collective-permute-done | bytes 16416 | tf_op jit(solution)/shard_map/ppermute | solution.py:219
  55.6 1.1 %convolution_add_fusion = f32[16,4096]{1,0:T(8,128)} fusion(f32[20,4096]{1,0:T(8,128)S(1)} %convolution_bitcast_fusion, f32[4,1,4096]{2,1,0:T(1,128)S(1)} %pad_maximum_fusion, s32[4]{0:T(128)S(1)} %gather_fusion.7), kind=kOutput, calls=%fused_computation.10 | convolution fusion | flops 3211328 | bytes 589840 | tf_op jit(solution)/shard_map/dot_general | solution.py:281
  (50 shorter events, 4.3 us)
Async XLA Ops:
  0.0 3.4 %copy-start = (bf16[16,32768]{1,0:T(8,128)(2,1)S(1)}, bf16[16,32768]{1,0:T(8,128)(2,1)}, u32[]{:S(2)}) copy-start(bf16[16,32768]{1,0:T(8,128)(2,1)} %param.11) | copy-start | bytes 3145732
  4.2 7.6 %copy-start.2 = (s32[1,1,4]{2,1,0:T(1,128)S(1)}, s32[1,1,4]{2,1,0:T(1,128)}, u32[]{:S(2)}) copy-start(s32[1,1,4]{2,1,0:T(1,128)} %param.15) | copy-start | bytes 52
  4.2 7.6 %copy-start.1 = (s32[1,1,4]{2,1,0:T(1,128)S(1)}, s32[1,1,4]{2,1,0:T(1,128)}, u32[]{:S(2)}) copy-start(s32[1,1,4]{2,1,0:T(1,128)} %param.14) | copy-start | bytes 52
  4.8 13.5 %collective-permute-start = (bf16[1,32896]{1,0:T(2,128)(2,1)S(1)}, bf16[1,32896]{1,0:T(2,128)(2,1)S(1)}, u32[]{:S(2)}, u32[]{:S(2)}) collective-permute-start(bf16[1,32896]{1,0:T(2,128)(2,1)S(1)} %get-tuple-element.28), channel_id=1, source_target_pairs={{0,8},{8,16},{16,24},{24,0},{1,9},{9,17},{17,25},{25,1},{2,10},{10... | collective-permute-start | bytes 197384 | tf_op jit(solution)/shard_map/ppermute | solution.py:219
  7.8 11.3 %collective-permute-start.1 = (bf16[1,32896]{1,0:T(2,128)(2,1)S(1)}, bf16[1,32896]{1,0:T(2,128)(2,1)S(1)}, u32[]{:S(2)}, u32[]{:S(2)}) collective-permute-start(bf16[1,32896]{1,0:T(2,128)(2,1)S(1)} %get-tuple-element.27), channel_id=1, source_target_pairs={{0,16},{8,24},{16,0},{24,8},{1,17},{9,25},{17,1},{25,9},{2,18},{10... | collective-permute-start | bytes 197384 | tf_op jit(solution)/shard_map/ppermute | solution.py:219
  10.4 8.7 %collective-permute-start.2 = (bf16[1,32896]{1,0:T(2,128)(2,1)S(1)}, bf16[1,32896]{1,0:T(2,128)(2,1)S(1)}, u32[]{:S(2)}, u32[]{:S(2)}) collective-permute-start(bf16[1,32896]{1,0:T(2,128)(2,1)S(1)} %get-tuple-element.26), channel_id=1, source_target_pairs={{0,24},{8,0},{16,8},{24,16},{1,25},{9,1},{17,9},{25,17},{2,26},{10... | collective-permute-start | bytes 197384 | tf_op jit(solution)/shard_map/ppermute | solution.py:219
  29.8 5.5 %collective-permute-start.3 = (f32[8,4224]{1,0:T(8,128)}, f32[8,4224]{1,0:T(8,128)S(1)}, u32[]{:S(2)}, u32[]{:S(2)}) collective-permute-start(f32[8,4224]{1,0:T(8,128)} %get-tuple-element.18), channel_id=1, source_target_pairs={{0,1},{1,2},{2,3},{3,4},{4,5},{5,6},{6,7},{7,0},{8,9},{9,10},{10,1... | collective-permute-start | bytes 405512 | tf_op jit(solution)/shard_map/ppermute | solution.py:219
  30.7 7.1 %collective-permute-start.4 = (f32[8,4224]{1,0:T(8,128)}, f32[8,4224]{1,0:T(8,128)S(1)}, u32[]{:S(2)}, u32[]{:S(2)}) collective-permute-start(f32[8,4224]{1,0:T(8,128)} %get-tuple-element.19), channel_id=1, source_target_pairs={{0,2},{1,3},{2,4},{3,5},{4,6},{5,7},{6,0},{7,1},{8,10},{9,11},{10,... | collective-permute-start | bytes 405512 | tf_op jit(solution)/shard_map/ppermute | solution.py:219
  32.3 10.3 %collective-permute-start.5 = (f32[8,4224]{1,0:T(8,128)}, f32[8,4224]{1,0:T(8,128)S(1)}, u32[]{:S(2)}, u32[]{:S(2)}) collective-permute-start(f32[8,4224]{1,0:T(8,128)} %get-tuple-element.20), channel_id=1, source_target_pairs={{0,3},{1,4},{2,5},{3,6},{4,7},{5,0},{6,1},{7,2},{8,11},{9,12},{10,... | collective-permute-start | bytes 405512 | tf_op jit(solution)/shard_map/ppermute | solution.py:219
  34.7 8.1 %collective-permute-start.6 = (f32[8,4224]{1,0:T(8,128)}, f32[8,4224]{1,0:T(8,128)S(1)}, u32[]{:S(2)}, u32[]{:S(2)}) collective-permute-start(f32[8,4224]{1,0:T(8,128)} %get-tuple-element.21), channel_id=1, source_target_pairs={{0,4},{1,5},{2,6},{3,7},{4,0},{5,1},{6,2},{7,3},{8,12},{9,13},{10,... | collective-permute-start | bytes 405512 | tf_op jit(solution)/shard_map/ppermute | solution.py:219
  35.2 9.5 %collective-permute-start.7 = (f32[8,4224]{1,0:T(8,128)}, f32[8,4224]{1,0:T(8,128)S(1)}, u32[]{:S(2)}, u32[]{:S(2)}) collective-permute-start(f32[8,4224]{1,0:T(8,128)} %get-tuple-element.22), channel_id=1, source_target_pairs={{0,5},{1,6},{2,7},{3,0},{4,1},{5,2},{6,3},{7,4},{8,13},{9,14},{10,... | collective-permute-start | bytes 405512 | tf_op jit(solution)/shard_map/ppermute | solution.py:219
  35.4 9.4 %collective-permute-start.8 = (f32[8,4224]{1,0:T(8,128)}, f32[8,4224]{1,0:T(8,128)S(1)}, u32[]{:S(2)}, u32[]{:S(2)}) collective-permute-start(f32[8,4224]{1,0:T(8,128)} %get-tuple-element.23), channel_id=1, source_target_pairs={{0,6},{1,7},{2,0},{3,1},{4,2},{5,3},{6,4},{7,5},{8,14},{9,15},{10,... | collective-permute-start | bytes 405512 | tf_op jit(solution)/shard_map/ppermute | solution.py:219
  37.9 7.0 %collective-permute-start.9 = (f32[8,4224]{1,0:T(8,128)}, f32[8,4224]{1,0:T(8,128)S(1)}, u32[]{:S(2)}, u32[]{:S(2)}) collective-permute-start(f32[8,4224]{1,0:T(8,128)} %get-tuple-element.24), channel_id=1, source_target_pairs={{0,7},{1,0},{2,1},{3,2},{4,3},{5,4},{6,5},{7,6},{8,15},{9,8},{10,9... | collective-permute-start | bytes 405512 | tf_op jit(solution)/shard_map/ppermute | solution.py:219
  46.8 6.4 %collective-permute-start.10 = (f32[1,4096]{1,0:T(1,128)S(1)}, f32[1,4096]{1,0:T(1,128)S(1)}, u32[]{:S(2)}, u32[]{:S(2)}) collective-permute-start(f32[1,4096]{1,0:T(1,128)S(1)} %get-tuple-element.31), channel_id=1, source_target_pairs={{0,8},{8,16},{16,24},{24,0},{1,9},{9,17},{17,25},{25,1},{2,10},{10... | collective-permute-start | bytes 49160 | tf_op jit(solution)/shard_map/ppermute | solution.py:219
  50.1 4.7 %collective-permute-start.11 = (f32[1,4096]{1,0:T(1,128)S(1)}, f32[1,4096]{1,0:T(1,128)S(1)}, u32[]{:S(2)}, u32[]{:S(2)}) collective-permute-start(f32[1,4096]{1,0:T(1,128)S(1)} %get-tuple-element.30), channel_id=1, source_target_pairs={{0,16},{8,24},{16,0},{24,8},{1,17},{9,25},{17,1},{25,9},{2,18},{10... | collective-permute-start | bytes 49160 | tf_op jit(solution)/shard_map/ppermute | solution.py:219
  51.8 3.7 %collective-permute-start.12 = (f32[1,4096]{1,0:T(1,128)S(1)}, f32[1,4096]{1,0:T(1,128)S(1)}, u32[]{:S(2)}, u32[]{:S(2)}) collective-permute-start(f32[1,4096]{1,0:T(1,128)S(1)} %get-tuple-element.32), channel_id=1, source_target_pairs={{0,24},{8,0},{16,8},{24,16},{1,25},{9,1},{17,9},{25,17},{2,26},{10... | collective-permute-start | bytes 49160 | tf_op jit(solution)/shard_map/ppermute | solution.py:219

commit v9 on v7

--- a/solution.py
+++ b/solution.py
@@ -203,7 +203,7 @@
     for step in range(1, count):
         pairs = [(source, (source + step) % count) for source in range(count)]
         received.append(lax.ppermute(blocks[step], axis, pairs))
-    return jnp.stack(received)
+    return received
 
 
 def per_device(orbitals, offsets, sends, pair_home, pair_visit, pair_count):
@@ -225,17 +225,22 @@
         ],
         axis=1,
     ).reshape(section_total, per_target, cell_count + extra)
-    arrived = exchange(outgoing, "home").reshape(slot_total, cell_count + extra)
-    visitors = arrived[:, :cell_count]
-    visit_offsets = arrived[:, cell_count : cell_count + 3].astype(jnp.int32)
+    arrived = exchange(outgoing, "home")
+    visitors = jnp.stack(
+        [block[:, :cell_count].reshape(per_target, B, PLANE) for block in arrived]
+    ).reshape(slot_total, B, PLANE)
+    visit_offsets = jnp.stack(
+        [block[:, cell_count : cell_count + 3] for block in arrived]
+    ).reshape(slot_total, 3).astype(jnp.int32)
 
     home_slot = pair_home[0, 0]
     visit_code = pair_visit[0, 0]
     source = visit_code // per_target
     visit_slot = ((me - source) % section_total) * per_target + visit_code % per_target
+    return_slot = ((source - me) % section_total) * per_target + visit_code % per_target
     live = (jnp.arange(slots, dtype=jnp.int32) < pair_count[0, 0]).astype(jnp.int32)
     home_orb = orbitals[home_slot].reshape(slots, B, PLANE)
-    part_orb = visitors[visit_slot].reshape(slots, B, PLANE)
+    part_orb = visitors[visit_slot]
     delta = offsets[home_slot] - visit_offsets[visit_slot]
     pair_total = lax.psum(1, "pair")
     chunk = cell_count // pair_total
@@ -245,21 +250,20 @@
             delta.reshape(-1),
             live,
             home_slot,
-            home_count + visit_slot,
+            home_count + return_slot,
             jnp.reshape(pair_me, (1,)).astype(jnp.int32),
         ]
     )
     payload = pair_fields(meta, home_orb, part_orb, pair_total, chunk)
-    got = exchange(payload, "pair")
+    got = jnp.stack(exchange(payload, "pair"))
     got_ids = got[:, :, chunk].astype(jnp.int32)
     all_rows = jnp.arange(home_count + slot_total, dtype=jnp.int32)
     picker = (got_ids[:, :, None] == all_rows[None, None, :]).astype(jnp.float32)
     totals = jnp.einsum("srk,srl->kl", picker, got[:, :, :chunk], precision=PRECISE)
     home_totals = totals[:home_count]
     back = (-jnp.arange(section_total, dtype=jnp.int32)) % section_total
-    back_rows = (back[:, None] * per_target + jnp.arange(per_target)[None, :]).reshape(-1)
-    visit_totals = totals[home_count:][back_rows].reshape(section_total, per_target, chunk)
-    returned = exchange(visit_totals, "home").reshape(slot_total, chunk)
+    visit_totals = totals[home_count:].reshape(section_total, per_target, chunk)
+    returned = jnp.stack(exchange(visit_totals, "home")).reshape(slot_total, chunk)
     owners = chosen[back].reshape(-1)
     chooser = (owners[:, None] == jnp.arange(home_count, dtype=jnp.int32)[None, :]).astype(
         jnp.float32

time: 55.8 us -> 55.8 us (level)
  starting transfers between devices: 20.4 us -> 17 us
  waiting for transfers between devices: 13.1 us -> 16.4 us
  local copies, waits for them, and re-layouts: 11.4 us -> 12 us
    ppermute x13, starting transfers between devices: 20.4 us -> 17 us  [exchange(): received.append(lax.ppermute(blocks[step], axis, pairs))]
    ppermute x13, waiting for transfers between devices: 13.1 us -> 16.4 us  [exchange(): received.append(lax.ppermute(blocks[step], axis, pairs))]
    slice x2 -> x5, local copies, waits for them, and re-layouts: 0.1 us -> 1.83 us  [the longest x4 1.48 us: per_device(): block[:, :cell_count].reshape(per_target, B, PLANE)]
    unnamed x16 -> x15, local copies, waits for them, and re-layouts: 3.31 us -> 2.54 us
    reshape x1, other arithmetic: 0.62 us -> 0.04 us  [per_device(): visitors = jnp.stack([block[:, :cell_count].reshape(per_target, B, PLANE)...]
    gather x2 -> x1, local copies, waits for them, and re-layouts: 1.39 us -> 1.26 us  [per_device(): part_orb = visitors[visit_slot]]
  transfers between devices with their start and end apart: 13 -> 13, of which waited for: 8 -> 9; matrix products, arithmetic and copies ran while one was open for 7% -> 9% of each run, Pallas kernels for 0% -> 0%
where the time goes in v9:
time: 55.8 us; the launch traced here: 55.6 us
  starting transfers between devices  17 us (30%)
  waiting for transfers between devices  16.4 us (29%)
  local copies, waits for them, and re-layouts  12 us (22%)
  Pallas kernels  6.05 us (11%)
  matrix products  2.18 us (4%)
  other arithmetic  1.08 us (2%)
  between operations  0.91 us (2%)
    ppermute x13, starting transfers between devices, exchange(): received.append(lax.ppermute(blocks[step], axis, pairs))  17 us
    ppermute x13, waiting for transfers between devices, exchange(): received.append(lax.ppermute(blocks[step], axis, pairs))  16.4 us
    pallas_call x1, Pallas kernels, pair_fields(): pl.pallas_call(functools.partial(pair_kernel, count), out_shape=tuple([bo...  6.05 us
    unnamed x15, local copies, waits for them, and re-layouts  2.54 us
    slice x4, local copies, waits for them, and re-layouts, per_device(): block[:, :cell_count].reshape(per_target, B, PLANE)  1.48 us
    gather x1, local copies, waits for them, and re-layouts, per_device(): chosen = sends[0][ahead]  1.3 us
    gather x1, local copies, waits for them, and re-layouts, per_device(): part_orb = visitors[visit_slot]  1.26 us
    dot_general x1, matrix products, per_device(): return home_totals + jnp.dot(chooser.T, returned, precision=PRECISE)  1.14 us
  transfers between devices with their start and end apart: 13, of which 9 were waited for; matrix products, arithmetic and copies ran while one was open for 9% of the time, Pallas kernels for 0%

profile of v9, /device:TPU:0, one launch (start us, length us, event | category | flops | bytes accessed | tf_op | source)
XLA Modules:
  0.0 55.6 jit_solution(6681911612789349554)
XLA Ops:
  0.0 0.8 %fusion.16 = s32[4]{0:T(128)S(1)} fusion(s32[1,1,4]{2,1,0:T(1,128)} %param.15, s32[]{:T(128)S(6)} %axis_index.23), kind=kLoop, calls=%fused_computation.71 | loop fusion | flops 60 | bytes 36 | tf_op jit(solution)/shard_map/select_n | solution.py:244
  0.8 1.3 %gather_fusion.1 = s32[4]{0:T(128)S(1)} fusion(s32[4]{0:T(128)} %bitcast.65, s32[1024]{0:T(1024)S(1)} %pad_clamp_fusion.3), kind=kCustom, calls=%fused_computation.1 | custom fusion | bytes 48 | tf_op jit(solution)/shard_map/gather | solution.py:219
  2.1 0.8 %copy.16 = s32[16,3]{1,0:T(8,128)S(1)} copy(s32[16,3]{0,1:T(4,128)} %param.12) | data formatting | bytes 384 | tf_op args[1]
  3.4 0.8 %gather_fusion.3 = bf16[4,32768]{1,0:T(4,128)(2,1)S(1)} fusion(bf16[16,32768]{1,0:T(8,128)(2,1)S(1)} %copy-done, s32[1024]{0:T(1024)S(1)} %get-tuple-element.29), kind=kCustom, calls=%fused_computation.3 | custom fusion | bytes 524304 | tf_op jit(solution)/shard_map/gather | solution.py:223
  4.7 3.1 %collective-permute-start = (bf16[1,32896]{1,0:T(2,128)(2,1)S(1)}, bf16[1,32896]{1,0:T(2,128)(2,1)S(1)}, u32[]{:S(2)}, u32[]{:S(2)}) collective-permute-start(bf16[1,32896]{1,0:T(2,128)(2,1)S(1)} %get-tuple-element.25), channel_id=1, source_target_pairs={{0,8},{8,16},{16,24},{24,0},{1,9},{9,17},{17,25},{25,1},{2,10},{10... | collective-permute-start | bytes 197384 | tf_op jit(solution)/shard_map/ppermute | solution.py:205
  7.8 2.1 %collective-permute-start.2 = (bf16[1,32896]{1,0:T(2,128)(2,1)S(1)}, bf16[1,32896]{1,0:T(2,128)(2,1)S(1)}, u32[]{:S(2)}, u32[]{:S(2)}) collective-permute-start(bf16[1,32896]{1,0:T(2,128)(2,1)S(1)} %get-tuple-element.26), channel_id=1, source_target_pairs={{0,24},{8,0},{16,8},{24,16},{1,25},{9,1},{17,9},{25,17},{2,26},{10... | collective-permute-start | bytes 197384 | tf_op jit(solution)/shard_map/ppermute | solution.py:205
  9.9 0.9 %collective-permute-start.1 = (bf16[1,32896]{1,0:T(2,128)(2,1)S(1)}, bf16[1,32896]{1,0:T(2,128)(2,1)S(1)}, u32[]{:S(2)}, u32[]{:S(2)}) collective-permute-start(bf16[1,32896]{1,0:T(2,128)(2,1)S(1)} %get-tuple-element.27), channel_id=1, source_target_pairs={{0,16},{8,24},{16,0},{24,8},{1,17},{9,25},{17,1},{25,9},{2,18},{10... | collective-permute-start | bytes 197384 | tf_op jit(solution)/shard_map/ppermute | solution.py:205
  11.3 0.6 %gather_fusion = s32[4,3]{1,0:T(4,128)S(1)} fusion(s32[16,3]{1,0:T(8,128)S(1)} %copy.16, s32[1024]{0:T(1024)S(1)} %pad_clamp_fusion.4), kind=kCustom, calls=%fused_computation | custom fusion | bytes 112 | tf_op jit(solution)/shard_map/gather | solution.py:244
  11.9 0.8 %gather_fusion.5 = bf16[4,32768]{1,0:T(4,128)(2,1)S(1)} fusion(bf16[16,32768]{1,0:T(8,128)(2,1)S(1)} %copy-done, s32[1024]{0:T(1024)S(1)} %pad_clamp_fusion.4), kind=kCustom, calls=%fused_computation.5 | custom fusion | bytes 524304 | tf_op jit(solution)/shard_map/gather | solution.py:242
  13.4 0.8 %copy.30 = bf16[1,4,32,1024]{3,2,1,0:T(8,128)(2,1)} copy(bf16[1,4,32,1024]{3,1,2,0:T(4,128)(2,1)S(1)} %bitcast.67) | data formatting | bytes 524288
  14.6 1.0 %collective-permute-done.2 = bf16[1,32896]{1,0:T(2,128)(2,1)S(1)} collective-permute-done((bf16[1,32896]{1,0:T(2,128)(2,1)S(1)}, bf16[1,32896]{1,0:T(2,128)(2,1)S(1)}, u32[]{:S(2)}, u32[]{:S(2)}) %collective-permute-start.2) | collective-permute-done | bytes 65824 | tf_op jit(solution)/shard_map/ppermute | solution.py:205
  16.1 5.8 %collective-permute-done.1 = bf16[1,32896]{1,0:T(2,128)(2,1)S(1)} collective-permute-done((bf16[1,32896]{1,0:T(2,128)(2,1)S(1)}, bf16[1,32896]{1,0:T(2,128)(2,1)S(1)}, u32[]{:S(2)}, u32[]{:S(2)}) %collective-permute-start.1) | collective-permute-done | bytes 65824 | tf_op jit(solution)/shard_map/ppermute | solution.py:205
  22.3 1.3 %gather_fusion.6 = bf16[4,32,1024]{2,1,0:T(8,128)(2,1)} fusion(bf16[4,32,1024]{2,1,0:T(8,128)(2,1)S(1)} %maximum_bitcast_fusion, s32[1024]{0:T(1024)S(1)} %get-tuple-element.28), kind=kCustom, calls=%fused_computation.6 | custom fusion | bytes 524304 | tf_op jit(solution)/shard_map/gather | solution.py:243
  23.6 0.6 %gather_fusion.4 = s32[4,3]{1,0:T(4,128)S(1)} fusion(s32[4,3]{1,0:T(4,128)S(1)} %bitcast.68, s32[1024]{0:T(1024)S(1)} %get-tuple-element.28), kind=kCustom, calls=%fused_computation.4 | custom fusion | bytes 112 | tf_op jit(solution)/shard_map/gather | solution.py:244
  24.2 0.7 %concatenate.7.meta_ref = s32[25]{0:T(128)} concatenate(s32[12]{0:T(128)S(1)} %sub.33, s32[4]{0:T(128)S(1)} %compare_convert_fusion, s32[4]{0:T(128)S(1)} %bitcast.73, s32[4]{0:T(128)S(1)} %fusion.9, s32[1]{0:T(128)} %bitcast.16), dimensions={0} | concatenate | bytes 200 | tf_op jit(solution)/shard_map/concatenate | solution.py:248
  24.9 6.1 %shard_map.109 = (f32[8,4224]{1,0:T(8,128)}, f32[8,4224]{1,0:T(8,128)}, f32[8,4224]{1,0:T(8,128)}, f32[8,4224]{1,0:T(8,128)}, f32[8,4224]{1,0:T(8,128)}, /*index...) custom-call(s32[25]{0:T(128)} %concatenate.7.meta_ref, bf16[4,32,1024]{2,1,0:T(8,128)(2,1)} %bitcast.66, ...), custom_call_target="tpu_custom_call" | custom-call | tf_op jit(solution)/shard_map/pallas_call | solution.py:185
  30.9 1.5 %collective-permute-start.4 = (f32[8,4224]{1,0:T(8,128)}, f32[8,4224]{1,0:T(8,128)S(1)}, u32[]{:S(2)}, u32[]{:S(2)}) collective-permute-start(f32[8,4224]{1,0:T(8,128)} %get-tuple-element.15), channel_id=1, source_target_pairs={{0,2},{1,3},{2,4},{3,5},{4,6},{5,7},{6,0},{7,1},{8,10},{9,11},{10,... | collective-permute-start | bytes 405512 | tf_op jit(solution)/shard_map/ppermute | solution.py:205
  32.5 2.4 %collective-permute-start.5 = (f32[8,4224]{1,0:T(8,128)}, f32[8,4224]{1,0:T(8,128)S(1)}, u32[]{:S(2)}, u32[]{:S(2)}) collective-permute-start(f32[8,4224]{1,0:T(8,128)} %get-tuple-element.16), channel_id=1, source_target_pairs={{0,3},{1,4},{2,5},{3,6},{4,7},{5,0},{6,1},{7,2},{8,11},{9,12},{10,... | collective-permute-start | bytes 405512 | tf_op jit(solution)/shard_map/ppermute | solution.py:205
  35.5 0.9 %bitcast_dynamic-update-slice_fusion.7 = f32[8,8,4224]{2,1,0:T(8,128)S(1)} fusion(f32[8,4224]{1,0:T(8,128)} %get-tuple-element.13), kind=kLoop, calls=%fused_computation.23 | loop fusion | bytes 270336
  36.4 1.1 %collective-permute-done.3 = f32[8,4224]{1,0:T(8,128)S(1)} collective-permute-done((f32[8,4224]{1,0:T(8,128)}, f32[8,4224]{1,0:T(8,128)S(1)}, u32[]{:S(2)}, u32[]{:S(2)}) %collective-permute-start.3) | collective-permute-done | bytes 135200 | tf_op jit(solution)/shard_map/ppermute | solution.py:205
  37.4 1.5 %collective-permute-start.8 = (f32[8,4224]{1,0:T(8,128)}, f32[8,4224]{1,0:T(8,128)S(1)}, u32[]{:S(2)}, u32[]{:S(2)}) collective-permute-start(f32[8,4224]{1,0:T(8,128)} %get-tuple-element.19), channel_id=1, source_target_pairs={{0,6},{1,7},{2,0},{3,1},{4,2},{5,3},{6,4},{7,5},{8,14},{9,15},{10,... | collective-permute-start | bytes 405512 | tf_op jit(solution)/shard_map/ppermute | solution.py:205
  38.9 2.6 %collective-permute-start.9 = (f32[8,4224]{1,0:T(8,128)}, f32[8,4224]{1,0:T(8,128)S(1)}, u32[]{:S(2)}, u32[]{:S(2)}) collective-permute-start(f32[8,4224]{1,0:T(8,128)} %get-tuple-element.20), channel_id=1, source_target_pairs={{0,7},{1,0},{2,1},{3,2},{4,3},{5,4},{6,5},{7,6},{8,15},{9,8},{10,9... | collective-permute-start | bytes 405512 | tf_op jit(solution)/shard_map/ppermute | solution.py:205
  41.5 2.1 %collective-permute-done.5 = f32[8,4224]{1,0:T(8,128)S(1)} collective-permute-done((f32[8,4224]{1,0:T(8,128)}, f32[8,4224]{1,0:T(8,128)S(1)}, u32[]{:S(2)}, u32[]{:S(2)}) %collective-permute-start.5) | collective-permute-done | bytes 135200 | tf_op jit(solution)/shard_map/ppermute | solution.py:205
  43.8 1.9 %collective-permute-done.7 = f32[8,4224]{1,0:T(8,128)S(1)} collective-permute-done((f32[8,4224]{1,0:T(8,128)}, f32[8,4224]{1,0:T(8,128)S(1)}, u32[]{:S(2)}, u32[]{:S(2)}) %collective-permute-start.7) | collective-permute-done | bytes 135200 | tf_op jit(solution)/shard_map/ppermute | solution.py:205
  46.1 1.0 %convolution_bitcast_fusion = f32[20,4096]{1,0:T(8,128)S(1)} fusion(f32[8,8,4096]{2,1,0:T(8,128)S(1)} %slice.121, s32[8,8]{0,1:T(8,128)S(1)} %bitcast.69), kind=kOutput, calls=%fused_computation.8 | convolution fusion | flops 62915840 | bytes 1376512 | tf_op jit(solution)/shard_map/srk,srl->kl/dot_general | solution.py:262
  47.2 1.7 %collective-permute-start.12 = (f32[1,4096]{1,0:T(1,128)S(1)}, f32[1,4096]{1,0:T(1,128)S(1)}, u32[]{:S(2)}, u32[]{:S(2)}) collective-permute-start(f32[1,4096]{1,0:T(1,128)S(1)} %get-tuple-element.22), channel_id=1, source_target_pairs={{0,24},{8,0},{16,8},{24,16},{1,25},{9,1},{17,9},{25,17},{2,26},{10... | collective-permute-start | bytes 49160 | tf_op jit(solution)/shard_map/ppermute | solution.py:205
  48.8 0.6 %collective-permute-start.10 = (f32[1,4096]{1,0:T(1,128)S(1)}, f32[1,4096]{1,0:T(1,128)S(1)}, u32[]{:S(2)}, u32[]{:S(2)}) collective-permute-start(f32[1,4096]{1,0:T(1,128)S(1)} %get-tuple-element.24), channel_id=1, source_target_pairs={{0,8},{8,16},{16,24},{24,0},{1,9},{9,17},{17,25},{25,1},{2,10},{10... | collective-permute-start | bytes 49160 | tf_op jit(solution)/shard_map/ppermute | solution.py:205
  49.5 0.6 %gather_fusion.7 = s32[4]{0:T(128)S(1)} fusion(s32[4]{0:T(128)S(1)} %gather_fusion.1, s32[1024]{0:T(1024)S(1)} %pad_clamp_fusion), kind=kCustom, calls=%fused_computation.7 | custom fusion | bytes 48 | tf_op jit(solution)/shard_map/gather | solution.py:267
  50.1 0.8 %collective-permute-done.12 = f32[1,4096]{1,0:T(1,128)S(1)} collective-permute-done((f32[1,4096]{1,0:T(1,128)S(1)}, f32[1,4096]{1,0:T(1,128)S(1)}, u32[]{:S(2)}, u32[]{:S(2)}) %collective-permute-start.12) | collective-permute-done | bytes 16416 | tf_op jit(solution)/shard_map/ppermute | solution.py:205
  51.0 2.5 %collective-permute-done.11 = f32[1,4096]{1,0:T(1,128)S(1)} collective-permute-done((f32[1,4096]{1,0:T(1,128)S(1)}, f32[1,4096]{1,0:T(1,128)S(1)}, u32[]{:S(2)}, u32[]{:S(2)}) %collective-permute-start.11) | collective-permute-done | bytes 16416 | tf_op jit(solution)/shard_map/ppermute | solution.py:205
  53.5 0.9 %collective-permute-done.10 = f32[1,4096]{1,0:T(1,128)S(1)} collective-permute-done((f32[1,4096]{1,0:T(1,128)S(1)}, f32[1,4096]{1,0:T(1,128)S(1)}, u32[]{:S(2)}, u32[]{:S(2)}) %collective-permute-start.10) | collective-permute-done | bytes 16416 | tf_op jit(solution)/shard_map/ppermute | solution.py:205
  54.4 1.1 %convolution_add_fusion = f32[16,4096]{1,0:T(8,128)} fusion(f32[20,4096]{1,0:T(8,128)S(1)} %convolution_bitcast_fusion, f32[4,1,4096]{2,1,0:T(1,128)S(1)} %pad_maximum_fusion, s32[4]{0:T(128)S(1)} %gather_fusion.7), kind=kOutput, calls=%fused_computation.9 | convolution fusion | flops 3211328 | bytes 589840 | tf_op jit(solution)/shard_map/dot_general | solution.py:271
  (57 shorter events, 4.1 us)
Async XLA Ops:
  0.0 3.4 %copy-start = (bf16[16,32768]{1,0:T(8,128)(2,1)S(1)}, bf16[16,32768]{1,0:T(8,128)(2,1)}, u32[]{:S(2)}) copy-start(bf16[16,32768]{1,0:T(8,128)(2,1)} %param.11) | copy-start | bytes 3145732
  4.2 6.6 %copy-start.2 = (s32[1,1,4]{2,1,0:T(1,128)S(1)}, s32[1,1,4]{2,1,0:T(1,128)}, u32[]{:S(2)}) copy-start(s32[1,1,4]{2,1,0:T(1,128)} %param.15) | copy-start | bytes 52
  4.2 7.0 %copy-start.1 = (s32[1,1,4]{2,1,0:T(1,128)S(1)}, s32[1,1,4]{2,1,0:T(1,128)}, u32[]{:S(2)}) copy-start(s32[1,1,4]{2,1,0:T(1,128)} %param.14) | copy-start | bytes 52
  4.7 9.4 %collective-permute-start = (bf16[1,32896]{1,0:T(2,128)(2,1)S(1)}, bf16[1,32896]{1,0:T(2,128)(2,1)S(1)}, u32[]{:S(2)}, u32[]{:S(2)}) collective-permute-start(bf16[1,32896]{1,0:T(2,128)(2,1)S(1)} %get-tuple-element.25), channel_id=1, source_target_pairs={{0,8},{8,16},{16,24},{24,0},{1,9},{9,17},{17,25},{25,1},{2,10},{10... | collective-permute-start | bytes 197384 | tf_op jit(solution)/shard_map/ppermute | solution.py:205
  7.8 7.8 %collective-permute-start.2 = (bf16[1,32896]{1,0:T(2,128)(2,1)S(1)}, bf16[1,32896]{1,0:T(2,128)(2,1)S(1)}, u32[]{:S(2)}, u32[]{:S(2)}) collective-permute-start(bf16[1,32896]{1,0:T(2,128)(2,1)S(1)} %get-tuple-element.26), channel_id=1, source_target_pairs={{0,24},{8,0},{16,8},{24,16},{1,25},{9,1},{17,9},{25,17},{2,26},{10... | collective-permute-start | bytes 197384 | tf_op jit(solution)/shard_map/ppermute | solution.py:205
  9.9 11.9 %collective-permute-start.1 = (bf16[1,32896]{1,0:T(2,128)(2,1)S(1)}, bf16[1,32896]{1,0:T(2,128)(2,1)S(1)}, u32[]{:S(2)}, u32[]{:S(2)}) collective-permute-start(bf16[1,32896]{1,0:T(2,128)(2,1)S(1)} %get-tuple-element.27), channel_id=1, source_target_pairs={{0,16},{8,24},{16,0},{24,8},{1,17},{9,25},{17,1},{25,9},{2,18},{10... | collective-permute-start | bytes 197384 | tf_op jit(solution)/shard_map/ppermute | solution.py:205
  30.9 6.5 %collective-permute-start.3 = (f32[8,4224]{1,0:T(8,128)}, f32[8,4224]{1,0:T(8,128)S(1)}, u32[]{:S(2)}, u32[]{:S(2)}) collective-permute-start(f32[8,4224]{1,0:T(8,128)} %get-tuple-element.14), channel_id=1, source_target_pairs={{0,1},{1,2},{2,3},{3,4},{4,5},{5,6},{6,7},{7,0},{8,9},{9,10},{10,1... | collective-permute-start | bytes 405512 | tf_op jit(solution)/shard_map/ppermute | solution.py:205
  30.9 8.0 %collective-permute-start.4 = (f32[8,4224]{1,0:T(8,128)}, f32[8,4224]{1,0:T(8,128)S(1)}, u32[]{:S(2)}, u32[]{:S(2)}) collective-permute-start(f32[8,4224]{1,0:T(8,128)} %get-tuple-element.15), channel_id=1, source_target_pairs={{0,2},{1,3},{2,4},{3,5},{4,6},{5,7},{6,0},{7,1},{8,10},{9,11},{10,... | collective-permute-start | bytes 405512 | tf_op jit(solution)/shard_map/ppermute | solution.py:205
  32.5 11.1 %collective-permute-start.5 = (f32[8,4224]{1,0:T(8,128)}, f32[8,4224]{1,0:T(8,128)S(1)}, u32[]{:S(2)}, u32[]{:S(2)}) collective-permute-start(f32[8,4224]{1,0:T(8,128)} %get-tuple-element.16), channel_id=1, source_target_pairs={{0,3},{1,4},{2,5},{3,6},{4,7},{5,0},{6,1},{7,2},{8,11},{9,12},{10,... | collective-permute-start | bytes 405512 | tf_op jit(solution)/shard_map/ppermute | solution.py:205
  34.8 9.0 %collective-permute-start.6 = (f32[8,4224]{1,0:T(8,128)}, f32[8,4224]{1,0:T(8,128)S(1)}, u32[]{:S(2)}, u32[]{:S(2)}) collective-permute-start(f32[8,4224]{1,0:T(8,128)} %get-tuple-element.17), channel_id=1, source_target_pairs={{0,4},{1,5},{2,6},{3,7},{4,0},{5,1},{6,2},{7,3},{8,12},{9,13},{10,... | collective-permute-start | bytes 405512 | tf_op jit(solution)/shard_map/ppermute | solution.py:205
  35.4 10.4 %collective-permute-start.7 = (f32[8,4224]{1,0:T(8,128)}, f32[8,4224]{1,0:T(8,128)S(1)}, u32[]{:S(2)}, u32[]{:S(2)}) collective-permute-start(f32[8,4224]{1,0:T(8,128)} %get-tuple-element.18), channel_id=1, source_target_pairs={{0,5},{1,6},{2,7},{3,0},{4,1},{5,2},{6,3},{7,4},{8,13},{9,14},{10,... | collective-permute-start | bytes 405512 | tf_op jit(solution)/shard_map/ppermute | solution.py:205
  37.4 8.3 %collective-permute-start.8 = (f32[8,4224]{1,0:T(8,128)}, f32[8,4224]{1,0:T(8,128)S(1)}, u32[]{:S(2)}, u32[]{:S(2)}) collective-permute-start(f32[8,4224]{1,0:T(8,128)} %get-tuple-element.19), channel_id=1, source_target_pairs={{0,6},{1,7},{2,0},{3,1},{4,2},{5,3},{6,4},{7,5},{8,14},{9,15},{10,... | collective-permute-start | bytes 405512 | tf_op jit(solution)/shard_map/ppermute | solution.py:205
  38.9 6.9 %collective-permute-start.9 = (f32[8,4224]{1,0:T(8,128)}, f32[8,4224]{1,0:T(8,128)S(1)}, u32[]{:S(2)}, u32[]{:S(2)}) collective-permute-start(f32[8,4224]{1,0:T(8,128)} %get-tuple-element.20), channel_id=1, source_target_pairs={{0,7},{1,0},{2,1},{3,2},{4,3},{5,4},{6,5},{7,6},{8,15},{9,8},{10,9... | collective-permute-start | bytes 405512 | tf_op jit(solution)/shard_map/ppermute | solution.py:205
  47.2 3.8 %collective-permute-start.12 = (f32[1,4096]{1,0:T(1,128)S(1)}, f32[1,4096]{1,0:T(1,128)S(1)}, u32[]{:S(2)}, u32[]{:S(2)}) collective-permute-start(f32[1,4096]{1,0:T(1,128)S(1)} %get-tuple-element.22), channel_id=1, source_target_pairs={{0,24},{8,0},{16,8},{24,16},{1,25},{9,1},{17,9},{25,17},{2,26},{10... | collective-permute-start | bytes 49160 | tf_op jit(solution)/shard_map/ppermute | solution.py:205
  48.8 4.7 %collective-permute-start.11 = (f32[1,4096]{1,0:T(1,128)S(1)}, f32[1,4096]{1,0:T(1,128)S(1)}, u32[]{:S(2)}, u32[]{:S(2)}) collective-permute-start(f32[1,4096]{1,0:T(1,128)S(1)} %get-tuple-element.23), channel_id=1, source_target_pairs={{0,16},{8,24},{16,0},{24,8},{1,17},{9,25},{17,1},{25,9},{2,18},{10... | collective-permute-start | bytes 49160 | tf_op jit(solution)/shard_map/ppermute | solution.py:205
  48.8 5.5 %collective-permute-start.10 = (f32[1,4096]{1,0:T(1,128)S(1)}, f32[1,4096]{1,0:T(1,128)S(1)}, u32[]{:S(2)}, u32[]{:S(2)}) collective-permute-start(f32[1,4096]{1,0:T(1,128)S(1)} %get-tuple-element.24), channel_id=1, source_target_pairs={{0,8},{8,16},{16,24},{24,0},{1,9},{9,17},{17,25},{25,1},{2,10},{10... | collective-permute-start | bytes 49160 | tf_op jit(solution)/shard_map/ppermute | solution.py:205

commit v10 on v9

--- a/solution.py
+++ b/solution.py
@@ -215,8 +215,7 @@
     slots = pair_home.shape[2]
     extra = 128
     me = lax.axis_index("home")
-    ahead = (me + jnp.arange(section_total, dtype=jnp.int32)) % section_total
-    chosen = sends[0][ahead]
+    chosen = lax.dynamic_slice_in_dim(jnp.concatenate([sends[0], sends[0]]), me, section_total)
     flat_chosen = chosen.reshape(-1)
     outgoing = jnp.concatenate(
         [
@@ -259,7 +258,7 @@
     got_ids = got[:, :, chunk].astype(jnp.int32)
     all_rows = jnp.arange(home_count + slot_total, dtype=jnp.int32)
     picker = (got_ids[:, :, None] == all_rows[None, None, :]).astype(jnp.float32)
-    totals = jnp.einsum("srk,srl->kl", picker, got[:, :, :chunk], precision=PRECISE)
+    totals = jnp.einsum("srk,srl->kl", picker, got[:, :, :chunk], precision=lax.Precision.HIGH)
     home_totals = totals[:home_count]
     back = (-jnp.arange(section_total, dtype=jnp.int32)) % section_total
     visit_totals = totals[home_count:].reshape(section_total, per_target, chunk)
@@ -268,7 +267,7 @@
     chooser = (owners[:, None] == jnp.arange(home_count, dtype=jnp.int32)[None, :]).astype(
         jnp.float32
     )
-    return home_totals + jnp.dot(chooser.T, returned, precision=PRECISE)
+    return home_totals + jnp.dot(chooser.T, returned, precision=lax.Precision.HIGH)
 
 
 def solution(mesh):

time: 55.8 us -> 55 us (0.986)
  local copies, waits for them, and re-layouts: 12 us -> 10.6 us
  other arithmetic: 1.08 us -> 1.88 us
    gather x1 -> x0, local copies, waits for them, and re-layouts: 1.3 us -> none  [per_device(): chosen = sends[0][ahead]]
    concatenate x0 -> x1, other arithmetic: none -> 0.83 us  [per_device(): jnp.concatenate([sends[0], sends[0]])]
where the time goes in v10:
time: 55 us; the launch traced here: 54.7 us
  starting transfers between devices  17 us (31%)
  waiting for transfers between devices  16.4 us (30%)
  local copies, waits for them, and re-layouts  10.6 us (19%)
  Pallas kernels  6.04 us (11%)
  matrix products  1.91 us (3%)
  other arithmetic  1.88 us (3%)
  between operations  0.91 us (2%)
    ppermute x13, starting transfers between devices, exchange(): received.append(lax.ppermute(blocks[step], axis, pairs))  17 us
    ppermute x13, waiting for transfers between devices, exchange(): received.append(lax.ppermute(blocks[step], axis, pairs))  16.4 us
    pallas_call x1, Pallas kernels, pair_fields(): pl.pallas_call(functools.partial(pair_kernel, count), out_shape=tuple([bo...  6.04 us
    unnamed x15, local copies, waits for them, and re-layouts  2.53 us
    slice x4, local copies, waits for them, and re-layouts, per_device(): block[:, :cell_count].reshape(per_target, B, PLANE)  1.48 us
    gather x1, local copies, waits for them, and re-layouts, per_device(): part_orb = visitors[visit_slot]  1.26 us
    gather x2, local copies, waits for them, and re-layouts, per_device(): delta = offsets[home_slot] - visit_offsets[visit_slot]  1.12 us
  transfers between devices with their start and end apart: 13, of which 9 were waited for; matrix products, arithmetic and copies ran while one was open for 9% of the time, Pallas kernels for 0%

profile of v10, /device:TPU:0, one launch (start us, length us, event | category | flops | bytes accessed | tf_op | source)
XLA Modules:
  0.0 54.7 jit_solution(2973001559389204980)
XLA Ops:
  0.0 0.8 %pad_add_fusion = s32[8,1]{0,1:T(1,128)S(1)} fusion(s32[4,1]{0,1:T(1,128)} %bitcast.71), kind=kLoop, calls=%fused_computation.67 | loop fusion | flops 8 | bytes 48 | tf_op jit(solution)/shard_map/concatenate | solution.py:218
  0.8 0.7 %fusion.14 = s32[4]{0:T(128)S(1)} fusion(s32[1,1,4]{2,1,0:T(1,128)} %param.15, s32[]{:T(128)S(6)} %axis_index.23), kind=kLoop, calls=%fused_computation.63 | loop fusion | flops 60 | bytes 36 | tf_op jit(solution)/shard_map/select_n | solution.py:243
  1.5 0.8 %copy.16 = s32[16,3]{1,0:T(8,128)S(1)} copy(s32[16,3]{0,1:T(4,128)} %param.12) | data formatting | bytes 384 | tf_op args[1]
  2.9 0.8 %gather_fusion.2 = bf16[4,32768]{1,0:T(4,128)(2,1)S(1)} fusion(bf16[16,32768]{1,0:T(8,128)(2,1)S(1)} %copy-done, s32[1024]{0:T(1024)S(1)} %get-tuple-element.31), kind=kCustom, calls=%fused_computation.2 | custom fusion | bytes 524304 | tf_op jit(solution)/shard_map/gather | solution.py:222
  4.2 3.1 %collective-permute-start = (bf16[1,32896]{1,0:T(2,128)(2,1)S(1)}, bf16[1,32896]{1,0:T(2,128)(2,1)S(1)}, u32[]{:S(2)}, u32[]{:S(2)}) collective-permute-start(bf16[1,32896]{1,0:T(2,128)(2,1)S(1)} %get-tuple-element.25), channel_id=1, source_target_pairs={{0,8},{8,16},{16,24},{24,0},{1,9},{9,17},{17,25},{25,1},{2,10},{10... | collective-permute-start | bytes 197384 | tf_op jit(solution)/shard_map/ppermute | solution.py:205
  7.3 2.1 %collective-permute-start.2 = (bf16[1,32896]{1,0:T(2,128)(2,1)S(1)}, bf16[1,32896]{1,0:T(2,128)(2,1)S(1)}, u32[]{:S(2)}, u32[]{:S(2)}) collective-permute-start(bf16[1,32896]{1,0:T(2,128)(2,1)S(1)} %get-tuple-element.26), channel_id=1, source_target_pairs={{0,24},{8,0},{16,8},{24,16},{1,25},{9,1},{17,9},{25,17},{2,26},{10... | collective-permute-start | bytes 197384 | tf_op jit(solution)/shard_map/ppermute | solution.py:205
  9.4 0.9 %collective-permute-start.1 = (bf16[1,32896]{1,0:T(2,128)(2,1)S(1)}, bf16[1,32896]{1,0:T(2,128)(2,1)S(1)}, u32[]{:S(2)}, u32[]{:S(2)}) collective-permute-start(bf16[1,32896]{1,0:T(2,128)(2,1)S(1)} %get-tuple-element.27), channel_id=1, source_target_pairs={{0,16},{8,24},{16,0},{24,8},{1,17},{9,25},{17,1},{25,9},{2,18},{10... | collective-permute-start | bytes 197384 | tf_op jit(solution)/shard_map/ppermute | solution.py:205
  10.8 0.6 %gather_fusion = s32[4,3]{1,0:T(4,128)S(1)} fusion(s32[16,3]{1,0:T(8,128)S(1)} %copy.16, s32[1024]{0:T(1024)S(1)} %pad_clamp_fusion.3), kind=kCustom, calls=%fused_computation | custom fusion | bytes 112 | tf_op jit(solution)/shard_map/gather | solution.py:243
  11.4 0.8 %gather_fusion.4 = bf16[4,32768]{1,0:T(4,128)(2,1)S(1)} fusion(bf16[16,32768]{1,0:T(8,128)(2,1)S(1)} %copy-done, s32[1024]{0:T(1024)S(1)} %pad_clamp_fusion.3), kind=kCustom, calls=%fused_computation.4 | custom fusion | bytes 524304 | tf_op jit(solution)/shard_map/gather | solution.py:241
  12.9 0.8 %copy.30 = bf16[1,4,32,1024]{3,2,1,0:T(8,128)(2,1)} copy(bf16[1,4,32,1024]{3,1,2,0:T(4,128)(2,1)S(1)} %bitcast.64) | data formatting | bytes 524288
  14.1 1.1 %collective-permute-done.2 = bf16[1,32896]{1,0:T(2,128)(2,1)S(1)} collective-permute-done((bf16[1,32896]{1,0:T(2,128)(2,1)S(1)}, bf16[1,32896]{1,0:T(2,128)(2,1)S(1)}, u32[]{:S(2)}, u32[]{:S(2)}) %collective-permute-start.2) | collective-permute-done | bytes 65824 | tf_op jit(solution)/shard_map/ppermute | solution.py:205
  15.5 5.8 %collective-permute-done.1 = bf16[1,32896]{1,0:T(2,128)(2,1)S(1)} collective-permute-done((bf16[1,32896]{1,0:T(2,128)(2,1)S(1)}, bf16[1,32896]{1,0:T(2,128)(2,1)S(1)}, u32[]{:S(2)}, u32[]{:S(2)}) %collective-permute-start.1) | collective-permute-done | bytes 65824 | tf_op jit(solution)/shard_map/ppermute | solution.py:205
  21.8 1.3 %gather_fusion.5 = bf16[4,32,1024]{2,1,0:T(8,128)(2,1)} fusion(bf16[4,32,1024]{2,1,0:T(8,128)(2,1)S(1)} %maximum_bitcast_fusion, s32[1024]{0:T(1024)S(1)} %get-tuple-element.30), kind=kCustom, calls=%fused_computation.5 | custom fusion | bytes 524304 | tf_op jit(solution)/shard_map/gather | solution.py:242
  23.1 0.6 %gather_fusion.3 = s32[4,3]{1,0:T(4,128)S(1)} fusion(s32[4,3]{1,0:T(4,128)S(1)} %bitcast.65, s32[1024]{0:T(1024)S(1)} %get-tuple-element.30), kind=kCustom, calls=%fused_computation.3 | custom fusion | bytes 112 | tf_op jit(solution)/shard_map/gather | solution.py:243
  23.7 0.6 %concatenate.11.meta_ref = s32[25]{0:T(128)} concatenate(s32[12]{0:T(128)S(1)} %sub.36, s32[4]{0:T(128)S(1)} %compare_convert_fusion, s32[4]{0:T(128)S(1)} %bitcast.70, s32[4]{0:T(128)S(1)} %fusion.9, s32[1]{0:T(128)} %bitcast.14), dimensions={0} | concatenate | bytes 200 | tf_op jit(solution)/shard_map/concatenate | solution.py:247
  24.3 6.0 %shard_map.109 = (f32[8,4224]{1,0:T(8,128)}, f32[8,4224]{1,0:T(8,128)}, f32[8,4224]{1,0:T(8,128)}, f32[8,4224]{1,0:T(8,128)}, f32[8,4224]{1,0:T(8,128)}, /*index...) custom-call(s32[25]{0:T(128)} %concatenate.11.meta_ref, bf16[4,32,1024]{2,1,0:T(8,128)(2,1)} %bitcast.63, ...), custom_call_target="tpu_custom_call" | custom-call | tf_op jit(solution)/shard_map/pallas_call | solution.py:185
  30.4 1.5 %collective-permute-start.4 = (f32[8,4224]{1,0:T(8,128)}, f32[8,4224]{1,0:T(8,128)S(1)}, u32[]{:S(2)}, u32[]{:S(2)}) collective-permute-start(f32[8,4224]{1,0:T(8,128)} %get-tuple-element.15), channel_id=1, source_target_pairs={{0,2},{1,3},{2,4},{3,5},{4,6},{5,7},{6,0},{7,1},{8,10},{9,11},{10,... | collective-permute-start | bytes 405512 | tf_op jit(solution)/shard_map/ppermute | solution.py:205
  31.9 2.4 %collective-permute-start.5 = (f32[8,4224]{1,0:T(8,128)}, f32[8,4224]{1,0:T(8,128)S(1)}, u32[]{:S(2)}, u32[]{:S(2)}) collective-permute-start(f32[8,4224]{1,0:T(8,128)} %get-tuple-element.16), channel_id=1, source_target_pairs={{0,3},{1,4},{2,5},{3,6},{4,7},{5,0},{6,1},{7,2},{8,11},{9,12},{10,... | collective-permute-start | bytes 405512 | tf_op jit(solution)/shard_map/ppermute | solution.py:205
  34.9 0.9 %bitcast_dynamic-update-slice_fusion.7 = f32[8,8,4224]{2,1,0:T(8,128)S(1)} fusion(f32[8,4224]{1,0:T(8,128)} %get-tuple-element.13), kind=kLoop, calls=%fused_computation.22 | loop fusion | bytes 270336
  35.8 1.1 %collective-permute-done.3 = f32[8,4224]{1,0:T(8,128)S(1)} collective-permute-done((f32[8,4224]{1,0:T(8,128)}, f32[8,4224]{1,0:T(8,128)S(1)}, u32[]{:S(2)}, u32[]{:S(2)}) %collective-permute-start.3) | collective-permute-done | bytes 135200 | tf_op jit(solution)/shard_map/ppermute | solution.py:205
  36.9 1.5 %collective-permute-start.8 = (f32[8,4224]{1,0:T(8,128)}, f32[8,4224]{1,0:T(8,128)S(1)}, u32[]{:S(2)}, u32[]{:S(2)}) collective-permute-start(f32[8,4224]{1,0:T(8,128)} %get-tuple-element.19), channel_id=1, source_target_pairs={{0,6},{1,7},{2,0},{3,1},{4,2},{5,3},{6,4},{7,5},{8,14},{9,15},{10,... | collective-permute-start | bytes 405512 | tf_op jit(solution)/shard_map/ppermute | solution.py:205
  38.4 2.6 %collective-permute-start.9 = (f32[8,4224]{1,0:T(8,128)}, f32[8,4224]{1,0:T(8,128)S(1)}, u32[]{:S(2)}, u32[]{:S(2)}) collective-permute-start(f32[8,4224]{1,0:T(8,128)} %get-tuple-element.20), channel_id=1, source_target_pairs={{0,7},{1,0},{2,1},{3,2},{4,3},{5,4},{6,5},{7,6},{8,15},{9,8},{10,9... | collective-permute-start | bytes 405512 | tf_op jit(solution)/shard_map/ppermute | solution.py:205
  41.0 2.1 %collective-permute-done.5 = f32[8,4224]{1,0:T(8,128)S(1)} collective-permute-done((f32[8,4224]{1,0:T(8,128)}, f32[8,4224]{1,0:T(8,128)S(1)}, u32[]{:S(2)}, u32[]{:S(2)}) %collective-permute-start.5) | collective-permute-done | bytes 135200 | tf_op jit(solution)/shard_map/ppermute | solution.py:205
  43.3 1.9 %collective-permute-done.7 = f32[8,4224]{1,0:T(8,128)S(1)} collective-permute-done((f32[8,4224]{1,0:T(8,128)}, f32[8,4224]{1,0:T(8,128)S(1)}, u32[]{:S(2)}, u32[]{:S(2)}) %collective-permute-start.7) | collective-permute-done | bytes 135200 | tf_op jit(solution)/shard_map/ppermute | solution.py:205
  45.5 0.8 %convolution_bitcast_fusion = f32[20,4096]{1,0:T(8,128)S(1)} fusion(f32[8,8,4096]{2,1,0:T(8,128)S(1)} %slice.119, s32[8,8]{0,1:T(8,128)S(1)} %bitcast.66), kind=kOutput, calls=%fused_computation.7 | convolution fusion | flops 31458560 | bytes 1376512 | tf_op jit(solution)/shard_map/srk,srl->kl/dot_general | solution.py:261
  46.4 1.7 %collective-permute-start.12 = (f32[1,4096]{1,0:T(1,128)S(1)}, f32[1,4096]{1,0:T(1,128)S(1)}, u32[]{:S(2)}, u32[]{:S(2)}) collective-permute-start(f32[1,4096]{1,0:T(1,128)S(1)} %get-tuple-element.22), channel_id=1, source_target_pairs={{0,24},{8,0},{16,8},{24,16},{1,25},{9,1},{17,9},{25,17},{2,26},{10... | collective-permute-start | bytes 49160 | tf_op jit(solution)/shard_map/ppermute | solution.py:205
  48.1 0.6 %collective-permute-start.10 = (f32[1,4096]{1,0:T(1,128)S(1)}, f32[1,4096]{1,0:T(1,128)S(1)}, u32[]{:S(2)}, u32[]{:S(2)}) collective-permute-start(f32[1,4096]{1,0:T(1,128)S(1)} %get-tuple-element.24), channel_id=1, source_target_pairs={{0,8},{8,16},{16,24},{24,0},{1,9},{9,17},{17,25},{25,1},{2,10},{10... | collective-permute-start | bytes 49160 | tf_op jit(solution)/shard_map/ppermute | solution.py:205
  48.7 0.6 %gather_fusion.6 = s32[4]{0:T(128)S(1)} fusion(s32[4]{0:T(128)S(1)} %get-tuple-element.28, s32[1024]{0:T(1024)S(1)} %pad_clamp_fusion), kind=kCustom, calls=%fused_computation.6 | custom fusion | bytes 48 | tf_op jit(solution)/shard_map/gather | solution.py:266
  49.4 0.8 %collective-permute-done.12 = f32[1,4096]{1,0:T(1,128)S(1)} collective-permute-done((f32[1,4096]{1,0:T(1,128)S(1)}, f32[1,4096]{1,0:T(1,128)S(1)}, u32[]{:S(2)}, u32[]{:S(2)}) %collective-permute-start.12) | collective-permute-done | bytes 16416 | tf_op jit(solution)/shard_map/ppermute | solution.py:205
  50.2 2.5 %collective-permute-done.11 = f32[1,4096]{1,0:T(1,128)S(1)} collective-permute-done((f32[1,4096]{1,0:T(1,128)S(1)}, f32[1,4096]{1,0:T(1,128)S(1)}, u32[]{:S(2)}, u32[]{:S(2)}) %collective-permute-start.11) | collective-permute-done | bytes 16416 | tf_op jit(solution)/shard_map/ppermute | solution.py:205
  52.7 0.9 %collective-permute-done.10 = f32[1,4096]{1,0:T(1,128)S(1)} collective-permute-done((f32[1,4096]{1,0:T(1,128)S(1)}, f32[1,4096]{1,0:T(1,128)S(1)}, u32[]{:S(2)}, u32[]{:S(2)}) %collective-permute-start.10) | collective-permute-done | bytes 16416 | tf_op jit(solution)/shard_map/ppermute | solution.py:205
  53.7 1.1 %convolution_add_fusion = f32[16,4096]{1,0:T(8,128)} fusion(f32[20,4096]{1,0:T(8,128)S(1)} %convolution_bitcast_fusion, f32[4,1,4096]{2,1,0:T(1,128)S(1)} %pad_maximum_fusion, s32[4]{0:T(128)S(1)} %gather_fusion.6), kind=kOutput, calls=%fused_computation.8 | convolution fusion | flops 1638464 | bytes 589840 | tf_op jit(solution)/shard_map/dot_general | solution.py:270
  (55 shorter events, 4.2 us)
Async XLA Ops:
  0.0 2.9 %copy-start = (bf16[16,32768]{1,0:T(8,128)(2,1)S(1)}, bf16[16,32768]{1,0:T(8,128)(2,1)}, u32[]{:S(2)}) copy-start(bf16[16,32768]{1,0:T(8,128)(2,1)} %param.11) | copy-start | bytes 3145732
  3.7 6.6 %copy-start.2 = (s32[1,1,4]{2,1,0:T(1,128)S(1)}, s32[1,1,4]{2,1,0:T(1,128)}, u32[]{:S(2)}) copy-start(s32[1,1,4]{2,1,0:T(1,128)} %param.15) | copy-start | bytes 52
  3.7 7.0 %copy-start.1 = (s32[1,1,4]{2,1,0:T(1,128)S(1)}, s32[1,1,4]{2,1,0:T(1,128)}, u32[]{:S(2)}) copy-start(s32[1,1,4]{2,1,0:T(1,128)} %param.14) | copy-start | bytes 52
  4.2 9.4 %collective-permute-start = (bf16[1,32896]{1,0:T(2,128)(2,1)S(1)}, bf16[1,32896]{1,0:T(2,128)(2,1)S(1)}, u32[]{:S(2)}, u32[]{:S(2)}) collective-permute-start(bf16[1,32896]{1,0:T(2,128)(2,1)S(1)} %get-tuple-element.25), channel_id=1, source_target_pairs={{0,8},{8,16},{16,24},{24,0},{1,9},{9,17},{17,25},{25,1},{2,10},{10... | collective-permute-start | bytes 197384 | tf_op jit(solution)/shard_map/ppermute | solution.py:205
  7.3 7.8 %collective-permute-start.2 = (bf16[1,32896]{1,0:T(2,128)(2,1)S(1)}, bf16[1,32896]{1,0:T(2,128)(2,1)S(1)}, u32[]{:S(2)}, u32[]{:S(2)}) collective-permute-start(bf16[1,32896]{1,0:T(2,128)(2,1)S(1)} %get-tuple-element.26), channel_id=1, source_target_pairs={{0,24},{8,0},{16,8},{24,16},{1,25},{9,1},{17,9},{25,17},{2,26},{10... | collective-permute-start | bytes 197384 | tf_op jit(solution)/shard_map/ppermute | solution.py:205
  9.4 11.9 %collective-permute-start.1 = (bf16[1,32896]{1,0:T(2,128)(2,1)S(1)}, bf16[1,32896]{1,0:T(2,128)(2,1)S(1)}, u32[]{:S(2)}, u32[]{:S(2)}) collective-permute-start(bf16[1,32896]{1,0:T(2,128)(2,1)S(1)} %get-tuple-element.27), channel_id=1, source_target_pairs={{0,16},{8,24},{16,0},{24,8},{1,17},{9,25},{17,1},{25,9},{2,18},{10... | collective-permute-start | bytes 197384 | tf_op jit(solution)/shard_map/ppermute | solution.py:205
  30.4 6.5 %collective-permute-start.3 = (f32[8,4224]{1,0:T(8,128)}, f32[8,4224]{1,0:T(8,128)S(1)}, u32[]{:S(2)}, u32[]{:S(2)}) collective-permute-start(f32[8,4224]{1,0:T(8,128)} %get-tuple-element.14), channel_id=1, source_target_pairs={{0,1},{1,2},{2,3},{3,4},{4,5},{5,6},{6,7},{7,0},{8,9},{9,10},{10,1... | collective-permute-start | bytes 405512 | tf_op jit(solution)/shard_map/ppermute | solution.py:205
  30.4 8.0 %collective-permute-start.4 = (f32[8,4224]{1,0:T(8,128)}, f32[8,4224]{1,0:T(8,128)S(1)}, u32[]{:S(2)}, u32[]{:S(2)}) collective-permute-start(f32[8,4224]{1,0:T(8,128)} %get-tuple-element.15), channel_id=1, source_target_pairs={{0,2},{1,3},{2,4},{3,5},{4,6},{5,7},{6,0},{7,1},{8,10},{9,11},{10,... | collective-permute-start | bytes 405512 | tf_op jit(solution)/shard_map/ppermute | solution.py:205
  31.9 11.1 %collective-permute-start.5 = (f32[8,4224]{1,0:T(8,128)}, f32[8,4224]{1,0:T(8,128)S(1)}, u32[]{:S(2)}, u32[]{:S(2)}) collective-permute-start(f32[8,4224]{1,0:T(8,128)} %get-tuple-element.16), channel_id=1, source_target_pairs={{0,3},{1,4},{2,5},{3,6},{4,7},{5,0},{6,1},{7,2},{8,11},{9,12},{10,... | collective-permute-start | bytes 405512 | tf_op jit(solution)/shard_map/ppermute | solution.py:205
  34.3 9.0 %collective-permute-start.6 = (f32[8,4224]{1,0:T(8,128)}, f32[8,4224]{1,0:T(8,128)S(1)}, u32[]{:S(2)}, u32[]{:S(2)}) collective-permute-start(f32[8,4224]{1,0:T(8,128)} %get-tuple-element.17), channel_id=1, source_target_pairs={{0,4},{1,5},{2,6},{3,7},{4,0},{5,1},{6,2},{7,3},{8,12},{9,13},{10,... | collective-permute-start | bytes 405512 | tf_op jit(solution)/shard_map/ppermute | solution.py:205
  34.8 10.4 %collective-permute-start.7 = (f32[8,4224]{1,0:T(8,128)}, f32[8,4224]{1,0:T(8,128)S(1)}, u32[]{:S(2)}, u32[]{:S(2)}) collective-permute-start(f32[8,4224]{1,0:T(8,128)} %get-tuple-element.18), channel_id=1, source_target_pairs={{0,5},{1,6},{2,7},{3,0},{4,1},{5,2},{6,3},{7,4},{8,13},{9,14},{10,... | collective-permute-start | bytes 405512 | tf_op jit(solution)/shard_map/ppermute | solution.py:205
  36.9 8.3 %collective-permute-start.8 = (f32[8,4224]{1,0:T(8,128)}, f32[8,4224]{1,0:T(8,128)S(1)}, u32[]{:S(2)}, u32[]{:S(2)}) collective-permute-start(f32[8,4224]{1,0:T(8,128)} %get-tuple-element.19), channel_id=1, source_target_pairs={{0,6},{1,7},{2,0},{3,1},{4,2},{5,3},{6,4},{7,5},{8,14},{9,15},{10,... | collective-permute-start | bytes 405512 | tf_op jit(solution)/shard_map/ppermute | solution.py:205
  38.4 6.9 %collective-permute-start.9 = (f32[8,4224]{1,0:T(8,128)}, f32[8,4224]{1,0:T(8,128)S(1)}, u32[]{:S(2)}, u32[]{:S(2)}) collective-permute-start(f32[8,4224]{1,0:T(8,128)} %get-tuple-element.20), channel_id=1, source_target_pairs={{0,7},{1,0},{2,1},{3,2},{4,3},{5,4},{6,5},{7,6},{8,15},{9,8},{10,9... | collective-permute-start | bytes 405512 | tf_op jit(solution)/shard_map/ppermute | solution.py:205
  46.4 3.8 %collective-permute-start.12 = (f32[1,4096]{1,0:T(1,128)S(1)}, f32[1,4096]{1,0:T(1,128)S(1)}, u32[]{:S(2)}, u32[]{:S(2)}) collective-permute-start(f32[1,4096]{1,0:T(1,128)S(1)} %get-tuple-element.22), channel_id=1, source_target_pairs={{0,24},{8,0},{16,8},{24,16},{1,25},{9,1},{17,9},{25,17},{2,26},{10... | collective-permute-start | bytes 49160 | tf_op jit(solution)/shard_map/ppermute | solution.py:205
  48.1 4.6 %collective-permute-start.11 = (f32[1,4096]{1,0:T(1,128)S(1)}, f32[1,4096]{1,0:T(1,128)S(1)}, u32[]{:S(2)}, u32[]{:S(2)}) collective-permute-start(f32[1,4096]{1,0:T(1,128)S(1)} %get-tuple-element.23), channel_id=1, source_target_pairs={{0,16},{8,24},{16,0},{24,8},{1,17},{9,25},{17,1},{25,9},{2,18},{10... | collective-permute-start | bytes 49160 | tf_op jit(solution)/shard_map/ppermute | solution.py:205
  48.1 5.5 %collective-permute-start.10 = (f32[1,4096]{1,0:T(1,128)S(1)}, f32[1,4096]{1,0:T(1,128)S(1)}, u32[]{:S(2)}, u32[]{:S(2)}) collective-permute-start(f32[1,4096]{1,0:T(1,128)S(1)} %get-tuple-element.24), channel_id=1, source_target_pairs={{0,8},{8,16},{16,24},{24,0},{1,9},{9,17},{17,25},{25,1},{2,10},{10... | collective-permute-start | bytes 49160 | tf_op jit(solution)/shard_map/ppermute | solution.py:205

commit v11 on v10

--- a/solution.py
+++ b/solution.py
@@ -206,6 +206,11 @@
     return received
 
 
+def pick_rows(indices, table):
+    chooser = (indices[:, None] == jnp.arange(table.shape[0], dtype=jnp.int32)[None, :])
+    return jnp.dot(chooser.astype(jnp.float32), table.astype(jnp.float32), precision=PRECISE)
+
+
 def per_device(orbitals, offsets, sends, pair_home, pair_visit, pair_count):
     home_count = orbitals.shape[0]
     cell_count = orbitals.shape[1]
@@ -220,7 +225,7 @@
     outgoing = jnp.concatenate(
         [
             orbitals[flat_chosen],
-            jnp.pad(offsets[flat_chosen].astype(jnp.bfloat16), ((0, 0), (0, extra - 3))),
+            jnp.pad(pick_rows(flat_chosen, offsets).astype(jnp.bfloat16), ((0, 0), (0, extra - 3))),
         ],
         axis=1,
     ).reshape(section_total, per_target, cell_count + extra)
@@ -240,7 +245,7 @@
     live = (jnp.arange(slots, dtype=jnp.int32) < pair_count[0, 0]).astype(jnp.int32)
     home_orb = orbitals[home_slot].reshape(slots, B, PLANE)
     part_orb = visitors[visit_slot]
-    delta = offsets[home_slot] - visit_offsets[visit_slot]
+    delta = pick_rows(home_slot, offsets).astype(jnp.int32) - visit_offsets[visit_slot]
     pair_total = lax.psum(1, "pair")
     chunk = cell_count // pair_total
     pair_me = lax.axis_index("pair")

time: 55 us -> 54.3 us (0.987)
  local copies, waits for them, and re-layouts: 10.6 us -> 9.19 us
  matrix products: 1.91 us -> 2.96 us
  other arithmetic: 1.88 us -> 1.21 us
    dot_general x0 -> x2, matrix products: none -> 1.05 us  [pick_rows(): jnp.dot(chooser.astype(jnp.float32), table.astype(jnp.float32), precision...]
    gather x3 -> x2, local copies, waits for them, and re-layouts: 1.68 us -> 0.65 us  [per_device(): visit_offsets[visit_slot]]
    unnamed x15 -> x17, local copies, waits for them, and re-layouts: 2.53 us -> 1.89 us
    select_n x2 -> x3, other arithmetic: 0.67 us -> 0.09 us  [the longest x1 0.08 us: per_device(): orbitals[flat_chosen]]
  transfers between devices with their start and end apart: 13 -> 13, of which waited for: 9 -> 10; matrix products, arithmetic and copies ran while one was open for 9% -> 8% of each run, Pallas kernels for 0% -> 0%
where the time goes in v11:
time: 54.3 us; the launch traced here: 54.1 us
  starting transfers between devices  17 us (31%)
  waiting for transfers between devices  16.8 us (31%)
  local copies, waits for them, and re-layouts  9.19 us (17%)
  Pallas kernels  6.07 us (11%)
  matrix products  2.96 us (5%)
  other arithmetic  1.21 us (2%)
  between operations  0.91 us (2%)
    ppermute x13, starting transfers between devices, exchange(): received.append(lax.ppermute(blocks[step], axis, pairs))  17 us
    ppermute x13, waiting for transfers between devices, exchange(): received.append(lax.ppermute(blocks[step], axis, pairs))  16.8 us
    pallas_call x1, Pallas kernels, pair_fields(): pl.pallas_call(functools.partial(pair_kernel, count), out_shape=tuple([bo...  6.07 us
    unnamed x17, local copies, waits for them, and re-layouts  1.89 us
    slice x4, local copies, waits for them, and re-layouts, per_device(): block[:, :cell_count].reshape(per_target, B, PLANE)  1.48 us
    gather x1, local copies, waits for them, and re-layouts, per_device(): part_orb = visitors[visit_slot]  1.26 us
  transfers between devices with their start and end apart: 13, of which 10 were waited for; matrix products, arithmetic and copies ran while one was open for 8% of the time, Pallas kernels for 0%

profile of v11, /device:TPU:0, one launch (start us, length us, event | category | flops | bytes accessed | tf_op | source)
XLA Modules:
  0.0 54.1 jit_solution(1744736081475217260)
XLA Ops:
  0.0 0.8 %pad_add_fusion = s32[8,1]{0,1:T(1,128)S(1)} fusion(s32[4,1]{0,1:T(1,128)} %bitcast.72), kind=kLoop, calls=%fused_computation.75 | loop fusion | flops 8 | bytes 48 | tf_op jit(solution)/shard_map/concatenate | solution.py:223
  0.9 0.9 %convolution_convert_fusion.1 = bf16[4,3]{0,1:T(4,128)(2,1)S(1)} fusion(s32[16,3]{0,1:T(4,128)} %param.12, s32[4]{0:T(128)S(1)} %get-tuple-element.29), kind=kOutput, calls=%fused_computation.9 | convolution fusion | flops 2428 | bytes 232 | tf_op jit(solution)/shard_map/dot_general | solution.py:211
  1.9 0.8 %gather_fusion = bf16[4,32768]{1,0:T(4,128)(2,1)S(1)} fusion(bf16[16,32768]{1,0:T(8,128)(2,1)S(1)} %copy-done, s32[1024]{0:T(1024)S(1)} %pad_clamp_fusion.3), kind=kCustom, calls=%fused_computation | custom fusion | bytes 524304 | tf_op jit(solution)/shard_map/gather | solution.py:227
  3.2 3.1 %collective-permute-start = (bf16[1,32896]{1,0:T(2,128)(2,1)S(1)}, bf16[1,32896]{1,0:T(2,128)(2,1)S(1)}, u32[]{:S(2)}, u32[]{:S(2)}) collective-permute-start(bf16[1,32896]{1,0:T(2,128)(2,1)S(1)} %get-tuple-element.25), channel_id=1, source_target_pairs={{0,8},{8,16},{16,24},{24,0},{1,9},{9,17},{17,25},{25,1},{2,10},{10... | collective-permute-start | bytes 197384 | tf_op jit(solution)/shard_map/ppermute | solution.py:205
  6.3 2.1 %collective-permute-start.2 = (bf16[1,32896]{1,0:T(2,128)(2,1)S(1)}, bf16[1,32896]{1,0:T(2,128)(2,1)S(1)}, u32[]{:S(2)}, u32[]{:S(2)}) collective-permute-start(bf16[1,32896]{1,0:T(2,128)(2,1)S(1)} %get-tuple-element.26), channel_id=1, source_target_pairs={{0,24},{8,0},{16,8},{24,16},{1,25},{9,1},{17,9},{25,17},{2,26},{10... | collective-permute-start | bytes 197384 | tf_op jit(solution)/shard_map/ppermute | solution.py:205
  8.4 0.9 %collective-permute-start.1 = (bf16[1,32896]{1,0:T(2,128)(2,1)S(1)}, bf16[1,32896]{1,0:T(2,128)(2,1)S(1)}, u32[]{:S(2)}, u32[]{:S(2)}) collective-permute-start(bf16[1,32896]{1,0:T(2,128)(2,1)S(1)} %get-tuple-element.27), channel_id=1, source_target_pairs={{0,16},{8,24},{16,0},{24,8},{1,17},{9,25},{17,1},{25,9},{2,18},{10... | collective-permute-start | bytes 197384 | tf_op jit(solution)/shard_map/ppermute | solution.py:205
  10.6 0.8 %gather_fusion.2 = bf16[4,32768]{1,0:T(4,128)(2,1)S(1)} fusion(bf16[16,32768]{1,0:T(8,128)(2,1)S(1)} %copy-done, s32[1024]{0:T(1024)S(1)} %get-tuple-element.30), kind=kCustom, calls=%fused_computation.2 | custom fusion | bytes 524304 | tf_op jit(solution)/shard_map/gather | solution.py:246
  11.4 0.8 %copy.33 = bf16[1,4,32,1024]{3,2,1,0:T(8,128)(2,1)} copy(bf16[1,4,32,1024]{3,1,2,0:T(4,128)(2,1)S(1)} %bitcast.63) | data formatting | bytes 524288
  12.2 0.5 collective-permute-done
  13.0 1.1 %collective-permute-done.2 = bf16[1,32896]{1,0:T(2,128)(2,1)S(1)} collective-permute-done((bf16[1,32896]{1,0:T(2,128)(2,1)S(1)}, bf16[1,32896]{1,0:T(2,128)(2,1)S(1)}, u32[]{:S(2)}, u32[]{:S(2)}) %collective-permute-start.2) | collective-permute-done | bytes 65824 | tf_op jit(solution)/shard_map/ppermute | solution.py:205
  14.5 5.8 %collective-permute-done.1 = bf16[1,32896]{1,0:T(2,128)(2,1)S(1)} collective-permute-done((bf16[1,32896]{1,0:T(2,128)(2,1)S(1)}, bf16[1,32896]{1,0:T(2,128)(2,1)S(1)}, u32[]{:S(2)}, u32[]{:S(2)}) %collective-permute-start.1) | collective-permute-done | bytes 65824 | tf_op jit(solution)/shard_map/ppermute | solution.py:205
  20.7 1.3 %gather_fusion.3 = bf16[4,32,1024]{2,1,0:T(8,128)(2,1)} fusion(bf16[4,32,1024]{2,1,0:T(8,128)(2,1)S(1)} %maximum_bitcast_fusion, s32[1024]{0:T(1024)S(1)} %get-tuple-element.31), kind=kCustom, calls=%fused_computation.3 | custom fusion | bytes 524304 | tf_op jit(solution)/shard_map/gather | solution.py:247
  22.0 0.6 %gather_fusion.1 = s32[4,3]{1,0:T(4,128)S(1)} fusion(s32[4,3]{1,0:T(4,128)S(1)} %bitcast.64, s32[1024]{0:T(1024)S(1)} %get-tuple-element.31), kind=kCustom, calls=%fused_computation.1 | custom fusion | bytes 112 | tf_op jit(solution)/shard_map/gather | solution.py:248
  23.1 0.6 %concatenate.11.meta_ref = s32[25]{0:T(128)} concatenate(s32[12]{0:T(128)S(1)} %reshape.172, s32[4]{0:T(128)S(1)} %compare_convert_fusion, s32[4]{0:T(128)S(1)} %bitcast.70, s32[4]{0:T(128)S(1)} %fusion.14, s32[1]{0:T(128)} %bitcast.12), dimensions={0} | concatenate | bytes 200 | tf_op jit(solution)/shard_map/concatenate | solution.py:252
  23.7 6.1 %shard_map.109 = (f32[8,4224]{1,0:T(8,128)}, f32[8,4224]{1,0:T(8,128)}, f32[8,4224]{1,0:T(8,128)}, f32[8,4224]{1,0:T(8,128)}, f32[8,4224]{1,0:T(8,128)}, /*index...) custom-call(s32[25]{0:T(128)} %concatenate.11.meta_ref, bf16[4,32,1024]{2,1,0:T(8,128)(2,1)} %bitcast.62, ...), custom_call_target="tpu_custom_call" | custom-call | tf_op jit(solution)/shard_map/pallas_call | solution.py:185
  29.8 1.5 %collective-permute-start.4 = (f32[8,4224]{1,0:T(8,128)}, f32[8,4224]{1,0:T(8,128)S(1)}, u32[]{:S(2)}, u32[]{:S(2)}) collective-permute-start(f32[8,4224]{1,0:T(8,128)} %get-tuple-element.15), channel_id=1, source_target_pairs={{0,2},{1,3},{2,4},{3,5},{4,6},{5,7},{6,0},{7,1},{8,10},{9,11},{10,... | collective-permute-start | bytes 405512 | tf_op jit(solution)/shard_map/ppermute | solution.py:205
  31.3 2.4 %collective-permute-start.5 = (f32[8,4224]{1,0:T(8,128)}, f32[8,4224]{1,0:T(8,128)S(1)}, u32[]{:S(2)}, u32[]{:S(2)}) collective-permute-start(f32[8,4224]{1,0:T(8,128)} %get-tuple-element.16), channel_id=1, source_target_pairs={{0,3},{1,4},{2,5},{3,6},{4,7},{5,0},{6,1},{7,2},{8,11},{9,12},{10,... | collective-permute-start | bytes 405512 | tf_op jit(solution)/shard_map/ppermute | solution.py:205
  33.7 0.5 collective-permute-start.6
  34.3 0.9 %bitcast_dynamic-update-slice_fusion.7 = f32[8,8,4224]{2,1,0:T(8,128)S(1)} fusion(f32[8,4224]{1,0:T(8,128)} %get-tuple-element.13), kind=kLoop, calls=%fused_computation.23 | loop fusion | bytes 270336
  35.2 1.1 %collective-permute-done.3 = f32[8,4224]{1,0:T(8,128)S(1)} collective-permute-done((f32[8,4224]{1,0:T(8,128)}, f32[8,4224]{1,0:T(8,128)S(1)}, u32[]{:S(2)}, u32[]{:S(2)}) %collective-permute-start.3) | collective-permute-done | bytes 135200 | tf_op jit(solution)/shard_map/ppermute | solution.py:205
  36.3 1.5 %collective-permute-start.8 = (f32[8,4224]{1,0:T(8,128)}, f32[8,4224]{1,0:T(8,128)S(1)}, u32[]{:S(2)}, u32[]{:S(2)}) collective-permute-start(f32[8,4224]{1,0:T(8,128)} %get-tuple-element.19), channel_id=1, source_target_pairs={{0,6},{1,7},{2,0},{3,1},{4,2},{5,3},{6,4},{7,5},{8,14},{9,15},{10,... | collective-permute-start | bytes 405512 | tf_op jit(solution)/shard_map/ppermute | solution.py:205
  37.8 2.6 %collective-permute-start.9 = (f32[8,4224]{1,0:T(8,128)}, f32[8,4224]{1,0:T(8,128)S(1)}, u32[]{:S(2)}, u32[]{:S(2)}) collective-permute-start(f32[8,4224]{1,0:T(8,128)} %get-tuple-element.20), channel_id=1, source_target_pairs={{0,7},{1,0},{2,1},{3,2},{4,3},{5,4},{6,5},{7,6},{8,15},{9,8},{10,9... | collective-permute-start | bytes 405512 | tf_op jit(solution)/shard_map/ppermute | solution.py:205
  40.4 2.1 %collective-permute-done.5 = f32[8,4224]{1,0:T(8,128)S(1)} collective-permute-done((f32[8,4224]{1,0:T(8,128)}, f32[8,4224]{1,0:T(8,128)S(1)}, u32[]{:S(2)}, u32[]{:S(2)}) %collective-permute-start.5) | collective-permute-done | bytes 135200 | tf_op jit(solution)/shard_map/ppermute | solution.py:205
  42.7 1.9 %collective-permute-done.7 = f32[8,4224]{1,0:T(8,128)S(1)} collective-permute-done((f32[8,4224]{1,0:T(8,128)}, f32[8,4224]{1,0:T(8,128)S(1)}, u32[]{:S(2)}, u32[]{:S(2)}) %collective-permute-start.7) | collective-permute-done | bytes 135200 | tf_op jit(solution)/shard_map/ppermute | solution.py:205
  44.9 0.8 %convolution_bitcast_fusion = f32[20,4096]{1,0:T(8,128)S(1)} fusion(f32[8,8,4096]{2,1,0:T(8,128)S(1)} %slice.115, s32[8,8]{0,1:T(8,128)S(1)} %bitcast.65), kind=kOutput, calls=%fused_computation.5 | convolution fusion | flops 31458560 | bytes 1376512 | tf_op jit(solution)/shard_map/srk,srl->kl/dot_general | solution.py:266
  45.8 1.7 %collective-permute-start.12 = (f32[1,4096]{1,0:T(1,128)S(1)}, f32[1,4096]{1,0:T(1,128)S(1)}, u32[]{:S(2)}, u32[]{:S(2)}) collective-permute-start(f32[1,4096]{1,0:T(1,128)S(1)} %get-tuple-element.22), channel_id=1, source_target_pairs={{0,24},{8,0},{16,8},{24,16},{1,25},{9,1},{17,9},{25,17},{2,26},{10... | collective-permute-start | bytes 49160 | tf_op jit(solution)/shard_map/ppermute | solution.py:205
  47.5 0.6 %collective-permute-start.10 = (f32[1,4096]{1,0:T(1,128)S(1)}, f32[1,4096]{1,0:T(1,128)S(1)}, u32[]{:S(2)}, u32[]{:S(2)}) collective-permute-start(f32[1,4096]{1,0:T(1,128)S(1)} %get-tuple-element.24), channel_id=1, source_target_pairs={{0,8},{8,16},{16,24},{24,0},{1,9},{9,17},{17,25},{25,1},{2,10},{10... | collective-permute-start | bytes 49160 | tf_op jit(solution)/shard_map/ppermute | solution.py:205
  48.1 0.6 %gather_fusion.4 = s32[4]{0:T(128)S(1)} fusion(s32[4]{0:T(128)S(1)} %get-tuple-element.29, s32[1024]{0:T(1024)S(1)} %pad_clamp_fusion), kind=kCustom, calls=%fused_computation.4 | custom fusion | bytes 48 | tf_op jit(solution)/shard_map/gather | solution.py:271
  48.8 0.8 %collective-permute-done.12 = f32[1,4096]{1,0:T(1,128)S(1)} collective-permute-done((f32[1,4096]{1,0:T(1,128)S(1)}, f32[1,4096]{1,0:T(1,128)S(1)}, u32[]{:S(2)}, u32[]{:S(2)}) %collective-permute-start.12) | collective-permute-done | bytes 16416 | tf_op jit(solution)/shard_map/ppermute | solution.py:205
  49.6 2.5 %collective-permute-done.11 = f32[1,4096]{1,0:T(1,128)S(1)} collective-permute-done((f32[1,4096]{1,0:T(1,128)S(1)}, f32[1,4096]{1,0:T(1,128)S(1)}, u32[]{:S(2)}, u32[]{:S(2)}) %collective-permute-start.11) | collective-permute-done | bytes 16416 | tf_op jit(solution)/shard_map/ppermute | solution.py:205
  52.1 0.9 %collective-permute-done.10 = f32[1,4096]{1,0:T(1,128)S(1)} collective-permute-done((f32[1,4096]{1,0:T(1,128)S(1)}, f32[1,4096]{1,0:T(1,128)S(1)}, u32[]{:S(2)}, u32[]{:S(2)}) %collective-permute-start.10) | collective-permute-done | bytes 16416 | tf_op jit(solution)/shard_map/ppermute | solution.py:205
  53.1 1.1 %convolution_add_fusion = f32[16,4096]{1,0:T(8,128)} fusion(f32[20,4096]{1,0:T(8,128)S(1)} %convolution_bitcast_fusion, f32[4,1,4096]{2,1,0:T(1,128)S(1)} %pad_maximum_fusion, s32[4]{0:T(128)S(1)} %gather_fusion.4), kind=kOutput, calls=%fused_computation.6 | convolution fusion | flops 1638464 | bytes 589840 | tf_op jit(solution)/shard_map/dot_general | solution.py:275
  (57 shorter events, 3.7 us)
Async XLA Ops:
  0.0 1.9 %copy-start = (bf16[16,32768]{1,0:T(8,128)(2,1)S(1)}, bf16[16,32768]{1,0:T(8,128)(2,1)}, u32[]{:S(2)}) copy-start(bf16[16,32768]{1,0:T(8,128)(2,1)} %param.11) | copy-start | bytes 3145732
  2.7 6.6 %copy-start.3 = (s32[1,1,4]{2,1,0:T(1,128)S(1)}, s32[1,1,4]{2,1,0:T(1,128)}, u32[]{:S(2)}) copy-start(s32[1,1,4]{2,1,0:T(1,128)} %param.15) | copy-start | bytes 52
  2.7 7.8 %copy-start.1 = (s32[1,1,4]{2,1,0:T(1,128)S(1)}, s32[1,1,4]{2,1,0:T(1,128)}, u32[]{:S(2)}) copy-start(s32[1,1,4]{2,1,0:T(1,128)} %param.14) | copy-start | bytes 52
  3.2 9.4 %collective-permute-start = (bf16[1,32896]{1,0:T(2,128)(2,1)S(1)}, bf16[1,32896]{1,0:T(2,128)(2,1)S(1)}, u32[]{:S(2)}, u32[]{:S(2)}) collective-permute-start(bf16[1,32896]{1,0:T(2,128)(2,1)S(1)} %get-tuple-element.25), channel_id=1, source_target_pairs={{0,8},{8,16},{16,24},{24,0},{1,9},{9,17},{17,25},{25,1},{2,10},{10... | collective-permute-start | bytes 197384 | tf_op jit(solution)/shard_map/ppermute | solution.py:205
  6.3 7.8 %collective-permute-start.2 = (bf16[1,32896]{1,0:T(2,128)(2,1)S(1)}, bf16[1,32896]{1,0:T(2,128)(2,1)S(1)}, u32[]{:S(2)}, u32[]{:S(2)}) collective-permute-start(bf16[1,32896]{1,0:T(2,128)(2,1)S(1)} %get-tuple-element.26), channel_id=1, source_target_pairs={{0,24},{8,0},{16,8},{24,16},{1,25},{9,1},{17,9},{25,17},{2,26},{10... | collective-permute-start | bytes 197384 | tf_op jit(solution)/shard_map/ppermute | solution.py:205
  8.4 11.9 %collective-permute-start.1 = (bf16[1,32896]{1,0:T(2,128)(2,1)S(1)}, bf16[1,32896]{1,0:T(2,128)(2,1)S(1)}, u32[]{:S(2)}, u32[]{:S(2)}) collective-permute-start(bf16[1,32896]{1,0:T(2,128)(2,1)S(1)} %get-tuple-element.27), channel_id=1, source_target_pairs={{0,16},{8,24},{16,0},{24,8},{1,17},{9,25},{17,1},{25,9},{2,18},{10... | collective-permute-start | bytes 197384 | tf_op jit(solution)/shard_map/ppermute | solution.py:205
  12.2 10.5 %copy-start.2 = (s32[16,3]{0,1:T(4,128)S(1)}, s32[16,3]{0,1:T(4,128)}, u32[]{:S(2)}) copy-start(s32[16,3]{0,1:T(4,128)} %param.12) | copy-start | bytes 580
  29.8 6.5 %collective-permute-start.3 = (f32[8,4224]{1,0:T(8,128)}, f32[8,4224]{1,0:T(8,128)S(1)}, u32[]{:S(2)}, u32[]{:S(2)}) collective-permute-start(f32[8,4224]{1,0:T(8,128)} %get-tuple-element.14), channel_id=1, source_target_pairs={{0,1},{1,2},{2,3},{3,4},{4,5},{5,6},{6,7},{7,0},{8,9},{9,10},{10,1... | collective-permute-start | bytes 405512 | tf_op jit(solution)/shard_map/ppermute | solution.py:205
  29.8 8.0 %collective-permute-start.4 = (f32[8,4224]{1,0:T(8,128)}, f32[8,4224]{1,0:T(8,128)S(1)}, u32[]{:S(2)}, u32[]{:S(2)}) collective-permute-start(f32[8,4224]{1,0:T(8,128)} %get-tuple-element.15), channel_id=1, source_target_pairs={{0,2},{1,3},{2,4},{3,5},{4,6},{5,7},{6,0},{7,1},{8,10},{9,11},{10,... | collective-permute-start | bytes 405512 | tf_op jit(solution)/shard_map/ppermute | solution.py:205
  31.3 11.1 %collective-permute-start.5 = (f32[8,4224]{1,0:T(8,128)}, f32[8,4224]{1,0:T(8,128)S(1)}, u32[]{:S(2)}, u32[]{:S(2)}) collective-permute-start(f32[8,4224]{1,0:T(8,128)} %get-tuple-element.16), channel_id=1, source_target_pairs={{0,3},{1,4},{2,5},{3,6},{4,7},{5,0},{6,1},{7,2},{8,11},{9,12},{10,... | collective-permute-start | bytes 405512 | tf_op jit(solution)/shard_map/ppermute | solution.py:205
  33.7 9.0 %collective-permute-start.6 = (f32[8,4224]{1,0:T(8,128)}, f32[8,4224]{1,0:T(8,128)S(1)}, u32[]{:S(2)}, u32[]{:S(2)}) collective-permute-start(f32[8,4224]{1,0:T(8,128)} %get-tuple-element.17), channel_id=1, source_target_pairs={{0,4},{1,5},{2,6},{3,7},{4,0},{5,1},{6,2},{7,3},{8,12},{9,13},{10,... | collective-permute-start | bytes 405512 | tf_op jit(solution)/shard_map/ppermute | solution.py:205
  34.2 10.4 %collective-permute-start.7 = (f32[8,4224]{1,0:T(8,128)}, f32[8,4224]{1,0:T(8,128)S(1)}, u32[]{:S(2)}, u32[]{:S(2)}) collective-permute-start(f32[8,4224]{1,0:T(8,128)} %get-tuple-element.18), channel_id=1, source_target_pairs={{0,5},{1,6},{2,7},{3,0},{4,1},{5,2},{6,3},{7,4},{8,13},{9,14},{10,... | collective-permute-start | bytes 405512 | tf_op jit(solution)/shard_map/ppermute | solution.py:205
  36.3 8.3 %collective-permute-start.8 = (f32[8,4224]{1,0:T(8,128)}, f32[8,4224]{1,0:T(8,128)S(1)}, u32[]{:S(2)}, u32[]{:S(2)}) collective-permute-start(f32[8,4224]{1,0:T(8,128)} %get-tuple-element.19), channel_id=1, source_target_pairs={{0,6},{1,7},{2,0},{3,1},{4,2},{5,3},{6,4},{7,5},{8,14},{9,15},{10,... | collective-permute-start | bytes 405512 | tf_op jit(solution)/shard_map/ppermute | solution.py:205
  37.8 6.9 %collective-permute-start.9 = (f32[8,4224]{1,0:T(8,128)}, f32[8,4224]{1,0:T(8,128)S(1)}, u32[]{:S(2)}, u32[]{:S(2)}) collective-permute-start(f32[8,4224]{1,0:T(8,128)} %get-tuple-element.20), channel_id=1, source_target_pairs={{0,7},{1,0},{2,1},{3,2},{4,3},{5,4},{6,5},{7,6},{8,15},{9,8},{10,9... | collective-permute-start | bytes 405512 | tf_op jit(solution)/shard_map/ppermute | solution.py:205
  45.8 3.8 %collective-permute-start.12 = (f32[1,4096]{1,0:T(1,128)S(1)}, f32[1,4096]{1,0:T(1,128)S(1)}, u32[]{:S(2)}, u32[]{:S(2)}) collective-permute-start(f32[1,4096]{1,0:T(1,128)S(1)} %get-tuple-element.22), channel_id=1, source_target_pairs={{0,24},{8,0},{16,8},{24,16},{1,25},{9,1},{17,9},{25,17},{2,26},{10... | collective-permute-start | bytes 49160 | tf_op jit(solution)/shard_map/ppermute | solution.py:205
  47.5 4.6 %collective-permute-start.11 = (f32[1,4096]{1,0:T(1,128)S(1)}, f32[1,4096]{1,0:T(1,128)S(1)}, u32[]{:S(2)}, u32[]{:S(2)}) collective-permute-start(f32[1,4096]{1,0:T(1,128)S(1)} %get-tuple-element.23), channel_id=1, source_target_pairs={{0,16},{8,24},{16,0},{24,8},{1,17},{9,25},{17,1},{25,9},{2,18},{10... | collective-permute-start | bytes 49160 | tf_op jit(solution)/shard_map/ppermute | solution.py:205
  47.5 5.5 %collective-permute-start.10 = (f32[1,4096]{1,0:T(1,128)S(1)}, f32[1,4096]{1,0:T(1,128)S(1)}, u32[]{:S(2)}, u32[]{:S(2)}) collective-permute-start(f32[1,4096]{1,0:T(1,128)S(1)} %get-tuple-element.24), channel_id=1, source_target_pairs={{0,8},{8,16},{16,24},{24,0},{1,9},{9,17},{17,25},{25,1},{2,10},{10... | collective-permute-start | bytes 49160 | tf_op jit(solution)/shard_map/ppermute | solution.py:205

commit v12 on v11

--- a/solution.py
+++ b/solution.py
@@ -102,9 +102,20 @@
 
 def pair_kernel(
     count,
+    boxes,
     meta_ref,
     home_ref,
-    part_ref,
+    *rest,
+):
+    box_refs = rest[:boxes]
+    pair_kernel_body(count, meta_ref, home_ref, box_refs, *rest[boxes:])
+
+
+def pair_kernel_body(
+    count,
+    meta_ref,
+    home_ref,
+    box_refs,
     tiled_ref,
     spread_ref,
     rows_high_ref,
@@ -133,8 +144,13 @@
         d_a = meta_ref[3 * slot]
         d_b = meta_ref[3 * slot + 1]
         d_c = meta_ref[3 * slot + 2]
+        visit = meta_ref[6 * slots + 1 + slot]
+        per_box = box_refs[0].shape[0]
+        part = box_refs[0][0]
+        for index in range(1, len(box_refs) * per_box):
+            part = jnp.where(visit == index, box_refs[index // per_box][index % per_box], part)
         pick = (col == row + d_a).astype(jnp.bfloat16)
-        moved = jnp.dot(pick, part_ref[slot], preferred_element_type=jnp.float32)
+        moved = jnp.dot(pick, part, preferred_element_type=jnp.float32)
         step = d_b * B + d_c
         moved = pltpu.roll(moved, (PLANE - step) % PLANE, 1)
         inside = (
@@ -176,16 +192,16 @@
         )
 
 
-def pair_fields(meta, home, part, count, chunk):
+def pair_fields(meta, home, boxes, count, chunk):
     slots = home.shape[0]
     tiled, spread, rows_high, rows_low, eigen = host_tables(slots)
     smem = pl.BlockSpec(memory_space=pltpu.SMEM)
     vmem = pl.BlockSpec(memory_space=pltpu.VMEM)
     box = jax.ShapeDtypeStruct((2 * slots, chunk + 128), jnp.float32)
     return pl.pallas_call(
-        functools.partial(pair_kernel, count),
+        functools.partial(pair_kernel, count, len(boxes)),
         out_shape=tuple([box] * count),
-        in_specs=[smem] + [vmem] * 7,
+        in_specs=[smem] + [vmem] * (6 + len(boxes)),
         out_specs=tuple([vmem] * count),
         scratch_shapes=[
             pltpu.VMEM((slots, B, PLANE), jnp.float32),
@@ -194,7 +210,7 @@
             pltpu.VMEM((PLANE, PLANE), jnp.bfloat16),
             pltpu.VMEM((B, PLANE), jnp.float32),
         ],
-    )(meta, home, part, tiled, spread, rows_high, rows_low, eigen)
+    )(meta, home, *boxes, tiled, spread, rows_high, rows_low, eigen)
 
 
 def exchange(blocks, axis):
@@ -230,9 +246,7 @@
         axis=1,
     ).reshape(section_total, per_target, cell_count + extra)
     arrived = exchange(outgoing, "home")
-    visitors = jnp.stack(
-        [block[:, :cell_count].reshape(per_target, B, PLANE) for block in arrived]
-    ).reshape(slot_total, B, PLANE)
+    visitors = [block[:, :cell_count].reshape(per_target, B, PLANE) for block in arrived]
     visit_offsets = jnp.stack(
         [block[:, cell_count : cell_count + 3] for block in arrived]
     ).reshape(slot_total, 3).astype(jnp.int32)
@@ -244,7 +258,6 @@
     return_slot = ((source - me) % section_total) * per_target + visit_code % per_target
     live = (jnp.arange(slots, dtype=jnp.int32) < pair_count[0, 0]).astype(jnp.int32)
     home_orb = orbitals[home_slot].reshape(slots, B, PLANE)
-    part_orb = visitors[visit_slot]
     delta = pick_rows(home_slot, offsets).astype(jnp.int32) - visit_offsets[visit_slot]
     pair_total = lax.psum(1, "pair")
     chunk = cell_count // pair_total
@@ -256,9 +269,10 @@
             home_slot,
             home_count + return_slot,
             jnp.reshape(pair_me, (1,)).astype(jnp.int32),
+            visit_slot,
         ]
     )
-    payload = pair_fields(meta, home_orb, part_orb, pair_total, chunk)
+    payload = pair_fields(meta, home_orb, visitors, pair_total, chunk)
     got = jnp.stack(exchange(payload, "pair"))
     got_ids = got[:, :, chunk].astype(jnp.int32)
     all_rows = jnp.arange(home_count + slot_total, dtype=jnp.int32)

time: 54.3 us -> 53.7 us (0.989)
  waiting for transfers between devices: 16.8 us -> 14.7 us
  local copies, waits for them, and re-layouts: 9.19 us -> 10.5 us
    reshape x0 -> x4, local copies, waits for them, and re-layouts: none -> 2.62 us  [per_device(): block[:, :cell_count].reshape(per_target, B, PLANE)]
    ppermute x13, waiting for transfers between devices: 16.8 us -> 14.7 us  [exchange(): received.append(lax.ppermute(blocks[step], axis, pairs))]
    gather x1 -> x0, local copies, waits for them, and re-layouts: 1.26 us -> none  [per_device(): part_orb = visitors[visit_slot]]
  transfers between devices with their start and end apart: 13 -> 13, of which waited for: 10 -> 9; matrix products, arithmetic and copies ran while one was open for 8% -> 12% of each run, Pallas kernels for 0% -> 0%
where the time goes in v12:
time: 53.7 us; the launch traced here: 53.6 us
  starting transfers between devices  17.3 us (32%)
  waiting for transfers between devices  14.7 us (27%)
  local copies, waits for them, and re-layouts  10.5 us (20%)
  Pallas kernels  6.12 us (11%)
  matrix products  2.96 us (6%)
  other arithmetic  1.17 us (2%)
  between operations  0.88 us (2%)
    ppermute x13, starting transfers between devices, exchange(): received.append(lax.ppermute(blocks[step], axis, pairs))  17.3 us
    ppermute x13, waiting for transfers between devices, exchange(): received.append(lax.ppermute(blocks[step], axis, pairs))  14.7 us
    pallas_call x1, Pallas kernels, pair_fields(): pl.pallas_call(functools.partial(pair_kernel, count, len(boxes)), out_sha...  6.12 us
    reshape x4, local copies, waits for them, and re-layouts, per_device(): block[:, :cell_count].reshape(per_target, B, PLANE)  2.62 us
    unnamed x17, local copies, waits for them, and re-layouts  1.89 us
    slice x4, local copies, waits for them, and re-layouts, per_device(): block[:, :cell_count].reshape(per_target, B, PLANE)  1.48 us
  transfers between devices with their start and end apart: 13, of which 9 were waited for; matrix products, arithmetic and copies ran while one was open for 12% of the time, Pallas kernels for 0%

profile of v12, /device:TPU:0, one launch (start us, length us, event | category | flops | bytes accessed | tf_op | source)
XLA Modules:
  0.0 53.6 jit_solution(10122486941381052659)
XLA Ops:
  0.0 0.8 %pad_add_fusion = s32[8,1]{0,1:T(1,128)S(1)} fusion(s32[4,1]{0,1:T(1,128)} %bitcast.72), kind=kLoop, calls=%fused_computation.77 | loop fusion | flops 8 | bytes 48 | tf_op jit(solution)/shard_map/concatenate | solution.py:239
  0.9 0.9 %convolution_convert_fusion.1 = bf16[4,3]{0,1:T(4,128)(2,1)S(1)} fusion(s32[16,3]{0,1:T(4,128)} %param.12, s32[4]{0:T(128)S(1)} %get-tuple-element.31), kind=kOutput, calls=%fused_computation.8 | convolution fusion | flops 2428 | bytes 232 | tf_op jit(solution)/shard_map/dot_general | solution.py:227
  1.9 0.8 %gather_fusion = bf16[4,32768]{1,0:T(4,128)(2,1)S(1)} fusion(bf16[16,32768]{1,0:T(8,128)(2,1)S(1)} %copy-done, s32[1024]{0:T(1024)S(1)} %pad_clamp_fusion.3), kind=kCustom, calls=%fused_computation | custom fusion | bytes 524304 | tf_op jit(solution)/shard_map/gather | solution.py:243
  3.2 3.1 %collective-permute-start = (bf16[1,32896]{1,0:T(2,128)(2,1)S(1)}, bf16[1,32896]{1,0:T(2,128)(2,1)S(1)}, u32[]{:S(2)}, u32[]{:S(2)}) collective-permute-start(bf16[1,32896]{1,0:T(2,128)(2,1)S(1)} %get-tuple-element.25), channel_id=1, source_target_pairs={{0,8},{8,16},{16,24},{24,0},{1,9},{9,17},{17,25},{25,1},{2,10},{10... | collective-permute-start | bytes 197384 | tf_op jit(solution)/shard_map/ppermute | solution.py:221
  6.3 2.1 %collective-permute-start.2 = (bf16[1,32896]{1,0:T(2,128)(2,1)S(1)}, bf16[1,32896]{1,0:T(2,128)(2,1)S(1)}, u32[]{:S(2)}, u32[]{:S(2)}) collective-permute-start(bf16[1,32896]{1,0:T(2,128)(2,1)S(1)} %get-tuple-element.26), channel_id=1, source_target_pairs={{0,24},{8,0},{16,8},{24,16},{1,25},{9,1},{17,9},{25,17},{2,26},{10... | collective-permute-start | bytes 197384 | tf_op jit(solution)/shard_map/ppermute | solution.py:221
  8.4 0.9 %collective-permute-start.1 = (bf16[1,32896]{1,0:T(2,128)(2,1)S(1)}, bf16[1,32896]{1,0:T(2,128)(2,1)S(1)}, u32[]{:S(2)}, u32[]{:S(2)}) collective-permute-start(bf16[1,32896]{1,0:T(2,128)(2,1)S(1)} %get-tuple-element.27), channel_id=1, source_target_pairs={{0,16},{8,24},{16,0},{24,8},{1,17},{9,25},{17,1},{25,9},{2,18},{10... | collective-permute-start | bytes 197384 | tf_op jit(solution)/shard_map/ppermute | solution.py:221
  10.6 0.7 %reshape.186.rest_0_ = bf16[1,32,1024]{2,1,0:T(8,128)(2,1)} reshape(bf16[32768]{0:T(1024)(128)(2,1)S(1)} %slice_reduce_fusion.3) | data formatting | bytes 131072 | tf_op jit(solution)/shard_map/reshape | solution.py:249
  11.2 0.8 %gather_fusion.2 = bf16[4,32768]{1,0:T(4,128)(2,1)S(1)} fusion(bf16[16,32768]{1,0:T(8,128)(2,1)S(1)} %copy-done, s32[1024]{0:T(1024)S(1)} %get-tuple-element.32), kind=kCustom, calls=%fused_computation.2 | custom fusion | bytes 524304 | tf_op jit(solution)/shard_map/gather | solution.py:260
  12.0 0.8 %copy.33 = bf16[1,4,32,1024]{3,2,1,0:T(8,128)(2,1)} copy(bf16[1,4,32,1024]{3,1,2,0:T(4,128)(2,1)S(1)} %bitcast.63) | data formatting | bytes 524288
  13.2 0.9 %collective-permute-done.2 = bf16[1,32896]{1,0:T(2,128)(2,1)S(1)} collective-permute-done((bf16[1,32896]{1,0:T(2,128)(2,1)S(1)}, bf16[1,32896]{1,0:T(2,128)(2,1)S(1)}, u32[]{:S(2)}, u32[]{:S(2)}) %collective-permute-start.2) | collective-permute-done | bytes 65824 | tf_op jit(solution)/shard_map/ppermute | solution.py:221
  14.5 0.7 %reshape.187.rest_1_ = bf16[1,32,1024]{2,1,0:T(8,128)(2,1)} reshape(bf16[32768]{0:T(1024)(128)(2,1)S(1)} %slice_reduce_fusion.2) | data formatting | bytes 131072 | tf_op jit(solution)/shard_map/reshape | solution.py:249
  15.1 0.7 %reshape.189.rest_3_ = bf16[1,32,1024]{2,1,0:T(8,128)(2,1)} reshape(bf16[32768]{0:T(1024)(128)(2,1)S(1)} %slice_reduce_fusion) | data formatting | bytes 131072 | tf_op jit(solution)/shard_map/reshape | solution.py:249
  15.8 4.5 %collective-permute-done.1 = bf16[1,32896]{1,0:T(2,128)(2,1)S(1)} collective-permute-done((bf16[1,32896]{1,0:T(2,128)(2,1)S(1)}, bf16[1,32896]{1,0:T(2,128)(2,1)S(1)}, u32[]{:S(2)}, u32[]{:S(2)}) %collective-permute-start.1) | collective-permute-done | bytes 65824 | tf_op jit(solution)/shard_map/ppermute | solution.py:221
  20.7 0.7 %reshape.188.rest_2_ = bf16[1,32,1024]{2,1,0:T(8,128)(2,1)} reshape(bf16[32768]{0:T(1024)(128)(2,1)S(1)} %slice_reduce_fusion.1) | data formatting | bytes 131072 | tf_op jit(solution)/shard_map/reshape | solution.py:249
  21.3 0.6 %gather_fusion.1 = s32[4,3]{1,0:T(4,128)S(1)} fusion(s32[4,3]{1,0:T(4,128)S(1)} %bitcast.64, s32[1024]{0:T(1024)S(1)} %get-tuple-element.33), kind=kCustom, calls=%fused_computation.1 | custom fusion | bytes 112 | tf_op jit(solution)/shard_map/gather | solution.py:261
  22.4 0.7 %concatenate.11.meta_ref = s32[29]{0:T(128)} concatenate(s32[12]{0:T(128)S(1)} %reshape.183, s32[4]{0:T(128)S(1)} %compare_convert_fusion, s32[4]{0:T(128)S(1)} %bitcast.70, s32[4]{0:T(128)S(1)} %get-tuple-element.29, s32[1]{0:T(128)} %bitcast.12, s32[4]{0:T(128)S(1)} %get-tuple-element.28), dimensions={0} | concatenate | bytes 232 | tf_op jit(solution)/shard_map/concatenate | solution.py:265
  23.1 6.1 %shard_map.109 = (f32[8,4224]{1,0:T(8,128)}, f32[8,4224]{1,0:T(8,128)}, f32[8,4224]{1,0:T(8,128)}, f32[8,4224]{1,0:T(8,128)}, f32[8,4224]{1,0:T(8,128)}, /*index...) custom-call(s32[29]{0:T(128)} %concatenate.11.meta_ref, bf16[4,32,1024]{2,1,0:T(8,128)(2,1)} %bitcast.62, ...), custom_call_target="tpu_custom_call" | custom-call | tf_op jit(solution)/shard_map/pallas_call | solution.py:201
  29.2 1.5 %collective-permute-start.4 = (f32[8,4224]{1,0:T(8,128)}, f32[8,4224]{1,0:T(8,128)S(1)}, u32[]{:S(2)}, u32[]{:S(2)}) collective-permute-start(f32[8,4224]{1,0:T(8,128)} %get-tuple-element.15), channel_id=1, source_target_pairs={{0,2},{1,3},{2,4},{3,5},{4,6},{5,7},{6,0},{7,1},{8,10},{9,11},{10,... | collective-permute-start | bytes 405512 | tf_op jit(solution)/shard_map/ppermute | solution.py:221
  30.7 2.4 %collective-permute-start.5 = (f32[8,4224]{1,0:T(8,128)}, f32[8,4224]{1,0:T(8,128)S(1)}, u32[]{:S(2)}, u32[]{:S(2)}) collective-permute-start(f32[8,4224]{1,0:T(8,128)} %get-tuple-element.16), channel_id=1, source_target_pairs={{0,3},{1,4},{2,5},{3,6},{4,7},{5,0},{6,1},{7,2},{8,11},{9,12},{10,... | collective-permute-start | bytes 405512 | tf_op jit(solution)/shard_map/ppermute | solution.py:221
  33.7 0.9 %bitcast_dynamic-update-slice_fusion.7 = f32[8,8,4224]{2,1,0:T(8,128)S(1)} fusion(f32[8,4224]{1,0:T(8,128)} %get-tuple-element.13), kind=kLoop, calls=%fused_computation.21 | loop fusion | bytes 270336
  34.6 1.0 %collective-permute-done.3 = f32[8,4224]{1,0:T(8,128)S(1)} collective-permute-done((f32[8,4224]{1,0:T(8,128)}, f32[8,4224]{1,0:T(8,128)S(1)}, u32[]{:S(2)}, u32[]{:S(2)}) %collective-permute-start.3) | collective-permute-done | bytes 135200 | tf_op jit(solution)/shard_map/ppermute | solution.py:221
  35.7 1.5 %collective-permute-start.8 = (f32[8,4224]{1,0:T(8,128)}, f32[8,4224]{1,0:T(8,128)S(1)}, u32[]{:S(2)}, u32[]{:S(2)}) collective-permute-start(f32[8,4224]{1,0:T(8,128)} %get-tuple-element.19), channel_id=1, source_target_pairs={{0,6},{1,7},{2,0},{3,1},{4,2},{5,3},{6,4},{7,5},{8,14},{9,15},{10,... | collective-permute-start | bytes 405512 | tf_op jit(solution)/shard_map/ppermute | solution.py:221
  37.2 2.6 %collective-permute-start.9 = (f32[8,4224]{1,0:T(8,128)}, f32[8,4224]{1,0:T(8,128)S(1)}, u32[]{:S(2)}, u32[]{:S(2)}) collective-permute-start(f32[8,4224]{1,0:T(8,128)} %get-tuple-element.20), channel_id=1, source_target_pairs={{0,7},{1,0},{2,1},{3,2},{4,3},{5,4},{6,5},{7,6},{8,15},{9,8},{10,9... | collective-permute-start | bytes 405512 | tf_op jit(solution)/shard_map/ppermute | solution.py:221
  39.8 2.1 %collective-permute-done.5 = f32[8,4224]{1,0:T(8,128)S(1)} collective-permute-done((f32[8,4224]{1,0:T(8,128)}, f32[8,4224]{1,0:T(8,128)S(1)}, u32[]{:S(2)}, u32[]{:S(2)}) %collective-permute-start.5) | collective-permute-done | bytes 135200 | tf_op jit(solution)/shard_map/ppermute | solution.py:221
  42.1 1.9 %collective-permute-done.7 = f32[8,4224]{1,0:T(8,128)S(1)} collective-permute-done((f32[8,4224]{1,0:T(8,128)}, f32[8,4224]{1,0:T(8,128)S(1)}, u32[]{:S(2)}, u32[]{:S(2)}) %collective-permute-start.7) | collective-permute-done | bytes 135200 | tf_op jit(solution)/shard_map/ppermute | solution.py:221
  44.3 0.8 %convolution_bitcast_fusion = f32[20,4096]{1,0:T(8,128)S(1)} fusion(f32[8,8,4096]{2,1,0:T(8,128)S(1)} %slice.113, s32[8,8]{0,1:T(8,128)S(1)} %bitcast.65), kind=kOutput, calls=%fused_computation.4 | convolution fusion | flops 31458560 | bytes 1376512 | tf_op jit(solution)/shard_map/srk,srl->kl/dot_general | solution.py:280
  45.2 1.7 %collective-permute-start.12 = (f32[1,4096]{1,0:T(1,128)S(1)}, f32[1,4096]{1,0:T(1,128)S(1)}, u32[]{:S(2)}, u32[]{:S(2)}) collective-permute-start(f32[1,4096]{1,0:T(1,128)S(1)} %get-tuple-element.22), channel_id=1, source_target_pairs={{0,24},{8,0},{16,8},{24,16},{1,25},{9,1},{17,9},{25,17},{2,26},{10... | collective-permute-start | bytes 49160 | tf_op jit(solution)/shard_map/ppermute | solution.py:221
  46.9 0.9 %collective-permute-start.10 = (f32[1,4096]{1,0:T(1,128)S(1)}, f32[1,4096]{1,0:T(1,128)S(1)}, u32[]{:S(2)}, u32[]{:S(2)}) collective-permute-start(f32[1,4096]{1,0:T(1,128)S(1)} %get-tuple-element.24), channel_id=1, source_target_pairs={{0,8},{8,16},{16,24},{24,0},{1,9},{9,17},{17,25},{25,1},{2,10},{10... | collective-permute-start | bytes 49160 | tf_op jit(solution)/shard_map/ppermute | solution.py:221
  47.8 0.6 %gather_fusion.3 = s32[4]{0:T(128)S(1)} fusion(s32[4]{0:T(128)S(1)} %get-tuple-element.31, s32[1024]{0:T(1024)S(1)} %pad_clamp_fusion), kind=kCustom, calls=%fused_computation.3 | custom fusion | bytes 48 | tf_op jit(solution)/shard_map/gather | solution.py:285
  49.0 2.5 %collective-permute-done.11 = f32[1,4096]{1,0:T(1,128)S(1)} collective-permute-done((f32[1,4096]{1,0:T(1,128)S(1)}, f32[1,4096]{1,0:T(1,128)S(1)}, u32[]{:S(2)}, u32[]{:S(2)}) %collective-permute-start.11) | collective-permute-done | bytes 16416 | tf_op jit(solution)/shard_map/ppermute | solution.py:221
  51.5 0.9 %collective-permute-done.10 = f32[1,4096]{1,0:T(1,128)S(1)} collective-permute-done((f32[1,4096]{1,0:T(1,128)S(1)}, f32[1,4096]{1,0:T(1,128)S(1)}, u32[]{:S(2)}, u32[]{:S(2)}) %collective-permute-start.10) | collective-permute-done | bytes 16416 | tf_op jit(solution)/shard_map/ppermute | solution.py:221
  52.5 1.1 %convolution_add_fusion = f32[16,4096]{1,0:T(8,128)} fusion(f32[20,4096]{1,0:T(8,128)S(1)} %convolution_bitcast_fusion, f32[4,1,4096]{2,1,0:T(1,128)S(1)} %pad_maximum_fusion, s32[4]{0:T(128)S(1)} %gather_fusion.3), kind=kOutput, calls=%fused_computation.5 | convolution fusion | flops 1638464 | bytes 589840 | tf_op jit(solution)/shard_map/dot_general | solution.py:289
  (55 shorter events, 4.6 us)
Async XLA Ops:
  0.0 1.9 %copy-start = (bf16[16,32768]{1,0:T(8,128)(2,1)S(1)}, bf16[16,32768]{1,0:T(8,128)(2,1)}, u32[]{:S(2)}) copy-start(bf16[16,32768]{1,0:T(8,128)(2,1)} %param.11) | copy-start | bytes 3145732
  2.7 6.6 %copy-start.2 = (s32[1,1,4]{2,1,0:T(1,128)S(1)}, s32[1,1,4]{2,1,0:T(1,128)}, u32[]{:S(2)}) copy-start(s32[1,1,4]{2,1,0:T(1,128)} %param.15) | copy-start | bytes 52
  2.7 7.8 %copy-start.1 = (s32[1,1,4]{2,1,0:T(1,128)S(1)}, s32[1,1,4]{2,1,0:T(1,128)}, u32[]{:S(2)}) copy-start(s32[1,1,4]{2,1,0:T(1,128)} %param.14) | copy-start | bytes 52
  3.2 9.6 %collective-permute-start = (bf16[1,32896]{1,0:T(2,128)(2,1)S(1)}, bf16[1,32896]{1,0:T(2,128)(2,1)S(1)}, u32[]{:S(2)}, u32[]{:S(2)}) collective-permute-start(bf16[1,32896]{1,0:T(2,128)(2,1)S(1)} %get-tuple-element.25), channel_id=1, source_target_pairs={{0,8},{8,16},{16,24},{24,0},{1,9},{9,17},{17,25},{25,1},{2,10},{10... | collective-permute-start | bytes 197384 | tf_op jit(solution)/shard_map/ppermute | solution.py:221
  6.3 7.8 %collective-permute-start.2 = (bf16[1,32896]{1,0:T(2,128)(2,1)S(1)}, bf16[1,32896]{1,0:T(2,128)(2,1)S(1)}, u32[]{:S(2)}, u32[]{:S(2)}) collective-permute-start(bf16[1,32896]{1,0:T(2,128)(2,1)S(1)} %get-tuple-element.26), channel_id=1, source_target_pairs={{0,24},{8,0},{16,8},{24,16},{1,25},{9,1},{17,9},{25,17},{2,26},{10... | collective-permute-start | bytes 197384 | tf_op jit(solution)/shard_map/ppermute | solution.py:221
  8.4 11.9 %collective-permute-start.1 = (bf16[1,32896]{1,0:T(2,128)(2,1)S(1)}, bf16[1,32896]{1,0:T(2,128)(2,1)S(1)}, u32[]{:S(2)}, u32[]{:S(2)}) collective-permute-start(bf16[1,32896]{1,0:T(2,128)(2,1)S(1)} %get-tuple-element.27), channel_id=1, source_target_pairs={{0,16},{8,24},{16,0},{24,8},{1,17},{9,25},{17,1},{25,9},{2,18},{10... | collective-permute-start | bytes 197384 | tf_op jit(solution)/shard_map/ppermute | solution.py:221
  12.0 10.0 %copy-start.3 = (s32[16,3]{0,1:T(4,128)S(1)}, s32[16,3]{0,1:T(4,128)}, u32[]{:S(2)}) copy-start(s32[16,3]{0,1:T(4,128)} %param.12) | copy-start | bytes 580
  29.2 6.5 %collective-permute-start.3 = (f32[8,4224]{1,0:T(8,128)}, f32[8,4224]{1,0:T(8,128)S(1)}, u32[]{:S(2)}, u32[]{:S(2)}) collective-permute-start(f32[8,4224]{1,0:T(8,128)} %get-tuple-element.14), channel_id=1, source_target_pairs={{0,1},{1,2},{2,3},{3,4},{4,5},{5,6},{6,7},{7,0},{8,9},{9,10},{10,1... | collective-permute-start | bytes 405512 | tf_op jit(solution)/shard_map/ppermute | solution.py:221
  29.2 8.0 %collective-permute-start.4 = (f32[8,4224]{1,0:T(8,128)}, f32[8,4224]{1,0:T(8,128)S(1)}, u32[]{:S(2)}, u32[]{:S(2)}) collective-permute-start(f32[8,4224]{1,0:T(8,128)} %get-tuple-element.15), channel_id=1, source_target_pairs={{0,2},{1,3},{2,4},{3,5},{4,6},{5,7},{6,0},{7,1},{8,10},{9,11},{10,... | collective-permute-start | bytes 405512 | tf_op jit(solution)/shard_map/ppermute | solution.py:221
  30.7 11.1 %collective-permute-start.5 = (f32[8,4224]{1,0:T(8,128)}, f32[8,4224]{1,0:T(8,128)S(1)}, u32[]{:S(2)}, u32[]{:S(2)}) collective-permute-start(f32[8,4224]{1,0:T(8,128)} %get-tuple-element.16), channel_id=1, source_target_pairs={{0,3},{1,4},{2,5},{3,6},{4,7},{5,0},{6,1},{7,2},{8,11},{9,12},{10,... | collective-permute-start | bytes 405512 | tf_op jit(solution)/shard_map/ppermute | solution.py:221
  33.1 9.0 %collective-permute-start.6 = (f32[8,4224]{1,0:T(8,128)}, f32[8,4224]{1,0:T(8,128)S(1)}, u32[]{:S(2)}, u32[]{:S(2)}) collective-permute-start(f32[8,4224]{1,0:T(8,128)} %get-tuple-element.17), channel_id=1, source_target_pairs={{0,4},{1,5},{2,6},{3,7},{4,0},{5,1},{6,2},{7,3},{8,12},{9,13},{10,... | collective-permute-start | bytes 405512 | tf_op jit(solution)/shard_map/ppermute | solution.py:221
  33.6 10.4 %collective-permute-start.7 = (f32[8,4224]{1,0:T(8,128)}, f32[8,4224]{1,0:T(8,128)S(1)}, u32[]{:S(2)}, u32[]{:S(2)}) collective-permute-start(f32[8,4224]{1,0:T(8,128)} %get-tuple-element.18), channel_id=1, source_target_pairs={{0,5},{1,6},{2,7},{3,0},{4,1},{5,2},{6,3},{7,4},{8,13},{9,14},{10,... | collective-permute-start | bytes 405512 | tf_op jit(solution)/shard_map/ppermute | solution.py:221
  35.7 8.3 %collective-permute-start.8 = (f32[8,4224]{1,0:T(8,128)}, f32[8,4224]{1,0:T(8,128)S(1)}, u32[]{:S(2)}, u32[]{:S(2)}) collective-permute-start(f32[8,4224]{1,0:T(8,128)} %get-tuple-element.19), channel_id=1, source_target_pairs={{0,6},{1,7},{2,0},{3,1},{4,2},{5,3},{6,4},{7,5},{8,14},{9,15},{10,... | collective-permute-start | bytes 405512 | tf_op jit(solution)/shard_map/ppermute | solution.py:221
  37.2 6.9 %collective-permute-start.9 = (f32[8,4224]{1,0:T(8,128)}, f32[8,4224]{1,0:T(8,128)S(1)}, u32[]{:S(2)}, u32[]{:S(2)}) collective-permute-start(f32[8,4224]{1,0:T(8,128)} %get-tuple-element.20), channel_id=1, source_target_pairs={{0,7},{1,0},{2,1},{3,2},{4,3},{5,4},{6,5},{7,6},{8,15},{9,8},{10,9... | collective-permute-start | bytes 405512 | tf_op jit(solution)/shard_map/ppermute | solution.py:221
  45.2 3.8 %collective-permute-start.12 = (f32[1,4096]{1,0:T(1,128)S(1)}, f32[1,4096]{1,0:T(1,128)S(1)}, u32[]{:S(2)}, u32[]{:S(2)}) collective-permute-start(f32[1,4096]{1,0:T(1,128)S(1)} %get-tuple-element.22), channel_id=1, source_target_pairs={{0,24},{8,0},{16,8},{24,16},{1,25},{9,1},{17,9},{25,17},{2,26},{10... | collective-permute-start | bytes 49160 | tf_op jit(solution)/shard_map/ppermute | solution.py:221
  46.9 4.7 %collective-permute-start.11 = (f32[1,4096]{1,0:T(1,128)S(1)}, f32[1,4096]{1,0:T(1,128)S(1)}, u32[]{:S(2)}, u32[]{:S(2)}) collective-permute-start(f32[1,4096]{1,0:T(1,128)S(1)} %get-tuple-element.23), channel_id=1, source_target_pairs={{0,16},{8,24},{16,0},{24,8},{1,17},{9,25},{17,1},{25,9},{2,18},{10... | collective-permute-start | bytes 49160 | tf_op jit(solution)/shard_map/ppermute | solution.py:221
  46.9 5.5 %collective-permute-start.10 = (f32[1,4096]{1,0:T(1,128)S(1)}, f32[1,4096]{1,0:T(1,128)S(1)}, u32[]{:S(2)}, u32[]{:S(2)}) collective-permute-start(f32[1,4096]{1,0:T(1,128)S(1)} %get-tuple-element.24), channel_id=1, source_target_pairs={{0,8},{8,16},{16,24},{24,0},{1,9},{9,17},{17,25},{25,1},{2,10},{10... | collective-permute-start | bytes 49160 | tf_op jit(solution)/shard_map/ppermute | solution.py:221

commit v13 on v12

--- a/solution.py
+++ b/solution.py
@@ -249,7 +249,7 @@
     visitors = [block[:, :cell_count].reshape(per_target, B, PLANE) for block in arrived]
     visit_offsets = jnp.stack(
         [block[:, cell_count : cell_count + 3] for block in arrived]
-    ).reshape(slot_total, 3).astype(jnp.int32)
+    ).reshape(slot_total, 3)
 
     home_slot = pair_home[0, 0]
     visit_code = pair_visit[0, 0]
@@ -258,7 +258,7 @@
     return_slot = ((source - me) % section_total) * per_target + visit_code % per_target
     live = (jnp.arange(slots, dtype=jnp.int32) < pair_count[0, 0]).astype(jnp.int32)
     home_orb = orbitals[home_slot].reshape(slots, B, PLANE)
-    delta = pick_rows(home_slot, offsets).astype(jnp.int32) - visit_offsets[visit_slot]
+    delta = (pick_rows(home_slot, offsets) - pick_rows(visit_slot, visit_offsets)).astype(jnp.int32)
     pair_total = lax.psum(1, "pair")
     chunk = cell_count // pair_total
     pair_me = lax.axis_index("pair")

time: 53.7 us -> 53.8 us (level)
  local copies, waits for them, and re-layouts: 10.5 us -> 9.81 us
  other arithmetic: 1.17 us -> 1.81 us
    gather x2 -> x0, local copies, waits for them, and re-layouts: 0.65 us -> none  [per_device(): visit_offsets[visit_slot]]
    select_n x1, other arithmetic: 0.01 us -> 0.66 us  [per_device(): home_orb = orbitals[home_slot].reshape(slots, B, PLANE)]
    dot_general x2 -> x3, matrix products: 1.05 us -> 1.24 us  [pick_rows(): jnp.dot(chooser.astype(jnp.float32), table.astype(jnp.float32), precision...]
where the time goes in v13:
time: 53.8 us; the launch traced here: 53.6 us
  starting transfers between devices  17.3 us (32%)
  waiting for transfers between devices  14.5 us (27%)
  local copies, waits for them, and re-layouts  9.81 us (18%)
  Pallas kernels  6.12 us (11%)
  matrix products  3.15 us (6%)
  other arithmetic  1.81 us (3%)
  between operations  0.88 us (2%)
    ppermute x13, starting transfers between devices, exchange(): received.append(lax.ppermute(blocks[step], axis, pairs))  17.3 us
    ppermute x13, waiting for transfers between devices, exchange(): received.append(lax.ppermute(blocks[step], axis, pairs))  14.5 us
    pallas_call x1, Pallas kernels, pair_fields(): pl.pallas_call(functools.partial(pair_kernel, count, len(boxes)), out_sha...  6.12 us
    reshape x4, local copies, waits for them, and re-layouts, per_device(): block[:, :cell_count].reshape(per_target, B, PLANE)  2.62 us
    unnamed x17, local copies, waits for them, and re-layouts  1.89 us
    slice x4, local copies, waits for them, and re-layouts, per_device(): block[:, :cell_count].reshape(per_target, B, PLANE)  1.48 us
    dot_general x3, matrix products, pick_rows(): jnp.dot(chooser.astype(jnp.float32), table.astype(jnp.float32), precision...  1.24 us
  transfers between devices with their start and end apart: 13, of which 9 were waited for; matrix products, arithmetic and copies ran while one was open for 12% of the time, Pallas kernels for 0%

profile of v13, /device:TPU:0, one launch (start us, length us, event | category | flops | bytes accessed | tf_op | source)
XLA Modules:
  0.0 53.6 jit_solution(13751347375502470605)
XLA Ops:
  0.0 0.8 %pad_add_fusion = s32[8,1]{0,1:T(1,128)S(1)} fusion(s32[4,1]{0,1:T(1,128)} %bitcast.69), kind=kLoop, calls=%fused_computation.74 | loop fusion | flops 8 | bytes 48 | tf_op jit(solution)/shard_map/concatenate | solution.py:239
  0.8 0.7 %fusion.22 = s32[4]{0:T(128)S(1)} fusion(s32[1,1,4]{2,1,0:T(1,128)} %param.14), kind=kLoop, calls=%fused_computation.70 | loop fusion | flops 12 | bytes 32 | tf_op jit(solution)/shard_map/select_n | solution.py:260
  1.6 0.9 %convolution_convert_fusion = bf16[4,3]{0,1:T(4,128)(2,1)S(1)} fusion(s32[16,3]{0,1:T(4,128)} %param.12, s32[4]{0:T(128)S(1)} %get-tuple-element.31), kind=kOutput, calls=%fused_computation.7 | convolution fusion | flops 2428 | bytes 232 | tf_op jit(solution)/shard_map/dot_general | solution.py:227
  2.6 0.8 %gather_fusion = bf16[4,32768]{1,0:T(4,128)(2,1)S(1)} fusion(bf16[16,32768]{1,0:T(8,128)(2,1)S(1)} %copy-done, s32[1024]{0:T(1024)S(1)} %get-tuple-element.33), kind=kCustom, calls=%fused_computation | custom fusion | bytes 524304 | tf_op jit(solution)/shard_map/gather | solution.py:243
  3.9 3.1 %collective-permute-start = (bf16[1,32896]{1,0:T(2,128)(2,1)S(1)}, bf16[1,32896]{1,0:T(2,128)(2,1)S(1)}, u32[]{:S(2)}, u32[]{:S(2)}) collective-permute-start(bf16[1,32896]{1,0:T(2,128)(2,1)S(1)} %get-tuple-element.25), channel_id=1, source_target_pairs={{0,8},{8,16},{16,24},{24,0},{1,9},{9,17},{17,25},{25,1},{2,10},{10... | collective-permute-start | bytes 197384 | tf_op jit(solution)/shard_map/ppermute | solution.py:221
  7.0 2.1 %collective-permute-start.2 = (bf16[1,32896]{1,0:T(2,128)(2,1)S(1)}, bf16[1,32896]{1,0:T(2,128)(2,1)S(1)}, u32[]{:S(2)}, u32[]{:S(2)}) collective-permute-start(bf16[1,32896]{1,0:T(2,128)(2,1)S(1)} %get-tuple-element.26), channel_id=1, source_target_pairs={{0,24},{8,0},{16,8},{24,16},{1,25},{9,1},{17,9},{25,17},{2,26},{10... | collective-permute-start | bytes 197384 | tf_op jit(solution)/shard_map/ppermute | solution.py:221
  9.1 0.9 %collective-permute-start.1 = (bf16[1,32896]{1,0:T(2,128)(2,1)S(1)}, bf16[1,32896]{1,0:T(2,128)(2,1)S(1)}, u32[]{:S(2)}, u32[]{:S(2)}) collective-permute-start(bf16[1,32896]{1,0:T(2,128)(2,1)S(1)} %get-tuple-element.27), channel_id=1, source_target_pairs={{0,16},{8,24},{16,0},{24,8},{1,17},{9,25},{17,1},{25,9},{2,18},{10... | collective-permute-start | bytes 197384 | tf_op jit(solution)/shard_map/ppermute | solution.py:221
  11.4 0.8 %gather_fusion.1 = bf16[4,32768]{1,0:T(4,128)(2,1)S(1)} fusion(bf16[16,32768]{1,0:T(8,128)(2,1)S(1)} %copy-done, s32[1024]{0:T(1024)S(1)} %get-tuple-element.32), kind=kCustom, calls=%fused_computation.1 | custom fusion | bytes 524304 | tf_op jit(solution)/shard_map/gather | solution.py:260
  12.2 0.8 %copy.36 = bf16[1,4,32,1024]{3,2,1,0:T(8,128)(2,1)} copy(bf16[1,4,32,1024]{3,1,2,0:T(4,128)(2,1)S(1)} %bitcast.61) | data formatting | bytes 524288
  13.0 0.7 %reshape.149.rest_0_ = bf16[1,32,1024]{2,1,0:T(8,128)(2,1)} reshape(bf16[32768]{0:T(1024)(128)(2,1)S(1)} %slice_reduce_fusion.3) | data formatting | bytes 131072 | tf_op jit(solution)/shard_map/reshape | solution.py:249
  14.0 0.7 %collective-permute-done.2 = bf16[1,32896]{1,0:T(2,128)(2,1)S(1)} collective-permute-done((bf16[1,32896]{1,0:T(2,128)(2,1)S(1)}, bf16[1,32896]{1,0:T(2,128)(2,1)S(1)}, u32[]{:S(2)}, u32[]{:S(2)}) %collective-permute-start.2) | collective-permute-done | bytes 65824 | tf_op jit(solution)/shard_map/ppermute | solution.py:221
  15.1 0.7 %reshape.150.rest_1_ = bf16[1,32,1024]{2,1,0:T(8,128)(2,1)} reshape(bf16[32768]{0:T(1024)(128)(2,1)S(1)} %slice_reduce_fusion.2) | data formatting | bytes 131072 | tf_op jit(solution)/shard_map/reshape | solution.py:249
  15.8 0.7 %reshape.152.rest_3_ = bf16[1,32,1024]{2,1,0:T(8,128)(2,1)} reshape(bf16[32768]{0:T(1024)(128)(2,1)S(1)} %slice_reduce_fusion) | data formatting | bytes 131072 | tf_op jit(solution)/shard_map/reshape | solution.py:249
  16.4 4.5 %collective-permute-done.1 = bf16[1,32896]{1,0:T(2,128)(2,1)S(1)} collective-permute-done((bf16[1,32896]{1,0:T(2,128)(2,1)S(1)}, bf16[1,32896]{1,0:T(2,128)(2,1)S(1)}, u32[]{:S(2)}, u32[]{:S(2)}) %collective-permute-start.1) | collective-permute-done | bytes 65824 | tf_op jit(solution)/shard_map/ppermute | solution.py:221
  21.3 0.7 %reshape.151.rest_2_ = bf16[1,32,1024]{2,1,0:T(8,128)(2,1)} reshape(bf16[32768]{0:T(1024)(128)(2,1)S(1)} %slice_reduce_fusion.1) | data formatting | bytes 131072 | tf_op jit(solution)/shard_map/reshape | solution.py:249
  22.4 0.7 %concatenate.11.meta_ref = s32[29]{0:T(128)} concatenate(s32[12]{0:T(128)S(1)} %reshape.146, s32[4]{0:T(128)S(1)} %compare_convert_fusion, s32[4]{0:T(128)S(1)} %bitcast.67, s32[4]{0:T(128)S(1)} %get-tuple-element.28, s32[1]{0:T(128)} %bitcast.10, s32[4]{0:T(128)S(1)} %get-tuple-element.29), dimensions={0} | concatenate | bytes 232 | tf_op jit(solution)/shard_map/concatenate | solution.py:265
  23.1 6.1 %shard_map.109 = (f32[8,4224]{1,0:T(8,128)}, f32[8,4224]{1,0:T(8,128)}, f32[8,4224]{1,0:T(8,128)}, f32[8,4224]{1,0:T(8,128)}, f32[8,4224]{1,0:T(8,128)}, /*index...) custom-call(s32[29]{0:T(128)} %concatenate.11.meta_ref, bf16[4,32,1024]{2,1,0:T(8,128)(2,1)} %bitcast.60, ...), custom_call_target="tpu_custom_call" | custom-call | tf_op jit(solution)/shard_map/pallas_call | solution.py:201
  29.2 1.5 %collective-permute-start.4 = (f32[8,4224]{1,0:T(8,128)}, f32[8,4224]{1,0:T(8,128)S(1)}, u32[]{:S(2)}, u32[]{:S(2)}) collective-permute-start(f32[8,4224]{1,0:T(8,128)} %get-tuple-element.15), channel_id=1, source_target_pairs={{0,2},{1,3},{2,4},{3,5},{4,6},{5,7},{6,0},{7,1},{8,10},{9,11},{10,... | collective-permute-start | bytes 405512 | tf_op jit(solution)/shard_map/ppermute | solution.py:221
  30.7 2.4 %collective-permute-start.5 = (f32[8,4224]{1,0:T(8,128)}, f32[8,4224]{1,0:T(8,128)S(1)}, u32[]{:S(2)}, u32[]{:S(2)}) collective-permute-start(f32[8,4224]{1,0:T(8,128)} %get-tuple-element.16), channel_id=1, source_target_pairs={{0,3},{1,4},{2,5},{3,6},{4,7},{5,0},{6,1},{7,2},{8,11},{9,12},{10,... | collective-permute-start | bytes 405512 | tf_op jit(solution)/shard_map/ppermute | solution.py:221
  33.7 0.9 %bitcast_dynamic-update-slice_fusion.7 = f32[8,8,4224]{2,1,0:T(8,128)S(1)} fusion(f32[8,4224]{1,0:T(8,128)} %get-tuple-element.13), kind=kLoop, calls=%fused_computation.20 | loop fusion | bytes 270336
  34.6 1.0 %collective-permute-done.3 = f32[8,4224]{1,0:T(8,128)S(1)} collective-permute-done((f32[8,4224]{1,0:T(8,128)}, f32[8,4224]{1,0:T(8,128)S(1)}, u32[]{:S(2)}, u32[]{:S(2)}) %collective-permute-start.3) | collective-permute-done | bytes 135200 | tf_op jit(solution)/shard_map/ppermute | solution.py:221
  35.7 1.5 %collective-permute-start.8 = (f32[8,4224]{1,0:T(8,128)}, f32[8,4224]{1,0:T(8,128)S(1)}, u32[]{:S(2)}, u32[]{:S(2)}) collective-permute-start(f32[8,4224]{1,0:T(8,128)} %get-tuple-element.19), channel_id=1, source_target_pairs={{0,6},{1,7},{2,0},{3,1},{4,2},{5,3},{6,4},{7,5},{8,14},{9,15},{10,... | collective-permute-start | bytes 405512 | tf_op jit(solution)/shard_map/ppermute | solution.py:221
  37.2 2.6 %collective-permute-start.9 = (f32[8,4224]{1,0:T(8,128)}, f32[8,4224]{1,0:T(8,128)S(1)}, u32[]{:S(2)}, u32[]{:S(2)}) collective-permute-start(f32[8,4224]{1,0:T(8,128)} %get-tuple-element.20), channel_id=1, source_target_pairs={{0,7},{1,0},{2,1},{3,2},{4,3},{5,4},{6,5},{7,6},{8,15},{9,8},{10,9... | collective-permute-start | bytes 405512 | tf_op jit(solution)/shard_map/ppermute | solution.py:221
  39.8 2.1 %collective-permute-done.5 = f32[8,4224]{1,0:T(8,128)S(1)} collective-permute-done((f32[8,4224]{1,0:T(8,128)}, f32[8,4224]{1,0:T(8,128)S(1)}, u32[]{:S(2)}, u32[]{:S(2)}) %collective-permute-start.5) | collective-permute-done | bytes 135200 | tf_op jit(solution)/shard_map/ppermute | solution.py:221
  42.1 1.9 %collective-permute-done.7 = f32[8,4224]{1,0:T(8,128)S(1)} collective-permute-done((f32[8,4224]{1,0:T(8,128)}, f32[8,4224]{1,0:T(8,128)S(1)}, u32[]{:S(2)}, u32[]{:S(2)}) %collective-permute-start.7) | collective-permute-done | bytes 135200 | tf_op jit(solution)/shard_map/ppermute | solution.py:221
  44.3 0.8 %convolution_bitcast_fusion = f32[20,4096]{1,0:T(8,128)S(1)} fusion(f32[8,8,4096]{2,1,0:T(8,128)S(1)} %slice.111, s32[8,8]{0,1:T(8,128)S(1)} %bitcast.62), kind=kOutput, calls=%fused_computation.3 | convolution fusion | flops 31458560 | bytes 1376512 | tf_op jit(solution)/shard_map/srk,srl->kl/dot_general | solution.py:280
  45.2 1.7 %collective-permute-start.12 = (f32[1,4096]{1,0:T(1,128)S(1)}, f32[1,4096]{1,0:T(1,128)S(1)}, u32[]{:S(2)}, u32[]{:S(2)}) collective-permute-start(f32[1,4096]{1,0:T(1,128)S(1)} %get-tuple-element.22), channel_id=1, source_target_pairs={{0,24},{8,0},{16,8},{24,16},{1,25},{9,1},{17,9},{25,17},{2,26},{10... | collective-permute-start | bytes 49160 | tf_op jit(solution)/shard_map/ppermute | solution.py:221
  46.9 0.9 %collective-permute-start.10 = (f32[1,4096]{1,0:T(1,128)S(1)}, f32[1,4096]{1,0:T(1,128)S(1)}, u32[]{:S(2)}, u32[]{:S(2)}) collective-permute-start(f32[1,4096]{1,0:T(1,128)S(1)} %get-tuple-element.24), channel_id=1, source_target_pairs={{0,8},{8,16},{16,24},{24,0},{1,9},{9,17},{17,25},{25,1},{2,10},{10... | collective-permute-start | bytes 49160 | tf_op jit(solution)/shard_map/ppermute | solution.py:221
  47.8 0.6 %gather_fusion.2 = s32[4]{0:T(128)S(1)} fusion(s32[4]{0:T(128)S(1)} %get-tuple-element.31, s32[1024]{0:T(1024)S(1)} %pad_clamp_fusion), kind=kCustom, calls=%fused_computation.2 | custom fusion | bytes 48 | tf_op jit(solution)/shard_map/gather | solution.py:285
  49.0 2.5 %collective-permute-done.11 = f32[1,4096]{1,0:T(1,128)S(1)} collective-permute-done((f32[1,4096]{1,0:T(1,128)S(1)}, f32[1,4096]{1,0:T(1,128)S(1)}, u32[]{:S(2)}, u32[]{:S(2)}) %collective-permute-start.11) | collective-permute-done | bytes 16416 | tf_op jit(solution)/shard_map/ppermute | solution.py:221
  51.5 0.9 %collective-permute-done.10 = f32[1,4096]{1,0:T(1,128)S(1)} collective-permute-done((f32[1,4096]{1,0:T(1,128)S(1)}, f32[1,4096]{1,0:T(1,128)S(1)}, u32[]{:S(2)}, u32[]{:S(2)}) %collective-permute-start.10) | collective-permute-done | bytes 16416 | tf_op jit(solution)/shard_map/ppermute | solution.py:221
  52.5 1.1 %convolution_add_fusion = f32[16,4096]{1,0:T(8,128)} fusion(f32[20,4096]{1,0:T(8,128)S(1)} %convolution_bitcast_fusion, f32[4,1,4096]{2,1,0:T(1,128)S(1)} %pad_maximum_fusion, s32[4]{0:T(128)S(1)} %gather_fusion.2), kind=kOutput, calls=%fused_computation.4 | convolution fusion | flops 1638464 | bytes 589840 | tf_op jit(solution)/shard_map/dot_general | solution.py:289
  (52 shorter events, 4.6 us)
Async XLA Ops:
  0.0 2.6 %copy-start = (bf16[16,32768]{1,0:T(8,128)(2,1)S(1)}, bf16[16,32768]{1,0:T(8,128)(2,1)}, u32[]{:S(2)}) copy-start(bf16[16,32768]{1,0:T(8,128)(2,1)} %param.11) | copy-start | bytes 3145732
  3.4 7.8 %copy-start.2 = (s32[1,1,4]{2,1,0:T(1,128)S(1)}, s32[1,1,4]{2,1,0:T(1,128)}, u32[]{:S(2)}) copy-start(s32[1,1,4]{2,1,0:T(1,128)} %param.15) | copy-start | bytes 52
  3.4 7.8 %copy-start.1 = (s32[1,1,4]{2,1,0:T(1,128)S(1)}, s32[1,1,4]{2,1,0:T(1,128)}, u32[]{:S(2)}) copy-start(s32[1,1,4]{2,1,0:T(1,128)} %param.14) | copy-start | bytes 52
  3.4 7.8 %copy-start.3 = (s32[16,3]{0,1:T(4,128)S(1)}, s32[16,3]{0,1:T(4,128)}, u32[]{:S(2)}) copy-start(s32[16,3]{0,1:T(4,128)} %param.12) | copy-start | bytes 580
  3.9 9.8 %collective-permute-start = (bf16[1,32896]{1,0:T(2,128)(2,1)S(1)}, bf16[1,32896]{1,0:T(2,128)(2,1)S(1)}, u32[]{:S(2)}, u32[]{:S(2)}) collective-permute-start(bf16[1,32896]{1,0:T(2,128)(2,1)S(1)} %get-tuple-element.25), channel_id=1, source_target_pairs={{0,8},{8,16},{16,24},{24,0},{1,9},{9,17},{17,25},{25,1},{2,10},{10... | collective-permute-start | bytes 197384 | tf_op jit(solution)/shard_map/ppermute | solution.py:221
  7.0 7.8 %collective-permute-start.2 = (bf16[1,32896]{1,0:T(2,128)(2,1)S(1)}, bf16[1,32896]{1,0:T(2,128)(2,1)S(1)}, u32[]{:S(2)}, u32[]{:S(2)}) collective-permute-start(bf16[1,32896]{1,0:T(2,128)(2,1)S(1)} %get-tuple-element.26), channel_id=1, source_target_pairs={{0,24},{8,0},{16,8},{24,16},{1,25},{9,1},{17,9},{25,17},{2,26},{10... | collective-permute-start | bytes 197384 | tf_op jit(solution)/shard_map/ppermute | solution.py:221
  9.1 11.9 %collective-permute-start.1 = (bf16[1,32896]{1,0:T(2,128)(2,1)S(1)}, bf16[1,32896]{1,0:T(2,128)(2,1)S(1)}, u32[]{:S(2)}, u32[]{:S(2)}) collective-permute-start(bf16[1,32896]{1,0:T(2,128)(2,1)S(1)} %get-tuple-element.27), channel_id=1, source_target_pairs={{0,16},{8,24},{16,0},{24,8},{1,17},{9,25},{17,1},{25,9},{2,18},{10... | collective-permute-start | bytes 197384 | tf_op jit(solution)/shard_map/ppermute | solution.py:221
  29.2 6.5 %collective-permute-start.3 = (f32[8,4224]{1,0:T(8,128)}, f32[8,4224]{1,0:T(8,128)S(1)}, u32[]{:S(2)}, u32[]{:S(2)}) collective-permute-start(f32[8,4224]{1,0:T(8,128)} %get-tuple-element.14), channel_id=1, source_target_pairs={{0,1},{1,2},{2,3},{3,4},{4,5},{5,6},{6,7},{7,0},{8,9},{9,10},{10,1... | collective-permute-start | bytes 405512 | tf_op jit(solution)/shard_map/ppermute | solution.py:221
  29.2 8.0 %collective-permute-start.4 = (f32[8,4224]{1,0:T(8,128)}, f32[8,4224]{1,0:T(8,128)S(1)}, u32[]{:S(2)}, u32[]{:S(2)}) collective-permute-start(f32[8,4224]{1,0:T(8,128)} %get-tuple-element.15), channel_id=1, source_target_pairs={{0,2},{1,3},{2,4},{3,5},{4,6},{5,7},{6,0},{7,1},{8,10},{9,11},{10,... | collective-permute-start | bytes 405512 | tf_op jit(solution)/shard_map/ppermute | solution.py:221
  30.7 11.1 %collective-permute-start.5 = (f32[8,4224]{1,0:T(8,128)}, f32[8,4224]{1,0:T(8,128)S(1)}, u32[]{:S(2)}, u32[]{:S(2)}) collective-permute-start(f32[8,4224]{1,0:T(8,128)} %get-tuple-element.16), channel_id=1, source_target_pairs={{0,3},{1,4},{2,5},{3,6},{4,7},{5,0},{6,1},{7,2},{8,11},{9,12},{10,... | collective-permute-start | bytes 405512 | tf_op jit(solution)/shard_map/ppermute | solution.py:221
  33.1 9.0 %collective-permute-start.6 = (f32[8,4224]{1,0:T(8,128)}, f32[8,4224]{1,0:T(8,128)S(1)}, u32[]{:S(2)}, u32[]{:S(2)}) collective-permute-start(f32[8,4224]{1,0:T(8,128)} %get-tuple-element.17), channel_id=1, source_target_pairs={{0,4},{1,5},{2,6},{3,7},{4,0},{5,1},{6,2},{7,3},{8,12},{9,13},{10,... | collective-permute-start | bytes 405512 | tf_op jit(solution)/shard_map/ppermute | solution.py:221
  33.6 10.4 %collective-permute-start.7 = (f32[8,4224]{1,0:T(8,128)}, f32[8,4224]{1,0:T(8,128)S(1)}, u32[]{:S(2)}, u32[]{:S(2)}) collective-permute-start(f32[8,4224]{1,0:T(8,128)} %get-tuple-element.18), channel_id=1, source_target_pairs={{0,5},{1,6},{2,7},{3,0},{4,1},{5,2},{6,3},{7,4},{8,13},{9,14},{10,... | collective-permute-start | bytes 405512 | tf_op jit(solution)/shard_map/ppermute | solution.py:221
  35.7 8.3 %collective-permute-start.8 = (f32[8,4224]{1,0:T(8,128)}, f32[8,4224]{1,0:T(8,128)S(1)}, u32[]{:S(2)}, u32[]{:S(2)}) collective-permute-start(f32[8,4224]{1,0:T(8,128)} %get-tuple-element.19), channel_id=1, source_target_pairs={{0,6},{1,7},{2,0},{3,1},{4,2},{5,3},{6,4},{7,5},{8,14},{9,15},{10,... | collective-permute-start | bytes 405512 | tf_op jit(solution)/shard_map/ppermute | solution.py:221
  37.2 6.9 %collective-permute-start.9 = (f32[8,4224]{1,0:T(8,128)}, f32[8,4224]{1,0:T(8,128)S(1)}, u32[]{:S(2)}, u32[]{:S(2)}) collective-permute-start(f32[8,4224]{1,0:T(8,128)} %get-tuple-element.20), channel_id=1, source_target_pairs={{0,7},{1,0},{2,1},{3,2},{4,3},{5,4},{6,5},{7,6},{8,15},{9,8},{10,9... | collective-permute-start | bytes 405512 | tf_op jit(solution)/shard_map/ppermute | solution.py:221
  45.2 3.8 %collective-permute-start.12 = (f32[1,4096]{1,0:T(1,128)S(1)}, f32[1,4096]{1,0:T(1,128)S(1)}, u32[]{:S(2)}, u32[]{:S(2)}) collective-permute-start(f32[1,4096]{1,0:T(1,128)S(1)} %get-tuple-element.22), channel_id=1, source_target_pairs={{0,24},{8,0},{16,8},{24,16},{1,25},{9,1},{17,9},{25,17},{2,26},{10... | collective-permute-start | bytes 49160 | tf_op jit(solution)/shard_map/ppermute | solution.py:221
  46.9 4.6 %collective-permute-start.11 = (f32[1,4096]{1,0:T(1,128)S(1)}, f32[1,4096]{1,0:T(1,128)S(1)}, u32[]{:S(2)}, u32[]{:S(2)}) collective-permute-start(f32[1,4096]{1,0:T(1,128)S(1)} %get-tuple-element.23), channel_id=1, source_target_pairs={{0,16},{8,24},{16,0},{24,8},{1,17},{9,25},{17,1},{25,9},{2,18},{10... | collective-permute-start | bytes 49160 | tf_op jit(solution)/shard_map/ppermute | solution.py:221
  46.9 5.5 %collective-permute-start.10 = (f32[1,4096]{1,0:T(1,128)S(1)}, f32[1,4096]{1,0:T(1,128)S(1)}, u32[]{:S(2)}, u32[]{:S(2)}) collective-permute-start(f32[1,4096]{1,0:T(1,128)S(1)} %get-tuple-element.24), channel_id=1, source_target_pairs={{0,8},{8,16},{16,24},{24,0},{1,9},{9,17},{17,25},{25,1},{2,10},{10... | collective-permute-start | bytes 49160 | tf_op jit(solution)/shard_map/ppermute | solution.py:221

commit v14 on v12

--- a/solution.py
+++ b/solution.py
@@ -277,10 +277,15 @@
     got_ids = got[:, :, chunk].astype(jnp.int32)
     all_rows = jnp.arange(home_count + slot_total, dtype=jnp.int32)
     picker = (got_ids[:, :, None] == all_rows[None, None, :]).astype(jnp.float32)
-    totals = jnp.einsum("srk,srl->kl", picker, got[:, :, :chunk], precision=lax.Precision.HIGH)
-    home_totals = totals[:home_count]
+    data = got[:, :, :chunk]
+    visit_part = jnp.einsum(
+        "srk,srl->kl", picker[:, :, home_count:], data, precision=lax.Precision.HIGH
+    )
+    home_totals = jnp.einsum(
+        "srk,srl->kl", picker[:, :, :home_count], data, precision=lax.Precision.HIGH
+    )
     back = (-jnp.arange(section_total, dtype=jnp.int32)) % section_total
-    visit_totals = totals[home_count:].reshape(section_total, per_target, chunk)
+    visit_totals = visit_part.reshape(section_total, per_target, chunk)
     returned = jnp.stack(exchange(visit_totals, "home")).reshape(slot_total, chunk)
     owners = chosen[back].reshape(-1)
     chooser = (owners[:, None] == jnp.arange(home_count, dtype=jnp.int32)[None, :]).astype(

time: 53.7 us -> 53.8 us (level)
  waiting for transfers between devices: 14.7 us -> 13.8 us
  matrix products: 2.96 us -> 3.74 us
    ppermute x13, waiting for transfers between devices: 14.7 us -> 13.8 us  [exchange(): received.append(lax.ppermute(blocks[step], axis, pairs))]
    dot_general x1 -> x2, matrix products: 0.83 us -> 1.62 us  [the longest x1 0.82 us: per_device(): jnp.einsum('srk,srl->kl', picker[:, :, home_count:], data, precision=lax....]
  transfers between devices with their start and end apart: 13 -> 13, of which waited for: 9 -> 9; matrix products, arithmetic and copies ran while one was open for 12% -> 14% of each run, Pallas kernels for 0% -> 0%
where the time goes in v14:
time: 53.8 us; the launch traced here: 53.6 us
  starting transfers between devices  17.3 us (32%)
  waiting for transfers between devices  13.8 us (26%)
  local copies, waits for them, and re-layouts  10.5 us (20%)
  Pallas kernels  6.12 us (11%)
  matrix products  3.74 us (7%)
  other arithmetic  1.25 us (2%)
  between operations  0.9 us (2%)
    ppermute x13, starting transfers between devices, exchange(): received.append(lax.ppermute(blocks[step], axis, pairs))  17.3 us
    ppermute x13, waiting for transfers between devices, exchange(): received.append(lax.ppermute(blocks[step], axis, pairs))  13.8 us
    pallas_call x1, Pallas kernels, pair_fields(): pl.pallas_call(functools.partial(pair_kernel, count, len(boxes)), out_sha...  6.12 us
    reshape x4, local copies, waits for them, and re-layouts, per_device(): block[:, :cell_count].reshape(per_target, B, PLANE)  2.62 us
    unnamed x17, local copies, waits for them, and re-layouts  1.89 us
    slice x4, local copies, waits for them, and re-layouts, per_device(): block[:, :cell_count].reshape(per_target, B, PLANE)  1.48 us
  transfers between devices with their start and end apart: 13, of which 9 were waited for; matrix products, arithmetic and copies ran while one was open for 14% of the time, Pallas kernels for 0%

profile of v14, /device:TPU:0, one launch (start us, length us, event | category | flops | bytes accessed | tf_op | source)
XLA Modules:
  0.0 53.6 jit_solution(5576602433574914810)
XLA Ops:
  0.0 0.8 %pad_add_fusion = s32[8,1]{0,1:T(1,128)S(1)} fusion(s32[4,1]{0,1:T(1,128)} %bitcast.74), kind=kLoop, calls=%fused_computation.80 | loop fusion | flops 8 | bytes 48 | tf_op jit(solution)/shard_map/concatenate | solution.py:239
  0.9 0.9 %convolution_convert_fusion.1 = bf16[4,3]{0,1:T(4,128)(2,1)S(1)} fusion(s32[16,3]{0,1:T(4,128)} %param.12, s32[4]{0:T(128)S(1)} %get-tuple-element.31), kind=kOutput, calls=%fused_computation.9 | convolution fusion | flops 2428 | bytes 232 | tf_op jit(solution)/shard_map/dot_general | solution.py:227
  1.9 0.8 %gather_fusion = bf16[4,32768]{1,0:T(4,128)(2,1)S(1)} fusion(bf16[16,32768]{1,0:T(8,128)(2,1)S(1)} %copy-done, s32[1024]{0:T(1024)S(1)} %pad_clamp_fusion.3), kind=kCustom, calls=%fused_computation | custom fusion | bytes 524304 | tf_op jit(solution)/shard_map/gather | solution.py:243
  3.2 3.1 %collective-permute-start = (bf16[1,32896]{1,0:T(2,128)(2,1)S(1)}, bf16[1,32896]{1,0:T(2,128)(2,1)S(1)}, u32[]{:S(2)}, u32[]{:S(2)}) collective-permute-start(bf16[1,32896]{1,0:T(2,128)(2,1)S(1)} %get-tuple-element.21), channel_id=1, source_target_pairs={{0,8},{8,16},{16,24},{24,0},{1,9},{9,17},{17,25},{25,1},{2,10},{10... | collective-permute-start | bytes 197384 | tf_op jit(solution)/shard_map/ppermute | solution.py:221
  6.3 2.1 %collective-permute-start.2 = (bf16[1,32896]{1,0:T(2,128)(2,1)S(1)}, bf16[1,32896]{1,0:T(2,128)(2,1)S(1)}, u32[]{:S(2)}, u32[]{:S(2)}) collective-permute-start(bf16[1,32896]{1,0:T(2,128)(2,1)S(1)} %get-tuple-element.22), channel_id=1, source_target_pairs={{0,24},{8,0},{16,8},{24,16},{1,25},{9,1},{17,9},{25,17},{2,26},{10... | collective-permute-start | bytes 197384 | tf_op jit(solution)/shard_map/ppermute | solution.py:221
  8.4 0.9 %collective-permute-start.1 = (bf16[1,32896]{1,0:T(2,128)(2,1)S(1)}, bf16[1,32896]{1,0:T(2,128)(2,1)S(1)}, u32[]{:S(2)}, u32[]{:S(2)}) collective-permute-start(bf16[1,32896]{1,0:T(2,128)(2,1)S(1)} %get-tuple-element.23), channel_id=1, source_target_pairs={{0,16},{8,24},{16,0},{24,8},{1,17},{9,25},{17,1},{25,9},{2,18},{10... | collective-permute-start | bytes 197384 | tf_op jit(solution)/shard_map/ppermute | solution.py:221
  10.6 0.6 %gather_fusion.3 = s32[4]{0:T(128)S(1)} fusion(s32[4]{0:T(128)S(1)} %get-tuple-element.31, s32[1024]{0:T(1024)S(1)} %pad_clamp_fusion), kind=kCustom, calls=%fused_computation.3 | custom fusion | bytes 48 | tf_op jit(solution)/shard_map/gather | solution.py:290
  11.2 0.7 %reshape.186.rest_0_ = bf16[1,32,1024]{2,1,0:T(8,128)(2,1)} reshape(bf16[32768]{0:T(1024)(128)(2,1)S(1)} %slice_reduce_fusion.3) | data formatting | bytes 131072 | tf_op jit(solution)/shard_map/reshape | solution.py:249
  11.9 0.8 %gather_fusion.2 = bf16[4,32768]{1,0:T(4,128)(2,1)S(1)} fusion(bf16[16,32768]{1,0:T(8,128)(2,1)S(1)} %copy-done, s32[1024]{0:T(1024)S(1)} %get-tuple-element.32), kind=kCustom, calls=%fused_computation.2 | custom fusion | bytes 524304 | tf_op jit(solution)/shard_map/gather | solution.py:260
  12.7 0.8 %copy.40 = bf16[1,4,32,1024]{3,2,1,0:T(8,128)(2,1)} copy(bf16[1,4,32,1024]{3,1,2,0:T(4,128)(2,1)S(1)} %bitcast.65) | data formatting | bytes 524288
  14.5 0.7 %reshape.187.rest_1_ = bf16[1,32,1024]{2,1,0:T(8,128)(2,1)} reshape(bf16[32768]{0:T(1024)(128)(2,1)S(1)} %slice_reduce_fusion.2) | data formatting | bytes 131072 | tf_op jit(solution)/shard_map/reshape | solution.py:249
  15.1 0.7 %reshape.189.rest_3_ = bf16[1,32,1024]{2,1,0:T(8,128)(2,1)} reshape(bf16[32768]{0:T(1024)(128)(2,1)S(1)} %slice_reduce_fusion) | data formatting | bytes 131072 | tf_op jit(solution)/shard_map/reshape | solution.py:249
  15.8 4.5 %collective-permute-done.1 = bf16[1,32896]{1,0:T(2,128)(2,1)S(1)} collective-permute-done((bf16[1,32896]{1,0:T(2,128)(2,1)S(1)}, bf16[1,32896]{1,0:T(2,128)(2,1)S(1)}, u32[]{:S(2)}, u32[]{:S(2)}) %collective-permute-start.1) | collective-permute-done | bytes 65824 | tf_op jit(solution)/shard_map/ppermute | solution.py:221
  20.7 0.7 %reshape.188.rest_2_ = bf16[1,32,1024]{2,1,0:T(8,128)(2,1)} reshape(bf16[32768]{0:T(1024)(128)(2,1)S(1)} %slice_reduce_fusion.1) | data formatting | bytes 131072 | tf_op jit(solution)/shard_map/reshape | solution.py:249
  21.4 0.6 %gather_fusion.1 = s32[4,3]{1,0:T(4,128)S(1)} fusion(s32[4,3]{1,0:T(4,128)S(1)} %bitcast.66, s32[1024]{0:T(1024)S(1)} %get-tuple-element.33), kind=kCustom, calls=%fused_computation.1 | custom fusion | bytes 112 | tf_op jit(solution)/shard_map/gather | solution.py:261
  22.4 0.7 %concatenate.11.meta_ref = s32[29]{0:T(128)} concatenate(s32[12]{0:T(128)S(1)} %reshape.183, s32[4]{0:T(128)S(1)} %compare_convert_fusion, s32[4]{0:T(128)S(1)} %bitcast.72, s32[4]{0:T(128)S(1)} %get-tuple-element.29, s32[1]{0:T(128)} %bitcast.12, s32[4]{0:T(128)S(1)} %get-tuple-element.28), dimensions={0} | concatenate | bytes 232 | tf_op jit(solution)/shard_map/concatenate | solution.py:265
  23.1 6.1 %shard_map.109 = (f32[8,4224]{1,0:T(8,128)}, f32[8,4224]{1,0:T(8,128)}, f32[8,4224]{1,0:T(8,128)}, f32[8,4224]{1,0:T(8,128)}, f32[8,4224]{1,0:T(8,128)}, /*index...) custom-call(s32[29]{0:T(128)} %concatenate.11.meta_ref, bf16[4,32,1024]{2,1,0:T(8,128)(2,1)} %bitcast.64, ...), custom_call_target="tpu_custom_call" | custom-call | tf_op jit(solution)/shard_map/pallas_call | solution.py:201
  29.2 1.5 %collective-permute-start.4 = (f32[8,4224]{1,0:T(8,128)}, f32[8,4224]{1,0:T(8,128)S(1)}, u32[]{:S(2)}, u32[]{:S(2)}) collective-permute-start(f32[8,4224]{1,0:T(8,128)} %get-tuple-element.15), channel_id=1, source_target_pairs={{0,2},{1,3},{2,4},{3,5},{4,6},{5,7},{6,0},{7,1},{8,10},{9,11},{10,... | collective-permute-start | bytes 405512 | tf_op jit(solution)/shard_map/ppermute | solution.py:221
  30.7 2.4 %collective-permute-start.5 = (f32[8,4224]{1,0:T(8,128)}, f32[8,4224]{1,0:T(8,128)S(1)}, u32[]{:S(2)}, u32[]{:S(2)}) collective-permute-start(f32[8,4224]{1,0:T(8,128)} %get-tuple-element.16), channel_id=1, source_target_pairs={{0,3},{1,4},{2,5},{3,6},{4,7},{5,0},{6,1},{7,2},{8,11},{9,12},{10,... | collective-permute-start | bytes 405512 | tf_op jit(solution)/shard_map/ppermute | solution.py:221
  33.7 0.9 %bitcast_dynamic-update-slice_fusion.7 = f32[8,8,4224]{2,1,0:T(8,128)S(1)} fusion(f32[8,4224]{1,0:T(8,128)} %get-tuple-element.13), kind=kLoop, calls=%fused_computation.23 | loop fusion | bytes 270336
  34.6 1.1 %collective-permute-done.3 = f32[8,4224]{1,0:T(8,128)S(1)} collective-permute-done((f32[8,4224]{1,0:T(8,128)}, f32[8,4224]{1,0:T(8,128)S(1)}, u32[]{:S(2)}, u32[]{:S(2)}) %collective-permute-start.3) | collective-permute-done | bytes 135200 | tf_op jit(solution)/shard_map/ppermute | solution.py:221
  35.7 1.5 %collective-permute-start.8 = (f32[8,4224]{1,0:T(8,128)}, f32[8,4224]{1,0:T(8,128)S(1)}, u32[]{:S(2)}, u32[]{:S(2)}) collective-permute-start(f32[8,4224]{1,0:T(8,128)} %get-tuple-element.19), channel_id=1, source_target_pairs={{0,6},{1,7},{2,0},{3,1},{4,2},{5,3},{6,4},{7,5},{8,14},{9,15},{10,... | collective-permute-start | bytes 405512 | tf_op jit(solution)/shard_map/ppermute | solution.py:221
  37.2 2.6 %collective-permute-start.9 = (f32[8,4224]{1,0:T(8,128)}, f32[8,4224]{1,0:T(8,128)S(1)}, u32[]{:S(2)}, u32[]{:S(2)}) collective-permute-start(f32[8,4224]{1,0:T(8,128)} %get-tuple-element.20), channel_id=1, source_target_pairs={{0,7},{1,0},{2,1},{3,2},{4,3},{5,4},{6,5},{7,6},{8,15},{9,8},{10,9... | collective-permute-start | bytes 405512 | tf_op jit(solution)/shard_map/ppermute | solution.py:221
  39.8 2.1 %collective-permute-done.5 = f32[8,4224]{1,0:T(8,128)S(1)} collective-permute-done((f32[8,4224]{1,0:T(8,128)}, f32[8,4224]{1,0:T(8,128)S(1)}, u32[]{:S(2)}, u32[]{:S(2)}) %collective-permute-start.5) | collective-permute-done | bytes 135200 | tf_op jit(solution)/shard_map/ppermute | solution.py:221
  42.1 1.9 %collective-permute-done.7 = f32[8,4224]{1,0:T(8,128)S(1)} collective-permute-done((f32[8,4224]{1,0:T(8,128)}, f32[8,4224]{1,0:T(8,128)S(1)}, u32[]{:S(2)}, u32[]{:S(2)}) %collective-permute-start.7) | collective-permute-done | bytes 135200 | tf_op jit(solution)/shard_map/ppermute | solution.py:221
  44.4 0.8 %convolution_bitcast_fusion.1 = f32[4,4096]{1,0:T(4,128)S(1)} fusion(f32[8,8,4096]{2,1,0:T(8,128)S(1)} %slice.113, pred[8,8,20]{2,0,1:T(8,128)(4,1)S(1)} %iota_compare_fusion.1), kind=kOutput, calls=%fused_computation.6 | convolution fusion | flops 6291456 | bytes 1115392 | tf_op jit(solution)/shard_map/srk,srl->kl/dot_general | solution.py:281
  45.3 1.7 %collective-permute-start.12 = (f32[1,4096]{1,0:T(1,128)S(1)}, f32[1,4096]{1,0:T(1,128)S(1)}, u32[]{:S(2)}, u32[]{:S(2)}) collective-permute-start(f32[1,4096]{1,0:T(1,128)S(1)} %get-tuple-element.25), channel_id=1, source_target_pairs={{0,24},{8,0},{16,8},{24,16},{1,25},{9,1},{17,9},{25,17},{2,26},{10... | collective-permute-start | bytes 49160 | tf_op jit(solution)/shard_map/ppermute | solution.py:221
  46.9 0.9 %collective-permute-start.10 = (f32[1,4096]{1,0:T(1,128)S(1)}, f32[1,4096]{1,0:T(1,128)S(1)}, u32[]{:S(2)}, u32[]{:S(2)}) collective-permute-start(f32[1,4096]{1,0:T(1,128)S(1)} %get-tuple-element.27), channel_id=1, source_target_pairs={{0,8},{8,16},{16,24},{24,0},{1,9},{9,17},{17,25},{25,1},{2,10},{10... | collective-permute-start | bytes 49160 | tf_op jit(solution)/shard_map/ppermute | solution.py:221
  47.9 0.8 %convolution_bitcast_fusion = f32[16,4096]{1,0:T(8,128)S(1)} fusion(f32[8,8,4096]{2,1,0:T(8,128)S(1)} %slice.113, pred[8,8,20]{2,0,1:T(8,128)(4,1)S(1)} %iota_compare_fusion.1), kind=kOutput, calls=%fused_computation.5 | convolution fusion | flops 25165824 | bytes 1312000 | tf_op jit(solution)/shard_map/srk,srl->kl/dot_general | solution.py:284
  49.0 2.5 %collective-permute-done.11 = f32[1,4096]{1,0:T(1,128)S(1)} collective-permute-done((f32[1,4096]{1,0:T(1,128)S(1)}, f32[1,4096]{1,0:T(1,128)S(1)}, u32[]{:S(2)}, u32[]{:S(2)}) %collective-permute-start.11) | collective-permute-done | bytes 16416 | tf_op jit(solution)/shard_map/ppermute | solution.py:221
  51.6 0.9 %collective-permute-done.10 = f32[1,4096]{1,0:T(1,128)S(1)} collective-permute-done((f32[1,4096]{1,0:T(1,128)S(1)}, f32[1,4096]{1,0:T(1,128)S(1)}, u32[]{:S(2)}, u32[]{:S(2)}) %collective-permute-start.10) | collective-permute-done | bytes 16416 | tf_op jit(solution)/shard_map/ppermute | solution.py:221
  52.5 1.1 %convolution_add_fusion = f32[16,4096]{1,0:T(8,128)} fusion(f32[16,4096]{1,0:T(8,128)S(1)} %convolution_bitcast_fusion, f32[4,1,4096]{2,1,0:T(1,128)S(1)} %pad_maximum_fusion, s32[4]{0:T(128)S(1)} %gather_fusion.3), kind=kOutput, calls=%fused_computation.4 | convolution fusion | flops 1638464 | bytes 589840 | tf_op jit(solution)/shard_map/dot_general | solution.py:294
  (57 shorter events, 4.7 us)
Async XLA Ops:
  0.0 1.9 %copy-start = (bf16[16,32768]{1,0:T(8,128)(2,1)S(1)}, bf16[16,32768]{1,0:T(8,128)(2,1)}, u32[]{:S(2)}) copy-start(bf16[16,32768]{1,0:T(8,128)(2,1)} %param.11) | copy-start | bytes 3145732
  2.7 6.6 %copy-start.2 = (s32[1,1,4]{2,1,0:T(1,128)S(1)}, s32[1,1,4]{2,1,0:T(1,128)}, u32[]{:S(2)}) copy-start(s32[1,1,4]{2,1,0:T(1,128)} %param.15) | copy-start | bytes 52
  2.7 7.8 %copy-start.1 = (s32[1,1,4]{2,1,0:T(1,128)S(1)}, s32[1,1,4]{2,1,0:T(1,128)}, u32[]{:S(2)}) copy-start(s32[1,1,4]{2,1,0:T(1,128)} %param.14) | copy-start | bytes 52
  3.2 10.3 %collective-permute-start = (bf16[1,32896]{1,0:T(2,128)(2,1)S(1)}, bf16[1,32896]{1,0:T(2,128)(2,1)S(1)}, u32[]{:S(2)}, u32[]{:S(2)}) collective-permute-start(bf16[1,32896]{1,0:T(2,128)(2,1)S(1)} %get-tuple-element.21), channel_id=1, source_target_pairs={{0,8},{8,16},{16,24},{24,0},{1,9},{9,17},{17,25},{25,1},{2,10},{10... | collective-permute-start | bytes 197384 | tf_op jit(solution)/shard_map/ppermute | solution.py:221
  6.3 7.8 %collective-permute-start.2 = (bf16[1,32896]{1,0:T(2,128)(2,1)S(1)}, bf16[1,32896]{1,0:T(2,128)(2,1)S(1)}, u32[]{:S(2)}, u32[]{:S(2)}) collective-permute-start(bf16[1,32896]{1,0:T(2,128)(2,1)S(1)} %get-tuple-element.22), channel_id=1, source_target_pairs={{0,24},{8,0},{16,8},{24,16},{1,25},{9,1},{17,9},{25,17},{2,26},{10... | collective-permute-start | bytes 197384 | tf_op jit(solution)/shard_map/ppermute | solution.py:221
  8.4 11.9 %collective-permute-start.1 = (bf16[1,32896]{1,0:T(2,128)(2,1)S(1)}, bf16[1,32896]{1,0:T(2,128)(2,1)S(1)}, u32[]{:S(2)}, u32[]{:S(2)}) collective-permute-start(bf16[1,32896]{1,0:T(2,128)(2,1)S(1)} %get-tuple-element.23), channel_id=1, source_target_pairs={{0,16},{8,24},{16,0},{24,8},{1,17},{9,25},{17,1},{25,9},{2,18},{10... | collective-permute-start | bytes 197384 | tf_op jit(solution)/shard_map/ppermute | solution.py:221
  12.7 9.3 %copy-start.3 = (s32[16,3]{0,1:T(4,128)S(1)}, s32[16,3]{0,1:T(4,128)}, u32[]{:S(2)}) copy-start(s32[16,3]{0,1:T(4,128)} %param.12) | copy-start | bytes 580
  29.2 6.5 %collective-permute-start.3 = (f32[8,4224]{1,0:T(8,128)}, f32[8,4224]{1,0:T(8,128)S(1)}, u32[]{:S(2)}, u32[]{:S(2)}) collective-permute-start(f32[8,4224]{1,0:T(8,128)} %get-tuple-element.14), channel_id=1, source_target_pairs={{0,1},{1,2},{2,3},{3,4},{4,5},{5,6},{6,7},{7,0},{8,9},{9,10},{10,1... | collective-permute-start | bytes 405512 | tf_op jit(solution)/shard_map/ppermute | solution.py:221
  29.2 8.0 %collective-permute-start.4 = (f32[8,4224]{1,0:T(8,128)}, f32[8,4224]{1,0:T(8,128)S(1)}, u32[]{:S(2)}, u32[]{:S(2)}) collective-permute-start(f32[8,4224]{1,0:T(8,128)} %get-tuple-element.15), channel_id=1, source_target_pairs={{0,2},{1,3},{2,4},{3,5},{4,6},{5,7},{6,0},{7,1},{8,10},{9,11},{10,... | collective-permute-start | bytes 405512 | tf_op jit(solution)/shard_map/ppermute | solution.py:221
  30.7 11.1 %collective-permute-start.5 = (f32[8,4224]{1,0:T(8,128)}, f32[8,4224]{1,0:T(8,128)S(1)}, u32[]{:S(2)}, u32[]{:S(2)}) collective-permute-start(f32[8,4224]{1,0:T(8,128)} %get-tuple-element.16), channel_id=1, source_target_pairs={{0,3},{1,4},{2,5},{3,6},{4,7},{5,0},{6,1},{7,2},{8,11},{9,12},{10,... | collective-permute-start | bytes 405512 | tf_op jit(solution)/shard_map/ppermute | solution.py:221
  33.1 9.0 %collective-permute-start.6 = (f32[8,4224]{1,0:T(8,128)}, f32[8,4224]{1,0:T(8,128)S(1)}, u32[]{:S(2)}, u32[]{:S(2)}) collective-permute-start(f32[8,4224]{1,0:T(8,128)} %get-tuple-element.17), channel_id=1, source_target_pairs={{0,4},{1,5},{2,6},{3,7},{4,0},{5,1},{6,2},{7,3},{8,12},{9,13},{10,... | collective-permute-start | bytes 405512 | tf_op jit(solution)/shard_map/ppermute | solution.py:221
  33.6 10.4 %collective-permute-start.7 = (f32[8,4224]{1,0:T(8,128)}, f32[8,4224]{1,0:T(8,128)S(1)}, u32[]{:S(2)}, u32[]{:S(2)}) collective-permute-start(f32[8,4224]{1,0:T(8,128)} %get-tuple-element.18), channel_id=1, source_target_pairs={{0,5},{1,6},{2,7},{3,0},{4,1},{5,2},{6,3},{7,4},{8,13},{9,14},{10,... | collective-permute-start | bytes 405512 | tf_op jit(solution)/shard_map/ppermute | solution.py:221
  35.7 8.3 %collective-permute-start.8 = (f32[8,4224]{1,0:T(8,128)}, f32[8,4224]{1,0:T(8,128)S(1)}, u32[]{:S(2)}, u32[]{:S(2)}) collective-permute-start(f32[8,4224]{1,0:T(8,128)} %get-tuple-element.19), channel_id=1, source_target_pairs={{0,6},{1,7},{2,0},{3,1},{4,2},{5,3},{6,4},{7,5},{8,14},{9,15},{10,... | collective-permute-start | bytes 405512 | tf_op jit(solution)/shard_map/ppermute | solution.py:221
  37.2 6.9 %collective-permute-start.9 = (f32[8,4224]{1,0:T(8,128)}, f32[8,4224]{1,0:T(8,128)S(1)}, u32[]{:S(2)}, u32[]{:S(2)}) collective-permute-start(f32[8,4224]{1,0:T(8,128)} %get-tuple-element.20), channel_id=1, source_target_pairs={{0,7},{1,0},{2,1},{3,2},{4,3},{5,4},{6,5},{7,6},{8,15},{9,8},{10,9... | collective-permute-start | bytes 405512 | tf_op jit(solution)/shard_map/ppermute | solution.py:221
  45.3 3.8 %collective-permute-start.12 = (f32[1,4096]{1,0:T(1,128)S(1)}, f32[1,4096]{1,0:T(1,128)S(1)}, u32[]{:S(2)}, u32[]{:S(2)}) collective-permute-start(f32[1,4096]{1,0:T(1,128)S(1)} %get-tuple-element.25), channel_id=1, source_target_pairs={{0,24},{8,0},{16,8},{24,16},{1,25},{9,1},{17,9},{25,17},{2,26},{10... | collective-permute-start | bytes 49160 | tf_op jit(solution)/shard_map/ppermute | solution.py:221
  46.9 4.7 %collective-permute-start.11 = (f32[1,4096]{1,0:T(1,128)S(1)}, f32[1,4096]{1,0:T(1,128)S(1)}, u32[]{:S(2)}, u32[]{:S(2)}) collective-permute-start(f32[1,4096]{1,0:T(1,128)S(1)} %get-tuple-element.26), channel_id=1, source_target_pairs={{0,16},{8,24},{16,0},{24,8},{1,17},{9,25},{17,1},{25,9},{2,18},{10... | collective-permute-start | bytes 49160 | tf_op jit(solution)/shard_map/ppermute | solution.py:221
  46.9 5.5 %collective-permute-start.10 = (f32[1,4096]{1,0:T(1,128)S(1)}, f32[1,4096]{1,0:T(1,128)S(1)}, u32[]{:S(2)}, u32[]{:S(2)}) collective-permute-start(f32[1,4096]{1,0:T(1,128)S(1)} %get-tuple-element.27), channel_id=1, source_target_pairs={{0,8},{8,16},{16,24},{24,0},{1,9},{9,17},{17,25},{25,1},{2,10},{10... | collective-permute-start | bytes 49160 | tf_op jit(solution)/shard_map/ppermute | solution.py:221

commit v15 on v12

--- a/solution.py
+++ b/solution.py
@@ -286,7 +286,9 @@
     chooser = (owners[:, None] == jnp.arange(home_count, dtype=jnp.int32)[None, :]).astype(
         jnp.float32
     )
-    return home_totals + jnp.dot(chooser.T, returned, precision=lax.Precision.HIGH)
+    return home_totals + jnp.sum(
+        jnp.where(chooser.T[:, :, None] > 0, returned[None, :, :], 0.0), axis=1
+    )
 
 
 def solution(mesh):

time: 53.7 us -> 54.2 us (level)
  other arithmetic: 1.17 us -> 2.77 us
  matrix products: 2.96 us -> 1.89 us
    dot_general x1 -> x0, matrix products: 1.07 us -> none  [per_device(): jnp.dot(chooser.T, returned, precision=lax.Precision.HIGH)]
    add x0 -> x1, other arithmetic: none -> 0.73 us  [per_device(): home_totals + jnp.sum(jnp.where(chooser.T[:, :, None] > 0, returned[None,...]
    select_n x1, other arithmetic: 0.01 us -> 0.67 us  [per_device(): visit_offsets[visit_slot]]
where the time goes in v15:
time: 54.2 us; the launch traced here: 54 us
  starting transfers between devices  17.3 us (32%)
  waiting for transfers between devices  14.6 us (27%)
  local copies, waits for them, and re-layouts  10.4 us (19%)
  Pallas kernels  6.12 us (11%)
  other arithmetic  2.77 us (5%)
  matrix products  1.89 us (3%)
  between operations  0.89 us (2%)
    ppermute x13, starting transfers between devices, exchange(): received.append(lax.ppermute(blocks[step], axis, pairs))  17.3 us
    ppermute x13, waiting for transfers between devices, exchange(): received.append(lax.ppermute(blocks[step], axis, pairs))  14.6 us
    pallas_call x1, Pallas kernels, pair_fields(): pl.pallas_call(functools.partial(pair_kernel, count, len(boxes)), out_sha...  6.12 us
    reshape x4, local copies, waits for them, and re-layouts, per_device(): block[:, :cell_count].reshape(per_target, B, PLANE)  2.63 us
    unnamed x17, local copies, waits for them, and re-layouts  1.89 us
    slice x4, local copies, waits for them, and re-layouts, per_device(): block[:, :cell_count].reshape(per_target, B, PLANE)  1.48 us
  transfers between devices with their start and end apart: 13, of which 9 were waited for; matrix products, arithmetic and copies ran while one was open for 12% of the time, Pallas kernels for 0%

profile of v15, /device:TPU:0, one launch (start us, length us, event | category | flops | bytes accessed | tf_op | source)
XLA Modules:
  0.0 54.0 jit_solution(8558073446721657827)
XLA Ops:
  0.0 0.8 %pad_add_fusion = s32[8,1]{0,1:T(1,128)S(1)} fusion(s32[4,1]{0,1:T(1,128)} %bitcast.71), kind=kLoop, calls=%fused_computation.76 | loop fusion | flops 8 | bytes 48 | tf_op jit(solution)/shard_map/concatenate | solution.py:239
  0.8 0.7 %fusion.16 = s32[4]{0:T(128)S(1)} fusion(s32[1,1,4]{2,1,0:T(1,128)} %param.15, s32[]{:T(128)S(6)} %axis_index.23), kind=kLoop, calls=%fused_computation.71 | loop fusion | flops 60 | bytes 36 | tf_op jit(solution)/shard_map/select_n | solution.py:261
  1.6 0.9 %convolution_convert_fusion.1 = bf16[4,3]{0,1:T(4,128)(2,1)S(1)} fusion(s32[16,3]{0,1:T(4,128)} %param.12, s32[4]{0:T(128)S(1)} %get-tuple-element.31), kind=kOutput, calls=%fused_computation.7 | convolution fusion | flops 2428 | bytes 232 | tf_op jit(solution)/shard_map/dot_general | solution.py:227
  2.6 0.8 %gather_fusion = bf16[4,32768]{1,0:T(4,128)(2,1)S(1)} fusion(bf16[16,32768]{1,0:T(8,128)(2,1)S(1)} %copy-done, s32[1024]{0:T(1024)S(1)} %get-tuple-element.35), kind=kCustom, calls=%fused_computation | custom fusion | bytes 524304 | tf_op jit(solution)/shard_map/gather | solution.py:243
  3.9 3.1 %collective-permute-start = (bf16[1,32896]{1,0:T(2,128)(2,1)S(1)}, bf16[1,32896]{1,0:T(2,128)(2,1)S(1)}, u32[]{:S(2)}, u32[]{:S(2)}) collective-permute-start(bf16[1,32896]{1,0:T(2,128)(2,1)S(1)} %get-tuple-element.25), channel_id=1, source_target_pairs={{0,8},{8,16},{16,24},{24,0},{1,9},{9,17},{17,25},{25,1},{2,10},{10... | collective-permute-start | bytes 197384 | tf_op jit(solution)/shard_map/ppermute | solution.py:221
  7.0 2.1 %collective-permute-start.2 = (bf16[1,32896]{1,0:T(2,128)(2,1)S(1)}, bf16[1,32896]{1,0:T(2,128)(2,1)S(1)}, u32[]{:S(2)}, u32[]{:S(2)}) collective-permute-start(bf16[1,32896]{1,0:T(2,128)(2,1)S(1)} %get-tuple-element.26), channel_id=1, source_target_pairs={{0,24},{8,0},{16,8},{24,16},{1,25},{9,1},{17,9},{25,17},{2,26},{10... | collective-permute-start | bytes 197384 | tf_op jit(solution)/shard_map/ppermute | solution.py:221
  9.1 0.9 %collective-permute-start.1 = (bf16[1,32896]{1,0:T(2,128)(2,1)S(1)}, bf16[1,32896]{1,0:T(2,128)(2,1)S(1)}, u32[]{:S(2)}, u32[]{:S(2)}) collective-permute-start(bf16[1,32896]{1,0:T(2,128)(2,1)S(1)} %get-tuple-element.27), channel_id=1, source_target_pairs={{0,16},{8,24},{16,0},{24,8},{1,17},{9,25},{17,1},{25,9},{2,18},{10... | collective-permute-start | bytes 197384 | tf_op jit(solution)/shard_map/ppermute | solution.py:221
  11.2 0.6 %gather_fusion.3 = s32[4]{0:T(128)S(1)} fusion(s32[4]{0:T(128)S(1)} %get-tuple-element.31, s32[1024]{0:T(1024)S(1)} %get-tuple-element.32), kind=kCustom, calls=%fused_computation.3 | custom fusion | bytes 48 | tf_op jit(solution)/shard_map/gather | solution.py:285
  11.9 0.6 %reshape.206.rest_0_ = bf16[1,32,1024]{2,1,0:T(8,128)(2,1)} reshape(bf16[32768]{0:T(1024)(128)(2,1)S(1)} %slice_reduce_fusion.3) | data formatting | bytes 131072 | tf_op jit(solution)/shard_map/reshape | solution.py:249
  12.5 0.8 %gather_fusion.2 = bf16[4,32768]{1,0:T(4,128)(2,1)S(1)} fusion(bf16[16,32768]{1,0:T(8,128)(2,1)S(1)} %copy-done, s32[1024]{0:T(1024)S(1)} %get-tuple-element.33), kind=kCustom, calls=%fused_computation.2 | custom fusion | bytes 524304 | tf_op jit(solution)/shard_map/gather | solution.py:260
  13.3 0.8 %copy.33 = bf16[1,4,32,1024]{3,2,1,0:T(8,128)(2,1)} copy(bf16[1,4,32,1024]{3,1,2,0:T(4,128)(2,1)S(1)} %bitcast.62) | data formatting | bytes 524288
  15.1 0.7 %reshape.207.rest_1_ = bf16[1,32,1024]{2,1,0:T(8,128)(2,1)} reshape(bf16[32768]{0:T(1024)(128)(2,1)S(1)} %slice_reduce_fusion.2) | data formatting | bytes 131072 | tf_op jit(solution)/shard_map/reshape | solution.py:249
  15.8 0.7 %reshape.209.rest_3_ = bf16[1,32,1024]{2,1,0:T(8,128)(2,1)} reshape(bf16[32768]{0:T(1024)(128)(2,1)S(1)} %slice_reduce_fusion) | data formatting | bytes 131072 | tf_op jit(solution)/shard_map/reshape | solution.py:249
  16.4 4.5 %collective-permute-done.1 = bf16[1,32896]{1,0:T(2,128)(2,1)S(1)} collective-permute-done((bf16[1,32896]{1,0:T(2,128)(2,1)S(1)}, bf16[1,32896]{1,0:T(2,128)(2,1)S(1)}, u32[]{:S(2)}, u32[]{:S(2)}) %collective-permute-start.1) | collective-permute-done | bytes 65824 | tf_op jit(solution)/shard_map/ppermute | solution.py:221
  21.3 0.7 %reshape.208.rest_2_ = bf16[1,32,1024]{2,1,0:T(8,128)(2,1)} reshape(bf16[32768]{0:T(1024)(128)(2,1)S(1)} %slice_reduce_fusion.1) | data formatting | bytes 131072 | tf_op jit(solution)/shard_map/reshape | solution.py:249
  23.0 0.6 %concatenate.11.meta_ref = s32[29]{0:T(128)} concatenate(s32[12]{0:T(128)S(1)} %reshape.203, s32[4]{0:T(128)S(1)} %compare_convert_fusion, s32[4]{0:T(128)S(1)} %bitcast.69, s32[4]{0:T(128)S(1)} %get-tuple-element.29, s32[1]{0:T(128)} %bitcast.12, s32[4]{0:T(128)S(1)} %get-tuple-element.28), dimensions={0} | concatenate | bytes 232 | tf_op jit(solution)/shard_map/concatenate | solution.py:265
  23.6 6.1 %shard_map.109 = (f32[8,4224]{1,0:T(8,128)}, f32[8,4224]{1,0:T(8,128)}, f32[8,4224]{1,0:T(8,128)}, f32[8,4224]{1,0:T(8,128)}, f32[8,4224]{1,0:T(8,128)}, /*index...) custom-call(s32[29]{0:T(128)} %concatenate.11.meta_ref, bf16[4,32,1024]{2,1,0:T(8,128)(2,1)} %bitcast.61, ...), custom_call_target="tpu_custom_call" | custom-call | tf_op jit(solution)/shard_map/pallas_call | solution.py:201
  29.8 1.5 %collective-permute-start.4 = (f32[8,4224]{1,0:T(8,128)}, f32[8,4224]{1,0:T(8,128)S(1)}, u32[]{:S(2)}, u32[]{:S(2)}) collective-permute-start(f32[8,4224]{1,0:T(8,128)} %get-tuple-element.15), channel_id=1, source_target_pairs={{0,2},{1,3},{2,4},{3,5},{4,6},{5,7},{6,0},{7,1},{8,10},{9,11},{10,... | collective-permute-start | bytes 405512 | tf_op jit(solution)/shard_map/ppermute | solution.py:221
  31.3 2.4 %collective-permute-start.5 = (f32[8,4224]{1,0:T(8,128)}, f32[8,4224]{1,0:T(8,128)S(1)}, u32[]{:S(2)}, u32[]{:S(2)}) collective-permute-start(f32[8,4224]{1,0:T(8,128)} %get-tuple-element.16), channel_id=1, source_target_pairs={{0,3},{1,4},{2,5},{3,6},{4,7},{5,0},{6,1},{7,2},{8,11},{9,12},{10,... | collective-permute-start | bytes 405512 | tf_op jit(solution)/shard_map/ppermute | solution.py:221
  34.3 0.9 %bitcast_dynamic-update-slice_fusion.7 = f32[8,8,4224]{2,1,0:T(8,128)S(1)} fusion(f32[8,4224]{1,0:T(8,128)} %get-tuple-element.13), kind=kLoop, calls=%fused_computation.22 | loop fusion | bytes 270336
  35.2 1.1 %collective-permute-done.3 = f32[8,4224]{1,0:T(8,128)S(1)} collective-permute-done((f32[8,4224]{1,0:T(8,128)}, f32[8,4224]{1,0:T(8,128)S(1)}, u32[]{:S(2)}, u32[]{:S(2)}) %collective-permute-start.3) | collective-permute-done | bytes 135200 | tf_op jit(solution)/shard_map/ppermute | solution.py:221
  36.3 1.5 %collective-permute-start.8 = (f32[8,4224]{1,0:T(8,128)}, f32[8,4224]{1,0:T(8,128)S(1)}, u32[]{:S(2)}, u32[]{:S(2)}) collective-permute-start(f32[8,4224]{1,0:T(8,128)} %get-tuple-element.19), channel_id=1, source_target_pairs={{0,6},{1,7},{2,0},{3,1},{4,2},{5,3},{6,4},{7,5},{8,14},{9,15},{10,... | collective-permute-start | bytes 405512 | tf_op jit(solution)/shard_map/ppermute | solution.py:221
  37.8 2.6 %collective-permute-start.9 = (f32[8,4224]{1,0:T(8,128)}, f32[8,4224]{1,0:T(8,128)S(1)}, u32[]{:S(2)}, u32[]{:S(2)}) collective-permute-start(f32[8,4224]{1,0:T(8,128)} %get-tuple-element.20), channel_id=1, source_target_pairs={{0,7},{1,0},{2,1},{3,2},{4,3},{5,4},{6,5},{7,6},{8,15},{9,8},{10,9... | collective-permute-start | bytes 405512 | tf_op jit(solution)/shard_map/ppermute | solution.py:221
  40.4 2.1 %collective-permute-done.5 = f32[8,4224]{1,0:T(8,128)S(1)} collective-permute-done((f32[8,4224]{1,0:T(8,128)}, f32[8,4224]{1,0:T(8,128)S(1)}, u32[]{:S(2)}, u32[]{:S(2)}) %collective-permute-start.5) | collective-permute-done | bytes 135200 | tf_op jit(solution)/shard_map/ppermute | solution.py:221
  42.7 1.9 %collective-permute-done.7 = f32[8,4224]{1,0:T(8,128)S(1)} collective-permute-done((f32[8,4224]{1,0:T(8,128)}, f32[8,4224]{1,0:T(8,128)S(1)}, u32[]{:S(2)}, u32[]{:S(2)}) %collective-permute-start.7) | collective-permute-done | bytes 135200 | tf_op jit(solution)/shard_map/ppermute | solution.py:221
  44.9 0.8 %convolution_bitcast_fusion = f32[20,4096]{1,0:T(8,128)S(1)} fusion(f32[8,8,4096]{2,1,0:T(8,128)S(1)} %slice.113, s32[8,8]{0,1:T(8,128)S(1)} %bitcast.64), kind=kOutput, calls=%fused_computation.4 | convolution fusion | flops 31458560 | bytes 1376512 | tf_op jit(solution)/shard_map/srk,srl->kl/dot_general | solution.py:280
  45.8 1.7 %collective-permute-start.12 = (f32[1,4096]{1,0:T(1,128)S(1)}, f32[1,4096]{1,0:T(1,128)S(1)}, u32[]{:S(2)}, u32[]{:S(2)}) collective-permute-start(f32[1,4096]{1,0:T(1,128)S(1)} %get-tuple-element.22), channel_id=1, source_target_pairs={{0,24},{8,0},{16,8},{24,16},{1,25},{9,1},{17,9},{25,17},{2,26},{10... | collective-permute-start | bytes 49160 | tf_op jit(solution)/shard_map/ppermute | solution.py:221
  47.5 0.9 %collective-permute-start.10 = (f32[1,4096]{1,0:T(1,128)S(1)}, f32[1,4096]{1,0:T(1,128)S(1)}, u32[]{:S(2)}, u32[]{:S(2)}) collective-permute-start(f32[1,4096]{1,0:T(1,128)S(1)} %get-tuple-element.24), channel_id=1, source_target_pairs={{0,8},{8,16},{16,24},{24,0},{1,9},{9,17},{17,25},{25,1},{2,10},{10... | collective-permute-start | bytes 49160 | tf_op jit(solution)/shard_map/ppermute | solution.py:221
  48.5 1.1 %collective-permute-done.12 = f32[1,4096]{1,0:T(1,128)S(1)} collective-permute-done((f32[1,4096]{1,0:T(1,128)S(1)}, f32[1,4096]{1,0:T(1,128)S(1)}, u32[]{:S(2)}, u32[]{:S(2)}) %collective-permute-start.12) | collective-permute-done | bytes 16416 | tf_op jit(solution)/shard_map/ppermute | solution.py:221
  49.6 2.5 %collective-permute-done.11 = f32[1,4096]{1,0:T(1,128)S(1)} collective-permute-done((f32[1,4096]{1,0:T(1,128)S(1)}, f32[1,4096]{1,0:T(1,128)S(1)}, u32[]{:S(2)}, u32[]{:S(2)}) %collective-permute-start.11) | collective-permute-done | bytes 16416 | tf_op jit(solution)/shard_map/ppermute | solution.py:221
  52.1 0.9 %collective-permute-done.10 = f32[1,4096]{1,0:T(1,128)S(1)} collective-permute-done((f32[1,4096]{1,0:T(1,128)S(1)}, f32[1,4096]{1,0:T(1,128)S(1)}, u32[]{:S(2)}, u32[]{:S(2)}) %collective-permute-start.10) | collective-permute-done | bytes 16416 | tf_op jit(solution)/shard_map/ppermute | solution.py:221
  53.2 0.7 %slice_add_fusion = f32[16,4096]{1,0:T(8,128)} fusion(f32[16,4096]{1,0:T(8,128)S(1)} %select_reduce_fusion, f32[20,4096]{1,0:T(8,128)S(1)} %convolution_bitcast_fusion), kind=kLoop, calls=%fused_computation.14 | loop fusion | flops 65536 | bytes 786432 | tf_op jit(solution)/shard_map/add | solution.py:289
  (56 shorter events, 5.1 us)
Async XLA Ops:
  0.0 2.6 %copy-start = (bf16[16,32768]{1,0:T(8,128)(2,1)S(1)}, bf16[16,32768]{1,0:T(8,128)(2,1)}, u32[]{:S(2)}) copy-start(bf16[16,32768]{1,0:T(8,128)(2,1)} %param.11) | copy-start | bytes 3145732
  3.4 6.6 %copy-start.2 = (s32[1,1,4]{2,1,0:T(1,128)S(1)}, s32[1,1,4]{2,1,0:T(1,128)}, u32[]{:S(2)}) copy-start(s32[1,1,4]{2,1,0:T(1,128)} %param.15) | copy-start | bytes 52
  3.4 7.8 %copy-start.1 = (s32[1,1,4]{2,1,0:T(1,128)S(1)}, s32[1,1,4]{2,1,0:T(1,128)}, u32[]{:S(2)}) copy-start(s32[1,1,4]{2,1,0:T(1,128)} %param.14) | copy-start | bytes 52
  3.9 10.2 %collective-permute-start = (bf16[1,32896]{1,0:T(2,128)(2,1)S(1)}, bf16[1,32896]{1,0:T(2,128)(2,1)S(1)}, u32[]{:S(2)}, u32[]{:S(2)}) collective-permute-start(bf16[1,32896]{1,0:T(2,128)(2,1)S(1)} %get-tuple-element.25), channel_id=1, source_target_pairs={{0,8},{8,16},{16,24},{24,0},{1,9},{9,17},{17,25},{25,1},{2,10},{10... | collective-permute-start | bytes 197384 | tf_op jit(solution)/shard_map/ppermute | solution.py:221
  7.0 7.8 %collective-permute-start.2 = (bf16[1,32896]{1,0:T(2,128)(2,1)S(1)}, bf16[1,32896]{1,0:T(2,128)(2,1)S(1)}, u32[]{:S(2)}, u32[]{:S(2)}) collective-permute-start(bf16[1,32896]{1,0:T(2,128)(2,1)S(1)} %get-tuple-element.26), channel_id=1, source_target_pairs={{0,24},{8,0},{16,8},{24,16},{1,25},{9,1},{17,9},{25,17},{2,26},{10... | collective-permute-start | bytes 197384 | tf_op jit(solution)/shard_map/ppermute | solution.py:221
  9.1 11.9 %collective-permute-start.1 = (bf16[1,32896]{1,0:T(2,128)(2,1)S(1)}, bf16[1,32896]{1,0:T(2,128)(2,1)S(1)}, u32[]{:S(2)}, u32[]{:S(2)}) collective-permute-start(bf16[1,32896]{1,0:T(2,128)(2,1)S(1)} %get-tuple-element.27), channel_id=1, source_target_pairs={{0,16},{8,24},{16,0},{24,8},{1,17},{9,25},{17,1},{25,9},{2,18},{10... | collective-permute-start | bytes 197384 | tf_op jit(solution)/shard_map/ppermute | solution.py:221
  13.3 9.4 %copy-start.3 = (s32[16,3]{0,1:T(4,128)S(1)}, s32[16,3]{0,1:T(4,128)}, u32[]{:S(2)}) copy-start(s32[16,3]{0,1:T(4,128)} %param.12) | copy-start | bytes 580
  29.8 6.5 %collective-permute-start.3 = (f32[8,4224]{1,0:T(8,128)}, f32[8,4224]{1,0:T(8,128)S(1)}, u32[]{:S(2)}, u32[]{:S(2)}) collective-permute-start(f32[8,4224]{1,0:T(8,128)} %get-tuple-element.14), channel_id=1, source_target_pairs={{0,1},{1,2},{2,3},{3,4},{4,5},{5,6},{6,7},{7,0},{8,9},{9,10},{10,1... | collective-permute-start | bytes 405512 | tf_op jit(solution)/shard_map/ppermute | solution.py:221
  29.8 8.0 %collective-permute-start.4 = (f32[8,4224]{1,0:T(8,128)}, f32[8,4224]{1,0:T(8,128)S(1)}, u32[]{:S(2)}, u32[]{:S(2)}) collective-permute-start(f32[8,4224]{1,0:T(8,128)} %get-tuple-element.15), channel_id=1, source_target_pairs={{0,2},{1,3},{2,4},{3,5},{4,6},{5,7},{6,0},{7,1},{8,10},{9,11},{10,... | collective-permute-start | bytes 405512 | tf_op jit(solution)/shard_map/ppermute | solution.py:221
  31.3 11.1 %collective-permute-start.5 = (f32[8,4224]{1,0:T(8,128)}, f32[8,4224]{1,0:T(8,128)S(1)}, u32[]{:S(2)}, u32[]{:S(2)}) collective-permute-start(f32[8,4224]{1,0:T(8,128)} %get-tuple-element.16), channel_id=1, source_target_pairs={{0,3},{1,4},{2,5},{3,6},{4,7},{5,0},{6,1},{7,2},{8,11},{9,12},{10,... | collective-permute-start | bytes 405512 | tf_op jit(solution)/shard_map/ppermute | solution.py:221
  33.7 9.0 %collective-permute-start.6 = (f32[8,4224]{1,0:T(8,128)}, f32[8,4224]{1,0:T(8,128)S(1)}, u32[]{:S(2)}, u32[]{:S(2)}) collective-permute-start(f32[8,4224]{1,0:T(8,128)} %get-tuple-element.17), channel_id=1, source_target_pairs={{0,4},{1,5},{2,6},{3,7},{4,0},{5,1},{6,2},{7,3},{8,12},{9,13},{10,... | collective-permute-start | bytes 405512 | tf_op jit(solution)/shard_map/ppermute | solution.py:221
  34.2 10.4 %collective-permute-start.7 = (f32[8,4224]{1,0:T(8,128)}, f32[8,4224]{1,0:T(8,128)S(1)}, u32[]{:S(2)}, u32[]{:S(2)}) collective-permute-start(f32[8,4224]{1,0:T(8,128)} %get-tuple-element.18), channel_id=1, source_target_pairs={{0,5},{1,6},{2,7},{3,0},{4,1},{5,2},{6,3},{7,4},{8,13},{9,14},{10,... | collective-permute-start | bytes 405512 | tf_op jit(solution)/shard_map/ppermute | solution.py:221
  36.3 8.3 %collective-permute-start.8 = (f32[8,4224]{1,0:T(8,128)}, f32[8,4224]{1,0:T(8,128)S(1)}, u32[]{:S(2)}, u32[]{:S(2)}) collective-permute-start(f32[8,4224]{1,0:T(8,128)} %get-tuple-element.19), channel_id=1, source_target_pairs={{0,6},{1,7},{2,0},{3,1},{4,2},{5,3},{6,4},{7,5},{8,14},{9,15},{10,... | collective-permute-start | bytes 405512 | tf_op jit(solution)/shard_map/ppermute | solution.py:221
  37.8 6.9 %collective-permute-start.9 = (f32[8,4224]{1,0:T(8,128)}, f32[8,4224]{1,0:T(8,128)S(1)}, u32[]{:S(2)}, u32[]{:S(2)}) collective-permute-start(f32[8,4224]{1,0:T(8,128)} %get-tuple-element.20), channel_id=1, source_target_pairs={{0,7},{1,0},{2,1},{3,2},{4,3},{5,4},{6,5},{7,6},{8,15},{9,8},{10,9... | collective-permute-start | bytes 405512 | tf_op jit(solution)/shard_map/ppermute | solution.py:221
  45.8 3.8 %collective-permute-start.12 = (f32[1,4096]{1,0:T(1,128)S(1)}, f32[1,4096]{1,0:T(1,128)S(1)}, u32[]{:S(2)}, u32[]{:S(2)}) collective-permute-start(f32[1,4096]{1,0:T(1,128)S(1)} %get-tuple-element.22), channel_id=1, source_target_pairs={{0,24},{8,0},{16,8},{24,16},{1,25},{9,1},{17,9},{25,17},{2,26},{10... | collective-permute-start | bytes 49160 | tf_op jit(solution)/shard_map/ppermute | solution.py:221
  47.5 4.7 %collective-permute-start.11 = (f32[1,4096]{1,0:T(1,128)S(1)}, f32[1,4096]{1,0:T(1,128)S(1)}, u32[]{:S(2)}, u32[]{:S(2)}) collective-permute-start(f32[1,4096]{1,0:T(1,128)S(1)} %get-tuple-element.23), channel_id=1, source_target_pairs={{0,16},{8,24},{16,0},{24,8},{1,17},{9,25},{17,1},{25,9},{2,18},{10... | collective-permute-start | bytes 49160 | tf_op jit(solution)/shard_map/ppermute | solution.py:221
  47.5 5.5 %collective-permute-start.10 = (f32[1,4096]{1,0:T(1,128)S(1)}, f32[1,4096]{1,0:T(1,128)S(1)}, u32[]{:S(2)}, u32[]{:S(2)}) collective-permute-start(f32[1,4096]{1,0:T(1,128)S(1)} %get-tuple-element.24), channel_id=1, source_target_pairs={{0,8},{8,16},{16,24},{24,0},{1,9},{9,17},{17,25},{25,1},{2,10},{10... | collective-permute-start | bytes 49160 | tf_op jit(solution)/shard_map/ppermute | solution.py:221

commit v16 on v12

--- a/solution.py
+++ b/solution.py
@@ -38,7 +38,7 @@
     rows_low = (rows - rows_high.astype(np.float32)).astype(ml_dtypes.bfloat16)
     single = (np.float32(2.0) - np.float32(2.0) * np.cos(np.float32(np.pi) * grid / np.float32(B + 1.0))).astype(np.float32)
     eigen = (single[:, None, None] + single[None, :, None] + single[None, None, :]).reshape(B, PLANE)
-    return tiled, spread, rows_high, rows_low, eigen.astype(np.float32)
+    return tiled, spread, rows_high, rows_low, (np.float32(1.0) / eigen).astype(np.float32)
 
 
 def split(values):
@@ -167,7 +167,7 @@
     coef = dot3_left(rows_high, rows_low, dot3(work_ref[...], kron_high, kron_low))
     eigen = eigen_ref[...]
     for slot in range(slots):
-        work_ref[slot * B : (slot + 1) * B, :] = coef[slot * B : (slot + 1) * B, :] / eigen
+        work_ref[slot * B : (slot + 1) * B, :] = coef[slot * B : (slot + 1) * B, :] * eigen
     potential = dot3_left(rows_high, rows_low, dot3(work_ref[...], kron_high, kron_low))
 
     for slot in range(slots):

time: 53.7 us -> 53.7 us (level)
  no operation moved by 1% of the time
where the time goes in v16:
time: 53.7 us; the launch traced here: 53.6 us
  starting transfers between devices  17.3 us (32%)
  waiting for transfers between devices  14.6 us (27%)
  local copies, waits for them, and re-layouts  10.5 us (20%)
  Pallas kernels  6.12 us (11%)
  matrix products  2.96 us (6%)
  other arithmetic  1.17 us (2%)
  between operations  0.88 us (2%)
    ppermute x13, starting transfers between devices, exchange(): received.append(lax.ppermute(blocks[step], axis, pairs))  17.3 us
    ppermute x13, waiting for transfers between devices, exchange(): received.append(lax.ppermute(blocks[step], axis, pairs))  14.6 us
    pallas_call x1, Pallas kernels, pair_fields(): pl.pallas_call(functools.partial(pair_kernel, count, len(boxes)), out_sha...  6.12 us
    reshape x4, local copies, waits for them, and re-layouts, per_device(): block[:, :cell_count].reshape(per_target, B, PLANE)  2.62 us
    unnamed x17, local copies, waits for them, and re-layouts  1.89 us
    slice x4, local copies, waits for them, and re-layouts, per_device(): block[:, :cell_count].reshape(per_target, B, PLANE)  1.48 us
    dot_general x1, matrix products, per_device(): jnp.dot(chooser.T, returned, precision=lax.Precision.HIGH)  1.07 us
  transfers between devices with their start and end apart: 13, of which 9 were waited for; matrix products, arithmetic and copies ran while one was open for 12% of the time, Pallas kernels for 0%

profile of v16, /device:TPU:0, one launch (start us, length us, event | category | flops | bytes accessed | tf_op | source)
XLA Modules:
  0.0 53.6 jit_solution(204656275292377133)
XLA Ops:
  0.0 0.8 %pad_add_fusion = s32[8,1]{0,1:T(1,128)S(1)} fusion(s32[4,1]{0,1:T(1,128)} %bitcast.72), kind=kLoop, calls=%fused_computation.77 | loop fusion | flops 8 | bytes 48 | tf_op jit(solution)/shard_map/concatenate | solution.py:239
  0.9 0.9 %convolution_convert_fusion.1 = bf16[4,3]{0,1:T(4,128)(2,1)S(1)} fusion(s32[16,3]{0,1:T(4,128)} %param.12, s32[4]{0:T(128)S(1)} %get-tuple-element.31), kind=kOutput, calls=%fused_computation.8 | convolution fusion | flops 2428 | bytes 232 | tf_op jit(solution)/shard_map/dot_general | solution.py:227
  1.9 0.8 %gather_fusion = bf16[4,32768]{1,0:T(4,128)(2,1)S(1)} fusion(bf16[16,32768]{1,0:T(8,128)(2,1)S(1)} %copy-done, s32[1024]{0:T(1024)S(1)} %pad_clamp_fusion.3), kind=kCustom, calls=%fused_computation | custom fusion | bytes 524304 | tf_op jit(solution)/shard_map/gather | solution.py:243
  3.2 3.1 %collective-permute-start = (bf16[1,32896]{1,0:T(2,128)(2,1)S(1)}, bf16[1,32896]{1,0:T(2,128)(2,1)S(1)}, u32[]{:S(2)}, u32[]{:S(2)}) collective-permute-start(bf16[1,32896]{1,0:T(2,128)(2,1)S(1)} %get-tuple-element.25), channel_id=1, source_target_pairs={{0,8},{8,16},{16,24},{24,0},{1,9},{9,17},{17,25},{25,1},{2,10},{10... | collective-permute-start | bytes 197384 | tf_op jit(solution)/shard_map/ppermute | solution.py:221
  6.3 2.1 %collective-permute-start.2 = (bf16[1,32896]{1,0:T(2,128)(2,1)S(1)}, bf16[1,32896]{1,0:T(2,128)(2,1)S(1)}, u32[]{:S(2)}, u32[]{:S(2)}) collective-permute-start(bf16[1,32896]{1,0:T(2,128)(2,1)S(1)} %get-tuple-element.26), channel_id=1, source_target_pairs={{0,24},{8,0},{16,8},{24,16},{1,25},{9,1},{17,9},{25,17},{2,26},{10... | collective-permute-start | bytes 197384 | tf_op jit(solution)/shard_map/ppermute | solution.py:221
  8.4 0.9 %collective-permute-start.1 = (bf16[1,32896]{1,0:T(2,128)(2,1)S(1)}, bf16[1,32896]{1,0:T(2,128)(2,1)S(1)}, u32[]{:S(2)}, u32[]{:S(2)}) collective-permute-start(bf16[1,32896]{1,0:T(2,128)(2,1)S(1)} %get-tuple-element.27), channel_id=1, source_target_pairs={{0,16},{8,24},{16,0},{24,8},{1,17},{9,25},{17,1},{25,9},{2,18},{10... | collective-permute-start | bytes 197384 | tf_op jit(solution)/shard_map/ppermute | solution.py:221
  10.6 0.7 %reshape.186.rest_0_ = bf16[1,32,1024]{2,1,0:T(8,128)(2,1)} reshape(bf16[32768]{0:T(1024)(128)(2,1)S(1)} %slice_reduce_fusion.3) | data formatting | bytes 131072 | tf_op jit(solution)/shard_map/reshape | solution.py:249
  11.2 0.8 %gather_fusion.2 = bf16[4,32768]{1,0:T(4,128)(2,1)S(1)} fusion(bf16[16,32768]{1,0:T(8,128)(2,1)S(1)} %copy-done, s32[1024]{0:T(1024)S(1)} %get-tuple-element.32), kind=kCustom, calls=%fused_computation.2 | custom fusion | bytes 524304 | tf_op jit(solution)/shard_map/gather | solution.py:260
  12.0 0.8 %copy.33 = bf16[1,4,32,1024]{3,2,1,0:T(8,128)(2,1)} copy(bf16[1,4,32,1024]{3,1,2,0:T(4,128)(2,1)S(1)} %bitcast.63) | data formatting | bytes 524288
  13.2 0.9 %collective-permute-done.2 = bf16[1,32896]{1,0:T(2,128)(2,1)S(1)} collective-permute-done((bf16[1,32896]{1,0:T(2,128)(2,1)S(1)}, bf16[1,32896]{1,0:T(2,128)(2,1)S(1)}, u32[]{:S(2)}, u32[]{:S(2)}) %collective-permute-start.2) | collective-permute-done | bytes 65824 | tf_op jit(solution)/shard_map/ppermute | solution.py:221
  14.5 0.7 %reshape.187.rest_1_ = bf16[1,32,1024]{2,1,0:T(8,128)(2,1)} reshape(bf16[32768]{0:T(1024)(128)(2,1)S(1)} %slice_reduce_fusion.2) | data formatting | bytes 131072 | tf_op jit(solution)/shard_map/reshape | solution.py:249
  15.1 0.7 %reshape.189.rest_3_ = bf16[1,32,1024]{2,1,0:T(8,128)(2,1)} reshape(bf16[32768]{0:T(1024)(128)(2,1)S(1)} %slice_reduce_fusion) | data formatting | bytes 131072 | tf_op jit(solution)/shard_map/reshape | solution.py:249
  15.8 4.5 %collective-permute-done.1 = bf16[1,32896]{1,0:T(2,128)(2,1)S(1)} collective-permute-done((bf16[1,32896]{1,0:T(2,128)(2,1)S(1)}, bf16[1,32896]{1,0:T(2,128)(2,1)S(1)}, u32[]{:S(2)}, u32[]{:S(2)}) %collective-permute-start.1) | collective-permute-done | bytes 65824 | tf_op jit(solution)/shard_map/ppermute | solution.py:221
  20.7 0.7 %reshape.188.rest_2_ = bf16[1,32,1024]{2,1,0:T(8,128)(2,1)} reshape(bf16[32768]{0:T(1024)(128)(2,1)S(1)} %slice_reduce_fusion.1) | data formatting | bytes 131072 | tf_op jit(solution)/shard_map/reshape | solution.py:249
  21.3 0.6 %gather_fusion.1 = s32[4,3]{1,0:T(4,128)S(1)} fusion(s32[4,3]{1,0:T(4,128)S(1)} %bitcast.64, s32[1024]{0:T(1024)S(1)} %get-tuple-element.33), kind=kCustom, calls=%fused_computation.1 | custom fusion | bytes 112 | tf_op jit(solution)/shard_map/gather | solution.py:261
  22.4 0.7 %concatenate.11.meta_ref = s32[29]{0:T(128)} concatenate(s32[12]{0:T(128)S(1)} %reshape.183, s32[4]{0:T(128)S(1)} %compare_convert_fusion, s32[4]{0:T(128)S(1)} %bitcast.70, s32[4]{0:T(128)S(1)} %get-tuple-element.29, s32[1]{0:T(128)} %bitcast.12, s32[4]{0:T(128)S(1)} %get-tuple-element.28), dimensions={0} | concatenate | bytes 232 | tf_op jit(solution)/shard_map/concatenate | solution.py:265
  23.1 6.1 %shard_map.109 = (f32[8,4224]{1,0:T(8,128)}, f32[8,4224]{1,0:T(8,128)}, f32[8,4224]{1,0:T(8,128)}, f32[8,4224]{1,0:T(8,128)}, f32[8,4224]{1,0:T(8,128)}, /*index...) custom-call(s32[29]{0:T(128)} %concatenate.11.meta_ref, bf16[4,32,1024]{2,1,0:T(8,128)(2,1)} %bitcast.62, ...), custom_call_target="tpu_custom_call" | custom-call | tf_op jit(solution)/shard_map/pallas_call | solution.py:201
  29.2 1.5 %collective-permute-start.4 = (f32[8,4224]{1,0:T(8,128)}, f32[8,4224]{1,0:T(8,128)S(1)}, u32[]{:S(2)}, u32[]{:S(2)}) collective-permute-start(f32[8,4224]{1,0:T(8,128)} %get-tuple-element.15), channel_id=1, source_target_pairs={{0,2},{1,3},{2,4},{3,5},{4,6},{5,7},{6,0},{7,1},{8,10},{9,11},{10,... | collective-permute-start | bytes 405512 | tf_op jit(solution)/shard_map/ppermute | solution.py:221
  30.7 2.4 %collective-permute-start.5 = (f32[8,4224]{1,0:T(8,128)}, f32[8,4224]{1,0:T(8,128)S(1)}, u32[]{:S(2)}, u32[]{:S(2)}) collective-permute-start(f32[8,4224]{1,0:T(8,128)} %get-tuple-element.16), channel_id=1, source_target_pairs={{0,3},{1,4},{2,5},{3,6},{4,7},{5,0},{6,1},{7,2},{8,11},{9,12},{10,... | collective-permute-start | bytes 405512 | tf_op jit(solution)/shard_map/ppermute | solution.py:221
  33.7 0.9 %bitcast_dynamic-update-slice_fusion.7 = f32[8,8,4224]{2,1,0:T(8,128)S(1)} fusion(f32[8,4224]{1,0:T(8,128)} %get-tuple-element.13), kind=kLoop, calls=%fused_computation.21 | loop fusion | bytes 270336
  34.6 1.0 %collective-permute-done.3 = f32[8,4224]{1,0:T(8,128)S(1)} collective-permute-done((f32[8,4224]{1,0:T(8,128)}, f32[8,4224]{1,0:T(8,128)S(1)}, u32[]{:S(2)}, u32[]{:S(2)}) %collective-permute-start.3) | collective-permute-done | bytes 135200 | tf_op jit(solution)/shard_map/ppermute | solution.py:221
  35.7 1.5 %collective-permute-start.8 = (f32[8,4224]{1,0:T(8,128)}, f32[8,4224]{1,0:T(8,128)S(1)}, u32[]{:S(2)}, u32[]{:S(2)}) collective-permute-start(f32[8,4224]{1,0:T(8,128)} %get-tuple-element.19), channel_id=1, source_target_pairs={{0,6},{1,7},{2,0},{3,1},{4,2},{5,3},{6,4},{7,5},{8,14},{9,15},{10,... | collective-permute-start | bytes 405512 | tf_op jit(solution)/shard_map/ppermute | solution.py:221
  37.2 2.6 %collective-permute-start.9 = (f32[8,4224]{1,0:T(8,128)}, f32[8,4224]{1,0:T(8,128)S(1)}, u32[]{:S(2)}, u32[]{:S(2)}) collective-permute-start(f32[8,4224]{1,0:T(8,128)} %get-tuple-element.20), channel_id=1, source_target_pairs={{0,7},{1,0},{2,1},{3,2},{4,3},{5,4},{6,5},{7,6},{8,15},{9,8},{10,9... | collective-permute-start | bytes 405512 | tf_op jit(solution)/shard_map/ppermute | solution.py:221
  39.8 2.1 %collective-permute-done.5 = f32[8,4224]{1,0:T(8,128)S(1)} collective-permute-done((f32[8,4224]{1,0:T(8,128)}, f32[8,4224]{1,0:T(8,128)S(1)}, u32[]{:S(2)}, u32[]{:S(2)}) %collective-permute-start.5) | collective-permute-done | bytes 135200 | tf_op jit(solution)/shard_map/ppermute | solution.py:221
  42.1 1.9 %collective-permute-done.7 = f32[8,4224]{1,0:T(8,128)S(1)} collective-permute-done((f32[8,4224]{1,0:T(8,128)}, f32[8,4224]{1,0:T(8,128)S(1)}, u32[]{:S(2)}, u32[]{:S(2)}) %collective-permute-start.7) | collective-permute-done | bytes 135200 | tf_op jit(solution)/shard_map/ppermute | solution.py:221
  44.3 0.8 %convolution_bitcast_fusion = f32[20,4096]{1,0:T(8,128)S(1)} fusion(f32[8,8,4096]{2,1,0:T(8,128)S(1)} %slice.113, s32[8,8]{0,1:T(8,128)S(1)} %bitcast.65), kind=kOutput, calls=%fused_computation.4 | convolution fusion | flops 31458560 | bytes 1376512 | tf_op jit(solution)/shard_map/srk,srl->kl/dot_general | solution.py:280
  45.2 1.7 %collective-permute-start.12 = (f32[1,4096]{1,0:T(1,128)S(1)}, f32[1,4096]{1,0:T(1,128)S(1)}, u32[]{:S(2)}, u32[]{:S(2)}) collective-permute-start(f32[1,4096]{1,0:T(1,128)S(1)} %get-tuple-element.22), channel_id=1, source_target_pairs={{0,24},{8,0},{16,8},{24,16},{1,25},{9,1},{17,9},{25,17},{2,26},{10... | collective-permute-start | bytes 49160 | tf_op jit(solution)/shard_map/ppermute | solution.py:221
  46.9 0.9 %collective-permute-start.10 = (f32[1,4096]{1,0:T(1,128)S(1)}, f32[1,4096]{1,0:T(1,128)S(1)}, u32[]{:S(2)}, u32[]{:S(2)}) collective-permute-start(f32[1,4096]{1,0:T(1,128)S(1)} %get-tuple-element.24), channel_id=1, source_target_pairs={{0,8},{8,16},{16,24},{24,0},{1,9},{9,17},{17,25},{25,1},{2,10},{10... | collective-permute-start | bytes 49160 | tf_op jit(solution)/shard_map/ppermute | solution.py:221
  47.8 0.6 %gather_fusion.3 = s32[4]{0:T(128)S(1)} fusion(s32[4]{0:T(128)S(1)} %get-tuple-element.31, s32[1024]{0:T(1024)S(1)} %pad_clamp_fusion), kind=kCustom, calls=%fused_computation.3 | custom fusion | bytes 48 | tf_op jit(solution)/shard_map/gather | solution.py:285
  49.0 2.5 %collective-permute-done.11 = f32[1,4096]{1,0:T(1,128)S(1)} collective-permute-done((f32[1,4096]{1,0:T(1,128)S(1)}, f32[1,4096]{1,0:T(1,128)S(1)}, u32[]{:S(2)}, u32[]{:S(2)}) %collective-permute-start.11) | collective-permute-done | bytes 16416 | tf_op jit(solution)/shard_map/ppermute | solution.py:221
  51.5 0.9 %collective-permute-done.10 = f32[1,4096]{1,0:T(1,128)S(1)} collective-permute-done((f32[1,4096]{1,0:T(1,128)S(1)}, f32[1,4096]{1,0:T(1,128)S(1)}, u32[]{:S(2)}, u32[]{:S(2)}) %collective-permute-start.10) | collective-permute-done | bytes 16416 | tf_op jit(solution)/shard_map/ppermute | solution.py:221
  52.5 1.1 %convolution_add_fusion = f32[16,4096]{1,0:T(8,128)} fusion(f32[20,4096]{1,0:T(8,128)S(1)} %convolution_bitcast_fusion, f32[4,1,4096]{2,1,0:T(1,128)S(1)} %pad_maximum_fusion, s32[4]{0:T(128)S(1)} %gather_fusion.3), kind=kOutput, calls=%fused_computation.5 | convolution fusion | flops 1638464 | bytes 589840 | tf_op jit(solution)/shard_map/dot_general | solution.py:289
  (55 shorter events, 4.6 us)
Async XLA Ops:
  0.0 1.9 %copy-start = (bf16[16,32768]{1,0:T(8,128)(2,1)S(1)}, bf16[16,32768]{1,0:T(8,128)(2,1)}, u32[]{:S(2)}) copy-start(bf16[16,32768]{1,0:T(8,128)(2,1)} %param.11) | copy-start | bytes 3145732
  2.7 6.6 %copy-start.2 = (s32[1,1,4]{2,1,0:T(1,128)S(1)}, s32[1,1,4]{2,1,0:T(1,128)}, u32[]{:S(2)}) copy-start(s32[1,1,4]{2,1,0:T(1,128)} %param.15) | copy-start | bytes 52
  2.7 7.8 %copy-start.1 = (s32[1,1,4]{2,1,0:T(1,128)S(1)}, s32[1,1,4]{2,1,0:T(1,128)}, u32[]{:S(2)}) copy-start(s32[1,1,4]{2,1,0:T(1,128)} %param.14) | copy-start | bytes 52
  3.2 9.6 %collective-permute-start = (bf16[1,32896]{1,0:T(2,128)(2,1)S(1)}, bf16[1,32896]{1,0:T(2,128)(2,1)S(1)}, u32[]{:S(2)}, u32[]{:S(2)}) collective-permute-start(bf16[1,32896]{1,0:T(2,128)(2,1)S(1)} %get-tuple-element.25), channel_id=1, source_target_pairs={{0,8},{8,16},{16,24},{24,0},{1,9},{9,17},{17,25},{25,1},{2,10},{10... | collective-permute-start | bytes 197384 | tf_op jit(solution)/shard_map/ppermute | solution.py:221
  6.3 7.8 %collective-permute-start.2 = (bf16[1,32896]{1,0:T(2,128)(2,1)S(1)}, bf16[1,32896]{1,0:T(2,128)(2,1)S(1)}, u32[]{:S(2)}, u32[]{:S(2)}) collective-permute-start(bf16[1,32896]{1,0:T(2,128)(2,1)S(1)} %get-tuple-element.26), channel_id=1, source_target_pairs={{0,24},{8,0},{16,8},{24,16},{1,25},{9,1},{17,9},{25,17},{2,26},{10... | collective-permute-start | bytes 197384 | tf_op jit(solution)/shard_map/ppermute | solution.py:221
  8.4 11.9 %collective-permute-start.1 = (bf16[1,32896]{1,0:T(2,128)(2,1)S(1)}, bf16[1,32896]{1,0:T(2,128)(2,1)S(1)}, u32[]{:S(2)}, u32[]{:S(2)}) collective-permute-start(bf16[1,32896]{1,0:T(2,128)(2,1)S(1)} %get-tuple-element.27), channel_id=1, source_target_pairs={{0,16},{8,24},{16,0},{24,8},{1,17},{9,25},{17,1},{25,9},{2,18},{10... | collective-permute-start | bytes 197384 | tf_op jit(solution)/shard_map/ppermute | solution.py:221
  12.0 10.0 %copy-start.3 = (s32[16,3]{0,1:T(4,128)S(1)}, s32[16,3]{0,1:T(4,128)}, u32[]{:S(2)}) copy-start(s32[16,3]{0,1:T(4,128)} %param.12) | copy-start | bytes 580
  29.2 6.5 %collective-permute-start.3 = (f32[8,4224]{1,0:T(8,128)}, f32[8,4224]{1,0:T(8,128)S(1)}, u32[]{:S(2)}, u32[]{:S(2)}) collective-permute-start(f32[8,4224]{1,0:T(8,128)} %get-tuple-element.14), channel_id=1, source_target_pairs={{0,1},{1,2},{2,3},{3,4},{4,5},{5,6},{6,7},{7,0},{8,9},{9,10},{10,1... | collective-permute-start | bytes 405512 | tf_op jit(solution)/shard_map/ppermute | solution.py:221
  29.2 8.0 %collective-permute-start.4 = (f32[8,4224]{1,0:T(8,128)}, f32[8,4224]{1,0:T(8,128)S(1)}, u32[]{:S(2)}, u32[]{:S(2)}) collective-permute-start(f32[8,4224]{1,0:T(8,128)} %get-tuple-element.15), channel_id=1, source_target_pairs={{0,2},{1,3},{2,4},{3,5},{4,6},{5,7},{6,0},{7,1},{8,10},{9,11},{10,... | collective-permute-start | bytes 405512 | tf_op jit(solution)/shard_map/ppermute | solution.py:221
  30.7 11.1 %collective-permute-start.5 = (f32[8,4224]{1,0:T(8,128)}, f32[8,4224]{1,0:T(8,128)S(1)}, u32[]{:S(2)}, u32[]{:S(2)}) collective-permute-start(f32[8,4224]{1,0:T(8,128)} %get-tuple-element.16), channel_id=1, source_target_pairs={{0,3},{1,4},{2,5},{3,6},{4,7},{5,0},{6,1},{7,2},{8,11},{9,12},{10,... | collective-permute-start | bytes 405512 | tf_op jit(solution)/shard_map/ppermute | solution.py:221
  33.1 9.0 %collective-permute-start.6 = (f32[8,4224]{1,0:T(8,128)}, f32[8,4224]{1,0:T(8,128)S(1)}, u32[]{:S(2)}, u32[]{:S(2)}) collective-permute-start(f32[8,4224]{1,0:T(8,128)} %get-tuple-element.17), channel_id=1, source_target_pairs={{0,4},{1,5},{2,6},{3,7},{4,0},{5,1},{6,2},{7,3},{8,12},{9,13},{10,... | collective-permute-start | bytes 405512 | tf_op jit(solution)/shard_map/ppermute | solution.py:221
  33.6 10.4 %collective-permute-start.7 = (f32[8,4224]{1,0:T(8,128)}, f32[8,4224]{1,0:T(8,128)S(1)}, u32[]{:S(2)}, u32[]{:S(2)}) collective-permute-start(f32[8,4224]{1,0:T(8,128)} %get-tuple-element.18), channel_id=1, source_target_pairs={{0,5},{1,6},{2,7},{3,0},{4,1},{5,2},{6,3},{7,4},{8,13},{9,14},{10,... | collective-permute-start | bytes 405512 | tf_op jit(solution)/shard_map/ppermute | solution.py:221
  35.7 8.3 %collective-permute-start.8 = (f32[8,4224]{1,0:T(8,128)}, f32[8,4224]{1,0:T(8,128)S(1)}, u32[]{:S(2)}, u32[]{:S(2)}) collective-permute-start(f32[8,4224]{1,0:T(8,128)} %get-tuple-element.19), channel_id=1, source_target_pairs={{0,6},{1,7},{2,0},{3,1},{4,2},{5,3},{6,4},{7,5},{8,14},{9,15},{10,... | collective-permute-start | bytes 405512 | tf_op jit(solution)/shard_map/ppermute | solution.py:221
  37.2 6.9 %collective-permute-start.9 = (f32[8,4224]{1,0:T(8,128)}, f32[8,4224]{1,0:T(8,128)S(1)}, u32[]{:S(2)}, u32[]{:S(2)}) collective-permute-start(f32[8,4224]{1,0:T(8,128)} %get-tuple-element.20), channel_id=1, source_target_pairs={{0,7},{1,0},{2,1},{3,2},{4,3},{5,4},{6,5},{7,6},{8,15},{9,8},{10,9... | collective-permute-start | bytes 405512 | tf_op jit(solution)/shard_map/ppermute | solution.py:221
  45.2 3.8 %collective-permute-start.12 = (f32[1,4096]{1,0:T(1,128)S(1)}, f32[1,4096]{1,0:T(1,128)S(1)}, u32[]{:S(2)}, u32[]{:S(2)}) collective-permute-start(f32[1,4096]{1,0:T(1,128)S(1)} %get-tuple-element.22), channel_id=1, source_target_pairs={{0,24},{8,0},{16,8},{24,16},{1,25},{9,1},{17,9},{25,17},{2,26},{10... | collective-permute-start | bytes 49160 | tf_op jit(solution)/shard_map/ppermute | solution.py:221
  46.9 4.6 %collective-permute-start.11 = (f32[1,4096]{1,0:T(1,128)S(1)}, f32[1,4096]{1,0:T(1,128)S(1)}, u32[]{:S(2)}, u32[]{:S(2)}) collective-permute-start(f32[1,4096]{1,0:T(1,128)S(1)} %get-tuple-element.23), channel_id=1, source_target_pairs={{0,16},{8,24},{16,0},{24,8},{1,17},{9,25},{17,1},{25,9},{2,18},{10... | collective-permute-start | bytes 49160 | tf_op jit(solution)/shard_map/ppermute | solution.py:221
  46.9 5.5 %collective-permute-start.10 = (f32[1,4096]{1,0:T(1,128)S(1)}, f32[1,4096]{1,0:T(1,128)S(1)}, u32[]{:S(2)}, u32[]{:S(2)}) collective-permute-start(f32[1,4096]{1,0:T(1,128)S(1)} %get-tuple-element.24), channel_id=1, source_target_pairs={{0,8},{8,16},{16,24},{24,0},{1,9},{9,17},{17,25},{25,1},{2,10},{10... | collective-permute-start | bytes 49160 | tf_op jit(solution)/shard_map/ppermute | solution.py:221

commit v17 on v12

--- a/solution.py
+++ b/solution.py
@@ -146,9 +146,11 @@
         d_c = meta_ref[3 * slot + 2]
         visit = meta_ref[6 * slots + 1 + slot]
         per_box = box_refs[0].shape[0]
-        part = box_refs[0][0]
+        part = box_refs[0][0, 0:B, :]
         for index in range(1, len(box_refs) * per_box):
-            part = jnp.where(visit == index, box_refs[index // per_box][index % per_box], part)
+            part = jnp.where(
+                visit == index, box_refs[index // per_box][index % per_box, 0:B, :], part
+            )
         pick = (col == row + d_a).astype(jnp.bfloat16)
         moved = jnp.dot(pick, part, preferred_element_type=jnp.float32)
         step = d_b * B + d_c
@@ -240,16 +242,17 @@
     flat_chosen = chosen.reshape(-1)
     outgoing = jnp.concatenate(
         [
-            orbitals[flat_chosen],
-            jnp.pad(pick_rows(flat_chosen, offsets).astype(jnp.bfloat16), ((0, 0), (0, extra - 3))),
+            orbitals[flat_chosen].reshape(slot_total, B, PLANE),
+            jnp.pad(
+                pick_rows(flat_chosen, offsets).astype(jnp.bfloat16), ((0, 0), (0, PLANE - 3))
+            )[:, None, :],
         ],
         axis=1,
-    ).reshape(section_total, per_target, cell_count + extra)
-    arrived = exchange(outgoing, "home")
-    visitors = [block[:, :cell_count].reshape(per_target, B, PLANE) for block in arrived]
-    visit_offsets = jnp.stack(
-        [block[:, cell_count : cell_count + 3] for block in arrived]
-    ).reshape(slot_total, 3).astype(jnp.int32)
+    ).reshape(section_total, per_target, B + 1, PLANE)
+    visitors = exchange(outgoing, "home")
+    visit_offsets = jnp.stack([block[:, B, 0:3] for block in visitors]).reshape(
+        slot_total, 3
+    ).astype(jnp.int32)
 
     home_slot = pair_home[0, 0]
     visit_code = pair_visit[0, 0]

time: 53.7 us -> 49 us (0.912)
  local copies, waits for them, and re-layouts: 10.5 us -> 6.63 us
  waiting for transfers between devices: 14.7 us -> 12.3 us
  starting transfers between devices: 17.3 us -> 18.8 us
    reshape x4 -> x0, local copies, waits for them, and re-layouts: 2.62 us -> none  [per_device(): block[:, :cell_count].reshape(per_target, B, PLANE)]
    ppermute x13, waiting for transfers between devices: 14.7 us -> 12.3 us  [exchange(): received.append(lax.ppermute(blocks[step], axis, pairs))]
    slice x6 -> x4, local copies, waits for them, and re-layouts: 1.94 us -> 0.01 us  [per_device(): block[:, B, 0:3]]
    ppermute x13, starting transfers between devices: 17.3 us -> 18.8 us  [exchange(): received.append(lax.ppermute(blocks[step], axis, pairs))]
    slice x1 -> x2, local copies, waits for them, and re-layouts: 0.05 us -> 0.7 us  [exchange(): received = [blocks[0]]]
    unnamed x17 -> x25, local copies, waits for them, and re-layouts: 1.89 us -> 1.99 us
  transfers between devices with their start and end apart: 13 -> 13, of which waited for: 9 -> 7; matrix products, arithmetic and copies ran while one was open for 12% -> 7% of each run, Pallas kernels for 0% -> 0%
where the time goes in v17:
time: 49 us; the launch traced here: 48.8 us
  starting transfers between devices  18.8 us (38%)
  waiting for transfers between devices  12.3 us (25%)
  local copies, waits for them, and re-layouts  6.63 us (14%)
  Pallas kernels  6.14 us (13%)
  matrix products  2.96 us (6%)
  other arithmetic  1.05 us (2%)
  between operations  0.93 us (2%)
    ppermute x13, starting transfers between devices, exchange(): received.append(lax.ppermute(blocks[step], axis, pairs))  18.8 us
    ppermute x13, waiting for transfers between devices, exchange(): received.append(lax.ppermute(blocks[step], axis, pairs))  12.3 us
    pallas_call x1, Pallas kernels, pair_fields(): pl.pallas_call(functools.partial(pair_kernel, count, len(boxes)), out_sha...  6.14 us
    unnamed x25, local copies, waits for them, and re-layouts  1.99 us
    dot_general x1, matrix products, per_device(): jnp.dot(chooser.T, returned, precision=lax.Precision.HIGH)  1.07 us
    dot_general x2, matrix products, pick_rows(): jnp.dot(chooser.astype(jnp.float32), table.astype(jnp.float32), precision...  1.05 us
  transfers between devices with their start and end apart: 13, of which 7 were waited for; matrix products, arithmetic and copies ran while one was open for 7% of the time, Pallas kernels for 0%

profile of v17, /device:TPU:0, one launch (start us, length us, event | category | flops | bytes accessed | tf_op | source)
XLA Modules:
  0.0 48.8 jit_solution(2880303977986747326)
XLA Ops:
  0.0 0.8 %pad_add_fusion = s32[8,1]{0,1:T(1,128)S(1)} fusion(s32[4,1]{0,1:T(1,128)} %bitcast.70), kind=kLoop, calls=%fused_computation.69 | loop fusion | flops 8 | bytes 48 | tf_op jit(solution)/shard_map/concatenate | solution.py:241
  0.9 0.9 %convolution_convert_fusion.1 = bf16[4,3]{0,1:T(4,128)(2,1)S(1)} fusion(s32[16,3]{0,1:T(4,128)} %param.12, s32[4]{0:T(128)S(1)} %get-tuple-element.31), kind=kOutput, calls=%fused_computation.8 | convolution fusion | flops 2428 | bytes 232 | tf_op jit(solution)/shard_map/dot_general | solution.py:229
  1.9 0.8 %gather_fusion = bf16[4,32768]{1,0:T(4,128)(2,1)S(1)} fusion(bf16[16,32768]{1,0:T(8,128)(2,1)S(1)} %copy-done, s32[1024]{0:T(1024)S(1)} %pad_clamp_fusion.3), kind=kCustom, calls=%fused_computation | custom fusion | bytes 524304 | tf_op jit(solution)/shard_map/gather | solution.py:245
  2.9 0.7 %fusion.20 = (bf16[1,33,1024]{2,1,0:T(8,128)(2,1)}, bf16[1,33,1024]{2,1,0:T(8,128)(2,1)S(1)}, bf16[1,33,1024]{2,1,0:T(8,128)(2,1)S(1)}, bf16[1,33,1024]{2,1,0:T(8,128)(2,1)S(1)}) fusion(bf16[4,33,1024]{2,1,0:T(8,128)(2,1)S(1)} %constant_dynamic-update-slice_fusion), kind=kLoop, calls=%fused_computation.72 | loop fusion | bytes 540672 | tf_op jit(solution)/shard_map/slice | solution.py:220
  3.5 5.0 %collective-permute-start.2 = (bf16[1,33,1024]{2,1,0:T(8,128)(2,1)S(1)}, bf16[1,33,1024]{2,1,0:T(8,128)(2,1)S(1)}, u32[]{:S(2)}, u32[]{:S(2)}) collective-permute-start(bf16[1,33,1024]{2,1,0:T(8,128)(2,1)S(1)} %get-tuple-element.26), channel_id=1, source_target_pairs={{0,24},{8,0},{16,8},{24,16},{1,25},{9,1},{17,9},{25,17},{2,26},{10... | collective-permute-start | bytes 202760 | tf_op jit(solution)/shard_map/ppermute | solution.py:223
  8.6 1.0 %collective-permute-start = (bf16[1,33,1024]{2,1,0:T(8,128)(2,1)S(1)}, bf16[1,33,1024]{2,1,0:T(8,128)(2,1)S(1)}, u32[]{:S(2)}, u32[]{:S(2)}) collective-permute-start(bf16[1,33,1024]{2,1,0:T(8,128)(2,1)S(1)} %get-tuple-element.28), channel_id=1, source_target_pairs={{0,8},{8,16},{16,24},{24,0},{1,9},{9,17},{17,25},{25,1},{2,10},{10... | collective-permute-start | bytes 202760 | tf_op jit(solution)/shard_map/ppermute | solution.py:223
  10.4 0.8 %gather_fusion.2 = bf16[4,32768]{1,0:T(4,128)(2,1)S(1)} fusion(bf16[16,32768]{1,0:T(8,128)(2,1)S(1)} %copy-done, s32[1024]{0:T(1024)S(1)} %get-tuple-element.33), kind=kCustom, calls=%fused_computation.2 | custom fusion | bytes 524304 | tf_op jit(solution)/shard_map/gather | solution.py:263
  11.2 0.8 %copy.39 = bf16[1,4,32,1024]{3,2,1,0:T(8,128)(2,1)} copy(bf16[1,4,32,1024]{3,1,2,0:T(4,128)(2,1)S(1)} %bitcast.61) | data formatting | bytes 524288
  12.0 4.1 %collective-permute-done.1.rest_2_ = bf16[1,33,1024]{2,1,0:T(8,128)(2,1)S(1)} collective-permute-done((bf16[1,33,1024]{2,1,0:T(8,128)(2,1)S(1)}, bf16[1,33,1024]{2,1,0:T(8,128)(2,1)S(1)}, u32[]{:S(2)}, u32[]{:S(2)}) %collective-permute-start.1) | collective-permute-done | bytes 67616 | tf_op jit(solution)/shard_map/ppermute | solution.py:223
  16.1 0.6 %gather_fusion.1 = s32[4,3]{1,0:T(4,128)S(1)} fusion(s32[4,3]{1,0:T(4,128)S(1)} %bitcast.63, s32[1024]{0:T(1024)S(1)} %get-tuple-element.34), kind=kCustom, calls=%fused_computation.1 | custom fusion | bytes 112 | tf_op jit(solution)/shard_map/gather | solution.py:264
  16.8 0.2 fusion
  17.2 0.6 %concatenate.11.meta_ref = s32[29]{0:T(128)} concatenate(s32[12]{0:T(128)S(1)} %reshape.175, s32[4]{0:T(128)S(1)} %compare_convert_fusion, s32[4]{0:T(128)S(1)} %bitcast.69, s32[4]{0:T(128)S(1)} %get-tuple-element.30, s32[1]{0:T(128)} %bitcast.10, s32[4]{0:T(128)S(1)} %get-tuple-element.29), dimensions={0} | concatenate | bytes 232 | tf_op jit(solution)/shard_map/concatenate | solution.py:268
  17.8 6.1 %shard_map.109 = (f32[8,4224]{1,0:T(8,128)}, f32[8,4224]{1,0:T(8,128)}, f32[8,4224]{1,0:T(8,128)}, f32[8,4224]{1,0:T(8,128)}, f32[8,4224]{1,0:T(8,128)}, /*index...) custom-call(s32[29]{0:T(128)} %concatenate.11.meta_ref, bf16[4,32,1024]{2,1,0:T(8,128)(2,1)} %bitcast.62, ...), custom_call_target="tpu_custom_call" | custom-call | tf_op jit(solution)/shard_map/pallas_call | solution.py:203
  23.9 1.5 %collective-permute-start.4 = (f32[8,4224]{1,0:T(8,128)}, f32[8,4224]{1,0:T(8,128)S(1)}, u32[]{:S(2)}, u32[]{:S(2)}) collective-permute-start(f32[8,4224]{1,0:T(8,128)} %get-tuple-element.15), channel_id=1, source_target_pairs={{0,2},{1,3},{2,4},{3,5},{4,6},{5,7},{6,0},{7,1},{8,10},{9,11},{10,... | collective-permute-start | bytes 405512 | tf_op jit(solution)/shard_map/ppermute | solution.py:223
  25.5 2.4 %collective-permute-start.5 = (f32[8,4224]{1,0:T(8,128)}, f32[8,4224]{1,0:T(8,128)S(1)}, u32[]{:S(2)}, u32[]{:S(2)}) collective-permute-start(f32[8,4224]{1,0:T(8,128)} %get-tuple-element.16), channel_id=1, source_target_pairs={{0,3},{1,4},{2,5},{3,6},{4,7},{5,0},{6,1},{7,2},{8,11},{9,12},{10,... | collective-permute-start | bytes 405512 | tf_op jit(solution)/shard_map/ppermute | solution.py:223
  27.8 0.5 %collective-permute-start.6 = (f32[8,4224]{1,0:T(8,128)}, f32[8,4224]{1,0:T(8,128)S(1)}, u32[]{:S(2)}, u32[]{:S(2)}) collective-permute-start(f32[8,4224]{1,0:T(8,128)} %get-tuple-element.17), channel_id=1, source_target_pairs={{0,4},{1,5},{2,6},{3,7},{4,0},{5,1},{6,2},{7,3},{8,12},{9,13},{10,... | collective-permute-start | bytes 405512 | tf_op jit(solution)/shard_map/ppermute | solution.py:223
  28.4 0.1 collective-permute-start.7
  28.5 0.9 %bitcast_dynamic-update-slice_fusion.8 = f32[8,8,4224]{2,1,0:T(8,128)S(1)} fusion(f32[8,4224]{1,0:T(8,128)} %get-tuple-element.13), kind=kLoop, calls=%fused_computation.19 | loop fusion | bytes 270336
  29.4 1.1 %collective-permute-done.3 = f32[8,4224]{1,0:T(8,128)S(1)} collective-permute-done((f32[8,4224]{1,0:T(8,128)}, f32[8,4224]{1,0:T(8,128)S(1)}, u32[]{:S(2)}, u32[]{:S(2)}) %collective-permute-start.3) | collective-permute-done | bytes 135200 | tf_op jit(solution)/shard_map/ppermute | solution.py:223
  30.4 1.4 %collective-permute-start.8 = (f32[8,4224]{1,0:T(8,128)}, f32[8,4224]{1,0:T(8,128)S(1)}, u32[]{:S(2)}, u32[]{:S(2)}) collective-permute-start(f32[8,4224]{1,0:T(8,128)} %get-tuple-element.19), channel_id=1, source_target_pairs={{0,6},{1,7},{2,0},{3,1},{4,2},{5,3},{6,4},{7,5},{8,14},{9,15},{10,... | collective-permute-start | bytes 405512 | tf_op jit(solution)/shard_map/ppermute | solution.py:223
  31.9 2.6 %collective-permute-start.9 = (f32[8,4224]{1,0:T(8,128)}, f32[8,4224]{1,0:T(8,128)S(1)}, u32[]{:S(2)}, u32[]{:S(2)}) collective-permute-start(f32[8,4224]{1,0:T(8,128)} %get-tuple-element.20), channel_id=1, source_target_pairs={{0,7},{1,0},{2,1},{3,2},{4,3},{5,4},{6,5},{7,6},{8,15},{9,8},{10,9... | collective-permute-start | bytes 405512 | tf_op jit(solution)/shard_map/ppermute | solution.py:223
  34.5 2.1 %collective-permute-done.5 = f32[8,4224]{1,0:T(8,128)S(1)} collective-permute-done((f32[8,4224]{1,0:T(8,128)}, f32[8,4224]{1,0:T(8,128)S(1)}, u32[]{:S(2)}, u32[]{:S(2)}) %collective-permute-start.5) | collective-permute-done | bytes 135200 | tf_op jit(solution)/shard_map/ppermute | solution.py:223
  36.6 0.2 collective-permute-done.6
  36.8 1.9 %collective-permute-done.7 = f32[8,4224]{1,0:T(8,128)S(1)} collective-permute-done((f32[8,4224]{1,0:T(8,128)}, f32[8,4224]{1,0:T(8,128)S(1)}, u32[]{:S(2)}, u32[]{:S(2)}) %collective-permute-start.7) | collective-permute-done | bytes 135200 | tf_op jit(solution)/shard_map/ppermute | solution.py:223
  38.9 0.1 copy.24
  39.1 0.8 %convolution_bitcast_fusion = f32[20,4096]{1,0:T(8,128)S(1)} fusion(f32[8,8,4096]{2,1,0:T(8,128)S(1)} %slice.95, s32[8,8]{0,1:T(8,128)S(1)} %bitcast.64), kind=kOutput, calls=%fused_computation.4 | convolution fusion | flops 31458560 | bytes 1376512 | tf_op jit(solution)/shard_map/srk,srl->kl/dot_general | solution.py:283
  40.0 2.2 %collective-permute-start.12 = (f32[1,4096]{1,0:T(1,128)S(1)}, f32[1,4096]{1,0:T(1,128)S(1)}, u32[]{:S(2)}, u32[]{:S(2)}) collective-permute-start(f32[1,4096]{1,0:T(1,128)S(1)} %get-tuple-element.22), channel_id=1, source_target_pairs={{0,24},{8,0},{16,8},{24,16},{1,25},{9,1},{17,9},{25,17},{2,26},{10... | collective-permute-start | bytes 49160 | tf_op jit(solution)/shard_map/ppermute | solution.py:223
  42.2 1.9 %collective-permute-start.10 = (f32[1,4096]{1,0:T(1,128)S(1)}, f32[1,4096]{1,0:T(1,128)S(1)}, u32[]{:S(2)}, u32[]{:S(2)}) collective-permute-start(f32[1,4096]{1,0:T(1,128)S(1)} %get-tuple-element.24), channel_id=1, source_target_pairs={{0,8},{8,16},{16,24},{24,0},{1,9},{9,17},{17,25},{25,1},{2,10},{10... | collective-permute-start | bytes 49160 | tf_op jit(solution)/shard_map/ppermute | solution.py:223
  44.1 0.6 %gather_fusion.3 = s32[4]{0:T(128)S(1)} fusion(s32[4]{0:T(128)S(1)} %get-tuple-element.31, s32[1024]{0:T(1024)S(1)} %pad_clamp_fusion), kind=kCustom, calls=%fused_computation.3 | custom fusion | bytes 48 | tf_op jit(solution)/shard_map/gather | solution.py:288
  44.8 2.0 %collective-permute-done.11 = f32[1,4096]{1,0:T(1,128)S(1)} collective-permute-done((f32[1,4096]{1,0:T(1,128)S(1)}, f32[1,4096]{1,0:T(1,128)S(1)}, u32[]{:S(2)}, u32[]{:S(2)}) %collective-permute-start.11) | collective-permute-done | bytes 16416 | tf_op jit(solution)/shard_map/ppermute | solution.py:223
  46.8 0.9 %collective-permute-done.10 = f32[1,4096]{1,0:T(1,128)S(1)} collective-permute-done((f32[1,4096]{1,0:T(1,128)S(1)}, f32[1,4096]{1,0:T(1,128)S(1)}, u32[]{:S(2)}, u32[]{:S(2)}) %collective-permute-start.10) | collective-permute-done | bytes 16416 | tf_op jit(solution)/shard_map/ppermute | solution.py:223
  47.8 1.1 %convolution_add_fusion = f32[16,4096]{1,0:T(8,128)} fusion(f32[20,4096]{1,0:T(8,128)S(1)} %convolution_bitcast_fusion, f32[4,1,4096]{2,1,0:T(1,128)S(1)} %pad_maximum_fusion, s32[4]{0:T(128)S(1)} %gather_fusion.3), kind=kOutput, calls=%fused_computation.5 | convolution fusion | flops 1638464 | bytes 589840 | tf_op jit(solution)/shard_map/dot_general | solution.py:292
  (56 shorter events, 1.0 us)
Async XLA Ops:
  0.0 1.9 %copy-start = (bf16[16,32768]{1,0:T(8,128)(2,1)S(1)}, bf16[16,32768]{1,0:T(8,128)(2,1)}, u32[]{:S(2)}) copy-start(bf16[16,32768]{1,0:T(8,128)(2,1)} %param.11) | copy-start | bytes 3145732
  2.7 6.9 %copy-start.5 = (s32[1,1,4]{2,1,0:T(1,128)S(1)}, s32[1,1,4]{2,1,0:T(1,128)}, u32[]{:S(2)}) copy-start(s32[1,1,4]{2,1,0:T(1,128)} %param.15) | copy-start | bytes 52
  2.7 7.6 %copy-start.4 = (s32[1,1,4]{2,1,0:T(1,128)S(1)}, s32[1,1,4]{2,1,0:T(1,128)}, u32[]{:S(2)}) copy-start(s32[1,1,4]{2,1,0:T(1,128)} %param.14) | copy-start | bytes 52
  3.5 8.4 %collective-permute-start.2 = (bf16[1,33,1024]{2,1,0:T(8,128)(2,1)S(1)}, bf16[1,33,1024]{2,1,0:T(8,128)(2,1)S(1)}, u32[]{:S(2)}, u32[]{:S(2)}) collective-permute-start(bf16[1,33,1024]{2,1,0:T(8,128)(2,1)S(1)} %get-tuple-element.26), channel_id=1, source_target_pairs={{0,24},{8,0},{16,8},{24,16},{1,25},{9,1},{17,9},{25,17},{2,26},{10... | collective-permute-start | bytes 202760 | tf_op jit(solution)/shard_map/ppermute | solution.py:223
  8.6 7.5 %collective-permute-start.1 = (bf16[1,33,1024]{2,1,0:T(8,128)(2,1)S(1)}, bf16[1,33,1024]{2,1,0:T(8,128)(2,1)S(1)}, u32[]{:S(2)}, u32[]{:S(2)}) collective-permute-start(bf16[1,33,1024]{2,1,0:T(8,128)(2,1)S(1)} %get-tuple-element.27), channel_id=1, source_target_pairs={{0,16},{8,24},{16,0},{24,8},{1,17},{9,25},{17,1},{25,9},{2,18},{10... | collective-permute-start | bytes 202760 | tf_op jit(solution)/shard_map/ppermute | solution.py:223
  8.6 7.5 %collective-permute-start = (bf16[1,33,1024]{2,1,0:T(8,128)(2,1)S(1)}, bf16[1,33,1024]{2,1,0:T(8,128)(2,1)S(1)}, u32[]{:S(2)}, u32[]{:S(2)}) collective-permute-start(bf16[1,33,1024]{2,1,0:T(8,128)(2,1)S(1)} %get-tuple-element.28), channel_id=1, source_target_pairs={{0,8},{8,16},{16,24},{24,0},{1,9},{9,17},{17,25},{25,1},{2,10},{10... | collective-permute-start | bytes 202760 | tf_op jit(solution)/shard_map/ppermute | solution.py:223
  10.4 6.4 %copy-start.6 = (s32[16,3]{0,1:T(4,128)S(1)}, s32[16,3]{0,1:T(4,128)}, u32[]{:S(2)}) copy-start(s32[16,3]{0,1:T(4,128)} %param.12) | copy-start | bytes 580
  12.0 5.8 %copy-start.1 = (bf16[1,33,1024]{2,1,0:T(8,128)(2,1)}, bf16[1,33,1024]{2,1,0:T(8,128)(2,1)S(1)}, u32[]{:S(2)}) copy-start(bf16[1,33,1024]{2,1,0:T(8,128)(2,1)S(1)} %collective-permute-done.2.rest_3_) | copy-start | bytes 202756
  16.1 1.7 %copy-start.2 = (bf16[1,33,1024]{2,1,0:T(8,128)(2,1)}, bf16[1,33,1024]{2,1,0:T(8,128)(2,1)S(1)}, u32[]{:S(2)}) copy-start(bf16[1,33,1024]{2,1,0:T(8,128)(2,1)S(1)} %collective-permute-done.1.rest_2_) | copy-start | bytes 202756
  16.1 1.7 %copy-start.3 = (bf16[1,33,1024]{2,1,0:T(8,128)(2,1)}, bf16[1,33,1024]{2,1,0:T(8,128)(2,1)S(1)}, u32[]{:S(2)}) copy-start(bf16[1,33,1024]{2,1,0:T(8,128)(2,1)S(1)} %collective-permute-done.rest_1_) | copy-start | bytes 202756
  23.9 6.5 %collective-permute-start.3 = (f32[8,4224]{1,0:T(8,128)}, f32[8,4224]{1,0:T(8,128)S(1)}, u32[]{:S(2)}, u32[]{:S(2)}) collective-permute-start(f32[8,4224]{1,0:T(8,128)} %get-tuple-element.14), channel_id=1, source_target_pairs={{0,1},{1,2},{2,3},{3,4},{4,5},{5,6},{6,7},{7,0},{8,9},{9,10},{10,1... | collective-permute-start | bytes 405512 | tf_op jit(solution)/shard_map/ppermute | solution.py:223
  23.9 8.0 %collective-permute-start.4 = (f32[8,4224]{1,0:T(8,128)}, f32[8,4224]{1,0:T(8,128)S(1)}, u32[]{:S(2)}, u32[]{:S(2)}) collective-permute-start(f32[8,4224]{1,0:T(8,128)} %get-tuple-element.15), channel_id=1, source_target_pairs={{0,2},{1,3},{2,4},{3,5},{4,6},{5,7},{6,0},{7,1},{8,10},{9,11},{10,... | collective-permute-start | bytes 405512 | tf_op jit(solution)/shard_map/ppermute | solution.py:223
  25.5 11.1 %collective-permute-start.5 = (f32[8,4224]{1,0:T(8,128)}, f32[8,4224]{1,0:T(8,128)S(1)}, u32[]{:S(2)}, u32[]{:S(2)}) collective-permute-start(f32[8,4224]{1,0:T(8,128)} %get-tuple-element.16), channel_id=1, source_target_pairs={{0,3},{1,4},{2,5},{3,6},{4,7},{5,0},{6,1},{7,2},{8,11},{9,12},{10,... | collective-permute-start | bytes 405512 | tf_op jit(solution)/shard_map/ppermute | solution.py:223
  27.8 9.0 %collective-permute-start.6 = (f32[8,4224]{1,0:T(8,128)}, f32[8,4224]{1,0:T(8,128)S(1)}, u32[]{:S(2)}, u32[]{:S(2)}) collective-permute-start(f32[8,4224]{1,0:T(8,128)} %get-tuple-element.17), channel_id=1, source_target_pairs={{0,4},{1,5},{2,6},{3,7},{4,0},{5,1},{6,2},{7,3},{8,12},{9,13},{10,... | collective-permute-start | bytes 405512 | tf_op jit(solution)/shard_map/ppermute | solution.py:223
  28.4 10.4 %collective-permute-start.7 = (f32[8,4224]{1,0:T(8,128)}, f32[8,4224]{1,0:T(8,128)S(1)}, u32[]{:S(2)}, u32[]{:S(2)}) collective-permute-start(f32[8,4224]{1,0:T(8,128)} %get-tuple-element.18), channel_id=1, source_target_pairs={{0,5},{1,6},{2,7},{3,0},{4,1},{5,2},{6,3},{7,4},{8,13},{9,14},{10,... | collective-permute-start | bytes 405512 | tf_op jit(solution)/shard_map/ppermute | solution.py:223
  30.4 8.3 %collective-permute-start.8 = (f32[8,4224]{1,0:T(8,128)}, f32[8,4224]{1,0:T(8,128)S(1)}, u32[]{:S(2)}, u32[]{:S(2)}) collective-permute-start(f32[8,4224]{1,0:T(8,128)} %get-tuple-element.19), channel_id=1, source_target_pairs={{0,6},{1,7},{2,0},{3,1},{4,2},{5,3},{6,4},{7,5},{8,14},{9,15},{10,... | collective-permute-start | bytes 405512 | tf_op jit(solution)/shard_map/ppermute | solution.py:223
  31.9 6.9 %collective-permute-start.9 = (f32[8,4224]{1,0:T(8,128)}, f32[8,4224]{1,0:T(8,128)S(1)}, u32[]{:S(2)}, u32[]{:S(2)}) collective-permute-start(f32[8,4224]{1,0:T(8,128)} %get-tuple-element.20), channel_id=1, source_target_pairs={{0,7},{1,0},{2,1},{3,2},{4,3},{5,4},{6,5},{7,6},{8,15},{9,8},{10,9... | collective-permute-start | bytes 405512 | tf_op jit(solution)/shard_map/ppermute | solution.py:223
  40.0 4.8 %collective-permute-start.12 = (f32[1,4096]{1,0:T(1,128)S(1)}, f32[1,4096]{1,0:T(1,128)S(1)}, u32[]{:S(2)}, u32[]{:S(2)}) collective-permute-start(f32[1,4096]{1,0:T(1,128)S(1)} %get-tuple-element.22), channel_id=1, source_target_pairs={{0,24},{8,0},{16,8},{24,16},{1,25},{9,1},{17,9},{25,17},{2,26},{10... | collective-permute-start | bytes 49160 | tf_op jit(solution)/shard_map/ppermute | solution.py:223
  42.1 4.6 %collective-permute-start.11 = (f32[1,4096]{1,0:T(1,128)S(1)}, f32[1,4096]{1,0:T(1,128)S(1)}, u32[]{:S(2)}, u32[]{:S(2)}) collective-permute-start(f32[1,4096]{1,0:T(1,128)S(1)} %get-tuple-element.23), channel_id=1, source_target_pairs={{0,16},{8,24},{16,0},{24,8},{1,17},{9,25},{17,1},{25,9},{2,18},{10... | collective-permute-start | bytes 49160 | tf_op jit(solution)/shard_map/ppermute | solution.py:223
  42.2 5.5 %collective-permute-start.10 = (f32[1,4096]{1,0:T(1,128)S(1)}, f32[1,4096]{1,0:T(1,128)S(1)}, u32[]{:S(2)}, u32[]{:S(2)}) collective-permute-start(f32[1,4096]{1,0:T(1,128)S(1)} %get-tuple-element.24), channel_id=1, source_target_pairs={{0,8},{8,16},{16,24},{24,0},{1,9},{9,17},{17,25},{25,1},{2,10},{10... | collective-permute-start | bytes 49160 | tf_op jit(solution)/shard_map/ppermute | solution.py:223

commit v18 on v17

--- a/solution.py
+++ b/solution.py
@@ -250,9 +250,7 @@
         axis=1,
     ).reshape(section_total, per_target, B + 1, PLANE)
     visitors = exchange(outgoing, "home")
-    visit_offsets = jnp.stack([block[:, B, 0:3] for block in visitors]).reshape(
-        slot_total, 3
-    ).astype(jnp.int32)
+    visit_offsets = jnp.stack([block[:, B, 0:3] for block in visitors]).reshape(slot_total, 3)
 
     home_slot = pair_home[0, 0]
     visit_code = pair_visit[0, 0]
@@ -261,7 +259,7 @@
     return_slot = ((source - me) % section_total) * per_target + visit_code % per_target
     live = (jnp.arange(slots, dtype=jnp.int32) < pair_count[0, 0]).astype(jnp.int32)
     home_orb = orbitals[home_slot].reshape(slots, B, PLANE)
-    delta = pick_rows(home_slot, offsets).astype(jnp.int32) - visit_offsets[visit_slot]
+    delta = (pick_rows(home_slot, offsets) - pick_rows(visit_slot, visit_offsets)).astype(jnp.int32)
     pair_total = lax.psum(1, "pair")
     chunk = cell_count // pair_total
     pair_me = lax.axis_index("pair")

time: 49 us -> 49.1 us (level)
  local copies, waits for them, and re-layouts: 6.63 us -> 5.98 us
  other arithmetic: 1.05 us -> 1.69 us
    gather x2 -> x0, local copies, waits for them, and re-layouts: 0.65 us -> none  [per_device(): visit_offsets[visit_slot]]
    select_n x1, other arithmetic: 0.01 us -> 0.66 us  [per_device(): home_orb = orbitals[home_slot].reshape(slots, B, PLANE)]
    dot_general x2 -> x3, matrix products: 1.05 us -> 1.24 us  [pick_rows(): jnp.dot(chooser.astype(jnp.float32), table.astype(jnp.float32), precision...]
where the time goes in v18:
time: 49.1 us; the launch traced here: 48.9 us
  starting transfers between devices  18.8 us (38%)
  waiting for transfers between devices  12.2 us (25%)
  Pallas kernels  6.14 us (13%)
  local copies, waits for them, and re-layouts  5.98 us (12%)
  matrix products  3.14 us (6%)
  other arithmetic  1.69 us (3%)
  between operations  0.91 us (2%)
    ppermute x13, starting transfers between devices, exchange(): received.append(lax.ppermute(blocks[step], axis, pairs))  18.8 us
    ppermute x13, waiting for transfers between devices, exchange(): received.append(lax.ppermute(blocks[step], axis, pairs))  12.2 us
    pallas_call x1, Pallas kernels, pair_fields(): pl.pallas_call(functools.partial(pair_kernel, count, len(boxes)), out_sha...  6.14 us
    unnamed x25, local copies, waits for them, and re-layouts  1.99 us
    dot_general x3, matrix products, pick_rows(): jnp.dot(chooser.astype(jnp.float32), table.astype(jnp.float32), precision...  1.24 us
    dot_general x1, matrix products, per_device(): jnp.dot(chooser.T, returned, precision=lax.Precision.HIGH)  1.07 us
  transfers between devices with their start and end apart: 13, of which 7 were waited for; matrix products, arithmetic and copies ran while one was open for 7% of the time, Pallas kernels for 0%

profile of v18, /device:TPU:0, one launch (start us, length us, event | category | flops | bytes accessed | tf_op | source)
XLA Modules:
  0.0 48.9 jit_solution(9027371574850877509)
XLA Ops:
  0.0 0.8 %pad_add_fusion = s32[8,1]{0,1:T(1,128)S(1)} fusion(s32[4,1]{0,1:T(1,128)} %bitcast.67), kind=kLoop, calls=%fused_computation.66 | loop fusion | flops 8 | bytes 48 | tf_op jit(solution)/shard_map/concatenate | solution.py:241
  0.8 0.7 %fusion.20 = s32[4]{0:T(128)S(1)} fusion(s32[1,1,4]{2,1,0:T(1,128)} %param.14), kind=kLoop, calls=%fused_computation.65 | loop fusion | flops 12 | bytes 32 | tf_op jit(solution)/shard_map/select_n | solution.py:261
  1.6 0.9 %convolution_convert_fusion = bf16[4,3]{0,1:T(4,128)(2,1)S(1)} fusion(s32[16,3]{0,1:T(4,128)} %param.12, s32[4]{0:T(128)S(1)} %get-tuple-element.31), kind=kOutput, calls=%fused_computation.7 | convolution fusion | flops 2428 | bytes 232 | tf_op jit(solution)/shard_map/dot_general | solution.py:229
  2.6 0.8 %gather_fusion = bf16[4,32768]{1,0:T(4,128)(2,1)S(1)} fusion(bf16[16,32768]{1,0:T(8,128)(2,1)S(1)} %copy-done, s32[1024]{0:T(1024)S(1)} %get-tuple-element.34), kind=kCustom, calls=%fused_computation | custom fusion | bytes 524304 | tf_op jit(solution)/shard_map/gather | solution.py:245
  3.5 0.7 %fusion.22 = (bf16[1,33,1024]{2,1,0:T(8,128)(2,1)}, bf16[1,33,1024]{2,1,0:T(8,128)(2,1)S(1)}, bf16[1,33,1024]{2,1,0:T(8,128)(2,1)S(1)}, bf16[1,33,1024]{2,1,0:T(8,128)(2,1)S(1)}) fusion(bf16[4,33,1024]{2,1,0:T(8,128)(2,1)S(1)} %constant_dynamic-update-slice_fusion), kind=kLoop, calls=%fused_computation.69 | loop fusion | bytes 540672 | tf_op jit(solution)/shard_map/slice | solution.py:220
  4.2 5.0 %collective-permute-start.2 = (bf16[1,33,1024]{2,1,0:T(8,128)(2,1)S(1)}, bf16[1,33,1024]{2,1,0:T(8,128)(2,1)S(1)}, u32[]{:S(2)}, u32[]{:S(2)}) collective-permute-start(bf16[1,33,1024]{2,1,0:T(8,128)(2,1)S(1)} %get-tuple-element.26), channel_id=1, source_target_pairs={{0,24},{8,0},{16,8},{24,16},{1,25},{9,1},{17,9},{25,17},{2,26},{10... | collective-permute-start | bytes 202760 | tf_op jit(solution)/shard_map/ppermute | solution.py:223
  9.3 1.0 %collective-permute-start = (bf16[1,33,1024]{2,1,0:T(8,128)(2,1)S(1)}, bf16[1,33,1024]{2,1,0:T(8,128)(2,1)S(1)}, u32[]{:S(2)}, u32[]{:S(2)}) collective-permute-start(bf16[1,33,1024]{2,1,0:T(8,128)(2,1)S(1)} %get-tuple-element.28), channel_id=1, source_target_pairs={{0,8},{8,16},{16,24},{24,0},{1,9},{9,17},{17,25},{25,1},{2,10},{10... | collective-permute-start | bytes 202760 | tf_op jit(solution)/shard_map/ppermute | solution.py:223
  11.0 0.2 fusion.6
  11.2 0.8 %gather_fusion.1 = bf16[4,32768]{1,0:T(4,128)(2,1)S(1)} fusion(bf16[16,32768]{1,0:T(8,128)(2,1)S(1)} %copy-done, s32[1024]{0:T(1024)S(1)} %get-tuple-element.33), kind=kCustom, calls=%fused_computation.1 | custom fusion | bytes 524304 | tf_op jit(solution)/shard_map/gather | solution.py:261
  12.0 0.8 %copy.42 = bf16[1,4,32,1024]{3,2,1,0:T(8,128)(2,1)} copy(bf16[1,4,32,1024]{3,1,2,0:T(4,128)(2,1)S(1)} %bitcast.59) | data formatting | bytes 524288
  12.8 4.0 %collective-permute-done.1.rest_2_ = bf16[1,33,1024]{2,1,0:T(8,128)(2,1)S(1)} collective-permute-done((bf16[1,33,1024]{2,1,0:T(8,128)(2,1)S(1)}, bf16[1,33,1024]{2,1,0:T(8,128)(2,1)S(1)}, u32[]{:S(2)}, u32[]{:S(2)}) %collective-permute-start.1) | collective-permute-done | bytes 67616 | tf_op jit(solution)/shard_map/ppermute | solution.py:223
  16.8 0.2 fusion
  17.2 0.6 %concatenate.11.meta_ref = s32[29]{0:T(128)} concatenate(s32[12]{0:T(128)S(1)} %reshape.138, s32[4]{0:T(128)S(1)} %compare_convert_fusion, s32[4]{0:T(128)S(1)} %bitcast.66, s32[4]{0:T(128)S(1)} %get-tuple-element.29, s32[1]{0:T(128)} %bitcast.8, s32[4]{0:T(128)S(1)} %get-tuple-element.30), dimensions={0} | concatenate | bytes 232 | tf_op jit(solution)/shard_map/concatenate | solution.py:266
  17.8 6.1 %shard_map.109 = (f32[8,4224]{1,0:T(8,128)}, f32[8,4224]{1,0:T(8,128)}, f32[8,4224]{1,0:T(8,128)}, f32[8,4224]{1,0:T(8,128)}, f32[8,4224]{1,0:T(8,128)}, /*index...) custom-call(s32[29]{0:T(128)} %concatenate.11.meta_ref, bf16[4,32,1024]{2,1,0:T(8,128)(2,1)} %bitcast.60, ...), custom_call_target="tpu_custom_call" | custom-call | tf_op jit(solution)/shard_map/pallas_call | solution.py:203
  24.0 1.5 %collective-permute-start.4 = (f32[8,4224]{1,0:T(8,128)}, f32[8,4224]{1,0:T(8,128)S(1)}, u32[]{:S(2)}, u32[]{:S(2)}) collective-permute-start(f32[8,4224]{1,0:T(8,128)} %get-tuple-element.15), channel_id=1, source_target_pairs={{0,2},{1,3},{2,4},{3,5},{4,6},{5,7},{6,0},{7,1},{8,10},{9,11},{10,... | collective-permute-start | bytes 405512 | tf_op jit(solution)/shard_map/ppermute | solution.py:223
  25.5 2.4 %collective-permute-start.5 = (f32[8,4224]{1,0:T(8,128)}, f32[8,4224]{1,0:T(8,128)S(1)}, u32[]{:S(2)}, u32[]{:S(2)}) collective-permute-start(f32[8,4224]{1,0:T(8,128)} %get-tuple-element.16), channel_id=1, source_target_pairs={{0,3},{1,4},{2,5},{3,6},{4,7},{5,0},{6,1},{7,2},{8,11},{9,12},{10,... | collective-permute-start | bytes 405512 | tf_op jit(solution)/shard_map/ppermute | solution.py:223
  27.9 0.5 %collective-permute-start.6 = (f32[8,4224]{1,0:T(8,128)}, f32[8,4224]{1,0:T(8,128)S(1)}, u32[]{:S(2)}, u32[]{:S(2)}) collective-permute-start(f32[8,4224]{1,0:T(8,128)} %get-tuple-element.17), channel_id=1, source_target_pairs={{0,4},{1,5},{2,6},{3,7},{4,0},{5,1},{6,2},{7,3},{8,12},{9,13},{10,... | collective-permute-start | bytes 405512 | tf_op jit(solution)/shard_map/ppermute | solution.py:223
  28.5 0.9 %bitcast_dynamic-update-slice_fusion.8 = f32[8,8,4224]{2,1,0:T(8,128)S(1)} fusion(f32[8,4224]{1,0:T(8,128)} %get-tuple-element.13), kind=kLoop, calls=%fused_computation.18 | loop fusion | bytes 270336
  29.4 1.1 %collective-permute-done.3 = f32[8,4224]{1,0:T(8,128)S(1)} collective-permute-done((f32[8,4224]{1,0:T(8,128)}, f32[8,4224]{1,0:T(8,128)S(1)}, u32[]{:S(2)}, u32[]{:S(2)}) %collective-permute-start.3) | collective-permute-done | bytes 135200 | tf_op jit(solution)/shard_map/ppermute | solution.py:223
  30.5 1.4 %collective-permute-start.8 = (f32[8,4224]{1,0:T(8,128)}, f32[8,4224]{1,0:T(8,128)S(1)}, u32[]{:S(2)}, u32[]{:S(2)}) collective-permute-start(f32[8,4224]{1,0:T(8,128)} %get-tuple-element.19), channel_id=1, source_target_pairs={{0,6},{1,7},{2,0},{3,1},{4,2},{5,3},{6,4},{7,5},{8,14},{9,15},{10,... | collective-permute-start | bytes 405512 | tf_op jit(solution)/shard_map/ppermute | solution.py:223
  31.9 2.6 %collective-permute-start.9 = (f32[8,4224]{1,0:T(8,128)}, f32[8,4224]{1,0:T(8,128)S(1)}, u32[]{:S(2)}, u32[]{:S(2)}) collective-permute-start(f32[8,4224]{1,0:T(8,128)} %get-tuple-element.20), channel_id=1, source_target_pairs={{0,7},{1,0},{2,1},{3,2},{4,3},{5,4},{6,5},{7,6},{8,15},{9,8},{10,9... | collective-permute-start | bytes 405512 | tf_op jit(solution)/shard_map/ppermute | solution.py:223
  34.5 2.1 %collective-permute-done.5 = f32[8,4224]{1,0:T(8,128)S(1)} collective-permute-done((f32[8,4224]{1,0:T(8,128)}, f32[8,4224]{1,0:T(8,128)S(1)}, u32[]{:S(2)}, u32[]{:S(2)}) %collective-permute-start.5) | collective-permute-done | bytes 135200 | tf_op jit(solution)/shard_map/ppermute | solution.py:223
  36.7 0.2 collective-permute-done.6
  36.8 1.9 %collective-permute-done.7 = f32[8,4224]{1,0:T(8,128)S(1)} collective-permute-done((f32[8,4224]{1,0:T(8,128)}, f32[8,4224]{1,0:T(8,128)S(1)}, u32[]{:S(2)}, u32[]{:S(2)}) %collective-permute-start.7) | collective-permute-done | bytes 135200 | tf_op jit(solution)/shard_map/ppermute | solution.py:223
  38.9 0.1 copy.22
  39.1 0.8 %convolution_bitcast_fusion = f32[20,4096]{1,0:T(8,128)S(1)} fusion(f32[8,8,4096]{2,1,0:T(8,128)S(1)} %slice.93, s32[8,8]{0,1:T(8,128)S(1)} %bitcast.61), kind=kOutput, calls=%fused_computation.3 | convolution fusion | flops 31458560 | bytes 1376512 | tf_op jit(solution)/shard_map/srk,srl->kl/dot_general | solution.py:281
  40.0 2.2 %collective-permute-start.12 = (f32[1,4096]{1,0:T(1,128)S(1)}, f32[1,4096]{1,0:T(1,128)S(1)}, u32[]{:S(2)}, u32[]{:S(2)}) collective-permute-start(f32[1,4096]{1,0:T(1,128)S(1)} %get-tuple-element.22), channel_id=1, source_target_pairs={{0,24},{8,0},{16,8},{24,16},{1,25},{9,1},{17,9},{25,17},{2,26},{10... | collective-permute-start | bytes 49160 | tf_op jit(solution)/shard_map/ppermute | solution.py:223
  42.2 1.9 %collective-permute-start.10 = (f32[1,4096]{1,0:T(1,128)S(1)}, f32[1,4096]{1,0:T(1,128)S(1)}, u32[]{:S(2)}, u32[]{:S(2)}) collective-permute-start(f32[1,4096]{1,0:T(1,128)S(1)} %get-tuple-element.24), channel_id=1, source_target_pairs={{0,8},{8,16},{16,24},{24,0},{1,9},{9,17},{17,25},{25,1},{2,10},{10... | collective-permute-start | bytes 49160 | tf_op jit(solution)/shard_map/ppermute | solution.py:223
  44.1 0.6 %gather_fusion.2 = s32[4]{0:T(128)S(1)} fusion(s32[4]{0:T(128)S(1)} %get-tuple-element.31, s32[1024]{0:T(1024)S(1)} %pad_clamp_fusion), kind=kCustom, calls=%fused_computation.2 | custom fusion | bytes 48 | tf_op jit(solution)/shard_map/gather | solution.py:286
  44.8 2.0 %collective-permute-done.11 = f32[1,4096]{1,0:T(1,128)S(1)} collective-permute-done((f32[1,4096]{1,0:T(1,128)S(1)}, f32[1,4096]{1,0:T(1,128)S(1)}, u32[]{:S(2)}, u32[]{:S(2)}) %collective-permute-start.11) | collective-permute-done | bytes 16416 | tf_op jit(solution)/shard_map/ppermute | solution.py:223
  46.8 0.9 %collective-permute-done.10 = f32[1,4096]{1,0:T(1,128)S(1)} collective-permute-done((f32[1,4096]{1,0:T(1,128)S(1)}, f32[1,4096]{1,0:T(1,128)S(1)}, u32[]{:S(2)}, u32[]{:S(2)}) %collective-permute-start.10) | collective-permute-done | bytes 16416 | tf_op jit(solution)/shard_map/ppermute | solution.py:223
  47.8 1.1 %convolution_add_fusion = f32[16,4096]{1,0:T(8,128)} fusion(f32[20,4096]{1,0:T(8,128)S(1)} %convolution_bitcast_fusion, f32[4,1,4096]{2,1,0:T(1,128)S(1)} %pad_maximum_fusion, s32[4]{0:T(128)S(1)} %gather_fusion.2), kind=kOutput, calls=%fused_computation.4 | convolution fusion | flops 1638464 | bytes 589840 | tf_op jit(solution)/shard_map/dot_general | solution.py:290
  (53 shorter events, 1.0 us)
Async XLA Ops:
  0.0 2.6 %copy-start = (bf16[16,32768]{1,0:T(8,128)(2,1)S(1)}, bf16[16,32768]{1,0:T(8,128)(2,1)}, u32[]{:S(2)}) copy-start(bf16[16,32768]{1,0:T(8,128)(2,1)} %param.11) | copy-start | bytes 3145732
  3.4 7.6 %copy-start.5 = (s32[1,1,4]{2,1,0:T(1,128)S(1)}, s32[1,1,4]{2,1,0:T(1,128)}, u32[]{:S(2)}) copy-start(s32[1,1,4]{2,1,0:T(1,128)} %param.15) | copy-start | bytes 52
  3.4 7.6 %copy-start.4 = (s32[1,1,4]{2,1,0:T(1,128)S(1)}, s32[1,1,4]{2,1,0:T(1,128)}, u32[]{:S(2)}) copy-start(s32[1,1,4]{2,1,0:T(1,128)} %param.14) | copy-start | bytes 52
  3.4 7.6 %copy-start.6 = (s32[16,3]{0,1:T(4,128)S(1)}, s32[16,3]{0,1:T(4,128)}, u32[]{:S(2)}) copy-start(s32[16,3]{0,1:T(4,128)} %param.12) | copy-start | bytes 580
  4.2 8.6 %collective-permute-start.2 = (bf16[1,33,1024]{2,1,0:T(8,128)(2,1)S(1)}, bf16[1,33,1024]{2,1,0:T(8,128)(2,1)S(1)}, u32[]{:S(2)}, u32[]{:S(2)}) collective-permute-start(bf16[1,33,1024]{2,1,0:T(8,128)(2,1)S(1)} %get-tuple-element.26), channel_id=1, source_target_pairs={{0,24},{8,0},{16,8},{24,16},{1,25},{9,1},{17,9},{25,17},{2,26},{10... | collective-permute-start | bytes 202760 | tf_op jit(solution)/shard_map/ppermute | solution.py:223
  9.3 7.5 %collective-permute-start.1 = (bf16[1,33,1024]{2,1,0:T(8,128)(2,1)S(1)}, bf16[1,33,1024]{2,1,0:T(8,128)(2,1)S(1)}, u32[]{:S(2)}, u32[]{:S(2)}) collective-permute-start(bf16[1,33,1024]{2,1,0:T(8,128)(2,1)S(1)} %get-tuple-element.27), channel_id=1, source_target_pairs={{0,16},{8,24},{16,0},{24,8},{1,17},{9,25},{17,1},{25,9},{2,18},{10... | collective-permute-start | bytes 202760 | tf_op jit(solution)/shard_map/ppermute | solution.py:223
  9.3 7.5 %collective-permute-start = (bf16[1,33,1024]{2,1,0:T(8,128)(2,1)S(1)}, bf16[1,33,1024]{2,1,0:T(8,128)(2,1)S(1)}, u32[]{:S(2)}, u32[]{:S(2)}) collective-permute-start(bf16[1,33,1024]{2,1,0:T(8,128)(2,1)S(1)} %get-tuple-element.28), channel_id=1, source_target_pairs={{0,8},{8,16},{16,24},{24,0},{1,9},{9,17},{17,25},{25,1},{2,10},{10... | collective-permute-start | bytes 202760 | tf_op jit(solution)/shard_map/ppermute | solution.py:223
  12.8 5.0 %copy-start.1 = (bf16[1,33,1024]{2,1,0:T(8,128)(2,1)}, bf16[1,33,1024]{2,1,0:T(8,128)(2,1)S(1)}, u32[]{:S(2)}) copy-start(bf16[1,33,1024]{2,1,0:T(8,128)(2,1)S(1)} %collective-permute-done.2.rest_3_) | copy-start | bytes 202756
  16.8 1.0 %copy-start.2 = (bf16[1,33,1024]{2,1,0:T(8,128)(2,1)}, bf16[1,33,1024]{2,1,0:T(8,128)(2,1)S(1)}, u32[]{:S(2)}) copy-start(bf16[1,33,1024]{2,1,0:T(8,128)(2,1)S(1)} %collective-permute-done.1.rest_2_) | copy-start | bytes 202756
  16.8 1.0 %copy-start.3 = (bf16[1,33,1024]{2,1,0:T(8,128)(2,1)}, bf16[1,33,1024]{2,1,0:T(8,128)(2,1)S(1)}, u32[]{:S(2)}) copy-start(bf16[1,33,1024]{2,1,0:T(8,128)(2,1)S(1)} %collective-permute-done.rest_1_) | copy-start | bytes 202756
  24.0 6.5 %collective-permute-start.3 = (f32[8,4224]{1,0:T(8,128)}, f32[8,4224]{1,0:T(8,128)S(1)}, u32[]{:S(2)}, u32[]{:S(2)}) collective-permute-start(f32[8,4224]{1,0:T(8,128)} %get-tuple-element.14), channel_id=1, source_target_pairs={{0,1},{1,2},{2,3},{3,4},{4,5},{5,6},{6,7},{7,0},{8,9},{9,10},{10,1... | collective-permute-start | bytes 405512 | tf_op jit(solution)/shard_map/ppermute | solution.py:223
  24.0 8.0 %collective-permute-start.4 = (f32[8,4224]{1,0:T(8,128)}, f32[8,4224]{1,0:T(8,128)S(1)}, u32[]{:S(2)}, u32[]{:S(2)}) collective-permute-start(f32[8,4224]{1,0:T(8,128)} %get-tuple-element.15), channel_id=1, source_target_pairs={{0,2},{1,3},{2,4},{3,5},{4,6},{5,7},{6,0},{7,1},{8,10},{9,11},{10,... | collective-permute-start | bytes 405512 | tf_op jit(solution)/shard_map/ppermute | solution.py:223
  25.5 11.1 %collective-permute-start.5 = (f32[8,4224]{1,0:T(8,128)}, f32[8,4224]{1,0:T(8,128)S(1)}, u32[]{:S(2)}, u32[]{:S(2)}) collective-permute-start(f32[8,4224]{1,0:T(8,128)} %get-tuple-element.16), channel_id=1, source_target_pairs={{0,3},{1,4},{2,5},{3,6},{4,7},{5,0},{6,1},{7,2},{8,11},{9,12},{10,... | collective-permute-start | bytes 405512 | tf_op jit(solution)/shard_map/ppermute | solution.py:223
  27.9 9.0 %collective-permute-start.6 = (f32[8,4224]{1,0:T(8,128)}, f32[8,4224]{1,0:T(8,128)S(1)}, u32[]{:S(2)}, u32[]{:S(2)}) collective-permute-start(f32[8,4224]{1,0:T(8,128)} %get-tuple-element.17), channel_id=1, source_target_pairs={{0,4},{1,5},{2,6},{3,7},{4,0},{5,1},{6,2},{7,3},{8,12},{9,13},{10,... | collective-permute-start | bytes 405512 | tf_op jit(solution)/shard_map/ppermute | solution.py:223
  28.4 10.4 %collective-permute-start.7 = (f32[8,4224]{1,0:T(8,128)}, f32[8,4224]{1,0:T(8,128)S(1)}, u32[]{:S(2)}, u32[]{:S(2)}) collective-permute-start(f32[8,4224]{1,0:T(8,128)} %get-tuple-element.18), channel_id=1, source_target_pairs={{0,5},{1,6},{2,7},{3,0},{4,1},{5,2},{6,3},{7,4},{8,13},{9,14},{10,... | collective-permute-start | bytes 405512 | tf_op jit(solution)/shard_map/ppermute | solution.py:223
  30.5 8.3 %collective-permute-start.8 = (f32[8,4224]{1,0:T(8,128)}, f32[8,4224]{1,0:T(8,128)S(1)}, u32[]{:S(2)}, u32[]{:S(2)}) collective-permute-start(f32[8,4224]{1,0:T(8,128)} %get-tuple-element.19), channel_id=1, source_target_pairs={{0,6},{1,7},{2,0},{3,1},{4,2},{5,3},{6,4},{7,5},{8,14},{9,15},{10,... | collective-permute-start | bytes 405512 | tf_op jit(solution)/shard_map/ppermute | solution.py:223
  31.9 6.9 %collective-permute-start.9 = (f32[8,4224]{1,0:T(8,128)}, f32[8,4224]{1,0:T(8,128)S(1)}, u32[]{:S(2)}, u32[]{:S(2)}) collective-permute-start(f32[8,4224]{1,0:T(8,128)} %get-tuple-element.20), channel_id=1, source_target_pairs={{0,7},{1,0},{2,1},{3,2},{4,3},{5,4},{6,5},{7,6},{8,15},{9,8},{10,9... | collective-permute-start | bytes 405512 | tf_op jit(solution)/shard_map/ppermute | solution.py:223
  40.0 4.8 %collective-permute-start.12 = (f32[1,4096]{1,0:T(1,128)S(1)}, f32[1,4096]{1,0:T(1,128)S(1)}, u32[]{:S(2)}, u32[]{:S(2)}) collective-permute-start(f32[1,4096]{1,0:T(1,128)S(1)} %get-tuple-element.22), channel_id=1, source_target_pairs={{0,24},{8,0},{16,8},{24,16},{1,25},{9,1},{17,9},{25,17},{2,26},{10... | collective-permute-start | bytes 49160 | tf_op jit(solution)/shard_map/ppermute | solution.py:223
  42.1 4.6 %collective-permute-start.11 = (f32[1,4096]{1,0:T(1,128)S(1)}, f32[1,4096]{1,0:T(1,128)S(1)}, u32[]{:S(2)}, u32[]{:S(2)}) collective-permute-start(f32[1,4096]{1,0:T(1,128)S(1)} %get-tuple-element.23), channel_id=1, source_target_pairs={{0,16},{8,24},{16,0},{24,8},{1,17},{9,25},{17,1},{25,9},{2,18},{10... | collective-permute-start | bytes 49160 | tf_op jit(solution)/shard_map/ppermute | solution.py:223
  42.2 5.5 %collective-permute-start.10 = (f32[1,4096]{1,0:T(1,128)S(1)}, f32[1,4096]{1,0:T(1,128)S(1)}, u32[]{:S(2)}, u32[]{:S(2)}) collective-permute-start(f32[1,4096]{1,0:T(1,128)S(1)} %get-tuple-element.24), channel_id=1, source_target_pairs={{0,8},{8,16},{16,24},{24,0},{1,9},{9,17},{17,25},{25,1},{2,10},{10... | collective-permute-start | bytes 49160 | tf_op jit(solution)/shard_map/ppermute | solution.py:223
